TPU v7x, 32 devices: a whole 2x2x4 slice. The times are simulated.
32 devices in a mesh: ctx: 8 (over z, core), tp: 4 (over y, x).
Axes of the slice: x: 2, y: 2, z: 4, core: 2. Of those that a mesh axis runs over, the one named last changes fastest.
Arguments:
- q_proj: bfloat16 [1024, 4096], P('ctx', 'tp'), may hold values from -6 to 6
- k_proj: bfloat16 [1024, 4096], P('ctx', 'tp'), may hold values from -6 to 6
- v_proj: bfloat16 [1024, 4096], P('ctx', 'tp'), may hold values from -6 to 6
- saved_conv: bfloat16 [1024, 4096], P('ctx', 'tp'), may hold values from -6 to 6
- out_grad: bfloat16 [1024, 4096], P('ctx', 'tp'), may hold values from -6 to 6
- out_weight: bfloat16 [4096, 4096], P('tp'), may hold values from -0.09375 to 0.09375
- filter_taps: bfloat16 [1024, 4096], P('ctx', 'tp'), may hold values from -1.1 to 1.1
Outputs:
- dq_grad: bfloat16 [1024, 4096], P('ctx', 'tp')
- dk_grad: bfloat16 [1024, 4096], P('ctx', 'tp')
- dv_grad: bfloat16 [1024, 4096], P('ctx', 'tp')
- filter_grad: float32 [1024, 4096], P('ctx', 'tp')
All inputs are finite; a program needn't handle non-finite values.
Results may differ from a plain program's by a relative error of at most 0.003.
Values may be sent and summed in bfloat16 or wider, within the bound.
No kernel may reach another device: no remote copies, remote signals or barrier semaphores. Data moves between devices by JAX's collectives and lax.ppermute only.
A program may use at most 128 MiB of HBM per device.

v0:
```python
import math

import jax
import jax.numpy as jnp
from jax import lax
from jax.sharding import PartitionSpec as P


def from_behind(value, axis, steps):
    count = lax.axis_size(axis)
    pairs = [(source, (source + steps) % count) for source in range(count)]
    return lax.ppermute(value, axis, pairs)


def passed_along(block, axis, distance):
    devices = range(lax.axis_size(axis))
    route = [(i - distance, i) for i in devices if i - distance in devices]
    return lax.ppermute(block, axis, route)


def matmul(left, right):
    return jnp.dot(left, right, precision=lax.Precision.HIGHEST, preferred_element_type=jnp.float32)


def split_table(table):
    upper = lax.optimization_barrier(table.astype(jnp.bfloat16))
    lower = (table - upper.astype(jnp.float32)).astype(jnp.bfloat16)
    return (upper, lower)


def half_matmul(table, signal):
    upper, lower = split_table(table)
    return jnp.dot(upper, signal, preferred_element_type=jnp.float32) + jnp.dot(
        lower, signal, preferred_element_type=jnp.float32
    )


def make_tables(rows):
    index = jnp.arange(rows, dtype=jnp.int32)
    long_index = jnp.arange(2 * rows, dtype=jnp.int32)
    angle = (index[:, None] * index[None, :] % (2 * rows)).astype(jnp.float32) * (math.pi / rows)
    angle_back = (long_index[:, None] * index[None, :] % (2 * rows)).astype(jnp.float32) * (
        math.pi / rows
    )
    weight = jnp.where(index == 0, 1.0, 2.0).astype(jnp.float32) / (2.0 * rows)
    alternate = (1 - 2 * (index % 2)).astype(jnp.float32)
    alternate_back = (1 - 2 * (long_index % 2)).astype(jnp.float32) / (2.0 * rows)
    return (
        jnp.cos(angle),
        -jnp.sin(angle),
        alternate,
        jnp.cos(angle_back) * weight[None, :],
        -jnp.sin(angle_back) * weight[None, :],
        alternate_back,
    )


def forward(signal, tables):
    fwd_cos, fwd_sin, alternate = (tables[0], tables[1], tables[2])
    return (matmul(fwd_cos, signal), matmul(fwd_sin, signal), matmul(alternate[None, :], signal))


def forward_half(signal, tables):
    fwd_cos, fwd_sin, alternate = (tables[0], tables[1], tables[2])
    signs = alternate[None, :].astype(jnp.bfloat16)
    return (
        half_matmul(fwd_cos, signal),
        half_matmul(fwd_sin, signal),
        jnp.dot(signs, signal, preferred_element_type=jnp.float32),
    )


def inverse(spectrum, tables, count):
    inv_cos, inv_sin, alternate_back = (tables[3], tables[4], tables[5])
    return (
        matmul(inv_cos[:count], spectrum[0])
        + matmul(inv_sin[:count], spectrum[1])
        + alternate_back[:count, None] * spectrum[2]
    )


def correlate(first, second):
    real_part = first[0] * second[0] + first[1] * second[1]
    imag_part = first[0] * second[1] - first[1] * second[0]
    return (real_part, imag_part, first[2] * second[2])


def add_lags(filter_terms, lagged, step, active, rows):
    later = jnp.asarray(step >= 1, jnp.float32)
    filter_terms = filter_terms.at[step].add(lagged[:rows] * active)
    return filter_terms.at[jnp.maximum(step - 1, 0)].add(lagged[rows:] * (active * later))


def body(q_proj, k_proj, v_proj, saved_conv, out_grad, out_weight, filter_taps):
    rows = q_proj.shape[0]
    chans = q_proj.shape[1]
    blocks = lax.axis_size("ctx")
    me_index = lax.axis_index("ctx")
    tables = make_tables(rows)
    empty = jnp.zeros((rows, chans), jnp.float32)
    d_gated = lax.dot_general(
        lax.all_gather(out_grad, "tp", axis=1, tiled=True),
        out_weight,
        (((1,), (1,)), ((), ())),
        preferred_element_type=jnp.float32,
    )
    dq_grad = (d_gated * saved_conv.astype(jnp.float32)).astype(jnp.bfloat16)
    dz_local = d_gated * q_proj.astype(jnp.float32)
    gated = (k_proj.astype(jnp.float32) * v_proj.astype(jnp.float32)).astype(jnp.bfloat16)
    whole_filter = lax.all_gather(filter_taps, "ctx", axis=0, tiled=True)
    filter_blocks = whole_filter.reshape(blocks, rows, chans)
    cos_upper, cos_lower = split_table(tables[0])
    sin_upper, sin_lower = split_table(tables[1])
    spec_real = jnp.einsum(
        "fn,bnc->bfc", cos_upper, filter_blocks, preferred_element_type=jnp.float32
    ) + jnp.einsum("fn,bnc->bfc", cos_lower, filter_blocks, preferred_element_type=jnp.float32)
    spec_imag = jnp.einsum(
        "fn,bnc->bfc", sin_upper, filter_blocks, preferred_element_type=jnp.float32
    ) + jnp.einsum("fn,bnc->bfc", sin_lower, filter_blocks, preferred_element_type=jnp.float32)
    spec_top = jnp.einsum(
        "n,bnc->bc",
        tables[2].astype(jnp.bfloat16),
        filter_blocks,
        preferred_element_type=jnp.float32,
    )[:, None, :]
    parity = tables[2][:, None]

    def lag_spectrum(step):
        earlier = jnp.maximum(step - 1, 0)
        keep = jnp.asarray(step >= 1, jnp.float32)
        pieces = []
        for stack, factor in ((spec_real, parity), (spec_imag, parity), (spec_top, 1.0)):
            current = lax.dynamic_index_in_dim(stack, step, 0, keepdims=False)
            before = lax.dynamic_index_in_dim(stack, earlier, 0, keepdims=False)
            pieces.append(current + keep * factor * before)
        return (pieces[0], pieces[1], pieces[2])

    filter_terms = jnp.zeros((blocks, rows, chans), jnp.float32)
    dz_spec = forward(dz_local, tables)

    def carried_step(step, state):
        partial_value, moving, terms = state
        active = jnp.asarray(me_index >= step, jnp.float32)
        partial_value = partial_value + active * inverse(
            correlate(lag_spectrum(step), dz_spec), tables, rows
        )
        moving_spec = forward_half(moving, tables)
        lagged = inverse(correlate(moving_spec, dz_spec), tables, 2 * rows)
        terms = add_lags(terms, lagged, step, active, rows)
        partial_value = from_behind(partial_value, "ctx", 1)
        moving = passed_along(moving, "ctx", 1)
        return (partial_value, moving, terms)

    du_local, moving_last, filter_terms = lax.fori_loop(
        0, blocks, carried_step, (empty, gated, filter_terms)
    )
    summed = lax.psum_scatter(
        filter_terms.reshape(blocks * rows, chans), "ctx", scatter_dimension=0, tiled=True
    )
    filter_grad = summed * float(rows * blocks) ** (-0.5)
    dk_grad = (du_local * v_proj.astype(jnp.float32)).astype(jnp.bfloat16)
    dv_grad = (du_local * k_proj.astype(jnp.float32)).astype(jnp.bfloat16)
    return (dq_grad, dk_grad, dv_grad, filter_grad)


def solution(mesh):
    in_specs = (
        P("ctx", "tp"),
        P("ctx", "tp"),
        P("ctx", "tp"),
        P("ctx", "tp"),
        P("ctx", "tp"),
        P("tp", None),
        P("ctx", "tp"),
    )
    out_specs = (P("ctx", "tp"), P("ctx", "tp"), P("ctx", "tp"), P("ctx", "tp"))
    return jax.shard_map(body, mesh=mesh, in_specs=in_specs, out_specs=out_specs, check_vma=False)
```

profile of v0, /device:TPU:0, one launch (start us, length us, event | category | flops | bytes accessed | tf_op | source)
XLA Modules:
  0.0 341.1 jit_solution(16660941688179493797)
XLA Ops:
  11.7 1.8 fusion.82
  13.5 25.6 %all-gather.3.cloned.1.call-done = bf16[128,4096]{1,0:T(8,128)(2,1)} async-done(((bf16[128,1024]{1,0:T(8,128)(2,1)}), bf16[128,4096]{1,0:T(8,128)(2,1)}) %all-gather.3.cloned.1.call-update) | async-done | bytes 1048592 | tf_op jit(solution)/shard_map/all_gather | solution.py:102
  39.1 7.2 %multiply_convert_fusion = (bf16[128,1024]{1,0:T(8,128)(2,1)}, f32[128,1024]{1,0:T(8,128)S(1)}) fusion(bf16[128,1024]{1,0:T(8,128)(2,1)} %param.16, bf16[128,4096]{1,0:T(8,128)(2,1)} %all-gather.3.cloned.1.call-done, bf16[1024,4096]{1,0:T(8,128)(2,1)} %param.18), kind=kOutput, calls=%fused_computation.101 | convolution fusion | flops 1074135040 | bytes 10485760 | tf_op jit(solution)/shard_map/dot_general | solution.py:101
  48.5 21.4 %all-gather.5.cloned.1.call-done = bf16[1024,1024]{1,0:T(8,128)(2,1)} async-done(((bf16[128,1024]{1,0:T(8,128)(2,1)}), bf16[1024,1024]{1,0:T(8,128)(2,1)}) %all-gather.5.cloned.1.call-update) | async-done | bytes 2097168 | tf_op jit(solution)/shard_map/all_gather | solution.py:110
  69.9 2.1 fusion.123
  72.6 2.3 fusion.104
  74.9 3.7 %add_bitcast_fusion = f32[8,128,1024]{2,1,0:T(8,128)} fusion(f32[128,8,1024]{2,0,1:T(8,128)S(1)} %fusion.104, bf16[8,128,1024]{2,1,0:T(8,128)(2,1)S(1)} %bitcast.168, bf16[128,128]{1,0:T(8,128)(2,1)} %fusion.99), kind=kOutput, calls=%fused_computation.92 | convolution fusion | flops 269778944 | bytes 10518528 | tf_op jit(solution)/shard_map/fn,bnc->bfc/dot_general | solution.py:119
  78.6 1.5 fusion.106
  80.1 3.6 %add_bitcast_fusion.1 = f32[8,128,1024]{2,1,0:T(8,128)} fusion(f32[128,8,1024]{2,0,1:T(8,128)S(1)} %fusion.106, bf16[8,128,1024]{2,1,0:T(8,128)(2,1)S(1)} %bitcast.170, bf16[128,128]{1,0:T(8,128)(2,1)} %fusion.113), kind=kOutput, calls=%fused_computation.93 | convolution fusion | flops 269762560 | bytes 10518528 | tf_op jit(solution)/shard_map/fn,bnc->bfc/dot_general | solution.py:116
  83.8 2.3 broadcast_in_dim.41
  86.1 189.9 %while.23 = (s32[]{:T(128)}, f32[128,1024]{0,1:T(8,128)S(1)}, bf16[128,1024]{1,0:T(8,128)(2,1)}, f32[8,128,1024]{1,2,0:T(8,128)}, s32[]{:T(128)}, /*index=5*/f32...) while((s32[]{:T(128)}, f32[128,1024]{0,1:T(8,128)S(1)}, ...), condition=%wide.region_3.4_spmd.clone.clone, body=%wide.region_0.3_spmd.clone.clone.sunk | while | flops 1348131328 | bytes 27578764 | solution.py:154
  87.0 2.8 collective-permute-start.1
  90.8 2.6 fusion.218
  93.4 2.7 fusion.221
  101.2 1.9 fusion.224
  105.0 2.6 fusion.226
  107.6 2.6 fusion.227
  111.1 2.8 collective-permute-start.1
  114.9 2.6 fusion.218
  117.5 2.7 fusion.221
  121.3 1.2 convolution_add_fusion.6
  124.7 1.9 fusion.224
  128.5 2.6 fusion.226
  131.1 2.6 fusion.227
  134.6 2.8 collective-permute-start.1
  138.3 2.6 fusion.218
  141.0 2.7 fusion.221
  148.1 1.9 fusion.224
  151.9 2.6 fusion.226
  154.5 2.6 fusion.227
  158.0 2.6 collective-permute-start.1
  161.5 2.6 fusion.218
  164.2 2.7 fusion.221
  171.3 1.9 fusion.224
  175.1 2.6 fusion.226
  177.7 2.5 fusion.227
  181.2 4.7 %collective-permute-start.1 = (bf16[128,1024]{1,0:T(8,128)(2,1)S(1)}, bf16[128,1024]{1,0:T(8,128)(2,1)}, u32[]{:S(2)}, u32[]{:S(2)}) collective-permute-start(bf16[128,1024]{1,0:T(8,128)(2,1)S(1)} %copy.25), channel_id=1, source_target_pairs={{0,4},{4,8},{8,12},{12,16},{16,20},{20,24},{24,28},{1,5},{5,9},{9,... | collective-permute-start | bytes 786440 | tf_op jit(solution)/shard_map/while/body/eval_jaxpr/ppermute | solution.py:18
  186.7 2.6 fusion.218
  189.4 2.7 fusion.221
  196.5 1.9 fusion.224
  200.3 2.6 fusion.226
  202.9 2.5 fusion.227
  206.4 3.5 %collective-permute-start.1 = (bf16[128,1024]{1,0:T(8,128)(2,1)S(1)}, bf16[128,1024]{1,0:T(8,128)(2,1)}, u32[]{:S(2)}, u32[]{:S(2)}) collective-permute-start(bf16[128,1024]{1,0:T(8,128)(2,1)S(1)} %copy.25), channel_id=1, source_target_pairs={{0,4},{4,8},{8,12},{12,16},{16,20},{20,24},{24,28},{1,5},{5,9},{9,... | collective-permute-start | bytes 786440 | tf_op jit(solution)/shard_map/while/body/eval_jaxpr/ppermute | solution.py:18
  210.8 2.6 fusion.218
  213.4 2.7 fusion.221
  220.5 1.9 fusion.224
  224.3 2.6 fusion.226
  226.9 2.5 fusion.227
  230.4 2.9 collective-permute-start.1
  234.2 2.6 fusion.218
  236.8 2.7 fusion.221
  240.6 1.2 convolution_add_fusion.6
  244.0 1.9 fusion.224
  247.8 2.6 fusion.226
  250.4 2.5 fusion.227
  253.8 2.6 collective-permute-start.1
  257.3 2.6 fusion.218
  260.0 2.7 fusion.221
  267.1 1.9 fusion.224
  270.9 2.6 fusion.226
  273.5 2.5 fusion.227
  276.0 5.4 %copy.13 = f32[8,128,1024]{2,1,0:T(8,128)} copy(f32[8,128,1024]{1,2,0:T(8,128)} %get-tuple-element.493) | data formatting | bytes 8388608 | tf_op jit(solution)/shard_map/while | solution.py:154
  283.3 49.3 %reduce-scatter.2.cloned.1.call-done = f32[128,1024]{1,0:T(8,128)} async-done(((f32[1024,1024]{1,0:T(8,128)}), f32[128,1024]{1,0:T(8,128)}) %reduce-scatter.2.cloned.1.call-update) | async-done | bytes 524304 | tf_op jit(solution)/shard_map/reduce_scatter | solution.py:157
  332.6 1.9 broadcast_multiply_fusion
  (147 shorter events, 72.2 us)
Async XLA Ops:
  7.2 31.9 %all-gather.3.cloned.1.call-start = ((), (), s32[]{:S(2)}) async-start(), calls=%async_computation.1 | async-start | bytes 1310720 | tf_op jit(solution)/shard_map/all_gather | solution.py:102
  7.9 62.0 %all-gather.5.cloned.1.call-start = ((), (), s32[]{:S(2)}) async-start(), calls=%async_computation.2 | async-start | bytes 2359296 | tf_op jit(solution)/shard_map/all_gather | solution.py:110
  8.6 324.0 %reduce-scatter.2.cloned.1.call-start = ((), (), s32[]{:S(2)}) async-start(), calls=%async_computation.3 | async-start | bytes 4718592 | tf_op jit(solution)/shard_map/reduce_scatter | solution.py:157
  13.5 32.8 %copy-start.1 = (bf16[128,1024]{1,0:T(8,128)(2,1)S(1)}, bf16[128,1024]{1,0:T(8,128)(2,1)}, u32[]{:S(2)}) copy-start(bf16[128,1024]{1,0:T(8,128)(2,1)} %param.13) | copy-start | bytes 786436
  69.9 5.1 %copy-start = (bf16[1024,1024]{1,0:T(8,128)(2,1)S(1)}, bf16[1024,1024]{1,0:T(8,128)(2,1)}, u32[]{:S(2)}) copy-start(bf16[1024,1024]{1,0:T(8,128)(2,1)} %all-gather.5.cloned.1.call-done) | copy-start | bytes 6291460
  83.7 2.4 copy-start.4
  87.0 23.2 %collective-permute-start.1 = (bf16[128,1024]{1,0:T(8,128)(2,1)S(1)}, bf16[128,1024]{1,0:T(8,128)(2,1)}, u32[]{:S(2)}, u32[]{:S(2)}) collective-permute-start(bf16[128,1024]{1,0:T(8,128)(2,1)S(1)} %copy.25), channel_id=1, source_target_pairs={{0,4},{4,8},{8,12},{12,16},{16,20},{20,24},{24,28},{1,5},{5,9},{9,... | collective-permute-start | bytes 786440 | tf_op jit(solution)/shard_map/while/body/eval_jaxpr/ppermute | solution.py:18
  96.1 14.1 %collective-permute-start = (f32[128,1024]{0,1:T(8,128)S(1)}, f32[128,1024]{0,1:T(8,128)S(1)}, u32[]{:S(2)}, u32[]{:S(2)}) collective-permute-start(f32[128,1024]{0,1:T(8,128)S(1)} %fusion.221), channel_id=1, source_target_pairs={{0,4},{4,8},{8,12},{12,16},{16,20},{20,24},{24,28},{28,0},{1,5},{5... | collective-permute-start | bytes 1572872 | tf_op jit(solution)/shard_map/while/body/eval_jaxpr/ppermute | solution.py:12
  111.1 22.5 %collective-permute-start.1 = (bf16[128,1024]{1,0:T(8,128)(2,1)S(1)}, bf16[128,1024]{1,0:T(8,128)(2,1)}, u32[]{:S(2)}, u32[]{:S(2)}) collective-permute-start(bf16[128,1024]{1,0:T(8,128)(2,1)S(1)} %copy.25), channel_id=1, source_target_pairs={{0,4},{4,8},{8,12},{12,16},{16,20},{20,24},{24,28},{1,5},{5,9},{9,... | collective-permute-start | bytes 786440 | tf_op jit(solution)/shard_map/while/body/eval_jaxpr/ppermute | solution.py:18
  120.2 13.5 %collective-permute-start = (f32[128,1024]{0,1:T(8,128)S(1)}, f32[128,1024]{0,1:T(8,128)S(1)}, u32[]{:S(2)}, u32[]{:S(2)}) collective-permute-start(f32[128,1024]{0,1:T(8,128)S(1)} %fusion.221), channel_id=1, source_target_pairs={{0,4},{4,8},{8,12},{12,16},{16,20},{20,24},{24,28},{28,0},{1,5},{5... | collective-permute-start | bytes 1572872 | tf_op jit(solution)/shard_map/while/body/eval_jaxpr/ppermute | solution.py:12
  134.6 22.4 %collective-permute-start.1 = (bf16[128,1024]{1,0:T(8,128)(2,1)S(1)}, bf16[128,1024]{1,0:T(8,128)(2,1)}, u32[]{:S(2)}, u32[]{:S(2)}) collective-permute-start(bf16[128,1024]{1,0:T(8,128)(2,1)S(1)} %copy.25), channel_id=1, source_target_pairs={{0,4},{4,8},{8,12},{12,16},{16,20},{20,24},{24,28},{1,5},{5,9},{9,... | collective-permute-start | bytes 786440 | tf_op jit(solution)/shard_map/while/body/eval_jaxpr/ppermute | solution.py:18
  143.7 13.4 %collective-permute-start = (f32[128,1024]{0,1:T(8,128)S(1)}, f32[128,1024]{0,1:T(8,128)S(1)}, u32[]{:S(2)}, u32[]{:S(2)}) collective-permute-start(f32[128,1024]{0,1:T(8,128)S(1)} %fusion.221), channel_id=1, source_target_pairs={{0,4},{4,8},{8,12},{12,16},{16,20},{20,24},{24,28},{28,0},{1,5},{5... | collective-permute-start | bytes 1572872 | tf_op jit(solution)/shard_map/while/body/eval_jaxpr/ppermute | solution.py:12
  158.0 22.2 %collective-permute-start.1 = (bf16[128,1024]{1,0:T(8,128)(2,1)S(1)}, bf16[128,1024]{1,0:T(8,128)(2,1)}, u32[]{:S(2)}, u32[]{:S(2)}) collective-permute-start(bf16[128,1024]{1,0:T(8,128)(2,1)S(1)} %copy.25), channel_id=1, source_target_pairs={{0,4},{4,8},{8,12},{12,16},{16,20},{20,24},{24,28},{1,5},{5,9},{9,... | collective-permute-start | bytes 786440 | tf_op jit(solution)/shard_map/while/body/eval_jaxpr/ppermute | solution.py:18
  166.8 13.4 %collective-permute-start = (f32[128,1024]{0,1:T(8,128)S(1)}, f32[128,1024]{0,1:T(8,128)S(1)}, u32[]{:S(2)}, u32[]{:S(2)}) collective-permute-start(f32[128,1024]{0,1:T(8,128)S(1)} %fusion.221), channel_id=1, source_target_pairs={{0,4},{4,8},{8,12},{12,16},{16,20},{20,24},{24,28},{28,0},{1,5},{5... | collective-permute-start | bytes 1572872 | tf_op jit(solution)/shard_map/while/body/eval_jaxpr/ppermute | solution.py:12
  181.2 24.3 %collective-permute-start.1 = (bf16[128,1024]{1,0:T(8,128)(2,1)S(1)}, bf16[128,1024]{1,0:T(8,128)(2,1)}, u32[]{:S(2)}, u32[]{:S(2)}) collective-permute-start(bf16[128,1024]{1,0:T(8,128)(2,1)S(1)} %copy.25), channel_id=1, source_target_pairs={{0,4},{4,8},{8,12},{12,16},{16,20},{20,24},{24,28},{1,5},{5,9},{9,... | collective-permute-start | bytes 786440 | tf_op jit(solution)/shard_map/while/body/eval_jaxpr/ppermute | solution.py:18
  192.1 13.4 %collective-permute-start = (f32[128,1024]{0,1:T(8,128)S(1)}, f32[128,1024]{0,1:T(8,128)S(1)}, u32[]{:S(2)}, u32[]{:S(2)}) collective-permute-start(f32[128,1024]{0,1:T(8,128)S(1)} %fusion.221), channel_id=1, source_target_pairs={{0,4},{4,8},{8,12},{12,16},{16,20},{20,24},{24,28},{28,0},{1,5},{5... | collective-permute-start | bytes 1572872 | tf_op jit(solution)/shard_map/while/body/eval_jaxpr/ppermute | solution.py:12
  206.4 23.0 %collective-permute-start.1 = (bf16[128,1024]{1,0:T(8,128)(2,1)S(1)}, bf16[128,1024]{1,0:T(8,128)(2,1)}, u32[]{:S(2)}, u32[]{:S(2)}) collective-permute-start(bf16[128,1024]{1,0:T(8,128)(2,1)S(1)} %copy.25), channel_id=1, source_target_pairs={{0,4},{4,8},{8,12},{12,16},{16,20},{20,24},{24,28},{1,5},{5,9},{9,... | collective-permute-start | bytes 786440 | tf_op jit(solution)/shard_map/while/body/eval_jaxpr/ppermute | solution.py:18
  216.1 13.4 %collective-permute-start = (f32[128,1024]{0,1:T(8,128)S(1)}, f32[128,1024]{0,1:T(8,128)S(1)}, u32[]{:S(2)}, u32[]{:S(2)}) collective-permute-start(f32[128,1024]{0,1:T(8,128)S(1)} %fusion.221), channel_id=1, source_target_pairs={{0,4},{4,8},{8,12},{12,16},{16,20},{20,24},{24,28},{28,0},{1,5},{5... | collective-permute-start | bytes 1572872 | tf_op jit(solution)/shard_map/while/body/eval_jaxpr/ppermute | solution.py:12
  230.4 22.5 %collective-permute-start.1 = (bf16[128,1024]{1,0:T(8,128)(2,1)S(1)}, bf16[128,1024]{1,0:T(8,128)(2,1)}, u32[]{:S(2)}, u32[]{:S(2)}) collective-permute-start(bf16[128,1024]{1,0:T(8,128)(2,1)S(1)} %copy.25), channel_id=1, source_target_pairs={{0,4},{4,8},{8,12},{12,16},{16,20},{20,24},{24,28},{1,5},{5,9},{9,... | collective-permute-start | bytes 786440 | tf_op jit(solution)/shard_map/while/body/eval_jaxpr/ppermute | solution.py:18
  239.5 13.4 %collective-permute-start = (f32[128,1024]{0,1:T(8,128)S(1)}, f32[128,1024]{0,1:T(8,128)S(1)}, u32[]{:S(2)}, u32[]{:S(2)}) collective-permute-start(f32[128,1024]{0,1:T(8,128)S(1)} %fusion.221), channel_id=1, source_target_pairs={{0,4},{4,8},{8,12},{12,16},{16,20},{20,24},{24,28},{28,0},{1,5},{5... | collective-permute-start | bytes 1572872 | tf_op jit(solution)/shard_map/while/body/eval_jaxpr/ppermute | solution.py:12
  253.8 22.2 %collective-permute-start.1 = (bf16[128,1024]{1,0:T(8,128)(2,1)S(1)}, bf16[128,1024]{1,0:T(8,128)(2,1)}, u32[]{:S(2)}, u32[]{:S(2)}) collective-permute-start(bf16[128,1024]{1,0:T(8,128)(2,1)S(1)} %copy.25), channel_id=1, source_target_pairs={{0,4},{4,8},{8,12},{12,16},{16,20},{20,24},{24,28},{1,5},{5,9},{9,... | collective-permute-start | bytes 786440 | tf_op jit(solution)/shard_map/while/body/eval_jaxpr/ppermute | solution.py:18
  262.6 13.4 %collective-permute-start = (f32[128,1024]{0,1:T(8,128)S(1)}, f32[128,1024]{0,1:T(8,128)S(1)}, u32[]{:S(2)}, u32[]{:S(2)}) collective-permute-start(f32[128,1024]{0,1:T(8,128)S(1)} %fusion.221), channel_id=1, source_target_pairs={{0,4},{4,8},{8,12},{12,16},{16,20},{20,24},{24,28},{28,0},{1,5},{5... | collective-permute-start | bytes 1572872 | tf_op jit(solution)/shard_map/while/body/eval_jaxpr/ppermute | solution.py:12
  281.4 0.9 copy-start.2
  281.4 1.0 copy-start.3
Sparse Core Ops, SparseCore 0:
  9.8 29.2 all-gather.2
  40.7 29.1 all-gather.4
  281.5 51.0 reduce-scatter.1
where the time goes:
time: 346 us; the launch traced here: 341 us
  matrix products  125 us (36%)
  waiting for transfers between devices  97.7 us (28%)
  other arithmetic  60.7 us (18%)
  starting transfers between devices  26.1 us (8%)
  local copies, waits for them, and re-layouts  17 us (5%)
  between operations  13.8 us (4%)
    dot_general x35, matrix products, matmul(): jnp.dot(left, right, precision=lax.Precision.HIGHEST, preferred_element_t...  68.8 us
    reduce_scatter x1, waiting for transfers between devices, body(): lax.psum_scatter(filter_terms.reshape(blocks * rows, chans), 'ctx', scatt...  49.3 us
    all_gather x1, waiting for transfers between devices, body(): lax.all_gather(out_grad, 'tp', axis=1, tiled=True)  25.6 us
    ppermute x8, starting transfers between devices, passed_along(): return lax.ppermute(block, axis, route)  24.8 us
    all_gather x1, waiting for transfers between devices, body(): whole_filter = lax.all_gather(filter_taps, 'ctx', axis=0, tiled=True)  21.4 us
    scatter-add x8, other arithmetic, add_lags(): filter_terms = filter_terms.at[step].add(lagged[:rows] * active)  20.8 us
    scatter-add x8, other arithmetic, add_lags(): filter_terms.at[jnp.maximum(step - 1, 0)]  20.3 us
    dot_general x16, matrix products, half_matmul(): jnp.dot(lower, signal, preferred_element_type=jnp.float32)  19.2 us
  transfers between devices with their start and end apart: 19, of which 3 were waited for; matrix products, arithmetic and copies ran while one was open for 50% of the time, Pallas kernels for 0%

commit v1 on v0

v1 whole, which is shorter than its diff:
```python
import math

import jax
import jax.numpy as jnp
from jax import lax
from jax.sharding import PartitionSpec as P


BLOCK = 128


def split_bf16(value):
    upper = lax.optimization_barrier(value.astype(jnp.bfloat16))
    lower = (value - upper.astype(jnp.float32)).astype(jnp.bfloat16)
    return upper, lower


def gather_matmul(out_grad, out_weight):
    count = lax.axis_size("tp")
    me = lax.axis_index("tp")
    width = out_grad.shape[1]
    total = None
    for shift in range(count):
        if shift == 0:
            piece = out_grad
        else:
            piece = lax.ppermute(out_grad, "tp", [(i, (i + shift) % count) for i in range(count)])
        source = (me - shift) % count
        weight = lax.dynamic_slice_in_dim(out_weight, source * width, width, axis=1)
        part = lax.dot_general(
            piece, weight, (((1,), (1,)), ((), ())), preferred_element_type=jnp.float32
        )
        total = part if total is None else total + part
    return total


def make_tables(size):
    index = jnp.arange(size, dtype=jnp.int32)
    long_index = jnp.arange(2 * size, dtype=jnp.int32)
    angle = (index[:, None] * index[None, :] % (2 * size)).astype(jnp.float32) * (math.pi / size)
    angle_back = (long_index[:, None] * index[None, :] % (2 * size)).astype(jnp.float32) * (
        math.pi / size
    )
    weight = jnp.where(index == 0, 1.0, 2.0).astype(jnp.float32) / (2.0 * size)
    alternate = (1 - 2 * (index % 2)).astype(jnp.float32)
    alternate_back = (1 - 2 * (long_index % 2)).astype(jnp.float32) / (2.0 * size)
    return {
        "cos": split_bf16(jnp.cos(angle)),
        "sin": split_bf16(-jnp.sin(angle)),
        "alt": alternate.astype(jnp.bfloat16),
        "icos": split_bf16(jnp.cos(angle_back) * weight[None, :]),
        "isin": split_bf16(-jnp.sin(angle_back) * weight[None, :]),
        "ialt": alternate_back,
    }


def apply(table, signal_hi, signal_lo=None):
    def one(left, right):
        return jnp.einsum("kn,bnc->bkc", left, right, preferred_element_type=jnp.float32)

    out = one(table[0], signal_hi) + one(table[1], signal_hi)
    if signal_lo is not None:
        out = out + one(table[0], signal_lo)
    return out


def forward(tables, signal_hi, signal_lo=None):
    real = apply(tables["cos"], signal_hi, signal_lo)
    imag = apply(tables["sin"], signal_hi, signal_lo)
    nyq = jnp.einsum("n,bnc->bc", tables["alt"], signal_hi, preferred_element_type=jnp.float32)
    if signal_lo is not None:
        nyq = nyq + jnp.einsum(
            "n,bnc->bc", tables["alt"], signal_lo, preferred_element_type=jnp.float32
        )
    return real, imag, nyq


def inverse(tables, spectrum, start, count):
    real_hi, real_lo = split_bf16(spectrum[0])
    imag_hi, imag_lo = split_bf16(spectrum[1])
    icos = tuple(t[start : start + count] for t in tables["icos"])
    isin = tuple(t[start : start + count] for t in tables["isin"])
    ialt = tables["ialt"][start : start + count]
    return (
        apply(icos, real_hi, real_lo)
        + apply(isin, imag_hi, imag_lo)
        + ialt[None, :, None] * spectrum[2][:, None, :]
    )


def conj_times(first, second):
    real = first[0][None] * second[0] + first[1][None] * second[1]
    imag = first[0][None] * second[1] - first[1][None] * second[0]
    return real, imag, first[2][None] * second[2]


def long_correlations(dz_hi, dz_lo, gated, taps, seq_scale):
    seq, chans = gated.shape
    size = min(BLOCK, seq)
    blocks = seq // size
    tables = make_tables(size)
    shape = (blocks, size, chans)
    dz_spec = forward(tables, dz_hi.reshape(shape), dz_lo.reshape(shape))
    gated_spec = forward(tables, gated.reshape(shape))
    taps_spec = forward(tables, taps.reshape(shape))
    parity = (1 - 2 * (jnp.arange(size, dtype=jnp.int32) % 2)).astype(jnp.float32)[None, :, None]
    parity_top = float(1 - 2 * (size % 2))

    def earlier(stack):
        return jnp.concatenate([jnp.zeros_like(stack[:1]), stack[:-1]], axis=0)

    lag_spec = (
        earlier(taps_spec[0]) + parity * taps_spec[0],
        earlier(taps_spec[1]) + parity * taps_spec[1],
        earlier(taps_spec[2]) + parity_top * taps_spec[2],
    )
    padded = tuple(jnp.concatenate([part, jnp.zeros_like(part)], axis=0) for part in dz_spec)
    du_spec = None
    lag_sums = None
    for offset in range(blocks):
        window = tuple(part[offset : offset + blocks] for part in padded)
        du_term = conj_times(tuple(part[offset] for part in lag_spec), window)
        lag_term = conj_times(tuple(part[offset] for part in gated_spec), window)
        if du_spec is None:
            du_spec, lag_sums = du_term, lag_term
        else:
            du_spec = tuple(a + b for a, b in zip(du_spec, du_term))
            lag_sums = tuple(a + b for a, b in zip(lag_sums, lag_term))
    du = inverse(tables, du_spec, size, size).reshape(seq, chans)
    lagged = inverse(tables, lag_sums, 0, 2 * size)
    later_half = jnp.concatenate([lagged[1:, size:], jnp.zeros_like(lagged[:1, size:])], axis=0)
    filter_grad = (lagged[:, :size] + later_half).reshape(seq, chans) * seq_scale
    return du, filter_grad


def body(q_proj, k_proj, v_proj, saved_conv, out_grad, out_weight, filter_taps):
    rows = q_proj.shape[0]
    blocks = lax.axis_size("ctx")
    seq = rows * blocks
    d_gated = gather_matmul(out_grad, out_weight)
    dq_grad = (d_gated * saved_conv.astype(jnp.float32)).astype(jnp.bfloat16)
    dz = d_gated * q_proj.astype(jnp.float32)
    gated = (k_proj.astype(jnp.float32) * v_proj.astype(jnp.float32)).astype(jnp.bfloat16)
    dz_hi, dz_lo = split_bf16(dz)
    outgoing = jnp.stack([dz_hi, dz_lo, gated, filter_taps])
    incoming = lax.all_to_all(outgoing, "ctx", 2, 1, tiled=True)
    du_t, filter_t = long_correlations(
        incoming[0], incoming[1], incoming[2], incoming[3], float(seq) ** -0.5
    )
    back = lax.all_to_all(jnp.stack([du_t, filter_t]), "ctx", 1, 2, tiled=True)
    du_local = back[0]
    filter_grad = back[1]
    dk_grad = (du_local * v_proj.astype(jnp.float32)).astype(jnp.bfloat16)
    dv_grad = (du_local * k_proj.astype(jnp.float32)).astype(jnp.bfloat16)
    return (dq_grad, dk_grad, dv_grad, filter_grad)


def solution(mesh):
    in_specs = (
        P("ctx", "tp"),
        P("ctx", "tp"),
        P("ctx", "tp"),
        P("ctx", "tp"),
        P("ctx", "tp"),
        P("tp", None),
        P("ctx", "tp"),
    )
    out_specs = (P("ctx", "tp"), P("ctx", "tp"), P("ctx", "tp"), P("ctx", "tp"))
    return jax.shard_map(body, mesh=mesh, in_specs=in_specs, out_specs=out_specs, check_vma=False)
```

time: 346 us -> 107 us (0.31); the launches traced: 341 us -> 106 us
  matrix products: 125 us -> 19.8 us
  other arithmetic: 60.7 us -> 5.57 us
  waiting for transfers between devices: 97.7 us -> 51.9 us
  starting transfers between devices: 26.1 us -> 13.5 us
  between operations: 13.8 us -> 1.21 us
    dot_general x81 -> x30, matrix products: 125 us -> 19 us  [the longest x26 9.81 us: one(): jnp.einsum('kn,bnc->bkc', left, right, preferred_element_type=jnp.float32)]
    all_to_all x0 -> x2, waiting for transfers between devices: none -> 49.8 us  [the longest x1 25.6 us: body(): back = lax.all_to_all(jnp.stack([du_t, filter_t]), 'ctx', 1, 2, tiled=True)]
    reduce_scatter x1 -> x0, waiting for transfers between devices: 49.3 us -> none  [body(): lax.psum_scatter(filter_terms.reshape(blocks * rows, chans), 'ctx', scatt...]
    all_gather x2 -> x0, waiting for transfers between devices: 47 us -> none  [the longest x1 25.6 us: body(): lax.all_gather(out_grad, 'tp', axis=1, tiled=True)]
    scatter-add x16 -> x0, other arithmetic: 41.1 us -> none  [the longest x8 20.8 us: add_lags(): filter_terms = filter_terms.at[step].add(lagged[:rows] * active)]
    ppermute x16 -> x3, starting transfers between devices: 25.9 us -> 5.07 us  [gather_matmul(): lax.ppermute(out_grad, 'tp', [(i, (i + shift) % count) for i in range(cou...]
    while x10 -> x0, local copies, waits for them, and re-layouts: 13.2 us -> none
    all_to_all x0 -> x2, starting transfers between devices: none -> 8.43 us  [the longest x1 4.87 us: body(): incoming = lax.all_to_all(outgoing, 'ctx', 2, 1, tiled=True)]
  transfers between devices with their start and end apart: 19 -> 5, of which waited for: 3 -> 3; matrix products, arithmetic and copies ran while one was open for 50% -> 15% of each run, Pallas kernels for 0% -> 0%
where the time goes in v1:
time: 107 us; the launch traced here: 106 us
  waiting for transfers between devices  51.9 us (49%)
  matrix products  19.8 us (19%)
  local copies, waits for them, and re-layouts  14 us (13%)
  starting transfers between devices  13.5 us (13%)
  other arithmetic  5.57 us (5%)
  between operations  1.21 us (1%)
    all_to_all x1, waiting for transfers between devices, body(): back = lax.all_to_all(jnp.stack([du_t, filter_t]), 'ctx', 1, 2, tiled=True)  25.6 us
    all_to_all x1, waiting for transfers between devices, body(): incoming = lax.all_to_all(outgoing, 'ctx', 2, 1, tiled=True)  24.2 us
    dot_general x26, matrix products, one(): jnp.einsum('kn,bnc->bkc', left, right, preferred_element_type=jnp.float32)  9.81 us
    dot_general x4, matrix products, gather_matmul(): lax.dot_general(piece, weight, (((1,), (1,)), ((), ())), preferred_elemen...  9.23 us
    unnamed x13, local copies, waits for them, and re-layouts  9.16 us
    ppermute x3, starting transfers between devices, gather_matmul(): lax.ppermute(out_grad, 'tp', [(i, (i + shift) % count) for i in range(cou...  5.07 us
    all_to_all x1, starting transfers between devices, body(): incoming = lax.all_to_all(outgoing, 'ctx', 2, 1, tiled=True)  4.87 us
    convert_element_type x7, other arithmetic, split_bf16(): upper = lax.optimization_barrier(value.astype(jnp.bfloat16))  3.58 us
  transfers between devices with their start and end apart: 5, of which 3 were waited for; matrix products, arithmetic and copies ran while one was open for 15% of the time, Pallas kernels for 0%

profile of v1, /device:TPU:0, one launch (start us, length us, event | category | flops | bytes accessed | tf_op | source)
XLA Modules:
  0.0 106.0 jit_solution(2542255583113662484)
XLA Ops:
  0.6 4.0 %collective-permute-start.2 = (bf16[128,1024]{1,0:T(8,128)(2,1)}, bf16[128,1024]{1,0:T(8,128)(2,1)S(1)}, u32[]{:S(2)}, u32[]{:S(2)}) collective-permute-start(bf16[128,1024]{1,0:T(8,128)(2,1)} %param.11), channel_id=1, source_target_pairs={{0,3},{1,0},{2,1},{3,2},{4,7},{5,4},{6,5},{7,6},{8,11},{9,8},{10,9... | collective-permute-start | bytes 786440 | tf_op jit(solution)/shard_map/ppermute | solution.py:27
  4.6 0.5 collective-permute-start.1
  5.1 0.6 collective-permute-start
  5.7 2.3 %fusion.6 = f32[1024,128]{1,0:T(8,128)S(1)} fusion(bf16[128,1024]{1,0:T(8,128)(2,1)} %param.11, bf16[1024,4096]{1,0:T(8,128)(2,1)} %param.12, s32[]{:T(128)S(6)} %select_n.104), kind=kOutput, calls=%fused_computation.20 | convolution fusion | flops 268435456 | bytes 2883588 | tf_op jit(solution)/shard_map/dot_general | solution.py:30
  8.0 1.1 %copy.62 = bf16[128,1024]{0,1:T(8,128)(2,1)S(1)} copy(bf16[128,1024]{1,0:T(8,128)(2,1)} %param.8) | data formatting | bytes 524288 | tf_op args[1]
  9.1 1.1 %copy.63 = bf16[128,1024]{0,1:T(8,128)(2,1)S(1)} copy(bf16[128,1024]{1,0:T(8,128)(2,1)} %param.9) | data formatting | bytes 524288 | tf_op args[2]
  10.4 1.1 %copy.61 = bf16[128,1024]{0,1:T(8,128)(2,1)S(1)} copy(bf16[128,1024]{1,0:T(8,128)(2,1)} %param.7) | data formatting | bytes 524288 | tf_op args[0]
  11.5 1.1 %copy.60 = bf16[128,1024]{0,1:T(8,128)(2,1)S(1)} copy(bf16[128,1024]{1,0:T(8,128)(2,1)} %param.10) | data formatting | bytes 524288 | tf_op args[3]
  12.7 1.1 %copy.64 = bf16[128,1024]{0,1:T(8,128)(2,1)S(1)} copy(bf16[128,1024]{1,0:T(8,128)(2,1)} %param.13) | data formatting | bytes 524288 | tf_op args[6]
  13.8 2.3 %fusion = f32[1024,128]{1,0:T(8,128)S(1)} fusion(bf16[128,1024]{1,0:T(8,128)(2,1)S(1)} %collective-permute-done.2, bf16[1024,4096]{1,0:T(8,128)(2,1)} %param.12, s32[]{:T(128)S(6)} %select_n.110), kind=kOutput, calls=%fused_computation.14 | convolution fusion | flops 268435456 | bytes 2883588 | tf_op jit(solution)/shard_map/dot_general | solution.py:30
  16.1 2.1 %collective-permute-done.1 = bf16[128,1024]{1,0:T(8,128)(2,1)S(1)} collective-permute-done((bf16[128,1024]{1,0:T(8,128)(2,1)}, bf16[128,1024]{1,0:T(8,128)(2,1)S(1)}, u32[]{:S(2)}, u32[]{:S(2)}) %collective-permute-start.1) | collective-permute-done | bytes 262176 | tf_op jit(solution)/shard_map/ppermute | solution.py:27
  18.2 2.3 %fusion.2 = f32[1024,128]{1,0:T(8,128)S(1)} fusion(bf16[128,1024]{1,0:T(8,128)(2,1)S(1)} %collective-permute-done.1, bf16[1024,4096]{1,0:T(8,128)(2,1)} %param.12, s32[]{:T(128)S(6)} %select_n.108), kind=kOutput, calls=%fused_computation.16 | convolution fusion | flops 268435456 | bytes 2883588 | tf_op jit(solution)/shard_map/dot_general | solution.py:30
  20.5 2.3 %fusion.36 = (bf16[128,1024]{0,1:T(8,128)(2,1)S(1)}, f32[128,1024]{0,1:T(8,128)S(1)}) fusion(bf16[128,1024]{0,1:T(8,128)(2,1)S(1)} %copy.61, f32[1024,128]{1,0:T(8,128)S(1)} %fusion, f32[1024,128]{1,0:T(8,128)S(1)} %fusion.2, f32[1024,128]{1,0:T(8,128)S(1)} %fusion.6, bf16[128,1024]{1,0:T(8,128)(2,1)S(1)} %collective-permute-done, ...), kind=kOutput, calls=%fused_computation.77 | convolution fusion | flops 269221888 | bytes 4980740 | tf_op jit(solution)/shard_map/dot_general | solution.py:30
  23.1 1.8 %copy.65 = bf16[4,128,1024]{1,0,2:T(4,128)(2,1)} copy(bf16[4,128,1024]{1,2,0:T(8,128)(2,1)S(1)} %pad_maximum_fusion) | data formatting | bytes 2097152 | tf_op jit(solution)/shard_map/stack | solution.py:145
  25.0 4.9 %all-to-all-start = ((bf16[4,128,1024]{1,0,2:T(4,128)(2,1)}), bf16[4,128,1024]{1,0,2:T(4,128)(2,1)S(1)}, u32[]{:S(2)}, u32[]{:S(2)}) async-start(bf16[4,128,1024]{1,0,2:T(4,128)(2,1)} %copy.65), calls=%async_computation | async-start | bytes 2097152 | tf_op jit(solution)/shard_map/all_to_all | solution.py:146
  29.8 0.3 fusion.93
  30.1 0.3 fusion.81
  30.4 0.6 fusion.66
  31.0 1.2 %subtract_convert_fusion.9 = (bf16[256,128]{1,0:T(8,128)(2,1)}, bf16[256,128]{1,0:T(8,128)(2,1)}) fusion(bf16[256,128]{1,0:T(8,128)(2,1)S(1)} %get-tuple-element.92, f32[128]{0:T(128)S(1)} %fusion.119, bf16[256,128]{1,0:T(8,128)(2,1)S(1)} %get-tuple-element.93), kind=kLoop, calls=%fused_computation.106 | loop fusion | flops 753664 | bytes 262656 | tf_op jit(solution)/shard_map/convert_element_type | solution.py:14
  32.2 24.2 %all-to-all-done = bf16[4,128,1024]{1,0,2:T(4,128)(2,1)S(1)} async-done(((bf16[4,128,1024]{1,0,2:T(4,128)(2,1)}), bf16[4,128,1024]{1,0,2:T(4,128)(2,1)S(1)}, u32[]{:S(2)}, u32[]{:S(2)}) %all-to-all-start) | async-done | bytes 1048608 | tf_op jit(solution)/shard_map/all_to_all | solution.py:146
  56.5 0.2 fusion.57
  56.8 0.2 fusion.51
  57.0 0.2 fusion.54
  57.2 0.2 fusion.48
  57.4 0.5 fusion.19
  58.0 0.5 fusion.17
  58.5 0.5 convolution_add_fusion.14
  58.9 0.2 fusion.18
  59.2 0.5 convolution_add_fusion.11
  59.6 0.2 fusion.16
  60.1 1.2 %fusion.176 = (bf16[8,128,128]{1,2,0:T(8,128)(2,1)S(1)}, f32[8,128,128]{1,2,0:T(8,128)}) fusion(f32[128,128]{0,1:T(8,128)S(1)} %get-tuple-element.45, f32[128,128]{0,1:T(8,128)S(1)} %get-tuple-element.118, f32[128,128]{0,1:T(8,128)S(1)} %get-tuple-element.46, f32[128,128]{0,1:T(8,128)S(1)} %get-tuple-element.117, f32[128,128]{0,1:T(8,128)S(1)} %get-tuple-element.47, ...), kind=kLoop, calls=%fused_computation.285 | loop fusion | flops 4194304 | bytes 2883584 | tf_op jit(solution)/shard_map/convert_element_type | solution.py:13
  61.3 0.4 fusion.177
  61.9 0.2 fusion.43
  62.1 0.2 fusion.40
  62.3 0.5 fusion.15
  62.8 0.5 fusion.14
  63.4 0.4 fusion.178
  63.8 0.4 fusion.179
  64.3 0.2 fusion.94
  64.5 0.2 fusion.95
  64.7 0.2 fusion.126
  64.9 0.2 fusion.120
  65.1 0.2 fusion.124
  65.3 0.2 fusion.122
  65.4 0.3 fusion.72
  65.8 0.2 convolution_add_fusion.7
  66.0 0.3 convolution_add_fusion.1
  66.3 0.3 fusion.76
  66.6 1.0 convolution_add_fusion.9
  67.6 0.3 convolution_add_fusion.3
  68.0 0.3 convolution_add_fusion.2
  68.3 0.3 fusion.10
  68.8 0.2 copy.73
  69.0 0.2 convolution_add_fusion.6
  69.2 1.5 %fusion.22 = f32[8,128,128]{2,1,0:T(8,128)S(1)} fusion(f32[8,128,128]{1,2,0:T(8,128)S(1)} %convolution_add_fusion.6, f32[8,128,128]{1,2,0:T(8,128)} %convolution_add_fusion.9, f32[8,128,128]{1,2,0:T(8,128)} %get-tuple-element.21, bf16[8,128,128]{1,2,0:T(8,128)(2,1)S(1)} %get-tuple-element.20, f32[8,128]{1,0:T(8,128)S(1)} %get-tuple-element.70, ...), kind=kOutput, calls=%fused_computation.50 | convolution fusion | flops 34471936 | bytes 2396672 | tf_op jit(solution)/shard_map/kn,bnc->bkc/dot_general | solution.py:59
  70.8 1.8 %copy.74 = f32[2,1024,128]{2,0,1:T(2,128)} copy(f32[2,1024,128]{2,1,0:T(8,128)S(1)} %pad_maximum_fusion.1) | data formatting | bytes 2097152 | tf_op jit(solution)/shard_map/stack | solution.py:150
  72.6 3.6 %all-to-all-start.1 = ((f32[2,1024,128]{2,0,1:T(2,128)}), f32[2,1024,128]{2,0,1:T(2,128)S(1)}, u32[]{:S(2)}, u32[]{:S(2)}) async-start(f32[2,1024,128]{2,0,1:T(2,128)} %copy.74), calls=%async_computation.1 | async-start | bytes 2097152 | tf_op jit(solution)/shard_map/all_to_all | solution.py:150
  76.1 0.9 copy.78
  77.0 25.6 %all-to-all-done.1 = f32[2,1024,128]{2,0,1:T(2,128)S(1)} async-done(((f32[2,1024,128]{2,0,1:T(2,128)}), f32[2,1024,128]{2,0,1:T(2,128)S(1)}, u32[]{:S(2)}, u32[]{:S(2)}) %all-to-all-start.1) | async-done | bytes 1048608 | tf_op jit(solution)/shard_map/all_to_all | solution.py:150
  102.8 0.2 copy.76
  103.1 0.9 copy.79
  103.9 0.8 copy.80
  104.8 0.2 copy.77
  105.0 1.0 copy.81
  (30 shorter events, 1.4 us)
Async XLA Ops:
  0.6 13.2 %collective-permute-start.2 = (bf16[128,1024]{1,0:T(8,128)(2,1)}, bf16[128,1024]{1,0:T(8,128)(2,1)S(1)}, u32[]{:S(2)}, u32[]{:S(2)}) collective-permute-start(bf16[128,1024]{1,0:T(8,128)(2,1)} %param.11), channel_id=1, source_target_pairs={{0,3},{1,0},{2,1},{3,2},{4,7},{5,4},{6,5},{7,6},{8,11},{9,8},{10,9... | collective-permute-start | bytes 786440 | tf_op jit(solution)/shard_map/ppermute | solution.py:27
  4.6 13.6 %collective-permute-start.1 = (bf16[128,1024]{1,0:T(8,128)(2,1)}, bf16[128,1024]{1,0:T(8,128)(2,1)S(1)}, u32[]{:S(2)}, u32[]{:S(2)}) collective-permute-start(bf16[128,1024]{1,0:T(8,128)(2,1)} %param.11), channel_id=1, source_target_pairs={{0,2},{1,3},{2,0},{3,1},{4,6},{5,7},{6,4},{7,5},{8,10},{9,11},{10,... | collective-permute-start | bytes 786440 | tf_op jit(solution)/shard_map/ppermute | solution.py:27
  5.1 15.4 %collective-permute-start = (bf16[128,1024]{1,0:T(8,128)(2,1)}, bf16[128,1024]{1,0:T(8,128)(2,1)S(1)}, u32[]{:S(2)}, u32[]{:S(2)}) collective-permute-start(bf16[128,1024]{1,0:T(8,128)(2,1)} %param.11), channel_id=1, source_target_pairs={{0,1},{1,2},{2,3},{3,0},{4,5},{5,6},{6,7},{7,4},{8,9},{9,10},{10,1... | collective-permute-start | bytes 786440 | tf_op jit(solution)/shard_map/ppermute | solution.py:27
  25.0 31.4 %all-to-all-start = ((bf16[4,128,1024]{1,0,2:T(4,128)(2,1)}), bf16[4,128,1024]{1,0,2:T(4,128)(2,1)S(1)}, u32[]{:S(2)}, u32[]{:S(2)}) async-start(bf16[4,128,1024]{1,0,2:T(4,128)(2,1)} %copy.65), calls=%async_computation | async-start | bytes 2097152 | tf_op jit(solution)/shard_map/all_to_all | solution.py:146
  61.9 3.9 %copy-start.1 = (bf16[256,128]{1,0:T(8,128)(2,1)S(1)}, bf16[256,128]{1,0:T(8,128)(2,1)}, u32[]{:S(2)}) copy-start(bf16[256,128]{1,0:T(8,128)(2,1)} %get-tuple-element.90) | copy-start | bytes 196612
  63.3 3.3 %copy-start = (bf16[256,128]{1,0:T(8,128)(2,1)S(1)}, bf16[256,128]{1,0:T(8,128)(2,1)}, u32[]{:S(2)}) copy-start(bf16[256,128]{1,0:T(8,128)(2,1)} %get-tuple-element.91) | copy-start | bytes 196612
  72.6 30.1 %all-to-all-start.1 = ((f32[2,1024,128]{2,0,1:T(2,128)}), f32[2,1024,128]{2,0,1:T(2,128)S(1)}, u32[]{:S(2)}, u32[]{:S(2)}) async-start(f32[2,1024,128]{2,0,1:T(2,128)} %copy.74), calls=%async_computation.1 | async-start | bytes 2097152 | tf_op jit(solution)/shard_map/all_to_all | solution.py:150

commit v2 on v1

--- a/solution.py
+++ b/solution.py
@@ -133,23 +133,43 @@
     return du, filter_grad
 
 
+def to_groups(value, groups):
+    rows, chans = value.shape
+    return value.reshape(rows, groups, chans // groups).transpose(1, 0, 2)
+
+
+def from_groups(value):
+    groups, rows, chans = value.shape
+    return value.transpose(1, 0, 2).reshape(rows, groups * chans)
+
+
+def transpose_ctx(stacked):
+    return lax.all_to_all(stacked, "ctx", 0, 0, tiled=True)
+
+
 def body(q_proj, k_proj, v_proj, saved_conv, out_grad, out_weight, filter_taps):
-    rows = q_proj.shape[0]
+    rows, chans = q_proj.shape
     blocks = lax.axis_size("ctx")
     seq = rows * blocks
+    gated = (k_proj.astype(jnp.float32) * v_proj.astype(jnp.float32)).astype(jnp.bfloat16)
+    inputs_t = transpose_ctx(
+        jnp.stack([to_groups(gated, blocks), to_groups(filter_taps, blocks)], axis=1)
+    )
     d_gated = gather_matmul(out_grad, out_weight)
     dq_grad = (d_gated * saved_conv.astype(jnp.float32)).astype(jnp.bfloat16)
     dz = d_gated * q_proj.astype(jnp.float32)
-    gated = (k_proj.astype(jnp.float32) * v_proj.astype(jnp.float32)).astype(jnp.bfloat16)
     dz_hi, dz_lo = split_bf16(dz)
-    outgoing = jnp.stack([dz_hi, dz_lo, gated, filter_taps])
-    incoming = lax.all_to_all(outgoing, "ctx", 2, 1, tiled=True)
+    dz_t = transpose_ctx(jnp.stack([to_groups(dz_hi, blocks), to_groups(dz_lo, blocks)], axis=1))
+    sub = chans // blocks
     du_t, filter_t = long_correlations(
-        incoming[0], incoming[1], incoming[2], incoming[3], float(seq) ** -0.5
+        dz_t[:, 0].reshape(seq, sub),
+        dz_t[:, 1].reshape(seq, sub),
+        inputs_t[:, 0].reshape(seq, sub),
+        inputs_t[:, 1].reshape(seq, sub),
+        float(seq) ** -0.5,
     )
-    back = lax.all_to_all(jnp.stack([du_t, filter_t]), "ctx", 1, 2, tiled=True)
-    du_local = back[0]
-    filter_grad = back[1]
+    du_local = from_groups(transpose_ctx(du_t.reshape(blocks, rows, sub)))
+    filter_grad = from_groups(transpose_ctx(filter_t.reshape(blocks, rows, sub)))
     dk_grad = (du_local * v_proj.astype(jnp.float32)).astype(jnp.bfloat16)
     dv_grad = (du_local * k_proj.astype(jnp.float32)).astype(jnp.bfloat16)
     return (dq_grad, dk_grad, dv_grad, filter_grad)

time: 107 us -> 97.7 us (0.913)
  waiting for transfers between devices: 51.9 us -> 36.1 us
  starting transfers between devices: 13.5 us -> 22 us
  local copies, waits for them, and re-layouts: 14 us -> 7.88 us
  other arithmetic: 5.57 us -> 11 us
  matrix products: 19.8 us -> 18.5 us
    all_to_all x2 -> x4, waiting for transfers between devices: 49.8 us -> 36.1 us  [transpose_ctx(): return lax.all_to_all(stacked, 'ctx', 0, 0, tiled=True)]
    all_to_all x2 -> x4, starting transfers between devices: 8.43 us -> 17 us  [transpose_ctx(): return lax.all_to_all(stacked, 'ctx', 0, 0, tiled=True)]
    unnamed x13 -> x55, local copies, waits for them, and re-layouts: 9.16 us -> 5.32 us
    another operation x2 -> x0, local copies, waits for them, and re-layouts: 3.6 us -> none  [the longest x1 1.8 us: body(): outgoing = jnp.stack([dz_hi, dz_lo, gated, filter_taps])]
    ppermute x3, waiting for transfers between devices: 2.09 us -> 0.01 us  [gather_matmul(): lax.ppermute(out_grad, 'tp', [(i, (i + shift) % count) for i in range(cou...]
    another operation x4 -> x2, other arithmetic: 0.42 us -> 1.7 us  [the longest x1 0.85 us: body(): jnp.stack([to_groups(dz_hi, blocks), to_groups(dz_lo, blocks)], axis=1)]
    convert_element_type x1 -> x3, other arithmetic: 1.23 us -> 2.49 us  [split_bf16(): lower = (value - upper.astype(jnp.float32)).astype(jnp.bfloat16)]
    dot_general x26, matrix products: 9.81 us -> 8.58 us  [one(): jnp.einsum('kn,bnc->bkc', left, right, preferred_element_type=jnp.float32)]
  transfers between devices with their start and end apart: 5 -> 7, of which waited for: 3 -> 3; matrix products, arithmetic and copies ran while one was open for 15% -> 30% of each run, Pallas kernels for 0% -> 0%
where the time goes in v2:
time: 97.7 us; the launch traced here: 97 us
  waiting for transfers between devices  36.1 us (37%)
  starting transfers between devices  22 us (23%)
  matrix products  18.5 us (19%)
  other arithmetic  11 us (11%)
  local copies, waits for them, and re-layouts  7.88 us (8%)
  between operations  1.45 us (1%)
    all_to_all x4, waiting for transfers between devices, transpose_ctx(): return lax.all_to_all(stacked, 'ctx', 0, 0, tiled=True)  36.1 us
    all_to_all x4, starting transfers between devices, transpose_ctx(): return lax.all_to_all(stacked, 'ctx', 0, 0, tiled=True)  17 us
    dot_general x4, matrix products, gather_matmul(): lax.dot_general(piece, weight, (((1,), (1,)), ((), ())), preferred_elemen...  9.24 us
    dot_general x26, matrix products, one(): jnp.einsum('kn,bnc->bkc', left, right, preferred_element_type=jnp.float32)  8.58 us
    unnamed x55, local copies, waits for them, and re-layouts  5.32 us
    ppermute x3, starting transfers between devices, gather_matmul(): lax.ppermute(out_grad, 'tp', [(i, (i + shift) % count) for i in range(cou...  5.07 us
    convert_element_type x7, other arithmetic, split_bf16(): upper = lax.optimization_barrier(value.astype(jnp.bfloat16))  3.65 us
    convert_element_type x3, other arithmetic, split_bf16(): lower = (value - upper.astype(jnp.float32)).astype(jnp.bfloat16)  2.49 us
  transfers between devices with their start and end apart: 7, of which 3 were waited for; matrix products, arithmetic and copies ran while one was open for 30% of the time, Pallas kernels for 0%

profile of v2, /device:TPU:0, one launch (start us, length us, event | category | flops | bytes accessed | tf_op | source)
XLA Modules:
  0.0 97.0 jit_solution(4654849896061001604)
XLA Ops:
  0.6 4.0 %collective-permute-start.2 = (bf16[128,1024]{1,0:T(8,128)(2,1)}, bf16[128,1024]{1,0:T(8,128)(2,1)S(1)}, u32[]{:S(2)}, u32[]{:S(2)}) collective-permute-start(bf16[128,1024]{1,0:T(8,128)(2,1)} %param.11), channel_id=1, source_target_pairs={{0,3},{1,0},{2,1},{3,2},{4,7},{5,4},{6,5},{7,6},{8,11},{9,8},{10,9... | collective-permute-start | bytes 786440 | tf_op jit(solution)/shard_map/ppermute | solution.py:27
  4.6 0.5 collective-permute-start.1
  5.1 0.6 collective-permute-start
  5.7 1.1 %copy.21 = bf16[128,1024]{0,1:T(8,128)(2,1)S(1)} copy(bf16[128,1024]{1,0:T(8,128)(2,1)} %param.13) | data formatting | bytes 524288 | tf_op args[6]
  6.8 1.1 %fusion.33 = bf16[128,1024]{1,0:T(8,128)(2,1)S(1)} fusion(bf16[128,1024]{1,0:T(8,128)(2,1)} %param.9, bf16[128,1024]{1,0:T(8,128)(2,1)} %param.8), kind=kLoop, calls=%fused_computation.58 | loop fusion | flops 524288 | bytes 786432 | tf_op jit(solution)/shard_map/convert_element_type | solution.py:154
  8.1 0.8 pad_maximum_fusion
  9.0 4.9 %all-to-all-start = ((bf16[8,2,128,128]{2,3,1,0:T(8,128)(2,1)}), bf16[8,2,128,128]{2,3,1,0:T(8,128)(2,1)S(1)}, u32[]{:S(2)}, u32[]{:S(2)}) async-start(bf16[8,2,128,128]{2,3,1,0:T(8,128)(2,1)} %pad_maximum_fusion), calls=%async_computation | async-start | bytes 1048576 | tf_op jit(solution)/shard_map/all_to_all | solution.py:147
  13.8 0.3 fusion.91
  14.1 0.5 fusion.63
  14.6 1.2 %subtract_convert_fusion.10 = (bf16[256,128]{1,0:T(8,128)(2,1)}, bf16[256,128]{1,0:T(8,128)(2,1)S(1)}) fusion(bf16[256,128]{1,0:T(8,128)(2,1)S(1)} %fusion.63, f32[128]{0:T(128)S(1)} %fusion.117), kind=kLoop, calls=%fused_computation.106 | loop fusion | flops 688128 | bytes 197120 | tf_op jit(solution)/shard_map/convert_element_type | solution.py:14
  15.8 1.2 %subtract_convert_fusion.9 = bf16[256,128]{1,0:T(8,128)(2,1)} fusion(bf16[256,128]{1,0:T(8,128)(2,1)S(1)} %get-tuple-element.79, f32[128]{0:T(128)S(1)} %fusion.117), kind=kLoop, calls=%fused_computation.104 | loop fusion | flops 622592 | bytes 131584 | tf_op jit(solution)/shard_map/convert_element_type | solution.py:14
  17.0 2.3 %fusion.6 = f32[1024,128]{1,0:T(8,128)S(1)} fusion(bf16[128,1024]{1,0:T(8,128)(2,1)} %param.11, bf16[1024,4096]{1,0:T(8,128)(2,1)} %param.12, s32[]{:T(128)S(6)} %select_n.104), kind=kOutput, calls=%fused_computation.20 | convolution fusion | flops 268435456 | bytes 2883588 | tf_op jit(solution)/shard_map/dot_general | solution.py:30
  19.3 0.3 fusion.79
  19.6 1.1 %copy.23 = bf16[128,1024]{0,1:T(8,128)(2,1)S(1)} copy(bf16[128,1024]{1,0:T(8,128)(2,1)} %param.7) | data formatting | bytes 524288 | tf_op args[0]
  20.8 1.1 %copy.19 = bf16[128,1024]{0,1:T(8,128)(2,1)S(1)} copy(bf16[128,1024]{1,0:T(8,128)(2,1)} %param.10) | data formatting | bytes 524288 | tf_op args[3]
  21.9 0.6 slice.288
  22.5 2.3 %fusion = f32[1024,128]{1,0:T(8,128)S(1)} fusion(bf16[128,1024]{1,0:T(8,128)(2,1)S(1)} %collective-permute-done.2, bf16[1024,4096]{1,0:T(8,128)(2,1)} %param.12, s32[]{:T(128)S(6)} %select_n.110), kind=kOutput, calls=%fused_computation.14 | convolution fusion | flops 268435456 | bytes 2883588 | tf_op jit(solution)/shard_map/dot_general | solution.py:30
  24.8 2.3 %fusion.2 = f32[1024,128]{1,0:T(8,128)S(1)} fusion(bf16[128,1024]{1,0:T(8,128)(2,1)S(1)} %collective-permute-done.1, bf16[1024,4096]{1,0:T(8,128)(2,1)} %param.12, s32[]{:T(128)S(6)} %select_n.108), kind=kOutput, calls=%fused_computation.16 | convolution fusion | flops 268435456 | bytes 2883588 | tf_op jit(solution)/shard_map/dot_general | solution.py:30
  27.1 2.3 %fusion.36 = (bf16[128,1024]{0,1:T(8,128)(2,1)S(1)}, f32[128,1024]{0,1:T(8,128)S(1)}) fusion(bf16[128,1024]{0,1:T(8,128)(2,1)S(1)} %copy.23, f32[1024,128]{1,0:T(8,128)S(1)} %fusion, f32[1024,128]{1,0:T(8,128)S(1)} %fusion.2, f32[1024,128]{1,0:T(8,128)S(1)} %fusion.6, bf16[128,1024]{1,0:T(8,128)(2,1)S(1)} %collective-permute-done, ...), kind=kOutput, calls=%fused_computation.77 | convolution fusion | flops 269221888 | bytes 4980740 | tf_op jit(solution)/shard_map/dot_general | solution.py:30
  29.6 0.9 pad_maximum_fusion.1
  30.5 5.1 %all-to-all-start.1 = ((bf16[8,2,128,128]{2,3,1,0:T(8,128)(2,1)}), bf16[8,2,128,128]{2,3,1,0:T(8,128)(2,1)S(1)}, u32[]{:S(2)}, u32[]{:S(2)}) async-start(bf16[8,2,128,128]{2,3,1,0:T(8,128)(2,1)} %pad_maximum_fusion.1), calls=%async_computation.1 | async-start | bytes 1048576 | tf_op jit(solution)/shard_map/all_to_all | solution.py:147
  35.6 0.2 fusion.55
  35.8 0.5 fusion.19
  36.3 0.2 fusion.52
  36.6 0.5 fusion.17
  37.3 0.2 fusion.124
  37.7 0.2 fusion.38
  38.0 0.2 fusion.41
  38.2 0.6 slice_bitcast_fusion.49
  38.8 0.5 fusion.14
  39.3 0.5 fusion.15
  39.8 0.7 slice_bitcast_fusion.14
  40.5 10.4 %all-to-all-done.1 = bf16[8,2,128,128]{2,3,1,0:T(8,128)(2,1)S(1)} async-done(((bf16[8,2,128,128]{2,3,1,0:T(8,128)(2,1)}), bf16[8,2,128,128]{2,3,1,0:T(8,128)(2,1)S(1)}, u32[]{:S(2)}, u32[]{:S(2)}) %all-to-all-start.1) | async-done | bytes 524320 | tf_op jit(solution)/shard_map/all_to_all | solution.py:147
  50.9 0.2 fusion.49
  51.1 0.2 fusion.46
  51.4 0.5 convolution_add_fusion.14
  51.8 0.2 fusion.18
  52.1 0.5 convolution_add_fusion.11
  52.5 0.2 fusion.16
  52.8 0.4 fusion.177
  53.4 0.4 fusion.176
  53.8 0.4 fusion.175
  54.3 1.3 %fusion.174 = (bf16[8,128,128]{1,2,0:T(8,128)(2,1)S(1)}, f32[8,128,128]{1,2,0:T(8,128)S(1)}) fusion(f32[128,128]{0,1:T(8,128)S(1)} %get-tuple-element.31, f32[128,128]{0,1:T(8,128)} %copy-done.4, f32[128,128]{0,1:T(8,128)S(1)} %get-tuple-element.32, f32[128,128]{0,1:T(8,128)} %copy-done.3, f32[128,128]{0,1:T(8,128)S(1)} %get-tuple-element.33, ...), kind=kLoop, calls=%fused_computation.283 | loop fusion | flops 4194304 | bytes 2883584 | tf_op jit(solution)/shard_map/convert_element_type | solution.py:13
  55.6 0.2 fusion.93
  55.8 0.2 fusion.92
  56.5 0.2 convolution_add_fusion.7
  56.7 0.2 convolution_add_fusion.6
  57.0 0.2 convolution_add_fusion.9
  57.4 1.1 %fusion.22 = f32[8,128,128]{1,2,0:T(8,128)} fusion(f32[8,128,128]{2,1,0:T(8,128)S(1)} %convolution_add_fusion.6, f32[8,128,128]{2,1,0:T(8,128)S(1)} %convolution_add_fusion.9, f32[8,128,128]{1,2,0:T(8,128)S(1)} %get-tuple-element.17, bf16[8,128,128]{1,2,0:T(8,128)(2,1)S(1)} %get-tuple-element.16, f32[8,128]{1,0:T(8,128)S(1)} %get-tuple-element.61, ...), kind=kOutput, calls=%fused_computation.50 | convolution fusion | flops 34471936 | bytes 2396672 | tf_op jit(solution)/shard_map/kn,bnc->bkc/dot_general | solution.py:59
  58.5 3.5 %all-to-all-start.2 = ((f32[8,128,128]{1,2,0:T(8,128)}), f32[8,128,128]{1,2,0:T(8,128)S(1)}, u32[]{:S(2)}, u32[]{:S(2)}) async-start(f32[8,128,128]{1,2,0:T(8,128)} %fusion.22), calls=%async_computation.2 | async-start | bytes 1048576 | tf_op jit(solution)/shard_map/all_to_all | solution.py:147
  62.0 0.3 fusion.74
  62.3 0.3 convolution_add_fusion.3
  62.6 0.3 fusion.70
  62.9 0.3 convolution_add_fusion.1
  63.2 0.3 convolution_add_fusion.2
  63.5 0.3 fusion.10
  63.9 0.9 fusion.35
  64.8 12.4 %all-to-all-done.2 = f32[8,128,128]{1,2,0:T(8,128)S(1)} async-done(((f32[8,128,128]{1,2,0:T(8,128)}), f32[8,128,128]{1,2,0:T(8,128)S(1)}, u32[]{:S(2)}, u32[]{:S(2)}) %all-to-all-start.2) | async-done | bytes 524320 | tf_op jit(solution)/shard_map/all_to_all | solution.py:147
  77.2 3.5 %all-to-all-start.3 = ((f32[8,128,128]{1,2,0:T(8,128)}), f32[8,128,128]{1,2,0:T(8,128)S(1)}, u32[]{:S(2)}, u32[]{:S(2)}) async-start(f32[8,128,128]{1,2,0:T(8,128)} %fusion.35), calls=%async_computation.3 | async-start | bytes 1048576 | tf_op jit(solution)/shard_map/all_to_all | solution.py:147
  80.7 0.9 copy.29
  81.6 0.2 copy.26
  81.8 0.9 fusion.32
  82.7 13.2 %all-to-all-done.3 = f32[8,128,128]{1,2,0:T(8,128)S(1)} async-done(((f32[8,128,128]{1,2,0:T(8,128)}), f32[8,128,128]{1,2,0:T(8,128)S(1)}, u32[]{:S(2)}, u32[]{:S(2)}) %all-to-all-start.3) | async-done | bytes 524320 | tf_op jit(solution)/shard_map/all_to_all | solution.py:147
  96.0 1.0 %copy.30 = f32[128,1024]{1,0:T(8,128)} copy(f32[128,1024]{0,1:T(8,128)S(1)} %bitcast.305) | data formatting | bytes 1048576
  (72 shorter events, 1.4 us)
Async XLA Ops:
  0.6 21.9 %collective-permute-start.2 = (bf16[128,1024]{1,0:T(8,128)(2,1)}, bf16[128,1024]{1,0:T(8,128)(2,1)S(1)}, u32[]{:S(2)}, u32[]{:S(2)}) collective-permute-start(bf16[128,1024]{1,0:T(8,128)(2,1)} %param.11), channel_id=1, source_target_pairs={{0,3},{1,0},{2,1},{3,2},{4,7},{5,4},{6,5},{7,6},{8,11},{9,8},{10,9... | collective-permute-start | bytes 786440 | tf_op jit(solution)/shard_map/ppermute | solution.py:27
  4.6 20.2 %collective-permute-start.1 = (bf16[128,1024]{1,0:T(8,128)(2,1)}, bf16[128,1024]{1,0:T(8,128)(2,1)S(1)}, u32[]{:S(2)}, u32[]{:S(2)}) collective-permute-start(bf16[128,1024]{1,0:T(8,128)(2,1)} %param.11), channel_id=1, source_target_pairs={{0,2},{1,3},{2,0},{3,1},{4,6},{5,7},{6,4},{7,5},{8,10},{9,11},{10,... | collective-permute-start | bytes 786440 | tf_op jit(solution)/shard_map/ppermute | solution.py:27
  5.1 22.0 %collective-permute-start = (bf16[128,1024]{1,0:T(8,128)(2,1)}, bf16[128,1024]{1,0:T(8,128)(2,1)S(1)}, u32[]{:S(2)}, u32[]{:S(2)}) collective-permute-start(bf16[128,1024]{1,0:T(8,128)(2,1)} %param.11), channel_id=1, source_target_pairs={{0,1},{1,2},{2,3},{3,0},{4,5},{5,6},{6,7},{7,4},{8,9},{9,10},{10,1... | collective-permute-start | bytes 786440 | tf_op jit(solution)/shard_map/ppermute | solution.py:27
  9.0 21.5 %all-to-all-start = ((bf16[8,2,128,128]{2,3,1,0:T(8,128)(2,1)}), bf16[8,2,128,128]{2,3,1,0:T(8,128)(2,1)S(1)}, u32[]{:S(2)}, u32[]{:S(2)}) async-start(bf16[8,2,128,128]{2,3,1,0:T(8,128)(2,1)} %pad_maximum_fusion), calls=%async_computation | async-start | bytes 1048576 | tf_op jit(solution)/shard_map/all_to_all | solution.py:147
  19.3 17.0 %copy-start.22 = (f32[256]{0:T(256)}, f32[256]{0:T(256)S(1)}, u32[]{:S(2)}) copy-start(f32[256]{0:T(256)S(1)} %fusion.103) | copy-start | bytes 3076
  30.5 20.4 %all-to-all-start.1 = ((bf16[8,2,128,128]{2,3,1,0:T(8,128)(2,1)}), bf16[8,2,128,128]{2,3,1,0:T(8,128)(2,1)S(1)}, u32[]{:S(2)}, u32[]{:S(2)}) async-start(bf16[8,2,128,128]{2,3,1,0:T(8,128)(2,1)} %pad_maximum_fusion.1), calls=%async_computation.1 | async-start | bytes 1048576 | tf_op jit(solution)/shard_map/all_to_all | solution.py:147
  40.5 13.3 %copy-start.2 = (f32[128,128]{0,1:T(8,128)}, f32[128,128]{0,1:T(8,128)S(1)}, u32[]{:S(2)}) copy-start(f32[128,128]{0,1:T(8,128)S(1)} %get-tuple-element.104) | copy-start | bytes 196612
  40.5 13.3 %copy-start.3 = (f32[128,128]{0,1:T(8,128)}, f32[128,128]{0,1:T(8,128)S(1)}, u32[]{:S(2)}) copy-start(f32[128,128]{0,1:T(8,128)S(1)} %get-tuple-element.105) | copy-start | bytes 196612
  40.5 13.3 %copy-start.4 = (f32[128,128]{0,1:T(8,128)}, f32[128,128]{0,1:T(8,128)S(1)}, u32[]{:S(2)}) copy-start(f32[128,128]{0,1:T(8,128)S(1)} %get-tuple-element.106) | copy-start | bytes 196612
  50.9 2.9 %copy-start.5 = (f32[128,128]{0,1:T(8,128)S(1)}, f32[128,128]{0,1:T(8,128)}, u32[]{:S(2)}) copy-start(f32[128,128]{0,1:T(8,128)} %get-tuple-element.107) | copy-start | bytes 196612
  52.5 3.9 %copy-start.8 = (bf16[256,128]{1,0:T(8,128)(2,1)S(1)}, bf16[256,128]{1,0:T(8,128)(2,1)}, u32[]{:S(2)}) copy-start(bf16[256,128]{1,0:T(8,128)(2,1)} %subtract_convert_fusion.9) | copy-start | bytes 196612
  52.8 4.2 %copy-start.6 = (bf16[256,128]{1,0:T(8,128)(2,1)S(1)}, bf16[256,128]{1,0:T(8,128)(2,1)}, u32[]{:S(2)}) copy-start(bf16[256,128]{1,0:T(8,128)(2,1)} %get-tuple-element.78) | copy-start | bytes 196612
  53.2 4.0 %copy-start.10 = (f32[128]{0:T(128)S(1)}, f32[128]{0:T(128)}, u32[]{:S(2)}) copy-start(f32[128]{0:T(128)} %get-tuple-element.66) | copy-start | bytes 1540
  53.2 4.0 %copy-start.11 = (f32[128]{0:T(128)S(1)}, f32[128]{0:T(128)}, u32[]{:S(2)}) copy-start(f32[128]{0:T(128)} %get-tuple-element.67) | copy-start | bytes 1540
  53.2 4.0 %copy-start.12 = (f32[128]{0:T(128)S(1)}, f32[128]{0:T(128)}, u32[]{:S(2)}) copy-start(f32[128]{0:T(128)} %get-tuple-element.68) | copy-start | bytes 1540
  53.3 4.0 %copy-start.13 = (f32[128]{0:T(128)S(1)}, f32[128]{0:T(128)}, u32[]{:S(2)}) copy-start(f32[128]{0:T(128)} %get-tuple-element.69) | copy-start | bytes 1540
  53.3 4.0 %copy-start.14 = (f32[128]{0:T(128)S(1)}, f32[128]{0:T(128)}, u32[]{:S(2)}) copy-start(f32[128]{0:T(128)} %get-tuple-element.92) | copy-start | bytes 1540
  53.3 4.0 %copy-start.15 = (f32[128]{0:T(128)S(1)}, f32[128]{0:T(128)}, u32[]{:S(2)}) copy-start(f32[128]{0:T(128)} %get-tuple-element.93) | copy-start | bytes 1540
  53.3 4.0 %copy-start.16 = (f32[128]{0:T(128)S(1)}, f32[128]{0:T(128)}, u32[]{:S(2)}) copy-start(f32[128]{0:T(128)} %get-tuple-element.94) | copy-start | bytes 1540
  53.3 4.0 %copy-start.17 = (f32[128]{0:T(128)S(1)}, f32[128]{0:T(128)}, u32[]{:S(2)}) copy-start(f32[128]{0:T(128)} %get-tuple-element.95) | copy-start | bytes 1540
  53.3 4.0 %copy-start.18 = (f32[128]{0:T(128)S(1)}, f32[128]{0:T(128)}, u32[]{:S(2)}) copy-start(f32[128]{0:T(128)} %get-tuple-element.96) | copy-start | bytes 1540
  53.3 4.0 %copy-start.19 = (f32[128]{0:T(128)S(1)}, f32[128]{0:T(128)}, u32[]{:S(2)}) copy-start(f32[128]{0:T(128)} %get-tuple-element.97) | copy-start | bytes 1540
  53.3 4.0 %copy-start.20 = (f32[128]{0:T(128)S(1)}, f32[128]{0:T(128)}, u32[]{:S(2)}) copy-start(f32[128]{0:T(128)} %get-tuple-element.98) | copy-start | bytes 1540
  53.3 4.0 %copy-start.21 = (f32[128]{0:T(128)S(1)}, f32[128]{0:T(128)}, u32[]{:S(2)}) copy-start(f32[128]{0:T(128)} %get-tuple-element.99) | copy-start | bytes 1540
  53.3 4.0 %copy-start.24 = (f32[128]{0:T(128)S(1)}, f32[128]{0:T(128)}, u32[]{:S(2)}) copy-start(f32[128]{0:T(128)} %slice.288) | copy-start | bytes 1540
  55.6 6.6 %copy-start.7 = (bf16[256,128]{1,0:T(8,128)(2,1)S(1)}, bf16[256,128]{1,0:T(8,128)(2,1)}, u32[]{:S(2)}) copy-start(bf16[256,128]{1,0:T(8,128)(2,1)} %get-tuple-element.78) | copy-start | bytes 196612
  55.6 7.3 %copy-start.9 = (bf16[256,128]{1,0:T(8,128)(2,1)S(1)}, bf16[256,128]{1,0:T(8,128)(2,1)}, u32[]{:S(2)}) copy-start(bf16[256,128]{1,0:T(8,128)(2,1)} %subtract_convert_fusion.9) | copy-start | bytes 196612
  56.7 6.8 %copy-start.23 = (f32[256]{0:T(256)S(1)}, f32[256]{0:T(256)}, u32[]{:S(2)}) copy-start(f32[256]{0:T(256)} %copy-done.22) | copy-start | bytes 3076
  58.5 18.8 %all-to-all-start.2 = ((f32[8,128,128]{1,2,0:T(8,128)}), f32[8,128,128]{1,2,0:T(8,128)S(1)}, u32[]{:S(2)}, u32[]{:S(2)}) async-start(f32[8,128,128]{1,2,0:T(8,128)} %fusion.22), calls=%async_computation.2 | async-start | bytes 1048576 | tf_op jit(solution)/shard_map/all_to_all | solution.py:147
  62.6 19.2 %copy-start = (bf16[128,1024]{1,0:T(8,128)(2,1)S(1)}, bf16[128,1024]{1,0:T(8,128)(2,1)}, u32[]{:S(2)}) copy-start(bf16[128,1024]{1,0:T(8,128)(2,1)} %param.9) | copy-start | bytes 786436
  62.6 19.2 %copy-start.1 = (bf16[128,1024]{1,0:T(8,128)(2,1)S(1)}, bf16[128,1024]{1,0:T(8,128)(2,1)}, u32[]{:S(2)}) copy-start(bf16[128,1024]{1,0:T(8,128)(2,1)} %param.8) | copy-start | bytes 786436
  77.2 18.8 %all-to-all-start.3 = ((f32[8,128,128]{1,2,0:T(8,128)}), f32[8,128,128]{1,2,0:T(8,128)S(1)}, u32[]{:S(2)}, u32[]{:S(2)}) async-start(f32[8,128,128]{1,2,0:T(8,128)} %fusion.35), calls=%async_computation.3 | async-start | bytes 1048576 | tf_op jit(solution)/shard_map/all_to_all | solution.py:147

commit v3 on v2

--- a/solution.py
+++ b/solution.py
@@ -1,6 +1,7 @@
 import math
 
 import jax
+import numpy as np
 import jax.numpy as jnp
 from jax import lax
 from jax.sharding import PartitionSpec as P
@@ -18,39 +19,43 @@
 def gather_matmul(out_grad, out_weight):
     count = lax.axis_size("tp")
     me = lax.axis_index("tp")
-    width = out_grad.shape[1]
-    total = None
-    for shift in range(count):
-        if shift == 0:
-            piece = out_grad
-        else:
-            piece = lax.ppermute(out_grad, "tp", [(i, (i + shift) % count) for i in range(count)])
-        source = (me - shift) % count
-        weight = lax.dynamic_slice_in_dim(out_weight, source * width, width, axis=1)
-        part = lax.dot_general(
-            piece, weight, (((1,), (1,)), ((), ())), preferred_element_type=jnp.float32
+    pieces = [out_grad]
+    for shift in range(1, count):
+        pieces.append(
+            lax.ppermute(out_grad, "tp", [(i, (i + shift) % count) for i in range(count)])
         )
-        total = part if total is None else total + part
-    return total
+    stacked = jnp.stack(pieces)
+    ordered = [
+        lax.dynamic_index_in_dim(stacked, (me - source) % count, 0, keepdims=False)
+        for source in range(count)
+    ]
+    gathered = jnp.concatenate(ordered, axis=1)
+    return lax.dot_general(
+        gathered, out_weight, (((1,), (1,)), ((), ())), preferred_element_type=jnp.float32
+    )
+
+
+def split_constant(table):
+    upper = table.astype(jnp.bfloat16)
+    lower = (table - upper.astype(np.float64)).astype(jnp.bfloat16)
+    return jnp.asarray(upper), jnp.asarray(lower)
 
 
 def make_tables(size):
-    index = jnp.arange(size, dtype=jnp.int32)
-    long_index = jnp.arange(2 * size, dtype=jnp.int32)
-    angle = (index[:, None] * index[None, :] % (2 * size)).astype(jnp.float32) * (math.pi / size)
-    angle_back = (long_index[:, None] * index[None, :] % (2 * size)).astype(jnp.float32) * (
-        math.pi / size
-    )
-    weight = jnp.where(index == 0, 1.0, 2.0).astype(jnp.float32) / (2.0 * size)
-    alternate = (1 - 2 * (index % 2)).astype(jnp.float32)
-    alternate_back = (1 - 2 * (long_index % 2)).astype(jnp.float32) / (2.0 * size)
+    index = np.arange(size)
+    long_index = np.arange(2 * size)
+    angle = (index[:, None] * index[None, :] % (2 * size)) * (math.pi / size)
+    angle_back = (long_index[:, None] * index[None, :] % (2 * size)) * (math.pi / size)
+    weight = np.where(index == 0, 1.0, 2.0) / (2.0 * size)
+    alternate = 1.0 - 2.0 * (index % 2)
+    alternate_back = (1.0 - 2.0 * (long_index % 2)) / (2.0 * size)
     return {
-        "cos": split_bf16(jnp.cos(angle)),
-        "sin": split_bf16(-jnp.sin(angle)),
-        "alt": alternate.astype(jnp.bfloat16),
-        "icos": split_bf16(jnp.cos(angle_back) * weight[None, :]),
-        "isin": split_bf16(-jnp.sin(angle_back) * weight[None, :]),
-        "ialt": alternate_back,
+        "cos": split_constant(np.cos(angle)),
+        "sin": split_constant(-np.sin(angle)),
+        "alt": jnp.asarray(alternate.astype(jnp.bfloat16)),
+        "icos": split_constant(np.cos(angle_back) * weight[None, :]),
+        "isin": split_constant(-np.sin(angle_back) * weight[None, :]),
+        "ialt": jnp.asarray(alternate_back.astype(np.float32)),
     }
 
 
@@ -168,8 +173,9 @@
         inputs_t[:, 1].reshape(seq, sub),
         float(seq) ** -0.5,
     )
-    du_local = from_groups(transpose_ctx(du_t.reshape(blocks, rows, sub)))
-    filter_grad = from_groups(transpose_ctx(filter_t.reshape(blocks, rows, sub)))
+    back = transpose_ctx(jnp.stack([du_t, filter_t], axis=1).reshape(blocks, rows, 2, sub))
+    du_local = from_groups(back[:, :, 0])
+    filter_grad = from_groups(back[:, :, 1])
     dk_grad = (du_local * v_proj.astype(jnp.float32)).astype(jnp.bfloat16)
     dv_grad = (du_local * k_proj.astype(jnp.float32)).astype(jnp.bfloat16)
     return (dq_grad, dk_grad, dv_grad, filter_grad)

time: 97.7 us -> 89.1 us (0.912)
  blocking collectives: 0 us -> 29 us
  waiting for transfers between devices: 36.1 us -> 17.3 us
  starting transfers between devices: 22 us -> 13.4 us
  matrix products: 18.5 us -> 13.3 us
  other arithmetic: 11 us -> 6.78 us
    all_to_all x0 -> x1, blocking collectives: none -> 29 us  [transpose_ctx(): return lax.all_to_all(stacked, 'ctx', 0, 0, tiled=True)]
    all_to_all x4 -> x2, waiting for transfers between devices: 36.1 us -> 13 us  [transpose_ctx(): return lax.all_to_all(stacked, 'ctx', 0, 0, tiled=True)]
    all_to_all x4 -> x2, starting transfers between devices: 17 us -> 8.37 us  [transpose_ctx(): return lax.all_to_all(stacked, 'ctx', 0, 0, tiled=True)]
    ppermute x3, waiting for transfers between devices: 0.01 us -> 4.35 us  [gather_matmul(): lax.ppermute(out_grad, 'tp', [(i, (i + shift) % count) for i in range(cou...]
    dot_general x26, matrix products: 8.58 us -> 6.31 us  [one(): jnp.einsum('kn,bnc->bkc', left, right, preferred_element_type=jnp.float32)]
    dot_general x4 -> x5, matrix products: 9.24 us -> 6.97 us  [the longest x1 6.3 us: gather_matmul(): lax.dot_general(gathered, out_weight, (((1,), (1,)), ((), ())), preferred...]
    convert_element_type x7 -> x4, other arithmetic: 3.65 us -> 1.71 us  [split_bf16(): upper = lax.optimization_barrier(value.astype(jnp.bfloat16))]
    convert_element_type x3 -> x1, other arithmetic: 2.49 us -> 0.88 us  [split_bf16(): lower = (value - upper.astype(jnp.float32)).astype(jnp.bfloat16)]
  transfers between devices with their start and end apart: 7 -> 5, of which waited for: 3 -> 3; matrix products, arithmetic and copies ran while one was open for 30% -> 16% of each run, Pallas kernels for 0% -> 0%
where the time goes in v3:
time: 89.1 us; the launch traced here: 88.4 us
  blocking collectives  29 us (33%)
  waiting for transfers between devices  17.3 us (19%)
  starting transfers between devices  13.4 us (15%)
  matrix products  13.3 us (15%)
  local copies, waits for them, and re-layouts  7.31 us (8%)
  other arithmetic  6.78 us (8%)
  between operations  1.24 us (1%)
    all_to_all x1, blocking collectives, transpose_ctx(): return lax.all_to_all(stacked, 'ctx', 0, 0, tiled=True)  29 us
    all_to_all x2, waiting for transfers between devices, transpose_ctx(): return lax.all_to_all(stacked, 'ctx', 0, 0, tiled=True)  13 us
    all_to_all x2, starting transfers between devices, transpose_ctx(): return lax.all_to_all(stacked, 'ctx', 0, 0, tiled=True)  8.37 us
    dot_general x26, matrix products, one(): jnp.einsum('kn,bnc->bkc', left, right, preferred_element_type=jnp.float32)  6.31 us
    dot_general x1, matrix products, gather_matmul(): lax.dot_general(gathered, out_weight, (((1,), (1,)), ((), ())), preferred...  6.3 us
    unnamed x50, local copies, waits for them, and re-layouts  5.72 us
    ppermute x3, starting transfers between devices, gather_matmul(): lax.ppermute(out_grad, 'tp', [(i, (i + shift) % count) for i in range(cou...  5.07 us
    ppermute x3, waiting for transfers between devices, gather_matmul(): lax.ppermute(out_grad, 'tp', [(i, (i + shift) % count) for i in range(cou...  4.35 us
  transfers between devices with their start and end apart: 5, of which 3 were waited for; matrix products, arithmetic and copies ran while one was open for 16% of the time, Pallas kernels for 0%

profile of v3, /device:TPU:0, one launch (start us, length us, event | category | flops | bytes accessed | tf_op | source)
XLA Modules:
  0.0 88.4 jit_solution(9034837242223971923)
XLA Ops:
  0.6 4.0 %collective-permute-start.2 = (bf16[128,1024]{1,0:T(8,128)(2,1)}, bf16[128,1024]{1,0:T(8,128)(2,1)S(1)}, u32[]{:S(2)}, u32[]{:S(2)}) collective-permute-start(bf16[128,1024]{1,0:T(8,128)(2,1)} %param.21), channel_id=1, source_target_pairs={{0,3},{1,0},{2,1},{3,2},{4,7},{5,4},{6,5},{7,6},{8,11},{9,8},{10,9... | collective-permute-start | bytes 786440 | tf_op jit(solution)/shard_map/ppermute | solution.py:25
  4.6 0.5 collective-permute-start.1
  5.1 0.6 collective-permute-start
  5.7 1.1 %fusion.22 = bf16[128,1024]{1,0:T(8,128)(2,1)S(1)} fusion(bf16[128,1024]{1,0:T(8,128)(2,1)} %param.19, bf16[128,1024]{1,0:T(8,128)(2,1)} %param.18), kind=kLoop, calls=%fused_computation.57 | loop fusion | flops 524288 | bytes 786432 | tf_op jit(solution)/shard_map/convert_element_type | solution.py:159
  6.8 1.1 %copy.29 = bf16[128,1024]{0,1:T(8,128)(2,1)S(1)} copy(bf16[128,1024]{1,0:T(8,128)(2,1)} %param.23) | data formatting | bytes 524288 | tf_op args[6]
  7.9 0.2 copy.28
  8.1 0.8 pad_maximum_fusion.2
  9.0 4.9 %all-to-all-start = ((bf16[8,2,128,128]{2,3,1,0:T(8,128)(2,1)}), bf16[8,2,128,128]{2,3,1,0:T(8,128)(2,1)S(1)}, u32[]{:S(2)}, u32[]{:S(2)}) async-start(bf16[8,2,128,128]{2,3,1,0:T(8,128)(2,1)} %pad_maximum_fusion.2), calls=%async_computation | async-start | bytes 1048576 | tf_op jit(solution)/shard_map/all_to_all | solution.py:152
  13.9 4.3 %collective-permute-done.1 = bf16[128,1024]{1,0:T(8,128)(2,1)S(1)} collective-permute-done((bf16[128,1024]{1,0:T(8,128)(2,1)}, bf16[128,1024]{1,0:T(8,128)(2,1)S(1)}, u32[]{:S(2)}, u32[]{:S(2)}) %collective-permute-start.1) | collective-permute-done | bytes 262176 | tf_op jit(solution)/shard_map/ppermute | solution.py:25
  18.2 0.1 pad_maximum_fusion
  18.5 0.7 copy-done.10
  19.2 6.3 %fusion.26 = (bf16[128,1024]{1,0:T(8,128)(2,1)S(1)}, f32[128,1024]{1,0:T(8,128)S(1)}) fusion(bf16[128,1024]{1,0:T(8,128)(2,1)S(1)} %copy-done.10, bf16[1024,4096]{1,0:T(8,128)(2,1)} %param.22, bf16[128,1024]{1,0:T(8,128)(2,1)S(1)} %get-tuple-element.23, bf16[128,1024]{1,0:T(8,128)(2,1)S(1)} %get-tuple-element.24, ...), kind=kOutput, calls=%fused_computation.77 | convolution fusion | flops 1078329344 | bytes 10485760 | tf_op jit(solution)/shard_map/dot_general | solution.py:33
  25.5 0.2 copy.44
  25.7 0.9 subtract_convert_fusion.4
  26.6 0.2 copy.45
  26.7 0.9 pad_maximum_fusion.3
  27.6 1.6 %all-to-all-done = bf16[8,2,128,128]{2,3,1,0:T(8,128)(2,1)S(1)} async-done(((bf16[8,2,128,128]{2,3,1,0:T(8,128)(2,1)}), bf16[8,2,128,128]{2,3,1,0:T(8,128)(2,1)S(1)}, u32[]{:S(2)}, u32[]{:S(2)}) %all-to-all-start) | async-done | bytes 524320 | tf_op jit(solution)/shard_map/all_to_all | solution.py:152
  29.2 3.5 %all-to-all-start.1 = ((bf16[8,2,128,128]{2,3,1,0:T(8,128)(2,1)}), bf16[8,2,128,128]{2,3,1,0:T(8,128)(2,1)S(1)}, u32[]{:S(2)}, u32[]{:S(2)}) async-start(bf16[8,2,128,128]{2,3,1,0:T(8,128)(2,1)} %pad_maximum_fusion.3), calls=%async_computation.1 | async-start | bytes 1048576 | tf_op jit(solution)/shard_map/all_to_all | solution.py:152
  32.7 0.2 fusion.28
  32.9 0.2 fusion.30
  33.1 0.2 fusion.8
  33.4 0.2 fusion.29
  33.6 0.2 fusion.6
  33.9 0.2 fusion.35
  34.2 0.2 fusion.36
  34.4 0.2 fusion.34
  34.6 0.2 fusion.3
  34.8 0.2 fusion.4
  35.2 0.4 copy-done.1
  35.6 0.3 slice-done
  35.9 0.3 copy-done.3
  36.5 11.4 %all-to-all-done.1 = bf16[8,2,128,128]{2,3,1,0:T(8,128)(2,1)S(1)} async-done(((bf16[8,2,128,128]{2,3,1,0:T(8,128)(2,1)}), bf16[8,2,128,128]{2,3,1,0:T(8,128)(2,1)S(1)}, u32[]{:S(2)}, u32[]{:S(2)}) %all-to-all-start.1) | async-done | bytes 524320 | tf_op jit(solution)/shard_map/all_to_all | solution.py:152
  47.9 0.2 fusion.32
  48.2 0.2 fusion.33
  48.4 0.2 convolution_add_fusion.11
  48.6 0.2 fusion.5
  48.9 0.2 convolution_add_fusion.14
  49.1 0.2 fusion.7
  49.3 0.4 fusion.44
  49.8 0.4 fusion.43
  50.2 0.4 fusion.42
  50.7 0.4 fusion.41
  51.1 0.4 copy-done.13
  51.5 0.3 fusion.48
  51.8 0.3 convolution_add_fusion.3
  52.1 0.3 convolution_add_fusion.2
  52.4 0.2 copy-done.14
  52.6 0.3 fusion.49
  52.9 0.3 convolution_add_fusion.1
  53.2 0.2 fusion.31
  53.4 0.2 fusion.27
  53.6 0.3 fusion.2
  54.1 0.6 copy-done.16
  54.7 0.2 fusion.47
  55.0 0.2 convolution_add_fusion.7
  55.2 0.2 convolution_add_fusion.6
  55.5 0.2 fusion.46
  55.7 0.2 convolution_add_fusion.9
  56.0 0.3 fusion.12
  56.4 29.0 %all_to_all.15 = f32[8,128,2,128]{1,3,2,0:T(8,128)S(1)} all-to-all(f32[8,128,2,128]{1,3,2,0:T(8,128)S(1)} %copy.36), channel_id=1, replica_groups=mesh['ctx'=8,'tp'=4] {'ctx'}, dimensions={0} | all-to-all | bytes 2097152 | tf_op jit(solution)/shard_map/all_to_all | solution.py:152
  85.5 0.2 copy.37
  85.7 0.7 copy-done.4
  86.5 0.9 %fusion.21 = (bf16[128,1024]{1,0:T(8,128)(2,1)}, bf16[128,1024]{1,0:T(8,128)(2,1)}) fusion(f32[128,1024]{1,0:T(8,128)S(1)} %copy.37, bf16[128,1024]{1,0:T(8,128)(2,1)S(1)} %copy-done.5, bf16[128,1024]{1,0:T(8,128)(2,1)S(1)} %copy-done.4), kind=kLoop, calls=%fused_computation.56 | loop fusion | flops 786432 | bytes 1572864 | tf_op jit(solution)/shard_map/convert_element_type | solution.py:180
  87.4 1.0 %copy.39 = f32[128,1024]{1,0:T(8,128)} copy(f32[128,1024]{0,1:T(8,128)S(1)} %bitcast.262) | data formatting | bytes 1048576
  (60 shorter events, 1.3 us)
Async XLA Ops:
  0.6 17.6 %copy-start.12 = (bf16[128,1024]{1,0:T(8,128)(2,1)S(1)}, bf16[128,1024]{1,0:T(8,128)(2,1)}, u32[]{:S(2)}) copy-start(bf16[128,1024]{1,0:T(8,128)(2,1)} %param.21) | copy-start | bytes 786436
  0.6 13.2 %collective-permute-start.2 = (bf16[128,1024]{1,0:T(8,128)(2,1)}, bf16[128,1024]{1,0:T(8,128)(2,1)S(1)}, u32[]{:S(2)}, u32[]{:S(2)}) collective-permute-start(bf16[128,1024]{1,0:T(8,128)(2,1)} %param.21), channel_id=1, source_target_pairs={{0,3},{1,0},{2,1},{3,2},{4,7},{5,4},{6,5},{7,6},{8,11},{9,8},{10,9... | collective-permute-start | bytes 786440 | tf_op jit(solution)/shard_map/ppermute | solution.py:25
  4.6 13.6 %collective-permute-start.1 = (bf16[128,1024]{1,0:T(8,128)(2,1)}, bf16[128,1024]{1,0:T(8,128)(2,1)S(1)}, u32[]{:S(2)}, u32[]{:S(2)}) collective-permute-start(bf16[128,1024]{1,0:T(8,128)(2,1)} %param.21), channel_id=1, source_target_pairs={{0,2},{1,3},{2,0},{3,1},{4,6},{5,7},{6,4},{7,5},{8,10},{9,11},{10,... | collective-permute-start | bytes 786440 | tf_op jit(solution)/shard_map/ppermute | solution.py:25
  5.1 13.1 %collective-permute-start = (bf16[128,1024]{1,0:T(8,128)(2,1)}, bf16[128,1024]{1,0:T(8,128)(2,1)S(1)}, u32[]{:S(2)}, u32[]{:S(2)}) collective-permute-start(bf16[128,1024]{1,0:T(8,128)(2,1)} %param.21), channel_id=1, source_target_pairs={{0,1},{1,2},{2,3},{3,0},{4,5},{5,6},{6,7},{7,4},{8,9},{9,10},{10,1... | collective-permute-start | bytes 786440 | tf_op jit(solution)/shard_map/ppermute | solution.py:25
  9.0 20.2 %all-to-all-start = ((bf16[8,2,128,128]{2,3,1,0:T(8,128)(2,1)}), bf16[8,2,128,128]{2,3,1,0:T(8,128)(2,1)S(1)}, u32[]{:S(2)}, u32[]{:S(2)}) async-start(bf16[8,2,128,128]{2,3,1,0:T(8,128)(2,1)} %pad_maximum_fusion.2), calls=%async_computation | async-start | bytes 1048576 | tf_op jit(solution)/shard_map/all_to_all | solution.py:152
  18.2 1.0 %copy-start.10 = (bf16[128,1024]{1,0:T(8,128)(2,1)S(1)}, bf16[128,1024]{1,0:T(8,128)(2,1)}, u32[]{:S(2)}) copy-start(bf16[128,1024]{1,0:T(8,128)(2,1)} %param.17) | copy-start | bytes 786436
  19.2 6.5 %copy-start.11 = (bf16[128,1024]{1,0:T(8,128)(2,1)S(1)}, bf16[128,1024]{1,0:T(8,128)(2,1)}, u32[]{:S(2)}) copy-start(bf16[128,1024]{1,0:T(8,128)(2,1)} %param.20) | copy-start | bytes 786436
  25.7 7.0 %copy-start.23 = (bf16[128,1,1]{0,1,2:T(2,128)(2,1)S(1)}, bf16[128,1,1]{0,1,2:T(2,128)(2,1)}, u32[]{:S(2)}) copy-start(bf16[128,1,1]{0,1,2:T(2,128)(2,1)} %constant.128) | copy-start | bytes 772
  25.7 7.2 %copy-start.6 = (bf16[128,128,1]{1,0,2:T(8,128)(2,1)S(1)}, bf16[128,128,1]{1,0,2:T(8,128)(2,1)}, u32[]{:S(2)}) copy-start(bf16[128,128,1]{1,0,2:T(8,128)(2,1)} %constant.120) | copy-start | bytes 98308
  26.6 6.6 %copy-start.8 = (bf16[128,128,1]{1,0,2:T(8,128)(2,1)S(1)}, bf16[128,128,1]{1,0,2:T(8,128)(2,1)}, u32[]{:S(2)}) copy-start(bf16[128,128,1]{1,0,2:T(8,128)(2,1)} %constant.121) | copy-start | bytes 98308
  27.6 5.8 %copy-start.7 = (bf16[128,128,1]{1,0,2:T(8,128)(2,1)S(1)}, bf16[128,128,1]{1,0,2:T(8,128)(2,1)}, u32[]{:S(2)}) copy-start(bf16[128,128,1]{1,0,2:T(8,128)(2,1)} %constant.122) | copy-start | bytes 98308
  29.2 18.8 %all-to-all-start.1 = ((bf16[8,2,128,128]{2,3,1,0:T(8,128)(2,1)}), bf16[8,2,128,128]{2,3,1,0:T(8,128)(2,1)S(1)}, u32[]{:S(2)}, u32[]{:S(2)}) async-start(bf16[8,2,128,128]{2,3,1,0:T(8,128)(2,1)} %pad_maximum_fusion.3), calls=%async_computation.1 | async-start | bytes 1048576 | tf_op jit(solution)/shard_map/all_to_all | solution.py:152
  32.7 0.9 %copy-start.9 = (bf16[128,128,1]{1,0,2:T(8,128)(2,1)S(1)}, bf16[128,128,1]{1,0,2:T(8,128)(2,1)}, u32[]{:S(2)}) copy-start(bf16[128,128,1]{1,0,2:T(8,128)(2,1)} %constant.123) | copy-start | bytes 98308
  33.4 0.8 copy-start
  33.9 0.9 %copy-start.2 = (f32[8,128,128]{1,2,0:T(8,128)}, f32[8,128,128]{1,2,0:T(8,128)S(1)}, u32[]{:S(2)}) copy-start(f32[8,128,128]{1,2,0:T(8,128)S(1)} %fusion.6) | copy-start | bytes 1572868
  34.5 1.1 %copy-start.1 = (f32[8,128,128]{1,2,0:T(8,128)S(1)}, f32[8,128,128]{1,2,0:T(8,128)}, u32[]{:S(2)}) copy-start(f32[8,128,128]{1,2,0:T(8,128)} %copy-done) | copy-start | bytes 1572868
  34.5 1.3 %slice-start = ((f32[8,128,128]{1,2,0:T(8,128)}), f32[7,128,128]{1,2,0:T(8,128)S(1)}, s32[]{:S(2)}) async-start(f32[8,128,128]{1,2,0:T(8,128)} %copy-done), calls=%async_computation.3 | async-start | bytes 917504 | tf_op jit(solution)/shard_map/slice | solution.py:115
  35.0 1.1 %copy-start.3 = (f32[8,128,128]{1,2,0:T(8,128)S(1)}, f32[8,128,128]{1,2,0:T(8,128)}, u32[]{:S(2)}) copy-start(f32[8,128,128]{1,2,0:T(8,128)} %copy-done.2) | copy-start | bytes 1572868
  35.1 1.2 %slice-start.1 = ((f32[8,128,128]{1,2,0:T(8,128)}), f32[7,128,128]{1,2,0:T(8,128)S(1)}, s32[]{:S(2)}) async-start(f32[8,128,128]{1,2,0:T(8,128)} %copy-done.2), calls=%async_computation.4 | async-start | bytes 917504 | tf_op jit(solution)/shard_map/slice | solution.py:115
  50.6 0.8 copy-start.13
  50.6 1.1 %copy-start.18 = (bf16[256,128,1]{1,0,2:T(8,128)(2,1)S(1)}, bf16[256,128,1]{1,0,2:T(8,128)(2,1)}, u32[]{:S(2)}) copy-start(bf16[256,128,1]{1,0,2:T(8,128)(2,1)} %constant.130) | copy-start | bytes 196612
  51.8 0.8 copy-start.14
  52.1 0.9 copy-start.17
  52.6 1.0 %copy-start.21 = (f32[256]{0:T(256)S(1)}, f32[256]{0:T(256)}, u32[]{:S(2)}) copy-start(f32[256]{0:T(256)} %constant.100.clone) | copy-start | bytes 3076
  54.0 0.8 copy-start.16
  54.0 1.0 %copy-start.20 = (bf16[128,128,1]{1,0,2:T(8,128)(2,1)S(1)}, bf16[128,128,1]{1,0,2:T(8,128)(2,1)}, u32[]{:S(2)}) copy-start(bf16[128,128,1]{1,0,2:T(8,128)(2,1)} %constant.127) | copy-start | bytes 98308
  54.1 1.4 %copy-start.15 = (bf16[128,128,1]{1,0,2:T(8,128)(2,1)S(1)}, bf16[128,128,1]{1,0,2:T(8,128)(2,1)}, u32[]{:S(2)}) copy-start(bf16[128,128,1]{1,0,2:T(8,128)(2,1)} %constant.124) | copy-start | bytes 98308
  55.0 0.8 copy-start.19
  55.2 0.8 copy-start.22
  85.4 1.0 %copy-start.4 = (bf16[128,1024]{1,0:T(8,128)(2,1)S(1)}, bf16[128,1024]{1,0:T(8,128)(2,1)}, u32[]{:S(2)}) copy-start(bf16[128,1024]{1,0:T(8,128)(2,1)} %param.19) | copy-start | bytes 786436
  85.4 1.0 %copy-start.5 = (bf16[128,1024]{1,0:T(8,128)(2,1)S(1)}, bf16[128,1024]{1,0:T(8,128)(2,1)}, u32[]{:S(2)}) copy-start(bf16[128,1024]{1,0:T(8,128)(2,1)} %param.18) | copy-start | bytes 786436

commit v4 on v3

--- a/solution.py
+++ b/solution.py
@@ -16,7 +16,7 @@
     return upper, lower
 
 
-def gather_matmul(out_grad, out_weight):
+def gather_tp(out_grad):
     count = lax.axis_size("tp")
     me = lax.axis_index("tp")
     pieces = [out_grad]
@@ -29,10 +29,7 @@
         lax.dynamic_index_in_dim(stacked, (me - source) % count, 0, keepdims=False)
         for source in range(count)
     ]
-    gathered = jnp.concatenate(ordered, axis=1)
-    return lax.dot_general(
-        gathered, out_weight, (((1,), (1,)), ((), ())), preferred_element_type=jnp.float32
-    )
+    return jnp.concatenate(ordered, axis=1)
 
 
 def split_constant(table):
@@ -138,16 +135,6 @@
     return du, filter_grad
 
 
-def to_groups(value, groups):
-    rows, chans = value.shape
-    return value.reshape(rows, groups, chans // groups).transpose(1, 0, 2)
-
-
-def from_groups(value):
-    groups, rows, chans = value.shape
-    return value.transpose(1, 0, 2).reshape(rows, groups * chans)
-
-
 def transpose_ctx(stacked):
     return lax.all_to_all(stacked, "ctx", 0, 0, tiled=True)
 
@@ -156,26 +143,44 @@
     rows, chans = q_proj.shape
     blocks = lax.axis_size("ctx")
     seq = rows * blocks
+    sub = chans // blocks
+    halves = 2 if sub % 2 == 0 else 1
+    part = sub // halves
+    split = (rows, blocks, halves, part)
+
+    def grouped(value):
+        return value.reshape(split).transpose(1, 2, 0, 3)
+
     gated = (k_proj.astype(jnp.float32) * v_proj.astype(jnp.float32)).astype(jnp.bfloat16)
-    inputs_t = transpose_ctx(
-        jnp.stack([to_groups(gated, blocks), to_groups(filter_taps, blocks)], axis=1)
-    )
-    d_gated = gather_matmul(out_grad, out_weight)
-    dq_grad = (d_gated * saved_conv.astype(jnp.float32)).astype(jnp.bfloat16)
-    dz = d_gated * q_proj.astype(jnp.float32)
-    dz_hi, dz_lo = split_bf16(dz)
-    dz_t = transpose_ctx(jnp.stack([to_groups(dz_hi, blocks), to_groups(dz_lo, blocks)], axis=1))
-    sub = chans // blocks
-    du_t, filter_t = long_correlations(
-        dz_t[:, 0].reshape(seq, sub),
-        dz_t[:, 1].reshape(seq, sub),
-        inputs_t[:, 0].reshape(seq, sub),
-        inputs_t[:, 1].reshape(seq, sub),
-        float(seq) ** -0.5,
-    )
-    back = transpose_ctx(jnp.stack([du_t, filter_t], axis=1).reshape(blocks, rows, 2, sub))
-    du_local = from_groups(back[:, :, 0])
-    filter_grad = from_groups(back[:, :, 1])
+    inputs_t = transpose_ctx(jnp.stack([grouped(gated), grouped(filter_taps)], axis=2))
+    gathered = gather_tp(out_grad)
+    weight = out_weight.reshape(blocks, halves, part, out_weight.shape[1])
+    queries = q_proj.reshape(split)
+    saved = saved_conv.reshape(split)
+    dq_parts = []
+    back_parts = []
+    for half in range(halves):
+        d_gated = jnp.einsum(
+            "to,gjo->tgj", gathered, weight[:, half], preferred_element_type=jnp.float32
+        )
+        dq_parts.append((d_gated * saved[:, :, half].astype(jnp.float32)).astype(jnp.bfloat16))
+        dz = d_gated * queries[:, :, half].astype(jnp.float32)
+        dz_hi, dz_lo = split_bf16(dz)
+        dz_t = transpose_ctx(jnp.stack([dz_hi, dz_lo]).transpose(2, 0, 1, 3))
+        du_t, filter_t = long_correlations(
+            dz_t[:, 0].reshape(seq, part),
+            dz_t[:, 1].reshape(seq, part),
+            inputs_t[:, half, 0].reshape(seq, part),
+            inputs_t[:, half, 1].reshape(seq, part),
+            float(seq) ** -0.5,
+        )
+        back_parts.append(
+            transpose_ctx(jnp.stack([du_t, filter_t]).reshape(2, blocks, rows, part).transpose(1, 0, 2, 3))
+        )
+    dq_grad = jnp.stack(dq_parts, axis=2).reshape(rows, chans)
+    back = jnp.stack(back_parts, axis=2)
+    du_local = back[:, 0].transpose(2, 0, 1, 3).reshape(rows, chans)
+    filter_grad = back[:, 1].transpose(2, 0, 1, 3).reshape(rows, chans)
     dk_grad = (du_local * v_proj.astype(jnp.float32)).astype(jnp.bfloat16)
     dv_grad = (du_local * k_proj.astype(jnp.float32)).astype(jnp.bfloat16)
     return (dq_grad, dk_grad, dv_grad, filter_grad)

time: 89.1 us -> 127 us (1.43)
  waiting for transfers between devices: 17.3 us -> 62.6 us
  blocking collectives: 29 us -> 0 us
  starting transfers between devices: 13.4 us -> 23.8 us
  local copies, waits for them, and re-layouts: 7.31 us -> 13 us
  matrix products: 13.3 us -> 18.8 us
    all_to_all x2 -> x5, waiting for transfers between devices: 13 us -> 54.8 us  [transpose_ctx(): return lax.all_to_all(stacked, 'ctx', 0, 0, tiled=True)]
    all_to_all x1 -> x0, blocking collectives: 29 us -> none  [transpose_ctx(): return lax.all_to_all(stacked, 'ctx', 0, 0, tiled=True)]
    all_to_all x2 -> x5, starting transfers between devices: 8.37 us -> 18.8 us  [transpose_ctx(): return lax.all_to_all(stacked, 'ctx', 0, 0, tiled=True)]
    dot_general x26 -> x52, matrix products: 6.31 us -> 10.2 us  [one(): jnp.einsum('kn,bnc->bkc', left, right, preferred_element_type=jnp.float32)]
    ppermute x3, waiting for transfers between devices: 4.35 us -> 7.78 us  [gather_tp(): lax.ppermute(out_grad, 'tp', [(i, (i + shift) % count) for i in range(cou...]
    transpose x0 -> x4, local copies, waits for them, and re-layouts: none -> 3.11 us  [the longest x2 1.67 us: body(): jnp.stack([du_t, filter_t]).reshape(2, blocks, rows, part)]
    unnamed x50 -> x65, local copies, waits for them, and re-layouts: 5.72 us -> 8.57 us
    convert_element_type x4 -> x8, other arithmetic: 1.71 us -> 3.89 us  [split_bf16(): upper = lax.optimization_barrier(value.astype(jnp.bfloat16))]
  transfers between devices with their start and end apart: 5 -> 8, of which waited for: 3 -> 7; matrix products, arithmetic and copies ran while one was open for 16% -> 11% of each run, Pallas kernels for 0% -> 0%
where the time goes in v4:
time: 127 us; the launch traced here: 126 us
  waiting for transfers between devices  62.6 us (49%)
  starting transfers between devices  23.8 us (19%)
  matrix products  18.8 us (15%)
  local copies, waits for them, and re-layouts  13 us (10%)
  other arithmetic  5.71 us (4%)
  between operations  1.75 us (1%)
    all_to_all x5, waiting for transfers between devices, transpose_ctx(): return lax.all_to_all(stacked, 'ctx', 0, 0, tiled=True)  54.8 us
    all_to_all x5, starting transfers between devices, transpose_ctx(): return lax.all_to_all(stacked, 'ctx', 0, 0, tiled=True)  18.8 us
    dot_general x52, matrix products, one(): jnp.einsum('kn,bnc->bkc', left, right, preferred_element_type=jnp.float32)  10.2 us
    unnamed x65, local copies, waits for them, and re-layouts  8.57 us
    ppermute x3, waiting for transfers between devices, gather_tp(): lax.ppermute(out_grad, 'tp', [(i, (i + shift) % count) for i in range(cou...  7.78 us
    dot_general x2, matrix products, body(): jnp.einsum('to,gjo->tgj', gathered, weight[:, half], preferred_element_ty...  6.94 us
    ppermute x3, starting transfers between devices, gather_tp(): lax.ppermute(out_grad, 'tp', [(i, (i + shift) % count) for i in range(cou...  5.07 us
    convert_element_type x8, other arithmetic, split_bf16(): upper = lax.optimization_barrier(value.astype(jnp.bfloat16))  3.89 us
  transfers between devices with their start and end apart: 8, of which 7 were waited for; matrix products, arithmetic and copies ran while one was open for 11% of the time, Pallas kernels for 0%

profile of v4, /device:TPU:0, one launch (start us, length us, event | category | flops | bytes accessed | tf_op | source)
XLA Modules:
  0.0 125.7 jit_solution(16793854676664733504)
XLA Ops:
  0.7 4.0 %collective-permute-start.2 = (bf16[128,1024]{1,0:T(8,128)(2,1)}, bf16[128,1024]{1,0:T(8,128)(2,1)S(1)}, u32[]{:S(2)}, u32[]{:S(2)}) collective-permute-start(bf16[128,1024]{1,0:T(8,128)(2,1)} %param.31), channel_id=1, source_target_pairs={{0,3},{1,0},{2,1},{3,2},{4,7},{5,4},{6,5},{7,6},{8,11},{9,8},{10,9... | collective-permute-start | bytes 786440 | tf_op jit(solution)/shard_map/ppermute | solution.py:25
  4.6 0.5 collective-permute-start.1
  5.1 0.6 collective-permute-start
  5.7 1.1 copy.62
  6.8 1.1 copy.52
  8.0 1.1 copy.57
  9.1 1.1 copy.59
  10.4 1.2 collective-permute-done.2
  11.6 6.6 %collective-permute-done.1 = bf16[128,1024]{1,0:T(8,128)(2,1)S(1)} collective-permute-done((bf16[128,1024]{1,0:T(8,128)(2,1)}, bf16[128,1024]{1,0:T(8,128)(2,1)S(1)}, u32[]{:S(2)}, u32[]{:S(2)}) %collective-permute-start.1) | collective-permute-done | bytes 262176 | tf_op jit(solution)/shard_map/ppermute | solution.py:25
  18.5 3.4 %fusion.1 = f32[128,8,64]{0,2,1:T(8,128)S(1)} fusion(bf16[8,2,64,4096]{3,2,1,0:T(8,128)(2,1)} %bitcast.563, bf16[128,1024]{1,0:T(8,128)(2,1)S(1)} %get-tuple-element.31, bf16[128,1024]{1,0:T(8,128)(2,1)S(1)} %get-tuple-element.32, bf16[128,1024]{1,0:T(8,128)(2,1)S(1)} %get-tuple-element.33, bf16[128,1024]{1,0:T(8,128)(2,1)S(1)} %get-tuple-element.30), kind=kOutput, calls=%fused_computation.3 | convolution fusion | flops 541065216 | bytes 5505024 | tf_op jit(solution)/shard_map/to,gjo->tgj/dot_general | solution.py:163
  21.9 3.5 %fusion.39 = (bf16[128,8,64]{0,2,1:T(8,128)(2,1)S(1)}, bf16[128,8,64]{0,2,1:T(8,128)(2,1)S(1)}, f32[128,8,64]{0,2,1:T(8,128)S(1)}) fusion(bf16[128,8,2,64]{0,3,2,1:T(8,128)(2,1)S(1)} %bitcast.541, f32[128,8,64]{0,2,1:T(8,128)S(1)} %fusion.1, bf16[8,2,64,4096]{3,2,1,0:T(8,128)(2,1)} %bitcast.564, bf16[128,1024]{1,0:T(8,128)(2,1)S(1)} %get-tuple-element.31, ...), kind=kOutput, calls=%fused_computation.149 | convolution fusion | flops 541458432 | bytes 6291456 | tf_op jit(solution)/shard_map/to,gjo->tgj/dot_general | solution.py:163
  25.4 0.9 fusion.41
  26.3 0.7 copy.72
  27.0 4.9 %all-to-all-start.3 = ((bf16[8,2,128,64]{2,3,1,0:T(8,128)(2,1)}), bf16[8,2,128,64]{2,3,1,0:T(8,128)(2,1)S(1)}, u32[]{:S(2)}, u32[]{:S(2)}) async-start(bf16[8,2,128,64]{2,3,1,0:T(8,128)(2,1)} %copy.72), calls=%async_computation.3 | async-start | bytes 524288 | tf_op jit(solution)/shard_map/all_to_all | solution.py:139
  32.1 0.7 copy.64
  32.8 8.8 %all-to-all-done.3 = bf16[8,2,128,64]{2,3,1,0:T(8,128)(2,1)S(1)} async-done(((bf16[8,2,128,64]{2,3,1,0:T(8,128)(2,1)}), bf16[8,2,128,64]{2,3,1,0:T(8,128)(2,1)S(1)}, u32[]{:S(2)}, u32[]{:S(2)}) %all-to-all-start.3) | async-done | bytes 262176 | tf_op jit(solution)/shard_map/all_to_all | solution.py:139
  41.6 3.4 %all-to-all-start.1 = ((bf16[8,2,128,64]{2,3,1,0:T(8,128)(2,1)}), bf16[8,2,128,64]{2,3,1,0:T(8,128)(2,1)S(1)}, u32[]{:S(2)}, u32[]{:S(2)}) async-start(bf16[8,2,128,64]{2,3,1,0:T(8,128)(2,1)} %copy.64), calls=%async_computation.1 | async-start | bytes 524288 | tf_op jit(solution)/shard_map/all_to_all | solution.py:139
  45.1 0.8 copy.60
  45.9 0.2 fusion.58
  46.1 0.2 fusion.45
  46.3 8.4 %all-to-all-done.1 = bf16[8,2,128,64]{2,3,1,0:T(8,128)(2,1)S(1)} async-done(((bf16[8,2,128,64]{2,3,1,0:T(8,128)(2,1)}), bf16[8,2,128,64]{2,3,1,0:T(8,128)(2,1)S(1)}, u32[]{:S(2)}, u32[]{:S(2)}) %all-to-all-start.1) | async-done | bytes 262176 | tf_op jit(solution)/shard_map/all_to_all | solution.py:139
  54.7 3.5 %all-to-all-start = ((bf16[8,2,2,128,64]{3,4,2,1,0:T(8,128)(2,1)}), bf16[8,2,2,128,64]{3,4,2,1,0:T(8,128)(2,1)S(1)}, u32[]{:S(2)}, u32[]{:S(2)}) async-start(bf16[8,2,2,128,64]{3,4,2,1,0:T(8,128)(2,1)} %copy.60), calls=%async_computation | async-start | bytes 1048576 | tf_op jit(solution)/shard_map/all_to_all | solution.py:139
  58.2 0.2 fusion.49
  58.4 0.2 fusion.44
  58.6 0.2 fusion.60
  61.0 12.5 %all-to-all-done = bf16[8,2,2,128,64]{3,4,2,1,0:T(8,128)(2,1)S(1)} async-done(((bf16[8,2,2,128,64]{3,4,2,1,0:T(8,128)(2,1)}), bf16[8,2,2,128,64]{3,4,2,1,0:T(8,128)(2,1)S(1)}, u32[]{:S(2)}, u32[]{:S(2)}) %all-to-all-start) | async-done | bytes 524320 | tf_op jit(solution)/shard_map/all_to_all | solution.py:139
  74.3 0.2 fusion.72
  74.5 0.2 fusion.71
  74.9 0.2 fusion.17
  75.7 0.2 fusion.15
  76.6 0.2 fusion.70
  76.8 0.2 fusion.69
  77.9 0.9 fusion.76
  78.8 0.2 fusion.75
  79.1 0.9 fusion.74
  80.1 0.9 fusion.73
  81.0 0.2 fusion.55
  81.2 0.2 fusion.84
  81.4 0.2 convolution_add_fusion.1
  81.7 0.2 convolution_add_fusion
  81.9 0.2 fusion.83
  82.2 0.2 convolution_add_fusion.3
  82.4 0.2 fusion.61
  82.7 0.2 fusion.7
  84.1 0.2 fusion.13
  84.4 0.8 copy.76
  85.2 3.5 %all-to-all-start.4 = ((f32[8,2,128,64]{2,3,1,0:T(8,128)}), f32[8,2,128,64]{2,3,1,0:T(8,128)S(1)}, u32[]{:S(2)}, u32[]{:S(2)}) async-start(f32[8,2,128,64]{2,3,1,0:T(8,128)} %copy.76), calls=%async_computation.4 | async-start | bytes 1048576 | tf_op jit(solution)/shard_map/all_to_all | solution.py:139
  88.7 0.2 fusion.80
  89.0 0.2 convolution_add_fusion.5
  89.2 0.2 fusion.79
  89.6 0.2 convolution_add_fusion.7
  89.8 0.2 fusion.46
  90.0 0.2 convolution_add_fusion.4
  90.3 0.2 fusion.52
  90.6 0.2 fusion.4
  91.9 0.2 fusion.23
  92.2 0.8 copy.68
  93.0 10.9 %all-to-all-done.4 = f32[8,2,128,64]{2,3,1,0:T(8,128)S(1)} async-done(((f32[8,2,128,64]{2,3,1,0:T(8,128)}), f32[8,2,128,64]{2,3,1,0:T(8,128)S(1)}, u32[]{:S(2)}, u32[]{:S(2)}) %all-to-all-start.4) | async-done | bytes 524320 | tf_op jit(solution)/shard_map/all_to_all | solution.py:139
  104.0 3.5 %all-to-all-start.2 = ((f32[8,2,128,64]{2,3,1,0:T(8,128)}), f32[8,2,128,64]{2,3,1,0:T(8,128)S(1)}, u32[]{:S(2)}, u32[]{:S(2)}) async-start(f32[8,2,128,64]{2,3,1,0:T(8,128)} %copy.68), calls=%async_computation.2 | async-start | bytes 1048576 | tf_op jit(solution)/shard_map/all_to_all | solution.py:139
  107.5 0.9 copy.78
  108.4 14.3 %all-to-all-done.2 = f32[8,2,128,64]{2,3,1,0:T(8,128)S(1)} async-done(((f32[8,2,128,64]{2,3,1,0:T(8,128)}), f32[8,2,128,64]{2,3,1,0:T(8,128)S(1)}, u32[]{:S(2)}, u32[]{:S(2)}) %all-to-all-start.2) | async-done | bytes 524320 | tf_op jit(solution)/shard_map/all_to_all | solution.py:139
  123.0 0.9 copy.79
  123.8 0.9 copy.80
  124.7 1.0 copy.81
  (129 shorter events, 8.5 us)
Async XLA Ops:
  0.6 17.6 %copy-start.20 = (bf16[128,1024]{1,0:T(8,128)(2,1)S(1)}, bf16[128,1024]{1,0:T(8,128)(2,1)}, u32[]{:S(2)}) copy-start(bf16[128,1024]{1,0:T(8,128)(2,1)} %param.31) | copy-start | bytes 786436
  0.6 9.6 %copy-start.19 = (bf16[128,1024]{1,0:T(8,128)(2,1)S(1)}, bf16[128,1024]{1,0:T(8,128)(2,1)}, u32[]{:S(2)}) copy-start(bf16[128,1024]{1,0:T(8,128)(2,1)} %param.29) | copy-start | bytes 786436
  0.7 11.0 %collective-permute-start.2 = (bf16[128,1024]{1,0:T(8,128)(2,1)}, bf16[128,1024]{1,0:T(8,128)(2,1)S(1)}, u32[]{:S(2)}, u32[]{:S(2)}) collective-permute-start(bf16[128,1024]{1,0:T(8,128)(2,1)} %param.31), channel_id=1, source_target_pairs={{0,3},{1,0},{2,1},{3,2},{4,7},{5,4},{6,5},{7,6},{8,11},{9,8},{10,9... | collective-permute-start | bytes 786440 | tf_op jit(solution)/shard_map/ppermute | solution.py:25
  4.6 13.6 %collective-permute-start.1 = (bf16[128,1024]{1,0:T(8,128)(2,1)}, bf16[128,1024]{1,0:T(8,128)(2,1)S(1)}, u32[]{:S(2)}, u32[]{:S(2)}) collective-permute-start(bf16[128,1024]{1,0:T(8,128)(2,1)} %param.31), channel_id=1, source_target_pairs={{0,2},{1,3},{2,0},{3,1},{4,6},{5,7},{6,4},{7,5},{8,10},{9,11},{10,... | collective-permute-start | bytes 786440 | tf_op jit(solution)/shard_map/ppermute | solution.py:25
  5.1 13.1 %collective-permute-start = (bf16[128,1024]{1,0:T(8,128)(2,1)}, bf16[128,1024]{1,0:T(8,128)(2,1)S(1)}, u32[]{:S(2)}, u32[]{:S(2)}) collective-permute-start(bf16[128,1024]{1,0:T(8,128)(2,1)} %param.31), channel_id=1, source_target_pairs={{0,1},{1,2},{2,3},{3,0},{4,5},{5,6},{6,7},{7,4},{8,9},{9,10},{10,1... | collective-permute-start | bytes 786440 | tf_op jit(solution)/shard_map/ppermute | solution.py:25
  27.0 14.6 %all-to-all-start.3 = ((bf16[8,2,128,64]{2,3,1,0:T(8,128)(2,1)}), bf16[8,2,128,64]{2,3,1,0:T(8,128)(2,1)S(1)}, u32[]{:S(2)}, u32[]{:S(2)}) async-start(bf16[8,2,128,64]{2,3,1,0:T(8,128)(2,1)} %copy.72), calls=%async_computation.3 | async-start | bytes 524288 | tf_op jit(solution)/shard_map/all_to_all | solution.py:139
  31.9 14.0 %copy-start.27 = (bf16[128,1,1]{0,1,2:T(2,128)(2,1)S(1)}, bf16[128,1,1]{0,1,2:T(2,128)(2,1)}, u32[]{:S(2)}) copy-start(bf16[128,1,1]{0,1,2:T(2,128)(2,1)} %constant.145) | copy-start | bytes 772
  32.1 26.5 %copy-start = (bf16[128,128,1]{1,0,2:T(8,128)(2,1)S(1)}, bf16[128,128,1]{1,0,2:T(8,128)(2,1)}, u32[]{:S(2)}) copy-start(bf16[128,128,1]{1,0,2:T(8,128)(2,1)} %constant.137) | copy-start | bytes 98308
  32.8 26.2 %copy-start.2 = (bf16[128,128,1]{1,0,2:T(8,128)(2,1)S(1)}, bf16[128,128,1]{1,0,2:T(8,128)(2,1)}, u32[]{:S(2)}) copy-start(bf16[128,128,1]{1,0,2:T(8,128)(2,1)} %constant.138) | copy-start | bytes 98308
  41.6 13.1 %all-to-all-start.1 = ((bf16[8,2,128,64]{2,3,1,0:T(8,128)(2,1)}), bf16[8,2,128,64]{2,3,1,0:T(8,128)(2,1)S(1)}, u32[]{:S(2)}, u32[]{:S(2)}) async-start(bf16[8,2,128,64]{2,3,1,0:T(8,128)(2,1)} %copy.64), calls=%async_computation.1 | async-start | bytes 524288 | tf_op jit(solution)/shard_map/all_to_all | solution.py:139
  45.9 13.5 %copy-start.1 = (bf16[128,128,1]{1,0,2:T(8,128)(2,1)S(1)}, bf16[128,128,1]{1,0,2:T(8,128)(2,1)}, u32[]{:S(2)}) copy-start(bf16[128,128,1]{1,0,2:T(8,128)(2,1)} %constant.139) | copy-start | bytes 98308
  46.1 13.5 %copy-start.3 = (bf16[128,128,1]{1,0,2:T(8,128)(2,1)S(1)}, bf16[128,128,1]{1,0,2:T(8,128)(2,1)}, u32[]{:S(2)}) copy-start(bf16[128,128,1]{1,0,2:T(8,128)(2,1)} %constant.140) | copy-start | bytes 98308
  54.7 18.8 %all-to-all-start = ((bf16[8,2,2,128,64]{3,4,2,1,0:T(8,128)(2,1)}), bf16[8,2,2,128,64]{3,4,2,1,0:T(8,128)(2,1)S(1)}, u32[]{:S(2)}, u32[]{:S(2)}) async-start(bf16[8,2,2,128,64]{3,4,2,1,0:T(8,128)(2,1)} %copy.60), calls=%async_computation | async-start | bytes 1048576 | tf_op jit(solution)/shard_map/all_to_all | solution.py:139
  79.0 2.1 %copy-start.8 = (bf16[256,128,1]{1,0,2:T(8,128)(2,1)S(1)}, bf16[256,128,1]{1,0,2:T(8,128)(2,1)}, u32[]{:S(2)}) copy-start(bf16[256,128,1]{1,0,2:T(8,128)(2,1)} %constant.148) | copy-start | bytes 196612
  79.1 2.3 %copy-start.17 = (bf16[256,128,1]{1,0,2:T(8,128)(2,1)S(1)}, bf16[256,128,1]{1,0,2:T(8,128)(2,1)}, u32[]{:S(2)}) copy-start(bf16[256,128,1]{1,0,2:T(8,128)(2,1)} %constant.149) | copy-start | bytes 196612
  81.0 1.0 copy-start.7
  81.2 1.0 copy-start.15
  81.7 1.0 copy-start.25
  82.2 0.9 copy-start.13
  82.4 0.8 copy-start.23
  82.9 0.8 copy-start.11
  83.0 0.9 copy-start.21
  83.0 1.1 copy-start.26
  84.3 4.7 %copy-start.18 = (bf16[256,128,1]{1,0,2:T(8,128)(2,1)S(1)}, bf16[256,128,1]{1,0,2:T(8,128)(2,1)}, u32[]{:S(2)}) copy-start(bf16[256,128,1]{1,0,2:T(8,128)(2,1)} %constant.149) | copy-start | bytes 196612
  85.2 18.8 %all-to-all-start.4 = ((f32[8,2,128,64]{2,3,1,0:T(8,128)}), f32[8,2,128,64]{2,3,1,0:T(8,128)S(1)}, u32[]{:S(2)}, u32[]{:S(2)}) async-start(f32[8,2,128,64]{2,3,1,0:T(8,128)} %copy.76), calls=%async_computation.4 | async-start | bytes 1048576 | tf_op jit(solution)/shard_map/all_to_all | solution.py:139
  88.7 0.8 copy-start.16
  88.7 1.3 %copy-start.6 = (f32[8,128,64]{1,2,0:T(8,128)S(1)}, f32[8,128,64]{1,2,0:T(8,128)}, u32[]{:S(2)}) copy-start(f32[8,128,64]{1,2,0:T(8,128)} %get-tuple-element.27) | copy-start | bytes 786436
  90.0 0.8 copy-start.14
  90.0 1.0 copy-start.24
  90.3 1.0 copy-start.12
  90.3 1.2 copy-start.22
  90.6 1.1 copy-start.5
  90.8 1.1 copy-start.4
  92.1 15.4 %copy-start.9 = (bf16[128,8,1,64]{0,3,1,2:T(8,128)(2,1)S(1)}, bf16[128,8,1,64]{0,3,1,2:T(8,128)(2,1)}, u32[]{:S(2)}) copy-start(bf16[128,8,1,64]{0,3,1,2:T(8,128)(2,1)} %get-tuple-element.70) | copy-start | bytes 393220
  92.1 15.4 %copy-start.10 = (bf16[128,8,1,64]{0,3,1,2:T(8,128)(2,1)S(1)}, bf16[128,8,1,64]{0,3,1,2:T(8,128)(2,1)}, u32[]{:S(2)}) copy-start(bf16[128,8,1,64]{0,3,1,2:T(8,128)(2,1)} %get-tuple-element.71) | copy-start | bytes 393220
  104.0 18.8 %all-to-all-start.2 = ((f32[8,2,128,64]{2,3,1,0:T(8,128)}), f32[8,2,128,64]{2,3,1,0:T(8,128)S(1)}, u32[]{:S(2)}, u32[]{:S(2)}) async-start(f32[8,2,128,64]{2,3,1,0:T(8,128)} %copy.68), calls=%async_computation.2 | async-start | bytes 1048576 | tf_op jit(solution)/shard_map/all_to_all | solution.py:139

commit v5 on v3

--- a/solution.py
+++ b/solution.py
@@ -149,7 +149,21 @@
 
 
 def transpose_ctx(stacked):
-    return lax.all_to_all(stacked, "ctx", 0, 0, tiled=True)
+    count = lax.axis_size("ctx")
+    me = lax.axis_index("ctx")
+    received = []
+    for shift in range(count):
+        chunk = lax.dynamic_index_in_dim(stacked, (me + shift) % count, 0, keepdims=False)
+        if shift:
+            chunk = lax.ppermute(chunk, "ctx", [(i, (i + shift) % count) for i in range(count)])
+        received.append(chunk)
+    received = jnp.stack(received)
+    return jnp.stack(
+        [
+            lax.dynamic_index_in_dim(received, (me - source) % count, 0, keepdims=False)
+            for source in range(count)
+        ]
+    )
 
 
 def body(q_proj, k_proj, v_proj, saved_conv, out_grad, out_weight, filter_taps):

time: 89.1 us -> 90.5 us (1.016)
  the two profiles are of different devices: /device:TPU:0 before, /device:TPU:9 now
where the time goes in v5:
time: 90.5 us; the launch traced here: 89.1 us
  starting transfers between devices  31.5 us (35%)
  waiting for transfers between devices  30.6 us (34%)
  matrix products  13.3 us (15%)
  local copies, waits for them, and re-layouts  6.86 us (8%)
  other arithmetic  5.24 us (6%)
  between operations  1.64 us (2%)
    ppermute x21, waiting for transfers between devices, transpose_ctx(): lax.ppermute(chunk, 'ctx', [(i, (i + shift) % count) for i in range(count)])  30.6 us
    ppermute x21, starting transfers between devices, transpose_ctx(): lax.ppermute(chunk, 'ctx', [(i, (i + shift) % count) for i in range(count)])  28.7 us
    dot_general x1, matrix products, gather_matmul(): lax.dot_general(gathered, out_weight, (((1,), (1,)), ((), ())), preferred...  6.3 us
    dot_general x26, matrix products, one(): jnp.einsum('kn,bnc->bkc', left, right, preferred_element_type=jnp.float32)  6.29 us
    unnamed x80, local copies, waits for them, and re-layouts  5.62 us
    ppermute x3, starting transfers between devices, gather_matmul(): lax.ppermute(out_grad, 'tp', [(i, (i + shift) % count) for i in range(cou...  2.76 us
  transfers between devices with their start and end apart: 24, of which 11 were waited for; matrix products, arithmetic and copies ran while one was open for 3% of the time, Pallas kernels for 0%

profile of v5, /device:TPU:9, one launch (start us, length us, event | category | flops | bytes accessed | tf_op | source)
XLA Modules:
  0.0 89.1 jit_solution(17759339268656822524)
XLA Ops:
  0.6 2.2 %collective-permute-start.2 = (bf16[128,1024]{1,0:T(8,128)(2,1)}, bf16[128,1024]{1,0:T(8,128)(2,1)S(1)}, u32[]{:S(2)}, u32[]{:S(2)}) collective-permute-start(bf16[128,1024]{1,0:T(8,128)(2,1)} %param.21), channel_id=1, source_target_pairs={{0,3},{1,0},{2,1},{3,2},{4,7},{5,4},{6,5},{7,6},{8,11},{9,8},{10,9... | collective-permute-start | bytes 786440 | tf_op jit(solution)/shard_map/ppermute | solution.py:25
  2.8 0.2 collective-permute-start.1
  3.1 0.3 collective-permute-start
  3.4 1.1 %copy.22 = bf16[128,1024]{0,1:T(8,128)(2,1)S(1)} copy(bf16[128,1024]{1,0:T(8,128)(2,1)} %param.23) | data formatting | bytes 524288 | tf_op args[6]
  4.5 1.1 %fusion.22 = bf16[128,1024]{1,0:T(8,128)(2,1)S(1)} fusion(bf16[128,1024]{1,0:T(8,128)(2,1)} %param.19, bf16[128,1024]{1,0:T(8,128)(2,1)} %param.18), kind=kLoop, calls=%fused_computation.104 | loop fusion | flops 524288 | bytes 786432 | tf_op jit(solution)/shard_map/convert_element_type | solution.py:173
  5.9 2.8 %collective-permute-start.3 = (bf16[2,128,128]{1,2,0:T(8,128)(2,1)S(1)}, bf16[2,128,128]{1,2,0:T(8,128)(2,1)S(1)}, u32[]{:S(2)}, u32[]{:S(2)}) collective-permute-start(bf16[2,128,128]{1,2,0:T(8,128)(2,1)S(1)} %get-tuple-element.76), channel_id=1, source_target_pairs={{0,4},{4,8},{8,12},{12,16},{16,20},{20,24},{24,28},{28,0},{1,5},{5... | collective-permute-start | bytes 196616 | tf_op jit(solution)/shard_map/ppermute | solution.py:158
  8.7 1.3 %collective-permute-start.4 = (bf16[2,128,128]{1,2,0:T(8,128)(2,1)S(1)}, bf16[2,128,128]{1,2,0:T(8,128)(2,1)S(1)}, u32[]{:S(2)}, u32[]{:S(2)}) collective-permute-start(bf16[2,128,128]{1,2,0:T(8,128)(2,1)S(1)} %get-tuple-element.77), channel_id=1, source_target_pairs={{0,8},{4,12},{8,16},{12,20},{16,24},{20,28},{24,0},{28,4},{1,9},{5... | collective-permute-start | bytes 196616 | tf_op jit(solution)/shard_map/ppermute | solution.py:158
  10.1 3.4 %collective-permute-start.5 = (bf16[2,128,128]{1,2,0:T(8,128)(2,1)S(1)}, bf16[2,128,128]{1,2,0:T(8,128)(2,1)S(1)}, u32[]{:S(2)}, u32[]{:S(2)}) collective-permute-start(bf16[2,128,128]{1,2,0:T(8,128)(2,1)S(1)} %get-tuple-element.78), channel_id=1, source_target_pairs={{0,12},{4,16},{8,20},{12,24},{16,28},{20,0},{24,4},{28,8},{1,13},{... | collective-permute-start | bytes 196616 | tf_op jit(solution)/shard_map/ppermute | solution.py:158
  13.5 1.0 %collective-permute-start.6 = (bf16[2,128,128]{1,2,0:T(8,128)(2,1)S(1)}, bf16[2,128,128]{1,2,0:T(8,128)(2,1)S(1)}, u32[]{:S(2)}, u32[]{:S(2)}) collective-permute-start(bf16[2,128,128]{1,2,0:T(8,128)(2,1)S(1)} %get-tuple-element.79), channel_id=1, source_target_pairs={{0,16},{4,20},{8,24},{12,28},{16,0},{20,4},{24,8},{28,12},{1,17},{... | collective-permute-start | bytes 196616 | tf_op jit(solution)/shard_map/ppermute | solution.py:158
  14.5 1.3 %collective-permute-done.5 = bf16[2,128,128]{1,2,0:T(8,128)(2,1)S(1)} collective-permute-done((bf16[2,128,128]{1,2,0:T(8,128)(2,1)S(1)}, bf16[2,128,128]{1,2,0:T(8,128)(2,1)S(1)}, u32[]{:S(2)}, u32[]{:S(2)}) %collective-permute-start.5) | collective-permute-done | bytes 65568 | tf_op jit(solution)/shard_map/ppermute | solution.py:158
  15.8 4.5 %collective-permute-start.7 = (bf16[2,128,128]{1,2,0:T(8,128)(2,1)S(1)}, bf16[2,128,128]{1,2,0:T(8,128)(2,1)S(1)}, u32[]{:S(2)}, u32[]{:S(2)}) collective-permute-start(bf16[2,128,128]{1,2,0:T(8,128)(2,1)S(1)} %get-tuple-element.81), channel_id=1, source_target_pairs={{0,20},{4,24},{8,28},{12,0},{16,4},{20,8},{24,12},{28,16},{1,21},{... | collective-permute-start | bytes 196616 | tf_op jit(solution)/shard_map/ppermute | solution.py:158
  20.3 1.2 %collective-permute-start.8 = (bf16[2,128,128]{1,2,0:T(8,128)(2,1)S(1)}, bf16[2,128,128]{1,2,0:T(8,128)(2,1)S(1)}, u32[]{:S(2)}, u32[]{:S(2)}) collective-permute-start(bf16[2,128,128]{1,2,0:T(8,128)(2,1)S(1)} %get-tuple-element.80), channel_id=1, source_target_pairs={{0,24},{4,28},{8,0},{12,4},{16,8},{20,12},{24,16},{28,20},{1,25},{... | collective-permute-start | bytes 196616 | tf_op jit(solution)/shard_map/ppermute | solution.py:158
  21.5 0.8 collective-permute-done.7
  22.3 1.1 %collective-permute-done.8 = bf16[2,128,128]{1,2,0:T(8,128)(2,1)S(1)} collective-permute-done((bf16[2,128,128]{1,2,0:T(8,128)(2,1)S(1)}, bf16[2,128,128]{1,2,0:T(8,128)(2,1)S(1)}, u32[]{:S(2)}, u32[]{:S(2)}) %collective-permute-start.8) | collective-permute-done | bytes 65568 | tf_op jit(solution)/shard_map/ppermute | solution.py:158
  23.5 2.5 %collective-permute-done.9 = bf16[2,128,128]{1,2,0:T(8,128)(2,1)S(1)} collective-permute-done((bf16[2,128,128]{1,2,0:T(8,128)(2,1)S(1)}, bf16[2,128,128]{1,2,0:T(8,128)(2,1)S(1)}, u32[]{:S(2)}, u32[]{:S(2)}) %collective-permute-start.9) | collective-permute-done | bytes 65568 | tf_op jit(solution)/shard_map/ppermute | solution.py:158
  26.4 0.7 copy-done.6
  27.1 6.3 %fusion.26 = (bf16[128,1024]{1,0:T(8,128)(2,1)S(1)}, f32[128,1024]{1,0:T(8,128)S(1)}) fusion(bf16[128,1024]{1,0:T(8,128)(2,1)S(1)} %copy-done.6, bf16[1024,4096]{1,0:T(8,128)(2,1)} %param.22, bf16[128,1024]{1,0:T(8,128)(2,1)S(1)} %get-tuple-element.27, bf16[128,1024]{1,0:T(8,128)(2,1)S(1)} %get-tuple-element.28, ...), kind=kOutput, calls=%fused_computation.122 | convolution fusion | flops 1078329344 | bytes 10485760 | tf_op jit(solution)/shard_map/dot_general | solution.py:33
  33.6 0.9 subtract_convert_fusion.4
  34.7 2.0 %collective-permute-start.11 = (bf16[2,128,128]{1,2,0:T(8,128)(2,1)S(1)}, bf16[2,128,128]{1,2,0:T(8,128)(2,1)S(1)}, u32[]{:S(2)}, u32[]{:S(2)}) collective-permute-start(bf16[2,128,128]{1,2,0:T(8,128)(2,1)S(1)} %get-tuple-element.67), channel_id=1, source_target_pairs={{0,8},{4,12},{8,16},{12,20},{16,24},{20,28},{24,0},{28,4},{1,9},{5... | collective-permute-start | bytes 196616 | tf_op jit(solution)/shard_map/ppermute | solution.py:158
  36.7 1.2 %collective-permute-start.12 = (bf16[2,128,128]{1,2,0:T(8,128)(2,1)S(1)}, bf16[2,128,128]{1,2,0:T(8,128)(2,1)S(1)}, u32[]{:S(2)}, u32[]{:S(2)}) collective-permute-start(bf16[2,128,128]{1,2,0:T(8,128)(2,1)S(1)} %get-tuple-element.68), channel_id=1, source_target_pairs={{0,12},{4,16},{8,20},{12,24},{16,28},{20,0},{24,4},{28,8},{1,13},{... | collective-permute-start | bytes 196616 | tf_op jit(solution)/shard_map/ppermute | solution.py:158
  37.9 1.8 %collective-permute-start.13 = (bf16[2,128,128]{1,2,0:T(8,128)(2,1)S(1)}, bf16[2,128,128]{1,2,0:T(8,128)(2,1)S(1)}, u32[]{:S(2)}, u32[]{:S(2)}) collective-permute-start(bf16[2,128,128]{1,2,0:T(8,128)(2,1)S(1)} %get-tuple-element.69), channel_id=1, source_target_pairs={{0,16},{4,20},{8,24},{12,28},{16,0},{20,4},{24,8},{28,12},{1,17},{... | collective-permute-start | bytes 196616 | tf_op jit(solution)/shard_map/ppermute | solution.py:158
  39.8 1.5 %collective-permute-start.15 = (bf16[2,128,128]{1,2,0:T(8,128)(2,1)S(1)}, bf16[2,128,128]{1,2,0:T(8,128)(2,1)S(1)}, u32[]{:S(2)}, u32[]{:S(2)}) collective-permute-start(bf16[2,128,128]{1,2,0:T(8,128)(2,1)S(1)} %get-tuple-element.70), channel_id=1, source_target_pairs={{0,24},{4,28},{8,0},{12,4},{16,8},{20,12},{24,16},{28,20},{1,25},{... | collective-permute-start | bytes 196616 | tf_op jit(solution)/shard_map/ppermute | solution.py:158
  41.3 0.8 collective-permute-start.16
  42.1 4.7 %collective-permute-done.13 = bf16[2,128,128]{1,2,0:T(8,128)(2,1)S(1)} collective-permute-done((bf16[2,128,128]{1,2,0:T(8,128)(2,1)S(1)}, bf16[2,128,128]{1,2,0:T(8,128)(2,1)S(1)}, u32[]{:S(2)}, u32[]{:S(2)}) %collective-permute-start.13) | collective-permute-done | bytes 65568 | tf_op jit(solution)/shard_map/ppermute | solution.py:158
  46.9 1.9 %collective-permute-done.15 = bf16[2,128,128]{1,2,0:T(8,128)(2,1)S(1)} collective-permute-done((bf16[2,128,128]{1,2,0:T(8,128)(2,1)S(1)}, bf16[2,128,128]{1,2,0:T(8,128)(2,1)S(1)}, u32[]{:S(2)}, u32[]{:S(2)}) %collective-permute-start.15) | collective-permute-done | bytes 65568 | tf_op jit(solution)/shard_map/ppermute | solution.py:158
  49.4 0.2 fusion.29
  50.0 0.2 fusion.32
  50.3 0.2 fusion.8
  50.5 0.2 fusion.6
  51.0 0.2 convolution_add_fusion.14
  51.3 0.2 fusion.7
  51.5 0.2 convolution_add_fusion.11
  51.7 0.2 fusion.5
  52.0 0.4 fusion.90
  52.4 0.4 fusion.89
  53.8 0.2 fusion.35
  54.0 0.2 fusion.36
  54.2 0.2 fusion.3
  54.5 0.2 fusion.4
  54.8 0.4 fusion.88
  55.3 0.4 fusion.87
  55.7 0.3 copy-done.9
  56.1 0.3 fusion.94
  56.4 0.3 convolution_add_fusion.3
  56.7 0.3 convolution_add_fusion.2
  57.2 0.3 fusion.95
  57.5 0.3 convolution_add_fusion.1
  57.9 0.3 fusion.2
  58.4 0.6 copy-done.12
  59.2 0.2 convolution_add_fusion.7
  59.5 0.2 convolution_add_fusion.6
  59.8 0.2 fusion.92
  60.2 0.3 fusion.12
  60.6 2.1 %collective-permute-start.18 = (f32[128,2,128]{0,2,1:T(8,128)S(1)}, f32[128,2,128]{0,2,1:T(8,128)S(1)}, u32[]{:S(2)}, u32[]{:S(2)}) collective-permute-start(f32[128,2,128]{0,2,1:T(8,128)S(1)} %get-tuple-element.21), channel_id=1, source_target_pairs={{0,8},{4,12},{8,16},{12,20},{16,24},{20,28},{24,0},{28,4},{1,9},{5... | collective-permute-start | bytes 393224 | tf_op jit(solution)/shard_map/ppermute | solution.py:158
  62.9 0.6 collective-permute-start.20
  63.6 2.1 %collective-permute-start.21 = (f32[128,2,128]{0,2,1:T(8,128)S(1)}, f32[128,2,128]{0,2,1:T(8,128)S(1)}, u32[]{:S(2)}, u32[]{:S(2)}) collective-permute-start(f32[128,2,128]{0,2,1:T(8,128)S(1)} %get-tuple-element.25), channel_id=1, source_target_pairs={{0,20},{4,24},{8,28},{12,0},{16,4},{20,8},{24,12},{28,16},{1,21},{... | collective-permute-start | bytes 393224 | tf_op jit(solution)/shard_map/ppermute | solution.py:158
  65.7 1.4 %collective-permute-start.22 = (f32[128,2,128]{0,2,1:T(8,128)S(1)}, f32[128,2,128]{0,2,1:T(8,128)S(1)}, u32[]{:S(2)}, u32[]{:S(2)}) collective-permute-start(f32[128,2,128]{0,2,1:T(8,128)S(1)} %get-tuple-element.24), channel_id=1, source_target_pairs={{0,24},{4,28},{8,0},{12,4},{16,8},{20,12},{24,16},{28,20},{1,25},{... | collective-permute-start | bytes 393224 | tf_op jit(solution)/shard_map/ppermute | solution.py:158
  67.1 0.8 collective-permute-start.23
  67.9 12.2 %collective-permute-done.19 = f32[128,2,128]{0,2,1:T(8,128)S(1)} collective-permute-done((f32[128,2,128]{0,2,1:T(8,128)S(1)}, f32[128,2,128]{0,2,1:T(8,128)S(1)}, u32[]{:S(2)}, u32[]{:S(2)}) %collective-permute-start.19) | collective-permute-done | bytes 131104 | tf_op jit(solution)/shard_map/ppermute | solution.py:158
  80.1 2.8 %collective-permute-done.20 = f32[128,2,128]{0,2,1:T(8,128)S(1)} collective-permute-done((f32[128,2,128]{0,2,1:T(8,128)S(1)}, f32[128,2,128]{0,2,1:T(8,128)S(1)}, u32[]{:S(2)}, u32[]{:S(2)}) %collective-permute-start.20) | collective-permute-done | bytes 131104 | tf_op jit(solution)/shard_map/ppermute | solution.py:158
  83.0 2.9 %collective-permute-done.22 = f32[128,2,128]{0,2,1:T(8,128)S(1)} collective-permute-done((f32[128,2,128]{0,2,1:T(8,128)S(1)}, f32[128,2,128]{0,2,1:T(8,128)S(1)}, u32[]{:S(2)}, u32[]{:S(2)}) %collective-permute-start.22) | collective-permute-done | bytes 131104 | tf_op jit(solution)/shard_map/ppermute | solution.py:158
  86.5 0.5 copy-done
  87.1 0.9 %fusion.21 = (bf16[128,1024]{1,0:T(8,128)(2,1)}, bf16[128,1024]{1,0:T(8,128)(2,1)}) fusion(f32[128,1024]{1,0:T(8,128)S(1)} %copy.25, bf16[128,1024]{1,0:T(8,128)(2,1)S(1)} %copy-done.1, bf16[128,1024]{1,0:T(8,128)(2,1)S(1)} %copy-done), kind=kLoop, calls=%fused_computation.103 | loop fusion | flops 786432 | bytes 1572864 | tf_op jit(solution)/shard_map/convert_element_type | solution.py:194
  88.1 1.0 %copy.27 = f32[128,1024]{1,0:T(8,128)} copy(f32[128,1024]{0,1:T(8,128)S(1)} %bitcast.346) | data formatting | bytes 1048576
  (136 shorter events, 5.4 us)
Async XLA Ops:
  0.6 25.4 %collective-permute-start.2 = (bf16[128,1024]{1,0:T(8,128)(2,1)}, bf16[128,1024]{1,0:T(8,128)(2,1)S(1)}, u32[]{:S(2)}, u32[]{:S(2)}) collective-permute-start(bf16[128,1024]{1,0:T(8,128)(2,1)} %param.21), channel_id=1, source_target_pairs={{0,3},{1,0},{2,1},{3,2},{4,7},{5,4},{6,5},{7,6},{8,11},{9,8},{10,9... | collective-permute-start | bytes 786440 | tf_op jit(solution)/shard_map/ppermute | solution.py:25
  2.8 23.2 %collective-permute-start.1 = (bf16[128,1024]{1,0:T(8,128)(2,1)}, bf16[128,1024]{1,0:T(8,128)(2,1)S(1)}, u32[]{:S(2)}, u32[]{:S(2)}) collective-permute-start(bf16[128,1024]{1,0:T(8,128)(2,1)} %param.21), channel_id=1, source_target_pairs={{0,2},{1,3},{2,0},{3,1},{4,6},{5,7},{6,4},{7,5},{8,10},{9,11},{10,... | collective-permute-start | bytes 786440 | tf_op jit(solution)/shard_map/ppermute | solution.py:25
  3.1 23.0 %collective-permute-start = (bf16[128,1024]{1,0:T(8,128)(2,1)}, bf16[128,1024]{1,0:T(8,128)(2,1)S(1)}, u32[]{:S(2)}, u32[]{:S(2)}) collective-permute-start(bf16[128,1024]{1,0:T(8,128)(2,1)} %param.21), channel_id=1, source_target_pairs={{0,1},{1,2},{2,3},{3,0},{4,5},{5,6},{6,7},{7,4},{8,9},{9,10},{10,1... | collective-permute-start | bytes 786440 | tf_op jit(solution)/shard_map/ppermute | solution.py:25
  4.5 21.6 %copy-start.8 = (bf16[128,1024]{1,0:T(8,128)(2,1)S(1)}, bf16[128,1024]{1,0:T(8,128)(2,1)}, u32[]{:S(2)}) copy-start(bf16[128,1024]{1,0:T(8,128)(2,1)} %param.21) | copy-start | bytes 786436
  5.9 4.1 %collective-permute-start.3 = (bf16[2,128,128]{1,2,0:T(8,128)(2,1)S(1)}, bf16[2,128,128]{1,2,0:T(8,128)(2,1)S(1)}, u32[]{:S(2)}, u32[]{:S(2)}) collective-permute-start(bf16[2,128,128]{1,2,0:T(8,128)(2,1)S(1)} %get-tuple-element.76), channel_id=1, source_target_pairs={{0,4},{4,8},{8,12},{12,16},{16,20},{20,24},{24,28},{28,0},{1,5},{5... | collective-permute-start | bytes 196616 | tf_op jit(solution)/shard_map/ppermute | solution.py:158
  8.7 4.8 %collective-permute-start.4 = (bf16[2,128,128]{1,2,0:T(8,128)(2,1)S(1)}, bf16[2,128,128]{1,2,0:T(8,128)(2,1)S(1)}, u32[]{:S(2)}, u32[]{:S(2)}) collective-permute-start(bf16[2,128,128]{1,2,0:T(8,128)(2,1)S(1)} %get-tuple-element.77), channel_id=1, source_target_pairs={{0,8},{4,12},{8,16},{12,20},{16,24},{20,28},{24,0},{28,4},{1,9},{5... | collective-permute-start | bytes 196616 | tf_op jit(solution)/shard_map/ppermute | solution.py:158
  10.1 5.8 %collective-permute-start.5 = (bf16[2,128,128]{1,2,0:T(8,128)(2,1)S(1)}, bf16[2,128,128]{1,2,0:T(8,128)(2,1)S(1)}, u32[]{:S(2)}, u32[]{:S(2)}) collective-permute-start(bf16[2,128,128]{1,2,0:T(8,128)(2,1)S(1)} %get-tuple-element.78), channel_id=1, source_target_pairs={{0,12},{4,16},{8,20},{12,24},{16,28},{20,0},{24,4},{28,8},{1,13},{... | collective-permute-start | bytes 196616 | tf_op jit(solution)/shard_map/ppermute | solution.py:158
  13.5 6.8 %collective-permute-start.6 = (bf16[2,128,128]{1,2,0:T(8,128)(2,1)S(1)}, bf16[2,128,128]{1,2,0:T(8,128)(2,1)S(1)}, u32[]{:S(2)}, u32[]{:S(2)}) collective-permute-start(bf16[2,128,128]{1,2,0:T(8,128)(2,1)S(1)} %get-tuple-element.79), channel_id=1, source_target_pairs={{0,16},{4,20},{8,24},{12,28},{16,0},{20,4},{24,8},{28,12},{1,17},{... | collective-permute-start | bytes 196616 | tf_op jit(solution)/shard_map/ppermute | solution.py:158
  15.8 6.5 %collective-permute-start.7 = (bf16[2,128,128]{1,2,0:T(8,128)(2,1)S(1)}, bf16[2,128,128]{1,2,0:T(8,128)(2,1)S(1)}, u32[]{:S(2)}, u32[]{:S(2)}) collective-permute-start(bf16[2,128,128]{1,2,0:T(8,128)(2,1)S(1)} %get-tuple-element.81), channel_id=1, source_target_pairs={{0,20},{4,24},{8,28},{12,0},{16,4},{20,8},{24,12},{28,16},{1,21},{... | collective-permute-start | bytes 196616 | tf_op jit(solution)/shard_map/ppermute | solution.py:158
  20.3 3.2 %collective-permute-start.8 = (bf16[2,128,128]{1,2,0:T(8,128)(2,1)S(1)}, bf16[2,128,128]{1,2,0:T(8,128)(2,1)S(1)}, u32[]{:S(2)}, u32[]{:S(2)}) collective-permute-start(bf16[2,128,128]{1,2,0:T(8,128)(2,1)S(1)} %get-tuple-element.80), channel_id=1, source_target_pairs={{0,24},{4,28},{8,0},{12,4},{16,8},{20,12},{24,16},{28,20},{1,25},{... | collective-permute-start | bytes 196616 | tf_op jit(solution)/shard_map/ppermute | solution.py:158
  22.3 3.7 %collective-permute-start.9 = (bf16[2,128,128]{1,2,0:T(8,128)(2,1)S(1)}, bf16[2,128,128]{1,2,0:T(8,128)(2,1)S(1)}, u32[]{:S(2)}, u32[]{:S(2)}) collective-permute-start(bf16[2,128,128]{1,2,0:T(8,128)(2,1)S(1)} %get-tuple-element.74), channel_id=1, source_target_pairs={{0,28},{4,0},{8,4},{12,8},{16,12},{20,16},{24,20},{28,24},{1,29},{... | collective-permute-start | bytes 196616 | tf_op jit(solution)/shard_map/ppermute | solution.py:158
  26.1 1.0 %copy-start.6 = (bf16[128,1024]{1,0:T(8,128)(2,1)S(1)}, bf16[128,1024]{1,0:T(8,128)(2,1)}, u32[]{:S(2)}) copy-start(bf16[128,1024]{1,0:T(8,128)(2,1)} %param.17) | copy-start | bytes 786436
  27.1 6.5 %copy-start.7 = (bf16[128,1024]{1,0:T(8,128)(2,1)S(1)}, bf16[128,1024]{1,0:T(8,128)(2,1)}, u32[]{:S(2)}) copy-start(bf16[128,1024]{1,0:T(8,128)(2,1)} %param.20) | copy-start | bytes 786436
  34.4 14.7 %copy-start.2 = (bf16[128,128,1]{1,0,2:T(8,128)(2,1)S(1)}, bf16[128,128,1]{1,0,2:T(8,128)(2,1)}, u32[]{:S(2)}) copy-start(bf16[128,128,1]{1,0,2:T(8,128)(2,1)} %constant.373) | copy-start | bytes 98308
  34.6 14.8 %copy-start.3 = (bf16[128,128,1]{1,0,2:T(8,128)(2,1)S(1)}, bf16[128,128,1]{1,0,2:T(8,128)(2,1)}, u32[]{:S(2)}) copy-start(bf16[128,128,1]{1,0,2:T(8,128)(2,1)} %constant.375) | copy-start | bytes 98308
  34.7 5.1 %collective-permute-start.10 = (bf16[2,128,128]{1,2,0:T(8,128)(2,1)S(1)}, bf16[2,128,128]{1,2,0:T(8,128)(2,1)S(1)}, u32[]{:S(2)}, u32[]{:S(2)}) collective-permute-start(bf16[2,128,128]{1,2,0:T(8,128)(2,1)S(1)} %get-tuple-element.66), channel_id=1, source_target_pairs={{0,4},{4,8},{8,12},{12,16},{16,20},{20,24},{24,28},{28,0},{1,5},{5... | collective-permute-start | bytes 196616 | tf_op jit(solution)/shard_map/ppermute | solution.py:158
  34.7 6.5 %collective-permute-start.11 = (bf16[2,128,128]{1,2,0:T(8,128)(2,1)S(1)}, bf16[2,128,128]{1,2,0:T(8,128)(2,1)S(1)}, u32[]{:S(2)}, u32[]{:S(2)}) collective-permute-start(bf16[2,128,128]{1,2,0:T(8,128)(2,1)S(1)} %get-tuple-element.67), channel_id=1, source_target_pairs={{0,8},{4,12},{8,16},{12,20},{16,24},{20,28},{24,0},{28,4},{1,9},{5... | collective-permute-start | bytes 196616 | tf_op jit(solution)/shard_map/ppermute | solution.py:158
  36.7 5.4 %collective-permute-start.12 = (bf16[2,128,128]{1,2,0:T(8,128)(2,1)S(1)}, bf16[2,128,128]{1,2,0:T(8,128)(2,1)S(1)}, u32[]{:S(2)}, u32[]{:S(2)}) collective-permute-start(bf16[2,128,128]{1,2,0:T(8,128)(2,1)S(1)} %get-tuple-element.68), channel_id=1, source_target_pairs={{0,12},{4,16},{8,20},{12,24},{16,28},{20,0},{24,4},{28,8},{1,13},{... | collective-permute-start | bytes 196616 | tf_op jit(solution)/shard_map/ppermute | solution.py:158
  37.9 8.9 %collective-permute-start.13 = (bf16[2,128,128]{1,2,0:T(8,128)(2,1)S(1)}, bf16[2,128,128]{1,2,0:T(8,128)(2,1)S(1)}, u32[]{:S(2)}, u32[]{:S(2)}) collective-permute-start(bf16[2,128,128]{1,2,0:T(8,128)(2,1)S(1)} %get-tuple-element.69), channel_id=1, source_target_pairs={{0,16},{4,20},{8,24},{12,28},{16,0},{20,4},{24,8},{28,12},{1,17},{... | collective-permute-start | bytes 196616 | tf_op jit(solution)/shard_map/ppermute | solution.py:158
  39.7 7.1 %collective-permute-start.14 = (bf16[2,128,128]{1,2,0:T(8,128)(2,1)S(1)}, bf16[2,128,128]{1,2,0:T(8,128)(2,1)S(1)}, u32[]{:S(2)}, u32[]{:S(2)}) collective-permute-start(bf16[2,128,128]{1,2,0:T(8,128)(2,1)S(1)} %get-tuple-element.71), channel_id=1, source_target_pairs={{0,20},{4,24},{8,28},{12,0},{16,4},{20,8},{24,12},{28,16},{1,21},{... | collective-permute-start | bytes 196616 | tf_op jit(solution)/shard_map/ppermute | solution.py:158
  39.8 9.0 %collective-permute-start.15 = (bf16[2,128,128]{1,2,0:T(8,128)(2,1)S(1)}, bf16[2,128,128]{1,2,0:T(8,128)(2,1)S(1)}, u32[]{:S(2)}, u32[]{:S(2)}) collective-permute-start(bf16[2,128,128]{1,2,0:T(8,128)(2,1)S(1)} %get-tuple-element.70), channel_id=1, source_target_pairs={{0,24},{4,28},{8,0},{12,4},{16,8},{20,12},{24,16},{28,20},{1,25},{... | collective-permute-start | bytes 196616 | tf_op jit(solution)/shard_map/ppermute | solution.py:158
  41.3 7.6 %collective-permute-start.16 = (bf16[2,128,128]{1,2,0:T(8,128)(2,1)S(1)}, bf16[2,128,128]{1,2,0:T(8,128)(2,1)S(1)}, u32[]{:S(2)}, u32[]{:S(2)}) collective-permute-start(bf16[2,128,128]{1,2,0:T(8,128)(2,1)S(1)} %get-tuple-element.64), channel_id=1, source_target_pairs={{0,28},{4,0},{8,4},{12,8},{16,12},{20,16},{24,20},{28,24},{1,29},{... | collective-permute-start | bytes 196616 | tf_op jit(solution)/shard_map/ppermute | solution.py:158
  49.1 1.1 %copy-start.4 = (bf16[128,128,1]{1,0,2:T(8,128)(2,1)S(1)}, bf16[128,128,1]{1,0,2:T(8,128)(2,1)}, u32[]{:S(2)}) copy-start(bf16[128,128,1]{1,0,2:T(8,128)(2,1)} %constant.374) | copy-start | bytes 98308
  49.7 0.8 copy-start.5
  52.4 0.7 copy-start.19
  55.2 0.8 copy-start.9
  55.2 1.1 %copy-start.14 = (bf16[256,128,1]{1,0,2:T(8,128)(2,1)S(1)}, bf16[256,128,1]{1,0,2:T(8,128)(2,1)}, u32[]{:S(2)}) copy-start(bf16[256,128,1]{1,0,2:T(8,128)(2,1)} %constant.383) | copy-start | bytes 196612
  56.4 0.8 copy-start.10
  56.7 0.9 copy-start.13
  57.2 0.7 copy-start.17
  58.2 0.8 copy-start.12
  58.2 1.0 %copy-start.16 = (bf16[128,128,1]{1,0,2:T(8,128)(2,1)S(1)}, bf16[128,128,1]{1,0,2:T(8,128)(2,1)}, u32[]{:S(2)}) copy-start(bf16[128,128,1]{1,0,2:T(8,128)(2,1)} %constant.380) | copy-start | bytes 98308
  59.0 0.8 copy-start.11
  59.2 0.8 copy-start.15
  59.5 0.7 copy-start.18
  60.6 5.1 %collective-permute-start.17 = (f32[128,2,128]{0,2,1:T(8,128)S(1)}, f32[128,2,128]{0,2,1:T(8,128)S(1)}, u32[]{:S(2)}, u32[]{:S(2)}) collective-permute-start(f32[128,2,128]{0,2,1:T(8,128)S(1)} %get-tuple-element.20), channel_id=1, source_target_pairs={{0,4},{4,8},{8,12},{12,16},{16,20},{20,24},{24,28},{28,0},{1,5},{5... | collective-permute-start | bytes 393224 | tf_op jit(solution)/shard_map/ppermute | solution.py:158
  60.6 6.5 %collective-permute-start.18 = (f32[128,2,128]{0,2,1:T(8,128)S(1)}, f32[128,2,128]{0,2,1:T(8,128)S(1)}, u32[]{:S(2)}, u32[]{:S(2)}) collective-permute-start(f32[128,2,128]{0,2,1:T(8,128)S(1)} %get-tuple-element.21), channel_id=1, source_target_pairs={{0,8},{4,12},{8,16},{12,20},{16,24},{20,28},{24,0},{28,4},{1,9},{5... | collective-permute-start | bytes 393224 | tf_op jit(solution)/shard_map/ppermute | solution.py:158
  62.7 17.4 %collective-permute-start.19 = (f32[128,2,128]{0,2,1:T(8,128)S(1)}, f32[128,2,128]{0,2,1:T(8,128)S(1)}, u32[]{:S(2)}, u32[]{:S(2)}) collective-permute-start(f32[128,2,128]{0,2,1:T(8,128)S(1)} %get-tuple-element.22), channel_id=1, source_target_pairs={{0,12},{4,16},{8,20},{12,24},{16,28},{20,0},{24,4},{28,8},{1,13},{... | collective-permute-start | bytes 393224 | tf_op jit(solution)/shard_map/ppermute | solution.py:158
  62.9 20.0 %collective-permute-start.20 = (f32[128,2,128]{0,2,1:T(8,128)S(1)}, f32[128,2,128]{0,2,1:T(8,128)S(1)}, u32[]{:S(2)}, u32[]{:S(2)}) collective-permute-start(f32[128,2,128]{0,2,1:T(8,128)S(1)} %get-tuple-element.23), channel_id=1, source_target_pairs={{0,16},{4,20},{8,24},{12,28},{16,0},{20,4},{24,8},{28,12},{1,17},{... | collective-permute-start | bytes 393224 | tf_op jit(solution)/shard_map/ppermute | solution.py:158
  63.6 19.3 %collective-permute-start.21 = (f32[128,2,128]{0,2,1:T(8,128)S(1)}, f32[128,2,128]{0,2,1:T(8,128)S(1)}, u32[]{:S(2)}, u32[]{:S(2)}) collective-permute-start(f32[128,2,128]{0,2,1:T(8,128)S(1)} %get-tuple-element.25), channel_id=1, source_target_pairs={{0,20},{4,24},{8,28},{12,0},{16,4},{20,8},{24,12},{28,16},{1,21},{... | collective-permute-start | bytes 393224 | tf_op jit(solution)/shard_map/ppermute | solution.py:158
  65.7 20.2 %collective-permute-start.22 = (f32[128,2,128]{0,2,1:T(8,128)S(1)}, f32[128,2,128]{0,2,1:T(8,128)S(1)}, u32[]{:S(2)}, u32[]{:S(2)}) collective-permute-start(f32[128,2,128]{0,2,1:T(8,128)S(1)} %get-tuple-element.24), channel_id=1, source_target_pairs={{0,24},{4,28},{8,0},{12,4},{16,8},{20,12},{24,16},{28,20},{1,25},{... | collective-permute-start | bytes 393224 | tf_op jit(solution)/shard_map/ppermute | solution.py:158
  67.1 18.9 %collective-permute-start.23 = (f32[128,2,128]{0,2,1:T(8,128)S(1)}, f32[128,2,128]{0,2,1:T(8,128)S(1)}, u32[]{:S(2)}, u32[]{:S(2)}) collective-permute-start(f32[128,2,128]{0,2,1:T(8,128)S(1)} %get-tuple-element.18), channel_id=1, source_target_pairs={{0,28},{4,0},{8,4},{12,8},{16,12},{20,16},{24,20},{28,24},{1,29},{... | collective-permute-start | bytes 393224 | tf_op jit(solution)/shard_map/ppermute | solution.py:158
  86.1 1.0 %copy-start = (bf16[128,1024]{1,0:T(8,128)(2,1)S(1)}, bf16[128,1024]{1,0:T(8,128)(2,1)}, u32[]{:S(2)}) copy-start(bf16[128,1024]{1,0:T(8,128)(2,1)} %param.19) | copy-start | bytes 786436
  86.1 1.0 %copy-start.1 = (bf16[128,1024]{1,0:T(8,128)(2,1)S(1)}, bf16[128,1024]{1,0:T(8,128)(2,1)}, u32[]{:S(2)}) copy-start(bf16[128,1024]{1,0:T(8,128)(2,1)} %param.18) | copy-start | bytes 786436

commit v6 on v5

--- a/solution.py
+++ b/solution.py
@@ -16,7 +16,7 @@
     return upper, lower
 
 
-def gather_matmul(out_grad, out_weight):
+def gather_tp(out_grad):
     count = lax.axis_size("tp")
     me = lax.axis_index("tp")
     pieces = [out_grad]
@@ -29,10 +29,7 @@
         lax.dynamic_index_in_dim(stacked, (me - source) % count, 0, keepdims=False)
         for source in range(count)
     ]
-    gathered = jnp.concatenate(ordered, axis=1)
-    return lax.dot_general(
-        gathered, out_weight, (((1,), (1,)), ((), ())), preferred_element_type=jnp.float32
-    )
+    return jnp.concatenate(ordered, axis=1)
 
 
 def split_constant(table):
@@ -171,10 +168,13 @@
     blocks = lax.axis_size("ctx")
     seq = rows * blocks
     gated = (k_proj.astype(jnp.float32) * v_proj.astype(jnp.float32)).astype(jnp.bfloat16)
-    inputs_t = transpose_ctx(
-        jnp.stack([to_groups(gated, blocks), to_groups(filter_taps, blocks)], axis=1)
-    )
-    d_gated = gather_matmul(out_grad, out_weight)
+    inputs = jnp.stack([to_groups(gated, blocks), to_groups(filter_taps, blocks)], axis=1)
+    gathered = gather_tp(out_grad)
+    gathered, inputs = lax.optimization_barrier((gathered, inputs))
+    inputs_t = transpose_ctx(inputs)
+    d_gated = lax.dot_general(
+        gathered, out_weight, (((1,), (1,)), ((), ())), preferred_element_type=jnp.float32
+    )
     dq_grad = (d_gated * saved_conv.astype(jnp.float32)).astype(jnp.bfloat16)
     dz = d_gated * q_proj.astype(jnp.float32)
     dz_hi, dz_lo = split_bf16(dz)

time: 90.5 us -> 92 us (1.017); the launches traced: 89.1 us -> 91.5 us
  waiting for transfers between devices: 30.6 us -> 35.1 us
  starting transfers between devices: 31.5 us -> 28.8 us
    ppermute x3, waiting for transfers between devices: 0.01 us -> 8.44 us  [gather_tp(): lax.ppermute(out_grad, 'tp', [(i, (i + shift) % count) for i in range(cou...]
    ppermute x21, waiting for transfers between devices: 30.6 us -> 26.6 us  [transpose_ctx(): lax.ppermute(chunk, 'ctx', [(i, (i + shift) % count) for i in range(count)])]
    ppermute x21, starting transfers between devices: 28.7 us -> 26 us  [transpose_ctx(): lax.ppermute(chunk, 'ctx', [(i, (i + shift) % count) for i in range(count)])]
  transfers between devices with their start and end apart: 24 -> 24, of which waited for: 11 -> 12; matrix products, arithmetic and copies ran while one was open for 3% -> 4% of each run, Pallas kernels for 0% -> 0%
where the time goes in v6:
time: 92 us; the launch traced here: 91.5 us
  waiting for transfers between devices  35.1 us (38%)
  starting transfers between devices  28.8 us (31%)
  matrix products  13.4 us (15%)
  local copies, waits for them, and re-layouts  6.99 us (8%)
  other arithmetic  5.27 us (6%)
  between operations  1.97 us (2%)
    ppermute x21, waiting for transfers between devices, transpose_ctx(): lax.ppermute(chunk, 'ctx', [(i, (i + shift) % count) for i in range(count)])  26.6 us
    ppermute x21, starting transfers between devices, transpose_ctx(): lax.ppermute(chunk, 'ctx', [(i, (i + shift) % count) for i in range(count)])  26 us
    ppermute x3, waiting for transfers between devices, gather_tp(): lax.ppermute(out_grad, 'tp', [(i, (i + shift) % count) for i in range(cou...  8.44 us
    dot_general x1, matrix products, body(): lax.dot_general(gathered, out_weight, (((1,), (1,)), ((), ())), preferred...  6.37 us
    dot_general x26, matrix products, one(): jnp.einsum('kn,bnc->bkc', left, right, preferred_element_type=jnp.float32)  6.33 us
    unnamed x80, local copies, waits for them, and re-layouts  5.72 us
    ppermute x3, starting transfers between devices, gather_tp(): lax.ppermute(out_grad, 'tp', [(i, (i + shift) % count) for i in range(cou...  2.76 us
  transfers between devices with their start and end apart: 24, of which 12 were waited for; matrix products, arithmetic and copies ran while one was open for 4% of the time, Pallas kernels for 0%

profile of v6, /device:TPU:9, one launch (start us, length us, event | category | flops | bytes accessed | tf_op | source)
XLA Modules:
  0.0 91.5 jit_solution(6214928795536919203)
XLA Ops:
  0.6 2.2 %collective-permute-start.2 = (bf16[128,1024]{1,0:T(8,128)(2,1)}, bf16[128,1024]{1,0:T(8,128)(2,1)S(1)}, u32[]{:S(2)}, u32[]{:S(2)}) collective-permute-start(bf16[128,1024]{1,0:T(8,128)(2,1)} %param.21), channel_id=1, source_target_pairs={{0,3},{1,0},{2,1},{3,2},{4,7},{5,4},{6,5},{7,6},{8,11},{9,8},{10,9... | collective-permute-start | bytes 786440 | tf_op jit(solution)/shard_map/ppermute | solution.py:25
  2.9 0.2 collective-permute-start.1
  3.1 0.3 collective-permute-start
  3.4 1.1 %fusion.14 = bf16[128,1024]{1,0:T(8,128)(2,1)S(1)} fusion(bf16[128,1024]{1,0:T(8,128)(2,1)} %param.19, bf16[128,1024]{1,0:T(8,128)(2,1)} %param.18), kind=kLoop, calls=%fused_computation.81 | loop fusion | flops 524288 | bytes 786432 | tf_op jit(solution)/shard_map/convert_element_type | solution.py:170
  4.8 1.1 %copy.22 = bf16[128,1024]{0,1:T(8,128)(2,1)S(1)} copy(bf16[128,1024]{1,0:T(8,128)(2,1)} %param.23) | data formatting | bytes 524288 | tf_op args[6]
  6.3 2.0 %collective-permute-done.2 = bf16[128,1024]{1,0:T(8,128)(2,1)S(1)} collective-permute-done((bf16[128,1024]{1,0:T(8,128)(2,1)}, bf16[128,1024]{1,0:T(8,128)(2,1)S(1)}, u32[]{:S(2)}, u32[]{:S(2)}) %collective-permute-start.2) | collective-permute-done | bytes 262176 | tf_op jit(solution)/shard_map/ppermute | solution.py:25
  8.3 2.6 %collective-permute-done.1 = bf16[128,1024]{1,0:T(8,128)(2,1)S(1)} collective-permute-done((bf16[128,1024]{1,0:T(8,128)(2,1)}, bf16[128,1024]{1,0:T(8,128)(2,1)S(1)}, u32[]{:S(2)}, u32[]{:S(2)}) %collective-permute-start.1) | collective-permute-done | bytes 262176 | tf_op jit(solution)/shard_map/ppermute | solution.py:25
  10.9 3.8 %collective-permute-done = bf16[128,1024]{1,0:T(8,128)(2,1)S(1)} collective-permute-done((bf16[128,1024]{1,0:T(8,128)(2,1)}, bf16[128,1024]{1,0:T(8,128)(2,1)S(1)}, u32[]{:S(2)}, u32[]{:S(2)}) %collective-permute-start) | collective-permute-done | bytes 262176 | tf_op jit(solution)/shard_map/ppermute | solution.py:25
  15.0 0.8 copy-done
  15.8 6.4 %fusion.18 = (bf16[128,1024]{1,0:T(8,128)(2,1)S(1)}, f32[128,1024]{1,0:T(8,128)S(1)}) fusion(bf16[128,1024]{1,0:T(8,128)(2,1)S(1)} %copy-done, bf16[128,4096]{1,0:T(8,128)(2,1)S(1)} %pad_maximum_fusion.1, bf16[1024,4096]{1,0:T(8,128)(2,1)} %param.22), kind=kOutput, calls=%fused_computation.100 | convolution fusion | flops 1074135040 | bytes 10485760 | tf_op jit(solution)/shard_map/dot_general | solution.py:175
  22.3 3.9 %collective-permute-start.3 = (bf16[2,128,128]{1,2,0:T(8,128)(2,1)S(1)}, bf16[2,128,128]{1,2,0:T(8,128)(2,1)S(1)}, u32[]{:S(2)}, u32[]{:S(2)}) collective-permute-start(bf16[2,128,128]{1,2,0:T(8,128)(2,1)S(1)} %get-tuple-element.84), channel_id=1, source_target_pairs={{0,4},{4,8},{8,12},{12,16},{16,20},{20,24},{24,28},{28,0},{1,5},{5... | collective-permute-start | bytes 196616 | tf_op jit(solution)/shard_map/ppermute | solution.py:155
  26.2 1.3 %collective-permute-start.4 = (bf16[2,128,128]{1,2,0:T(8,128)(2,1)S(1)}, bf16[2,128,128]{1,2,0:T(8,128)(2,1)S(1)}, u32[]{:S(2)}, u32[]{:S(2)}) collective-permute-start(bf16[2,128,128]{1,2,0:T(8,128)(2,1)S(1)} %get-tuple-element.83), channel_id=1, source_target_pairs={{0,8},{4,12},{8,16},{12,20},{16,24},{20,28},{24,0},{28,4},{1,9},{5... | collective-permute-start | bytes 196616 | tf_op jit(solution)/shard_map/ppermute | solution.py:155
  27.5 1.4 %collective-permute-start.6 = (bf16[2,128,128]{1,2,0:T(8,128)(2,1)S(1)}, bf16[2,128,128]{1,2,0:T(8,128)(2,1)S(1)}, u32[]{:S(2)}, u32[]{:S(2)}) collective-permute-start(bf16[2,128,128]{1,2,0:T(8,128)(2,1)S(1)} %get-tuple-element.81), channel_id=1, source_target_pairs={{0,16},{4,20},{8,24},{12,28},{16,0},{20,4},{24,8},{28,12},{1,17},{... | collective-permute-start | bytes 196616 | tf_op jit(solution)/shard_map/ppermute | solution.py:155
  28.9 1.6 %collective-permute-start.7 = (bf16[2,128,128]{1,2,0:T(8,128)(2,1)S(1)}, bf16[2,128,128]{1,2,0:T(8,128)(2,1)S(1)}, u32[]{:S(2)}, u32[]{:S(2)}) collective-permute-start(bf16[2,128,128]{1,2,0:T(8,128)(2,1)S(1)} %get-tuple-element.80), channel_id=1, source_target_pairs={{0,20},{4,24},{8,28},{12,0},{16,4},{20,8},{24,12},{28,16},{1,21},{... | collective-permute-start | bytes 196616 | tf_op jit(solution)/shard_map/ppermute | solution.py:155
  30.6 0.9 subtract_convert_fusion.4
  31.8 1.2 %collective-permute-start.8 = (bf16[2,128,128]{1,2,0:T(8,128)(2,1)S(1)}, bf16[2,128,128]{1,2,0:T(8,128)(2,1)S(1)}, u32[]{:S(2)}, u32[]{:S(2)}) collective-permute-start(bf16[2,128,128]{1,2,0:T(8,128)(2,1)S(1)} %get-tuple-element.79), channel_id=1, source_target_pairs={{0,24},{4,28},{8,0},{12,4},{16,8},{20,12},{24,16},{28,20},{1,25},{... | collective-permute-start | bytes 196616 | tf_op jit(solution)/shard_map/ppermute | solution.py:155
  33.0 0.5 collective-permute-start.9
  33.5 0.3 collective-permute-done.5
  33.8 1.1 %collective-permute-start.10 = (bf16[2,128,128]{1,2,0:T(8,128)(2,1)S(1)}, bf16[2,128,128]{1,2,0:T(8,128)(2,1)S(1)}, u32[]{:S(2)}, u32[]{:S(2)}) collective-permute-start(bf16[2,128,128]{1,2,0:T(8,128)(2,1)S(1)} %get-tuple-element.70), channel_id=1, source_target_pairs={{0,4},{4,8},{8,12},{12,16},{16,20},{20,24},{24,28},{28,0},{1,5},{5... | collective-permute-start | bytes 196616 | tf_op jit(solution)/shard_map/ppermute | solution.py:155
  34.9 1.7 %collective-permute-done.6 = bf16[2,128,128]{1,2,0:T(8,128)(2,1)S(1)} collective-permute-done((bf16[2,128,128]{1,2,0:T(8,128)(2,1)S(1)}, bf16[2,128,128]{1,2,0:T(8,128)(2,1)S(1)}, u32[]{:S(2)}, u32[]{:S(2)}) %collective-permute-start.6) | collective-permute-done | bytes 65568 | tf_op jit(solution)/shard_map/ppermute | solution.py:155
  36.6 1.1 %collective-permute-start.11 = (bf16[2,128,128]{1,2,0:T(8,128)(2,1)S(1)}, bf16[2,128,128]{1,2,0:T(8,128)(2,1)S(1)}, u32[]{:S(2)}, u32[]{:S(2)}) collective-permute-start(bf16[2,128,128]{1,2,0:T(8,128)(2,1)S(1)} %get-tuple-element.71), channel_id=1, source_target_pairs={{0,8},{4,12},{8,16},{12,20},{16,24},{20,28},{24,0},{28,4},{1,9},{5... | collective-permute-start | bytes 196616 | tf_op jit(solution)/shard_map/ppermute | solution.py:155
  37.7 2.0 %collective-permute-start.12 = (bf16[2,128,128]{1,2,0:T(8,128)(2,1)S(1)}, bf16[2,128,128]{1,2,0:T(8,128)(2,1)S(1)}, u32[]{:S(2)}, u32[]{:S(2)}) collective-permute-start(bf16[2,128,128]{1,2,0:T(8,128)(2,1)S(1)} %get-tuple-element.72), channel_id=1, source_target_pairs={{0,12},{4,16},{8,20},{12,24},{16,28},{20,0},{24,4},{28,8},{1,13},{... | collective-permute-start | bytes 196616 | tf_op jit(solution)/shard_map/ppermute | solution.py:155
  39.8 1.5 %collective-permute-start.13 = (bf16[2,128,128]{1,2,0:T(8,128)(2,1)S(1)}, bf16[2,128,128]{1,2,0:T(8,128)(2,1)S(1)}, u32[]{:S(2)}, u32[]{:S(2)}) collective-permute-start(bf16[2,128,128]{1,2,0:T(8,128)(2,1)S(1)} %get-tuple-element.73), channel_id=1, source_target_pairs={{0,16},{4,20},{8,24},{12,28},{16,0},{20,4},{24,8},{28,12},{1,17},{... | collective-permute-start | bytes 196616 | tf_op jit(solution)/shard_map/ppermute | solution.py:155
  41.3 2.1 %collective-permute-start.14 = (bf16[2,128,128]{1,2,0:T(8,128)(2,1)S(1)}, bf16[2,128,128]{1,2,0:T(8,128)(2,1)S(1)}, u32[]{:S(2)}, u32[]{:S(2)}) collective-permute-start(bf16[2,128,128]{1,2,0:T(8,128)(2,1)S(1)} %get-tuple-element.75), channel_id=1, source_target_pairs={{0,20},{4,24},{8,28},{12,0},{16,4},{20,8},{24,12},{28,16},{1,21},{... | collective-permute-start | bytes 196616 | tf_op jit(solution)/shard_map/ppermute | solution.py:155
  43.4 1.4 %collective-permute-start.15 = (bf16[2,128,128]{1,2,0:T(8,128)(2,1)S(1)}, bf16[2,128,128]{1,2,0:T(8,128)(2,1)S(1)}, u32[]{:S(2)}, u32[]{:S(2)}) collective-permute-start(bf16[2,128,128]{1,2,0:T(8,128)(2,1)S(1)} %get-tuple-element.74), channel_id=1, source_target_pairs={{0,24},{4,28},{8,0},{12,4},{16,8},{20,12},{24,16},{28,20},{1,25},{... | collective-permute-start | bytes 196616 | tf_op jit(solution)/shard_map/ppermute | solution.py:155
  45.0 3.7 %collective-permute-done.13 = bf16[2,128,128]{1,2,0:T(8,128)(2,1)S(1)} collective-permute-done((bf16[2,128,128]{1,2,0:T(8,128)(2,1)S(1)}, bf16[2,128,128]{1,2,0:T(8,128)(2,1)S(1)}, u32[]{:S(2)}, u32[]{:S(2)}) %collective-permute-start.13) | collective-permute-done | bytes 65568 | tf_op jit(solution)/shard_map/ppermute | solution.py:155
  48.7 2.6 %collective-permute-done.15 = bf16[2,128,128]{1,2,0:T(8,128)(2,1)S(1)} collective-permute-done((bf16[2,128,128]{1,2,0:T(8,128)(2,1)S(1)}, bf16[2,128,128]{1,2,0:T(8,128)(2,1)S(1)}, u32[]{:S(2)}, u32[]{:S(2)}) %collective-permute-start.15) | collective-permute-done | bytes 65568 | tf_op jit(solution)/shard_map/ppermute | solution.py:155
  51.7 0.2 fusion.22
  52.6 0.2 fusion.24
  52.8 0.2 fusion.8
  53.1 0.2 fusion.6
  54.3 0.2 fusion.5
  54.5 0.4 fusion.66
  55.0 0.4 fusion.65
  56.3 0.2 fusion.27
  56.6 0.2 fusion.28
  56.8 0.2 fusion.3
  57.1 0.2 fusion.4
  57.4 0.4 fusion.64
  57.8 0.4 fusion.63
  58.3 0.3 copy-done.9
  58.7 0.3 fusion.70
  59.0 0.3 convolution_add_fusion.3
  59.3 0.3 convolution_add_fusion.2
  59.8 0.3 fusion.71
  60.1 0.3 convolution_add_fusion.1
  60.5 0.3 fusion.2
  60.9 0.6 copy-done.12
  61.6 0.2 fusion.69
  61.8 0.2 convolution_add_fusion.7
  62.1 0.2 convolution_add_fusion.6
  62.8 0.3 fusion.12
  63.2 1.6 %collective-permute-start.18 = (f32[128,2,128]{0,2,1:T(8,128)S(1)}, f32[128,2,128]{0,2,1:T(8,128)S(1)}, u32[]{:S(2)}, u32[]{:S(2)}) collective-permute-start(f32[128,2,128]{0,2,1:T(8,128)S(1)} %get-tuple-element.25), channel_id=1, source_target_pairs={{0,8},{4,12},{8,16},{12,20},{16,24},{20,28},{24,0},{28,4},{1,9},{5... | collective-permute-start | bytes 393224 | tf_op jit(solution)/shard_map/ppermute | solution.py:155
  64.8 0.9 %collective-permute-start.19 = (f32[128,2,128]{0,2,1:T(8,128)S(1)}, f32[128,2,128]{0,2,1:T(8,128)S(1)}, u32[]{:S(2)}, u32[]{:S(2)}) collective-permute-start(f32[128,2,128]{0,2,1:T(8,128)S(1)} %get-tuple-element.26), channel_id=1, source_target_pairs={{0,12},{4,16},{8,20},{12,24},{16,28},{20,0},{24,4},{28,8},{1,13},{... | collective-permute-start | bytes 393224 | tf_op jit(solution)/shard_map/ppermute | solution.py:155
  65.8 0.3 collective-permute-start.20
  66.1 2.1 %collective-permute-start.21 = (f32[128,2,128]{0,2,1:T(8,128)S(1)}, f32[128,2,128]{0,2,1:T(8,128)S(1)}, u32[]{:S(2)}, u32[]{:S(2)}) collective-permute-start(f32[128,2,128]{0,2,1:T(8,128)S(1)} %get-tuple-element.29), channel_id=1, source_target_pairs={{0,20},{4,24},{8,28},{12,0},{16,4},{20,8},{24,12},{28,16},{1,21},{... | collective-permute-start | bytes 393224 | tf_op jit(solution)/shard_map/ppermute | solution.py:155
  68.2 1.3 %collective-permute-start.22 = (f32[128,2,128]{0,2,1:T(8,128)S(1)}, f32[128,2,128]{0,2,1:T(8,128)S(1)}, u32[]{:S(2)}, u32[]{:S(2)}) collective-permute-start(f32[128,2,128]{0,2,1:T(8,128)S(1)} %get-tuple-element.28), channel_id=1, source_target_pairs={{0,24},{4,28},{8,0},{12,4},{16,8},{20,12},{24,16},{28,20},{1,25},{... | collective-permute-start | bytes 393224 | tf_op jit(solution)/shard_map/ppermute | solution.py:155
  69.5 0.6 collective-permute-start.23
  70.1 12.6 %collective-permute-done.19 = f32[128,2,128]{0,2,1:T(8,128)S(1)} collective-permute-done((f32[128,2,128]{0,2,1:T(8,128)S(1)}, f32[128,2,128]{0,2,1:T(8,128)S(1)}, u32[]{:S(2)}, u32[]{:S(2)}) %collective-permute-start.19) | collective-permute-done | bytes 131104 | tf_op jit(solution)/shard_map/ppermute | solution.py:155
  82.7 2.8 %collective-permute-done.20 = f32[128,2,128]{0,2,1:T(8,128)S(1)} collective-permute-done((f32[128,2,128]{0,2,1:T(8,128)S(1)}, f32[128,2,128]{0,2,1:T(8,128)S(1)}, u32[]{:S(2)}, u32[]{:S(2)}) %collective-permute-start.20) | collective-permute-done | bytes 131104 | tf_op jit(solution)/shard_map/ppermute | solution.py:155
  85.6 2.8 %collective-permute-done.22 = f32[128,2,128]{0,2,1:T(8,128)S(1)} collective-permute-done((f32[128,2,128]{0,2,1:T(8,128)S(1)}, f32[128,2,128]{0,2,1:T(8,128)S(1)}, u32[]{:S(2)}, u32[]{:S(2)}) %collective-permute-start.22) | collective-permute-done | bytes 131104 | tf_op jit(solution)/shard_map/ppermute | solution.py:155
  88.9 0.5 copy-done.1
  89.6 0.9 %fusion.13 = (bf16[128,1024]{1,0:T(8,128)(2,1)}, bf16[128,1024]{1,0:T(8,128)(2,1)}) fusion(f32[128,1024]{1,0:T(8,128)S(1)} %copy.25, bf16[128,1024]{1,0:T(8,128)(2,1)S(1)} %copy-done.2, bf16[128,1024]{1,0:T(8,128)(2,1)S(1)} %copy-done.1), kind=kLoop, calls=%fused_computation.80 | loop fusion | flops 786432 | bytes 1572864 | tf_op jit(solution)/shard_map/convert_element_type | solution.py:194
  90.5 1.0 %copy.27 = f32[128,1024]{1,0:T(8,128)} copy(f32[128,1024]{0,1:T(8,128)S(1)} %bitcast.343) | data formatting | bytes 1048576
  (137 shorter events, 5.8 us)
Async XLA Ops:
  0.6 14.1 %copy-start.8 = (bf16[128,1024]{1,0:T(8,128)(2,1)S(1)}, bf16[128,1024]{1,0:T(8,128)(2,1)}, u32[]{:S(2)}) copy-start(bf16[128,1024]{1,0:T(8,128)(2,1)} %param.21) | copy-start | bytes 786436
  0.6 7.6 %collective-permute-start.2 = (bf16[128,1024]{1,0:T(8,128)(2,1)}, bf16[128,1024]{1,0:T(8,128)(2,1)S(1)}, u32[]{:S(2)}, u32[]{:S(2)}) collective-permute-start(bf16[128,1024]{1,0:T(8,128)(2,1)} %param.21), channel_id=1, source_target_pairs={{0,3},{1,0},{2,1},{3,2},{4,7},{5,4},{6,5},{7,6},{8,11},{9,8},{10,9... | collective-permute-start | bytes 786440 | tf_op jit(solution)/shard_map/ppermute | solution.py:25
  2.9 8.0 %collective-permute-start.1 = (bf16[128,1024]{1,0:T(8,128)(2,1)}, bf16[128,1024]{1,0:T(8,128)(2,1)S(1)}, u32[]{:S(2)}, u32[]{:S(2)}) collective-permute-start(bf16[128,1024]{1,0:T(8,128)(2,1)} %param.21), channel_id=1, source_target_pairs={{0,2},{1,3},{2,0},{3,1},{4,6},{5,7},{6,4},{7,5},{8,10},{9,11},{10,... | collective-permute-start | bytes 786440 | tf_op jit(solution)/shard_map/ppermute | solution.py:25
  3.1 11.6 %collective-permute-start = (bf16[128,1024]{1,0:T(8,128)(2,1)}, bf16[128,1024]{1,0:T(8,128)(2,1)S(1)}, u32[]{:S(2)}, u32[]{:S(2)}) collective-permute-start(bf16[128,1024]{1,0:T(8,128)(2,1)} %param.21), channel_id=1, source_target_pairs={{0,1},{1,2},{2,3},{3,0},{4,5},{5,6},{6,7},{7,4},{8,9},{9,10},{10,1... | collective-permute-start | bytes 786440 | tf_op jit(solution)/shard_map/ppermute | solution.py:25
  14.9 1.0 %copy-start = (bf16[128,1024]{1,0:T(8,128)(2,1)S(1)}, bf16[128,1024]{1,0:T(8,128)(2,1)}, u32[]{:S(2)}) copy-start(bf16[128,1024]{1,0:T(8,128)(2,1)} %param.17) | copy-start | bytes 786436
  15.8 14.8 %copy-start.7 = (bf16[128,1024]{1,0:T(8,128)(2,1)S(1)}, bf16[128,1024]{1,0:T(8,128)(2,1)}, u32[]{:S(2)}) copy-start(bf16[128,1024]{1,0:T(8,128)(2,1)} %param.20) | copy-start | bytes 786436
  22.3 9.6 %collective-permute-start.3 = (bf16[2,128,128]{1,2,0:T(8,128)(2,1)S(1)}, bf16[2,128,128]{1,2,0:T(8,128)(2,1)S(1)}, u32[]{:S(2)}, u32[]{:S(2)}) collective-permute-start(bf16[2,128,128]{1,2,0:T(8,128)(2,1)S(1)} %get-tuple-element.84), channel_id=1, source_target_pairs={{0,4},{4,8},{8,12},{12,16},{16,20},{20,24},{24,28},{28,0},{1,5},{5... | collective-permute-start | bytes 196616 | tf_op jit(solution)/shard_map/ppermute | solution.py:155
  26.2 6.8 %collective-permute-start.4 = (bf16[2,128,128]{1,2,0:T(8,128)(2,1)S(1)}, bf16[2,128,128]{1,2,0:T(8,128)(2,1)S(1)}, u32[]{:S(2)}, u32[]{:S(2)}) collective-permute-start(bf16[2,128,128]{1,2,0:T(8,128)(2,1)S(1)} %get-tuple-element.83), channel_id=1, source_target_pairs={{0,8},{4,12},{8,16},{12,20},{16,24},{20,28},{24,0},{28,4},{1,9},{5... | collective-permute-start | bytes 196616 | tf_op jit(solution)/shard_map/ppermute | solution.py:155
  27.5 6.3 %collective-permute-start.5 = (bf16[2,128,128]{1,2,0:T(8,128)(2,1)S(1)}, bf16[2,128,128]{1,2,0:T(8,128)(2,1)S(1)}, u32[]{:S(2)}, u32[]{:S(2)}) collective-permute-start(bf16[2,128,128]{1,2,0:T(8,128)(2,1)S(1)} %get-tuple-element.82), channel_id=1, source_target_pairs={{0,12},{4,16},{8,20},{12,24},{16,28},{20,0},{24,4},{28,8},{1,13},{... | collective-permute-start | bytes 196616 | tf_op jit(solution)/shard_map/ppermute | solution.py:155
  27.5 9.1 %collective-permute-start.6 = (bf16[2,128,128]{1,2,0:T(8,128)(2,1)S(1)}, bf16[2,128,128]{1,2,0:T(8,128)(2,1)S(1)}, u32[]{:S(2)}, u32[]{:S(2)}) collective-permute-start(bf16[2,128,128]{1,2,0:T(8,128)(2,1)S(1)} %get-tuple-element.81), channel_id=1, source_target_pairs={{0,16},{4,20},{8,24},{12,28},{16,0},{20,4},{24,8},{28,12},{1,17},{... | collective-permute-start | bytes 196616 | tf_op jit(solution)/shard_map/ppermute | solution.py:155
  28.9 8.8 %collective-permute-start.7 = (bf16[2,128,128]{1,2,0:T(8,128)(2,1)S(1)}, bf16[2,128,128]{1,2,0:T(8,128)(2,1)S(1)}, u32[]{:S(2)}, u32[]{:S(2)}) collective-permute-start(bf16[2,128,128]{1,2,0:T(8,128)(2,1)S(1)} %get-tuple-element.80), channel_id=1, source_target_pairs={{0,20},{4,24},{8,28},{12,0},{16,4},{20,8},{24,12},{28,16},{1,21},{... | collective-permute-start | bytes 196616 | tf_op jit(solution)/shard_map/ppermute | solution.py:155
  31.7 20.0 %copy-start.3 = (bf16[128,128,1]{1,0,2:T(8,128)(2,1)S(1)}, bf16[128,128,1]{1,0,2:T(8,128)(2,1)}, u32[]{:S(2)}) copy-start(bf16[128,128,1]{1,0,2:T(8,128)(2,1)} %constant.373) | copy-start | bytes 98308
  31.8 20.2 %copy-start.4 = (bf16[128,128,1]{1,0,2:T(8,128)(2,1)S(1)}, bf16[128,128,1]{1,0,2:T(8,128)(2,1)}, u32[]{:S(2)}) copy-start(bf16[128,128,1]{1,0,2:T(8,128)(2,1)} %constant.375) | copy-start | bytes 98308
  31.8 7.9 %collective-permute-start.8 = (bf16[2,128,128]{1,2,0:T(8,128)(2,1)S(1)}, bf16[2,128,128]{1,2,0:T(8,128)(2,1)S(1)}, u32[]{:S(2)}, u32[]{:S(2)}) collective-permute-start(bf16[2,128,128]{1,2,0:T(8,128)(2,1)S(1)} %get-tuple-element.79), channel_id=1, source_target_pairs={{0,24},{4,28},{8,0},{12,4},{16,8},{20,12},{24,16},{28,20},{1,25},{... | collective-permute-start | bytes 196616 | tf_op jit(solution)/shard_map/ppermute | solution.py:155
  33.0 8.3 %collective-permute-start.9 = (bf16[2,128,128]{1,2,0:T(8,128)(2,1)S(1)}, bf16[2,128,128]{1,2,0:T(8,128)(2,1)S(1)}, u32[]{:S(2)}, u32[]{:S(2)}) collective-permute-start(bf16[2,128,128]{1,2,0:T(8,128)(2,1)S(1)} %get-tuple-element.78), channel_id=1, source_target_pairs={{0,28},{4,0},{8,4},{12,8},{16,12},{20,16},{24,20},{28,24},{1,29},{... | collective-permute-start | bytes 196616 | tf_op jit(solution)/shard_map/ppermute | solution.py:155
  33.8 9.6 %collective-permute-start.10 = (bf16[2,128,128]{1,2,0:T(8,128)(2,1)S(1)}, bf16[2,128,128]{1,2,0:T(8,128)(2,1)S(1)}, u32[]{:S(2)}, u32[]{:S(2)}) collective-permute-start(bf16[2,128,128]{1,2,0:T(8,128)(2,1)S(1)} %get-tuple-element.70), channel_id=1, source_target_pairs={{0,4},{4,8},{8,12},{12,16},{16,20},{20,24},{24,28},{28,0},{1,5},{5... | collective-permute-start | bytes 196616 | tf_op jit(solution)/shard_map/ppermute | solution.py:155
  36.6 8.2 %collective-permute-start.11 = (bf16[2,128,128]{1,2,0:T(8,128)(2,1)S(1)}, bf16[2,128,128]{1,2,0:T(8,128)(2,1)S(1)}, u32[]{:S(2)}, u32[]{:S(2)}) collective-permute-start(bf16[2,128,128]{1,2,0:T(8,128)(2,1)S(1)} %get-tuple-element.71), channel_id=1, source_target_pairs={{0,8},{4,12},{8,16},{12,20},{16,24},{20,28},{24,0},{28,4},{1,9},{5... | collective-permute-start | bytes 196616 | tf_op jit(solution)/shard_map/ppermute | solution.py:155
  37.7 7.2 %collective-permute-start.12 = (bf16[2,128,128]{1,2,0:T(8,128)(2,1)S(1)}, bf16[2,128,128]{1,2,0:T(8,128)(2,1)S(1)}, u32[]{:S(2)}, u32[]{:S(2)}) collective-permute-start(bf16[2,128,128]{1,2,0:T(8,128)(2,1)S(1)} %get-tuple-element.72), channel_id=1, source_target_pairs={{0,12},{4,16},{8,20},{12,24},{16,28},{20,0},{24,4},{28,8},{1,13},{... | collective-permute-start | bytes 196616 | tf_op jit(solution)/shard_map/ppermute | solution.py:155
  39.8 8.9 %collective-permute-start.13 = (bf16[2,128,128]{1,2,0:T(8,128)(2,1)S(1)}, bf16[2,128,128]{1,2,0:T(8,128)(2,1)S(1)}, u32[]{:S(2)}, u32[]{:S(2)}) collective-permute-start(bf16[2,128,128]{1,2,0:T(8,128)(2,1)S(1)} %get-tuple-element.73), channel_id=1, source_target_pairs={{0,16},{4,20},{8,24},{12,28},{16,0},{20,4},{24,8},{28,12},{1,17},{... | collective-permute-start | bytes 196616 | tf_op jit(solution)/shard_map/ppermute | solution.py:155
  41.3 7.4 %collective-permute-start.14 = (bf16[2,128,128]{1,2,0:T(8,128)(2,1)S(1)}, bf16[2,128,128]{1,2,0:T(8,128)(2,1)S(1)}, u32[]{:S(2)}, u32[]{:S(2)}) collective-permute-start(bf16[2,128,128]{1,2,0:T(8,128)(2,1)S(1)} %get-tuple-element.75), channel_id=1, source_target_pairs={{0,20},{4,24},{8,28},{12,0},{16,4},{20,8},{24,12},{28,16},{1,21},{... | collective-permute-start | bytes 196616 | tf_op jit(solution)/shard_map/ppermute | solution.py:155
  43.4 7.9 %collective-permute-start.15 = (bf16[2,128,128]{1,2,0:T(8,128)(2,1)S(1)}, bf16[2,128,128]{1,2,0:T(8,128)(2,1)S(1)}, u32[]{:S(2)}, u32[]{:S(2)}) collective-permute-start(bf16[2,128,128]{1,2,0:T(8,128)(2,1)S(1)} %get-tuple-element.74), channel_id=1, source_target_pairs={{0,24},{4,28},{8,0},{12,4},{16,8},{20,12},{24,16},{28,20},{1,25},{... | collective-permute-start | bytes 196616 | tf_op jit(solution)/shard_map/ppermute | solution.py:155
  44.8 6.6 %collective-permute-start.16 = (bf16[2,128,128]{1,2,0:T(8,128)(2,1)S(1)}, bf16[2,128,128]{1,2,0:T(8,128)(2,1)S(1)}, u32[]{:S(2)}, u32[]{:S(2)}) collective-permute-start(bf16[2,128,128]{1,2,0:T(8,128)(2,1)S(1)} %get-tuple-element.68), channel_id=1, source_target_pairs={{0,28},{4,0},{8,4},{12,8},{16,12},{20,16},{24,20},{28,24},{1,29},{... | collective-permute-start | bytes 196616 | tf_op jit(solution)/shard_map/ppermute | solution.py:155
  51.6 1.1 %copy-start.5 = (bf16[128,128,1]{1,0,2:T(8,128)(2,1)S(1)}, bf16[128,128,1]{1,0,2:T(8,128)(2,1)}, u32[]{:S(2)}) copy-start(bf16[128,128,1]{1,0,2:T(8,128)(2,1)} %constant.374) | copy-start | bytes 98308
  52.3 0.8 copy-start.6
  55.0 0.7 copy-start.19
  57.8 0.8 copy-start.9
  57.8 1.1 %copy-start.14 = (bf16[256,128,1]{1,0,2:T(8,128)(2,1)S(1)}, bf16[256,128,1]{1,0,2:T(8,128)(2,1)}, u32[]{:S(2)}) copy-start(bf16[256,128,1]{1,0,2:T(8,128)(2,1)} %constant.383) | copy-start | bytes 196612
  59.0 0.8 copy-start.10
  59.3 0.9 copy-start.13
  59.8 0.7 copy-start.17
  60.8 0.8 copy-start.12
  60.8 1.0 %copy-start.16 = (bf16[128,128,1]{1,0,2:T(8,128)(2,1)S(1)}, bf16[128,128,1]{1,0,2:T(8,128)(2,1)}, u32[]{:S(2)}) copy-start(bf16[128,128,1]{1,0,2:T(8,128)(2,1)} %constant.380) | copy-start | bytes 98308
  61.6 0.8 copy-start.11
  61.8 0.8 copy-start.15
  62.1 0.7 copy-start.18
  63.2 5.0 %collective-permute-start.17 = (f32[128,2,128]{0,2,1:T(8,128)S(1)}, f32[128,2,128]{0,2,1:T(8,128)S(1)}, u32[]{:S(2)}, u32[]{:S(2)}) collective-permute-start(f32[128,2,128]{0,2,1:T(8,128)S(1)} %get-tuple-element.24), channel_id=1, source_target_pairs={{0,4},{4,8},{8,12},{12,16},{16,20},{20,24},{24,28},{28,0},{1,5},{5... | collective-permute-start | bytes 393224 | tf_op jit(solution)/shard_map/ppermute | solution.py:155
  63.2 6.2 %collective-permute-start.18 = (f32[128,2,128]{0,2,1:T(8,128)S(1)}, f32[128,2,128]{0,2,1:T(8,128)S(1)}, u32[]{:S(2)}, u32[]{:S(2)}) collective-permute-start(f32[128,2,128]{0,2,1:T(8,128)S(1)} %get-tuple-element.25), channel_id=1, source_target_pairs={{0,8},{4,12},{8,16},{12,20},{16,24},{20,28},{24,0},{28,4},{1,9},{5... | collective-permute-start | bytes 393224 | tf_op jit(solution)/shard_map/ppermute | solution.py:155
  64.8 17.9 %collective-permute-start.19 = (f32[128,2,128]{0,2,1:T(8,128)S(1)}, f32[128,2,128]{0,2,1:T(8,128)S(1)}, u32[]{:S(2)}, u32[]{:S(2)}) collective-permute-start(f32[128,2,128]{0,2,1:T(8,128)S(1)} %get-tuple-element.26), channel_id=1, source_target_pairs={{0,12},{4,16},{8,20},{12,24},{16,28},{20,0},{24,4},{28,8},{1,13},{... | collective-permute-start | bytes 393224 | tf_op jit(solution)/shard_map/ppermute | solution.py:155
  65.8 19.8 %collective-permute-start.20 = (f32[128,2,128]{0,2,1:T(8,128)S(1)}, f32[128,2,128]{0,2,1:T(8,128)S(1)}, u32[]{:S(2)}, u32[]{:S(2)}) collective-permute-start(f32[128,2,128]{0,2,1:T(8,128)S(1)} %get-tuple-element.27), channel_id=1, source_target_pairs={{0,16},{4,20},{8,24},{12,28},{16,0},{20,4},{24,8},{28,12},{1,17},{... | collective-permute-start | bytes 393224 | tf_op jit(solution)/shard_map/ppermute | solution.py:155
  66.1 19.4 %collective-permute-start.21 = (f32[128,2,128]{0,2,1:T(8,128)S(1)}, f32[128,2,128]{0,2,1:T(8,128)S(1)}, u32[]{:S(2)}, u32[]{:S(2)}) collective-permute-start(f32[128,2,128]{0,2,1:T(8,128)S(1)} %get-tuple-element.29), channel_id=1, source_target_pairs={{0,20},{4,24},{8,28},{12,0},{16,4},{20,8},{24,12},{28,16},{1,21},{... | collective-permute-start | bytes 393224 | tf_op jit(solution)/shard_map/ppermute | solution.py:155
  68.2 20.1 %collective-permute-start.22 = (f32[128,2,128]{0,2,1:T(8,128)S(1)}, f32[128,2,128]{0,2,1:T(8,128)S(1)}, u32[]{:S(2)}, u32[]{:S(2)}) collective-permute-start(f32[128,2,128]{0,2,1:T(8,128)S(1)} %get-tuple-element.28), channel_id=1, source_target_pairs={{0,24},{4,28},{8,0},{12,4},{16,8},{20,12},{24,16},{28,20},{1,25},{... | collective-permute-start | bytes 393224 | tf_op jit(solution)/shard_map/ppermute | solution.py:155
  69.5 18.9 %collective-permute-start.23 = (f32[128,2,128]{0,2,1:T(8,128)S(1)}, f32[128,2,128]{0,2,1:T(8,128)S(1)}, u32[]{:S(2)}, u32[]{:S(2)}) collective-permute-start(f32[128,2,128]{0,2,1:T(8,128)S(1)} %get-tuple-element.22), channel_id=1, source_target_pairs={{0,28},{4,0},{8,4},{12,8},{16,12},{20,16},{24,20},{28,24},{1,29},{... | collective-permute-start | bytes 393224 | tf_op jit(solution)/shard_map/ppermute | solution.py:155
  88.5 1.0 %copy-start.1 = (bf16[128,1024]{1,0:T(8,128)(2,1)S(1)}, bf16[128,1024]{1,0:T(8,128)(2,1)}, u32[]{:S(2)}) copy-start(bf16[128,1024]{1,0:T(8,128)(2,1)} %param.19) | copy-start | bytes 786436
  88.5 1.0 %copy-start.2 = (bf16[128,1024]{1,0:T(8,128)(2,1)S(1)}, bf16[128,1024]{1,0:T(8,128)(2,1)}, u32[]{:S(2)}) copy-start(bf16[128,1024]{1,0:T(8,128)(2,1)} %param.18) | copy-start | bytes 786436

commit v7 on v5

--- a/solution.py
+++ b/solution.py
@@ -16,17 +16,30 @@
     return upper, lower
 
 
+def partner_of(index, step, count):
+    if count & (count - 1) == 0:
+        return index ^ step
+    return (index + step) % count
+
+
+def source_of(index, step, count):
+    if count & (count - 1) == 0:
+        return index ^ step
+    return (index - step) % count
+
+
+def exchange(value, axis, step):
+    count = lax.axis_size(axis)
+    return lax.ppermute(value, axis, [(i, partner_of(i, step, count)) for i in range(count)])
+
+
 def gather_matmul(out_grad, out_weight):
     count = lax.axis_size("tp")
     me = lax.axis_index("tp")
-    pieces = [out_grad]
-    for shift in range(1, count):
-        pieces.append(
-            lax.ppermute(out_grad, "tp", [(i, (i + shift) % count) for i in range(count)])
-        )
+    pieces = [out_grad] + [exchange(out_grad, "tp", step) for step in range(1, count)]
     stacked = jnp.stack(pieces)
     ordered = [
-        lax.dynamic_index_in_dim(stacked, (me - source) % count, 0, keepdims=False)
+        lax.dynamic_index_in_dim(stacked, source_of(me, source, count), 0, keepdims=False)
         for source in range(count)
     ]
     gathered = jnp.concatenate(ordered, axis=1)
@@ -152,15 +165,15 @@
     count = lax.axis_size("ctx")
     me = lax.axis_index("ctx")
     received = []
-    for shift in range(count):
-        chunk = lax.dynamic_index_in_dim(stacked, (me + shift) % count, 0, keepdims=False)
-        if shift:
-            chunk = lax.ppermute(chunk, "ctx", [(i, (i + shift) % count) for i in range(count)])
+    for step in range(count):
+        chunk = lax.dynamic_index_in_dim(stacked, partner_of(me, step, count), 0, keepdims=False)
+        if step:
+            chunk = exchange(chunk, "ctx", step)
         received.append(chunk)
     received = jnp.stack(received)
     return jnp.stack(
         [
-            lax.dynamic_index_in_dim(received, (me - source) % count, 0, keepdims=False)
+            lax.dynamic_index_in_dim(received, source_of(me, source, count), 0, keepdims=False)
             for source in range(count)
         ]
     )

time: 90.5 us -> 94.4 us (1.043)
  waiting for transfers between devices: 30.6 us -> 35.8 us
  matrix products: 13.3 us -> 9.93 us
  local copies, waits for them, and re-layouts: 6.86 us -> 8.62 us
  other arithmetic: 5.24 us -> 6.24 us
    ppermute x24, waiting for transfers between devices: 30.6 us -> 35.8 us  [exchange(): lax.ppermute(value, axis, [(i, partner_of(i, step, count)) for i in range...]
    dot_general x1, matrix products: 6.3 us -> 2.87 us  [gather_matmul(): lax.dot_general(gathered, out_weight, (((1,), (1,)), ((), ())), preferred...]
    unnamed x80 -> x109, local copies, waits for them, and re-layouts: 5.62 us -> 6.76 us
    convert_element_type x1, other arithmetic: 0.88 us -> 1.91 us  [split_bf16(): lower = (value - upper.astype(jnp.float32)).astype(jnp.bfloat16)]
  transfers between devices with their start and end apart: 24 -> 24, of which waited for: 11 -> 15; matrix products, arithmetic and copies ran while one was open for 3% -> 6% of each run, Pallas kernels for 0% -> 0%
where the time goes in v7:
time: 94.4 us; the launch traced here: 93.8 us
  waiting for transfers between devices  35.8 us (38%)
  starting transfers between devices  31.6 us (33%)
  matrix products  9.93 us (11%)
  local copies, waits for them, and re-layouts  8.62 us (9%)
  other arithmetic  6.24 us (7%)
  between operations  1.68 us (2%)
    ppermute x24, waiting for transfers between devices, exchange(): lax.ppermute(value, axis, [(i, partner_of(i, step, count)) for i in range...  35.8 us
    ppermute x24, starting transfers between devices, exchange(): lax.ppermute(value, axis, [(i, partner_of(i, step, count)) for i in range...  31.6 us
    unnamed x109, local copies, waits for them, and re-layouts  6.76 us
    dot_general x26, matrix products, one(): jnp.einsum('kn,bnc->bkc', left, right, preferred_element_type=jnp.float32)  6.37 us
    dot_general x1, matrix products, gather_matmul(): lax.dot_general(gathered, out_weight, (((1,), (1,)), ((), ())), preferred...  2.87 us
    convert_element_type x1, other arithmetic, split_bf16(): lower = (value - upper.astype(jnp.float32)).astype(jnp.bfloat16)  1.91 us
  transfers between devices with their start and end apart: 24, of which 15 were waited for; matrix products, arithmetic and copies ran while one was open for 6% of the time, Pallas kernels for 0%

profile of v7, /device:TPU:9, one launch (start us, length us, event | category | flops | bytes accessed | tf_op | source)
XLA Modules:
  0.0 93.8 jit_solution(4181630913543503301)
XLA Ops:
  0.6 2.2 %collective-permute-start.2 = (bf16[128,1024]{1,0:T(8,128)(2,1)}, bf16[128,1024]{1,0:T(8,128)(2,1)S(1)}, u32[]{:S(2)}, u32[]{:S(2)}) collective-permute-start(bf16[128,1024]{1,0:T(8,128)(2,1)} %param.21), channel_id=1, source_target_pairs={{0,3},{1,2},{2,1},{3,0},{4,7},{5,6},{6,5},{7,4},{8,11},{9,10},{10,... | collective-permute-start | bytes 786440 | tf_op jit(solution)/shard_map/ppermute | solution.py:33
  2.9 0.2 collective-permute-start.1
  3.1 0.3 collective-permute-start
  3.3 1.1 %copy.22 = bf16[128,1024]{0,1:T(8,128)(2,1)S(1)} copy(bf16[128,1024]{1,0:T(8,128)(2,1)} %param.23) | data formatting | bytes 524288 | tf_op args[6]
  4.5 1.1 %fusion.22 = bf16[128,1024]{1,0:T(8,128)(2,1)S(1)} fusion(bf16[128,1024]{1,0:T(8,128)(2,1)} %param.19, bf16[128,1024]{1,0:T(8,128)(2,1)} %param.18), kind=kLoop, calls=%fused_computation.104 | loop fusion | flops 524288 | bytes 786432 | tf_op jit(solution)/shard_map/convert_element_type | solution.py:186
  5.9 1.6 %collective-permute-start.3 = (bf16[2,128,128]{1,2,0:T(8,128)(2,1)S(1)}, bf16[2,128,128]{1,2,0:T(8,128)(2,1)S(1)}, u32[]{:S(2)}, u32[]{:S(2)}) collective-permute-start(bf16[2,128,128]{1,2,0:T(8,128)(2,1)S(1)} %get-tuple-element.76), channel_id=1, source_target_pairs={{0,4},{4,0},{8,12},{12,8},{16,20},{20,16},{24,28},{28,24},{1,5},{5... | collective-permute-start | bytes 196616 | tf_op jit(solution)/shard_map/ppermute | solution.py:33
  7.5 0.9 collective-permute-done.3
  8.3 0.9 collective-permute-start.5
  9.3 1.7 %collective-permute-done.4 = bf16[2,128,128]{1,2,0:T(8,128)(2,1)S(1)} collective-permute-done((bf16[2,128,128]{1,2,0:T(8,128)(2,1)S(1)}, bf16[2,128,128]{1,2,0:T(8,128)(2,1)S(1)}, u32[]{:S(2)}, u32[]{:S(2)}) %collective-permute-start.4) | collective-permute-done | bytes 65568 | tf_op jit(solution)/shard_map/ppermute | solution.py:33
  11.0 2.3 %collective-permute-start.6 = (bf16[2,128,128]{1,2,0:T(8,128)(2,1)S(1)}, bf16[2,128,128]{1,2,0:T(8,128)(2,1)S(1)}, u32[]{:S(2)}, u32[]{:S(2)}) collective-permute-start(bf16[2,128,128]{1,2,0:T(8,128)(2,1)S(1)} %get-tuple-element.79), channel_id=1, source_target_pairs={{0,16},{4,20},{8,24},{12,28},{16,0},{20,4},{24,8},{28,12},{1,17},{... | collective-permute-start | bytes 196616 | tf_op jit(solution)/shard_map/ppermute | solution.py:33
  13.3 1.9 %collective-permute-start.7 = (bf16[2,128,128]{1,2,0:T(8,128)(2,1)S(1)}, bf16[2,128,128]{1,2,0:T(8,128)(2,1)S(1)}, u32[]{:S(2)}, u32[]{:S(2)}) collective-permute-start(bf16[2,128,128]{1,2,0:T(8,128)(2,1)S(1)} %get-tuple-element.81), channel_id=1, source_target_pairs={{0,20},{4,16},{8,28},{12,24},{16,4},{20,0},{24,12},{28,8},{1,21},{... | collective-permute-start | bytes 196616 | tf_op jit(solution)/shard_map/ppermute | solution.py:33
  15.3 1.1 %collective-permute-start.8 = (bf16[2,128,128]{1,2,0:T(8,128)(2,1)S(1)}, bf16[2,128,128]{1,2,0:T(8,128)(2,1)S(1)}, u32[]{:S(2)}, u32[]{:S(2)}) collective-permute-start(bf16[2,128,128]{1,2,0:T(8,128)(2,1)S(1)} %get-tuple-element.80), channel_id=1, source_target_pairs={{0,24},{4,28},{8,16},{12,20},{16,8},{20,12},{24,0},{28,4},{1,25},{... | collective-permute-start | bytes 196616 | tf_op jit(solution)/shard_map/ppermute | solution.py:33
  16.4 2.3 %collective-permute-done.7 = bf16[2,128,128]{1,2,0:T(8,128)(2,1)S(1)} collective-permute-done((bf16[2,128,128]{1,2,0:T(8,128)(2,1)S(1)}, bf16[2,128,128]{1,2,0:T(8,128)(2,1)S(1)}, u32[]{:S(2)}, u32[]{:S(2)}) %collective-permute-start.7) | collective-permute-done | bytes 65568 | tf_op jit(solution)/shard_map/ppermute | solution.py:33
  18.6 2.1 %collective-permute-start.9 = (bf16[2,128,128]{1,2,0:T(8,128)(2,1)S(1)}, bf16[2,128,128]{1,2,0:T(8,128)(2,1)S(1)}, u32[]{:S(2)}, u32[]{:S(2)}) collective-permute-start(bf16[2,128,128]{1,2,0:T(8,128)(2,1)S(1)} %get-tuple-element.74), channel_id=1, source_target_pairs={{0,28},{4,24},{8,20},{12,16},{16,12},{20,8},{24,4},{28,0},{1,29},{... | collective-permute-start | bytes 196616 | tf_op jit(solution)/shard_map/ppermute | solution.py:33
  20.9 2.7 %collective-permute-done.9 = bf16[2,128,128]{1,2,0:T(8,128)(2,1)S(1)} collective-permute-done((bf16[2,128,128]{1,2,0:T(8,128)(2,1)S(1)}, bf16[2,128,128]{1,2,0:T(8,128)(2,1)S(1)}, u32[]{:S(2)}, u32[]{:S(2)}) %collective-permute-start.9) | collective-permute-done | bytes 65568 | tf_op jit(solution)/shard_map/ppermute | solution.py:33
  24.2 0.2 fusion.29
  25.1 0.2 fusion.8
  25.7 0.2 fusion.3
  26.4 0.6 slice_bitcast_fusion.61
  27.2 0.4 copy-done.7
  27.9 1.3 %slice-done.1 = s8[4194304]{0:T(1024)(128)(4,1)S(1)} async-done(((s8[8388608]{0:T(1024)(128)(4,1)}), s8[4194304]{0:T(1024)(128)(4,1)S(1)}, s32[]{:S(2)}) %slice-start.1) | async-done | bytes 4194328
  29.2 2.9 %fusion.26 = (bf16[128,1024]{1,0:T(8,128)(2,1)S(1)}, f32[128,1024]{1,0:T(8,128)S(1)}) fusion(bf16[128,1024]{1,0:T(8,128)(2,1)S(1)} %copy-done.6, bf16[1024,4096]{1,0:T(8,128)(2,1)S(1)} %bitcast.358, bf16[128,1024]{1,0:T(8,128)(2,1)S(1)} %get-tuple-element.27, bf16[128,1024]{1,0:T(8,128)(2,1)S(1)} %get-tuple-element.28, ...), kind=kOutput, calls=%fused_computation.122 | convolution fusion | flops 1078329344 | bytes 10485760 | tf_op jit(solution)/shard_map/dot_general | solution.py:46
  32.3 1.9 %subtract_convert_fusion.4 = (bf16[128,1024]{1,0:T(8,128)(2,1)S(1)}, bf16[128,1024]{1,0:T(8,128)(2,1)}) fusion(bf16[128,1024]{1,0:T(8,128)(2,1)S(1)} %get-tuple-element.102, f32[128,1024]{1,0:T(8,128)S(1)} %get-tuple-element.103, bf16[128,1024]{1,0:T(8,128)(2,1)} %param.17, bf16[128,1024]{1,0:T(8,128)(2,1)} %param.20), kind=kLoop, calls=%fused_computation.118 | loop fusion | flops 1048576 | bytes 1835008 | tf_op jit(solution)/shard_map/convert_element_type | solution.py:15
  34.4 1.8 %collective-permute-start.10 = (bf16[2,128,128]{1,2,0:T(8,128)(2,1)S(1)}, bf16[2,128,128]{1,2,0:T(8,128)(2,1)S(1)}, u32[]{:S(2)}, u32[]{:S(2)}) collective-permute-start(bf16[2,128,128]{1,2,0:T(8,128)(2,1)S(1)} %get-tuple-element.66), channel_id=1, source_target_pairs={{0,4},{4,0},{8,12},{12,8},{16,20},{20,16},{24,28},{28,24},{1,5},{5... | collective-permute-start | bytes 196616 | tf_op jit(solution)/shard_map/ppermute | solution.py:33
  36.2 3.8 %collective-permute-start.11 = (bf16[2,128,128]{1,2,0:T(8,128)(2,1)S(1)}, bf16[2,128,128]{1,2,0:T(8,128)(2,1)S(1)}, u32[]{:S(2)}, u32[]{:S(2)}) collective-permute-start(bf16[2,128,128]{1,2,0:T(8,128)(2,1)S(1)} %get-tuple-element.67), channel_id=1, source_target_pairs={{0,8},{4,12},{8,0},{12,4},{16,24},{20,28},{24,16},{28,20},{1,9},{5... | collective-permute-start | bytes 196616 | tf_op jit(solution)/shard_map/ppermute | solution.py:33
  40.1 2.0 %collective-permute-start.13 = (bf16[2,128,128]{1,2,0:T(8,128)(2,1)S(1)}, bf16[2,128,128]{1,2,0:T(8,128)(2,1)S(1)}, u32[]{:S(2)}, u32[]{:S(2)}) collective-permute-start(bf16[2,128,128]{1,2,0:T(8,128)(2,1)S(1)} %get-tuple-element.69), channel_id=1, source_target_pairs={{0,16},{4,20},{8,24},{12,28},{16,0},{20,4},{24,8},{28,12},{1,17},{... | collective-permute-start | bytes 196616 | tf_op jit(solution)/shard_map/ppermute | solution.py:33
  42.0 1.0 %collective-permute-start.14 = (bf16[2,128,128]{1,2,0:T(8,128)(2,1)S(1)}, bf16[2,128,128]{1,2,0:T(8,128)(2,1)S(1)}, u32[]{:S(2)}, u32[]{:S(2)}) collective-permute-start(bf16[2,128,128]{1,2,0:T(8,128)(2,1)S(1)} %get-tuple-element.71), channel_id=1, source_target_pairs={{0,20},{4,16},{8,28},{12,24},{16,4},{20,0},{24,12},{28,8},{1,21},{... | collective-permute-start | bytes 196616 | tf_op jit(solution)/shard_map/ppermute | solution.py:33
  43.0 0.5 collective-permute-start.15
  43.6 1.0 %collective-permute-start.16 = (bf16[2,128,128]{1,2,0:T(8,128)(2,1)S(1)}, bf16[2,128,128]{1,2,0:T(8,128)(2,1)S(1)}, u32[]{:S(2)}, u32[]{:S(2)}) collective-permute-start(bf16[2,128,128]{1,2,0:T(8,128)(2,1)S(1)} %get-tuple-element.64), channel_id=1, source_target_pairs={{0,28},{4,24},{8,20},{12,16},{16,12},{20,8},{24,4},{28,0},{1,29},{... | collective-permute-start | bytes 196616 | tf_op jit(solution)/shard_map/ppermute | solution.py:33
  44.7 1.4 %collective-permute-done.13 = bf16[2,128,128]{1,2,0:T(8,128)(2,1)S(1)} collective-permute-done((bf16[2,128,128]{1,2,0:T(8,128)(2,1)S(1)}, bf16[2,128,128]{1,2,0:T(8,128)(2,1)S(1)}, u32[]{:S(2)}, u32[]{:S(2)}) %collective-permute-start.13) | collective-permute-done | bytes 65568 | tf_op jit(solution)/shard_map/ppermute | solution.py:33
  46.1 4.6 %collective-permute-done.14 = bf16[2,128,128]{1,2,0:T(8,128)(2,1)S(1)} collective-permute-done((bf16[2,128,128]{1,2,0:T(8,128)(2,1)S(1)}, bf16[2,128,128]{1,2,0:T(8,128)(2,1)S(1)}, u32[]{:S(2)}, u32[]{:S(2)}) %collective-permute-start.14) | collective-permute-done | bytes 65568 | tf_op jit(solution)/shard_map/ppermute | solution.py:33
  50.7 2.7 %collective-permute-done.15 = bf16[2,128,128]{1,2,0:T(8,128)(2,1)S(1)} collective-permute-done((bf16[2,128,128]{1,2,0:T(8,128)(2,1)S(1)}, bf16[2,128,128]{1,2,0:T(8,128)(2,1)S(1)}, u32[]{:S(2)}, u32[]{:S(2)}) %collective-permute-start.15) | collective-permute-done | bytes 65568 | tf_op jit(solution)/shard_map/ppermute | solution.py:33
  53.4 1.7 %collective-permute-done.16 = bf16[2,128,128]{1,2,0:T(8,128)(2,1)S(1)} collective-permute-done((bf16[2,128,128]{1,2,0:T(8,128)(2,1)S(1)}, bf16[2,128,128]{1,2,0:T(8,128)(2,1)S(1)}, u32[]{:S(2)}, u32[]{:S(2)}) %collective-permute-start.16) | collective-permute-done | bytes 65568 | tf_op jit(solution)/shard_map/ppermute | solution.py:33
  55.3 0.2 fusion.33
  55.8 0.2 convolution_add_fusion.14
  56.0 0.2 fusion.7
  56.2 0.2 convolution_add_fusion.11
  56.5 0.2 fusion.5
  56.7 0.4 fusion.90
  57.2 0.4 fusion.89
  58.2 0.4 fusion.88
  58.6 0.4 fusion.87
  59.1 0.4 copy-done.8
  59.4 0.3 fusion.94
  59.8 0.3 convolution_add_fusion.3
  60.1 0.3 convolution_add_fusion.2
  60.7 0.3 fusion.95
  61.0 0.3 convolution_add_fusion.1
  61.5 0.4 fusion.2
  62.0 0.6 copy-done.11
  63.1 0.2 convolution_add_fusion.6
  63.9 0.2 fusion.12
  64.4 2.0 %collective-permute-start.19 = (f32[128,2,128]{0,2,1:T(8,128)S(1)}, f32[128,2,128]{0,2,1:T(8,128)S(1)}, u32[]{:S(2)}, u32[]{:S(2)}) collective-permute-start(f32[128,2,128]{0,2,1:T(8,128)S(1)} %get-tuple-element.22), channel_id=1, source_target_pairs={{0,12},{4,8},{8,4},{12,0},{16,28},{20,24},{24,20},{28,16},{1,13},{... | collective-permute-start | bytes 393224 | tf_op jit(solution)/shard_map/ppermute | solution.py:33
  66.5 2.3 %collective-permute-start.21 = (f32[128,2,128]{0,2,1:T(8,128)S(1)}, f32[128,2,128]{0,2,1:T(8,128)S(1)}, u32[]{:S(2)}, u32[]{:S(2)}) collective-permute-start(f32[128,2,128]{0,2,1:T(8,128)S(1)} %get-tuple-element.25), channel_id=1, source_target_pairs={{0,20},{4,16},{8,28},{12,24},{16,4},{20,0},{24,12},{28,8},{1,21},{... | collective-permute-start | bytes 393224 | tf_op jit(solution)/shard_map/ppermute | solution.py:33
  68.8 0.9 collective-permute-start.22
  69.8 3.3 %collective-permute-start.23 = (f32[128,2,128]{0,2,1:T(8,128)S(1)}, f32[128,2,128]{0,2,1:T(8,128)S(1)}, u32[]{:S(2)}, u32[]{:S(2)}) collective-permute-start(f32[128,2,128]{0,2,1:T(8,128)S(1)} %get-tuple-element.18), channel_id=1, source_target_pairs={{0,28},{4,24},{8,20},{12,16},{16,12},{20,8},{24,4},{28,0},{1,29},{... | collective-permute-start | bytes 393224 | tf_op jit(solution)/shard_map/ppermute | solution.py:33
  73.1 1.6 %collective-permute-done.19 = f32[128,2,128]{0,2,1:T(8,128)S(1)} collective-permute-done((f32[128,2,128]{0,2,1:T(8,128)S(1)}, f32[128,2,128]{0,2,1:T(8,128)S(1)}, u32[]{:S(2)}, u32[]{:S(2)}) %collective-permute-start.19) | collective-permute-done | bytes 131104 | tf_op jit(solution)/shard_map/ppermute | solution.py:33
  74.7 0.9 collective-permute-done.20
  75.6 7.7 %collective-permute-done.21 = f32[128,2,128]{0,2,1:T(8,128)S(1)} collective-permute-done((f32[128,2,128]{0,2,1:T(8,128)S(1)}, f32[128,2,128]{0,2,1:T(8,128)S(1)}, u32[]{:S(2)}, u32[]{:S(2)}) %collective-permute-start.21) | collective-permute-done | bytes 131104 | tf_op jit(solution)/shard_map/ppermute | solution.py:33
  83.2 4.6 %collective-permute-done.22 = f32[128,2,128]{0,2,1:T(8,128)S(1)} collective-permute-done((f32[128,2,128]{0,2,1:T(8,128)S(1)}, f32[128,2,128]{0,2,1:T(8,128)S(1)}, u32[]{:S(2)}, u32[]{:S(2)}) %collective-permute-start.22) | collective-permute-done | bytes 131104 | tf_op jit(solution)/shard_map/ppermute | solution.py:33
  87.8 2.9 %collective-permute-done.23 = f32[128,2,128]{0,2,1:T(8,128)S(1)} collective-permute-done((f32[128,2,128]{0,2,1:T(8,128)S(1)}, f32[128,2,128]{0,2,1:T(8,128)S(1)}, u32[]{:S(2)}, u32[]{:S(2)}) %collective-permute-start.23) | collective-permute-done | bytes 131104 | tf_op jit(solution)/shard_map/ppermute | solution.py:33
  91.3 0.5 copy-done
  91.9 0.9 fusion.21
  92.8 1.0 %copy.27 = f32[128,1024]{1,0:T(8,128)} copy(f32[128,1024]{0,1:T(8,128)S(1)} %bitcast.346) | data formatting | bytes 1048576
  (163 shorter events, 6.6 us)
Async XLA Ops:
  0.6 26.5 %collective-permute-start.2 = (bf16[128,1024]{1,0:T(8,128)(2,1)}, bf16[128,1024]{1,0:T(8,128)(2,1)S(1)}, u32[]{:S(2)}, u32[]{:S(2)}) collective-permute-start(bf16[128,1024]{1,0:T(8,128)(2,1)} %param.21), channel_id=1, source_target_pairs={{0,3},{1,2},{2,1},{3,0},{4,7},{5,6},{6,5},{7,4},{8,11},{9,10},{10,... | collective-permute-start | bytes 786440 | tf_op jit(solution)/shard_map/ppermute | solution.py:33
  2.9 24.3 %collective-permute-start.1 = (bf16[128,1024]{1,0:T(8,128)(2,1)}, bf16[128,1024]{1,0:T(8,128)(2,1)S(1)}, u32[]{:S(2)}, u32[]{:S(2)}) collective-permute-start(bf16[128,1024]{1,0:T(8,128)(2,1)} %param.21), channel_id=1, source_target_pairs={{0,2},{1,3},{2,0},{3,1},{4,6},{5,7},{6,4},{7,5},{8,10},{9,11},{10,... | collective-permute-start | bytes 786440 | tf_op jit(solution)/shard_map/ppermute | solution.py:33
  3.1 24.1 %collective-permute-start = (bf16[128,1024]{1,0:T(8,128)(2,1)}, bf16[128,1024]{1,0:T(8,128)(2,1)S(1)}, u32[]{:S(2)}, u32[]{:S(2)}) collective-permute-start(bf16[128,1024]{1,0:T(8,128)(2,1)} %param.21), channel_id=1, source_target_pairs={{0,1},{1,0},{2,3},{3,2},{4,5},{5,4},{6,7},{7,6},{8,9},{9,8},{10,11... | collective-permute-start | bytes 786440 | tf_op jit(solution)/shard_map/ppermute | solution.py:33
  5.6 18.3 %copy-start.30 = (bf16[128,1,1]{0,1,2:T(2,128)(2,1)S(1)}, bf16[128,1,1]{0,1,2:T(2,128)(2,1)}, u32[]{:S(2)}) copy-start(bf16[128,1,1]{0,1,2:T(2,128)(2,1)} %constant.213) | copy-start | bytes 772
  5.8 18.4 %copy-start.2 = (bf16[128,128,1]{1,0,2:T(8,128)(2,1)S(1)}, bf16[128,128,1]{1,0,2:T(8,128)(2,1)}, u32[]{:S(2)}) copy-start(bf16[128,128,1]{1,0,2:T(8,128)(2,1)} %constant.207) | copy-start | bytes 98308
  5.9 2.5 %collective-permute-start.3 = (bf16[2,128,128]{1,2,0:T(8,128)(2,1)S(1)}, bf16[2,128,128]{1,2,0:T(8,128)(2,1)S(1)}, u32[]{:S(2)}, u32[]{:S(2)}) collective-permute-start(bf16[2,128,128]{1,2,0:T(8,128)(2,1)S(1)} %get-tuple-element.76), channel_id=1, source_target_pairs={{0,4},{4,0},{8,12},{12,8},{16,20},{20,16},{24,28},{28,24},{1,5},{5... | collective-permute-start | bytes 196616 | tf_op jit(solution)/shard_map/ppermute | solution.py:33
  7.4 3.6 %collective-permute-start.4 = (bf16[2,128,128]{1,2,0:T(8,128)(2,1)S(1)}, bf16[2,128,128]{1,2,0:T(8,128)(2,1)S(1)}, u32[]{:S(2)}, u32[]{:S(2)}) collective-permute-start(bf16[2,128,128]{1,2,0:T(8,128)(2,1)S(1)} %get-tuple-element.77), channel_id=1, source_target_pairs={{0,8},{4,12},{8,0},{12,4},{16,24},{20,28},{24,16},{28,20},{1,9},{5... | collective-permute-start | bytes 196616 | tf_op jit(solution)/shard_map/ppermute | solution.py:33
  8.3 5.0 %collective-permute-start.5 = (bf16[2,128,128]{1,2,0:T(8,128)(2,1)S(1)}, bf16[2,128,128]{1,2,0:T(8,128)(2,1)S(1)}, u32[]{:S(2)}, u32[]{:S(2)}) collective-permute-start(bf16[2,128,128]{1,2,0:T(8,128)(2,1)S(1)} %get-tuple-element.78), channel_id=1, source_target_pairs={{0,12},{4,8},{8,4},{12,0},{16,28},{20,24},{24,20},{28,16},{1,13},{... | collective-permute-start | bytes 196616 | tf_op jit(solution)/shard_map/ppermute | solution.py:33
  9.2 15.4 %copy-start.3 = (bf16[128,128,1]{1,0,2:T(8,128)(2,1)S(1)}, bf16[128,128,1]{1,0,2:T(8,128)(2,1)}, u32[]{:S(2)}) copy-start(bf16[128,128,1]{1,0,2:T(8,128)(2,1)} %constant.205) | copy-start | bytes 98308
  11.0 4.3 %collective-permute-start.6 = (bf16[2,128,128]{1,2,0:T(8,128)(2,1)S(1)}, bf16[2,128,128]{1,2,0:T(8,128)(2,1)S(1)}, u32[]{:S(2)}, u32[]{:S(2)}) collective-permute-start(bf16[2,128,128]{1,2,0:T(8,128)(2,1)S(1)} %get-tuple-element.79), channel_id=1, source_target_pairs={{0,16},{4,20},{8,24},{12,28},{16,0},{20,4},{24,8},{28,12},{1,17},{... | collective-permute-start | bytes 196616 | tf_op jit(solution)/shard_map/ppermute | solution.py:33
  13.3 5.3 %collective-permute-start.7 = (bf16[2,128,128]{1,2,0:T(8,128)(2,1)S(1)}, bf16[2,128,128]{1,2,0:T(8,128)(2,1)S(1)}, u32[]{:S(2)}, u32[]{:S(2)}) collective-permute-start(bf16[2,128,128]{1,2,0:T(8,128)(2,1)S(1)} %get-tuple-element.81), channel_id=1, source_target_pairs={{0,20},{4,16},{8,28},{12,24},{16,4},{20,0},{24,12},{28,8},{1,21},{... | collective-permute-start | bytes 196616 | tf_op jit(solution)/shard_map/ppermute | solution.py:33
  15.3 5.6 %collective-permute-start.8 = (bf16[2,128,128]{1,2,0:T(8,128)(2,1)S(1)}, bf16[2,128,128]{1,2,0:T(8,128)(2,1)S(1)}, u32[]{:S(2)}, u32[]{:S(2)}) collective-permute-start(bf16[2,128,128]{1,2,0:T(8,128)(2,1)S(1)} %get-tuple-element.80), channel_id=1, source_target_pairs={{0,24},{4,28},{8,16},{12,20},{16,8},{20,12},{24,0},{28,4},{1,25},{... | collective-permute-start | bytes 196616 | tf_op jit(solution)/shard_map/ppermute | solution.py:33
  18.6 5.0 %collective-permute-start.9 = (bf16[2,128,128]{1,2,0:T(8,128)(2,1)S(1)}, bf16[2,128,128]{1,2,0:T(8,128)(2,1)S(1)}, u32[]{:S(2)}, u32[]{:S(2)}) collective-permute-start(bf16[2,128,128]{1,2,0:T(8,128)(2,1)S(1)} %get-tuple-element.74), channel_id=1, source_target_pairs={{0,28},{4,24},{8,20},{12,16},{16,12},{20,8},{24,4},{28,0},{1,29},{... | collective-permute-start | bytes 196616 | tf_op jit(solution)/shard_map/ppermute | solution.py:33
  23.8 1.4 %copy-start.5 = (bf16[128,128,1]{1,0,2:T(8,128)(2,1)S(1)}, bf16[128,128,1]{1,0,2:T(8,128)(2,1)}, u32[]{:S(2)}) copy-start(bf16[128,128,1]{1,0,2:T(8,128)(2,1)} %constant.206) | copy-start | bytes 98308
  24.7 0.8 copy-start.4
  25.4 2.5 %slice-start = ((s8[8388608]{0:T(1024)(128)(4,1)}), s8[4194304]{0:T(1024)(128)(4,1)S(1)}, s32[]{:S(2)}) async-start(s8[8388608]{0:T(1024)(128)(4,1)} %bitcast.357), calls=%async_computation | async-start | bytes 8388608
  26.3 1.3 %copy-start.7 = (bf16[128,1024]{1,0:T(8,128)(2,1)S(1)}, bf16[128,1024]{1,0:T(8,128)(2,1)}, u32[]{:S(2)}) copy-start(bf16[128,1024]{1,0:T(8,128)(2,1)} %param.21) | copy-start | bytes 786436
  26.3 2.9 %slice-start.1 = ((s8[8388608]{0:T(1024)(128)(4,1)}), s8[4194304]{0:T(1024)(128)(4,1)S(1)}, s32[]{:S(2)}) async-start(s8[8388608]{0:T(1024)(128)(4,1)} %bitcast.357), calls=%async_computation.1 | async-start | bytes 8388608
  27.7 1.6 %copy-start.6 = (bf16[128,1024]{1,0:T(8,128)(2,1)S(1)}, bf16[128,1024]{1,0:T(8,128)(2,1)}, u32[]{:S(2)}) copy-start(bf16[128,1024]{1,0:T(8,128)(2,1)} %param.17) | copy-start | bytes 786436
  34.4 8.6 %collective-permute-start.10 = (bf16[2,128,128]{1,2,0:T(8,128)(2,1)S(1)}, bf16[2,128,128]{1,2,0:T(8,128)(2,1)S(1)}, u32[]{:S(2)}, u32[]{:S(2)}) collective-permute-start(bf16[2,128,128]{1,2,0:T(8,128)(2,1)S(1)} %get-tuple-element.66), channel_id=1, source_target_pairs={{0,4},{4,0},{8,12},{12,8},{16,20},{20,16},{24,28},{28,24},{1,5},{5... | collective-permute-start | bytes 196616 | tf_op jit(solution)/shard_map/ppermute | solution.py:33
  36.2 7.3 %collective-permute-start.11 = (bf16[2,128,128]{1,2,0:T(8,128)(2,1)S(1)}, bf16[2,128,128]{1,2,0:T(8,128)(2,1)S(1)}, u32[]{:S(2)}, u32[]{:S(2)}) collective-permute-start(bf16[2,128,128]{1,2,0:T(8,128)(2,1)S(1)} %get-tuple-element.67), channel_id=1, source_target_pairs={{0,8},{4,12},{8,0},{12,4},{16,24},{20,28},{24,16},{28,20},{1,9},{5... | collective-permute-start | bytes 196616 | tf_op jit(solution)/shard_map/ppermute | solution.py:33
  40.0 4.7 %collective-permute-start.12 = (bf16[2,128,128]{1,2,0:T(8,128)(2,1)S(1)}, bf16[2,128,128]{1,2,0:T(8,128)(2,1)S(1)}, u32[]{:S(2)}, u32[]{:S(2)}) collective-permute-start(bf16[2,128,128]{1,2,0:T(8,128)(2,1)S(1)} %get-tuple-element.68), channel_id=1, source_target_pairs={{0,12},{4,8},{8,4},{12,0},{16,28},{20,24},{24,20},{28,16},{1,13},{... | collective-permute-start | bytes 196616 | tf_op jit(solution)/shard_map/ppermute | solution.py:33
  40.1 6.0 %collective-permute-start.13 = (bf16[2,128,128]{1,2,0:T(8,128)(2,1)S(1)}, bf16[2,128,128]{1,2,0:T(8,128)(2,1)S(1)}, u32[]{:S(2)}, u32[]{:S(2)}) collective-permute-start(bf16[2,128,128]{1,2,0:T(8,128)(2,1)S(1)} %get-tuple-element.69), channel_id=1, source_target_pairs={{0,16},{4,20},{8,24},{12,28},{16,0},{20,4},{24,8},{28,12},{1,17},{... | collective-permute-start | bytes 196616 | tf_op jit(solution)/shard_map/ppermute | solution.py:33
  42.0 8.7 %collective-permute-start.14 = (bf16[2,128,128]{1,2,0:T(8,128)(2,1)S(1)}, bf16[2,128,128]{1,2,0:T(8,128)(2,1)S(1)}, u32[]{:S(2)}, u32[]{:S(2)}) collective-permute-start(bf16[2,128,128]{1,2,0:T(8,128)(2,1)S(1)} %get-tuple-element.71), channel_id=1, source_target_pairs={{0,20},{4,16},{8,28},{12,24},{16,4},{20,0},{24,12},{28,8},{1,21},{... | collective-permute-start | bytes 196616 | tf_op jit(solution)/shard_map/ppermute | solution.py:33
  43.0 10.4 %collective-permute-start.15 = (bf16[2,128,128]{1,2,0:T(8,128)(2,1)S(1)}, bf16[2,128,128]{1,2,0:T(8,128)(2,1)S(1)}, u32[]{:S(2)}, u32[]{:S(2)}) collective-permute-start(bf16[2,128,128]{1,2,0:T(8,128)(2,1)S(1)} %get-tuple-element.70), channel_id=1, source_target_pairs={{0,24},{4,28},{8,16},{12,20},{16,8},{20,12},{24,0},{28,4},{1,25},{... | collective-permute-start | bytes 196616 | tf_op jit(solution)/shard_map/ppermute | solution.py:33
  43.6 11.5 %collective-permute-start.16 = (bf16[2,128,128]{1,2,0:T(8,128)(2,1)S(1)}, bf16[2,128,128]{1,2,0:T(8,128)(2,1)S(1)}, u32[]{:S(2)}, u32[]{:S(2)}) collective-permute-start(bf16[2,128,128]{1,2,0:T(8,128)(2,1)S(1)} %get-tuple-element.64), channel_id=1, source_target_pairs={{0,28},{4,24},{8,20},{12,16},{16,12},{20,8},{24,4},{28,0},{1,29},{... | collective-permute-start | bytes 196616 | tf_op jit(solution)/shard_map/ppermute | solution.py:33
  57.2 0.7 copy-start.31
  58.6 0.8 copy-start.8
  58.6 1.1 %copy-start.13 = (bf16[256,128,1]{1,0,2:T(8,128)(2,1)S(1)}, bf16[256,128,1]{1,0,2:T(8,128)(2,1)}, u32[]{:S(2)}) copy-start(bf16[256,128,1]{1,0,2:T(8,128)(2,1)} %constant.215) | copy-start | bytes 196612
  59.8 0.8 copy-start.9
  60.1 0.9 copy-start.12
  60.6 0.7 copy-start.16
  60.6 0.7 copy-start.17
  60.6 0.7 copy-start.18
  60.6 0.7 copy-start.19
  60.6 0.7 copy-start.20
  60.6 0.7 copy-start.21
  60.6 0.7 copy-start.22
  60.6 0.7 copy-start.23
  60.6 0.7 copy-start.24
  60.7 0.7 copy-start.25
  60.7 0.7 copy-start.26
  60.7 0.7 copy-start.27
  60.7 0.8 copy-start.28
  61.9 0.8 copy-start.11
  61.9 1.0 %copy-start.15 = (bf16[128,128,1]{1,0,2:T(8,128)(2,1)S(1)}, bf16[128,128,1]{1,0,2:T(8,128)(2,1)}, u32[]{:S(2)}) copy-start(bf16[128,128,1]{1,0,2:T(8,128)(2,1)} %constant.212) | copy-start | bytes 98308
  62.6 0.8 copy-start.10
  62.9 0.8 copy-start.14
  63.1 0.8 copy-start.29
  64.2 4.6 %collective-permute-start.17 = (f32[128,2,128]{0,2,1:T(8,128)S(1)}, f32[128,2,128]{0,2,1:T(8,128)S(1)}, u32[]{:S(2)}, u32[]{:S(2)}) collective-permute-start(f32[128,2,128]{0,2,1:T(8,128)S(1)} %get-tuple-element.20), channel_id=1, source_target_pairs={{0,4},{4,0},{8,12},{12,8},{16,20},{20,16},{24,28},{28,24},{1,5},{5... | collective-permute-start | bytes 393224 | tf_op jit(solution)/shard_map/ppermute | solution.py:33
  64.4 5.4 %collective-permute-start.18 = (f32[128,2,128]{0,2,1:T(8,128)S(1)}, f32[128,2,128]{0,2,1:T(8,128)S(1)}, u32[]{:S(2)}, u32[]{:S(2)}) collective-permute-start(f32[128,2,128]{0,2,1:T(8,128)S(1)} %get-tuple-element.21), channel_id=1, source_target_pairs={{0,8},{4,12},{8,0},{12,4},{16,24},{20,28},{24,16},{28,20},{1,9},{5... | collective-permute-start | bytes 393224 | tf_op jit(solution)/shard_map/ppermute | solution.py:33
  64.4 10.3 %collective-permute-start.19 = (f32[128,2,128]{0,2,1:T(8,128)S(1)}, f32[128,2,128]{0,2,1:T(8,128)S(1)}, u32[]{:S(2)}, u32[]{:S(2)}) collective-permute-start(f32[128,2,128]{0,2,1:T(8,128)S(1)} %get-tuple-element.22), channel_id=1, source_target_pairs={{0,12},{4,8},{8,4},{12,0},{16,28},{20,24},{24,20},{28,16},{1,13},{... | collective-permute-start | bytes 393224 | tf_op jit(solution)/shard_map/ppermute | solution.py:33
  66.4 9.2 %collective-permute-start.20 = (f32[128,2,128]{0,2,1:T(8,128)S(1)}, f32[128,2,128]{0,2,1:T(8,128)S(1)}, u32[]{:S(2)}, u32[]{:S(2)}) collective-permute-start(f32[128,2,128]{0,2,1:T(8,128)S(1)} %get-tuple-element.23), channel_id=1, source_target_pairs={{0,16},{4,20},{8,24},{12,28},{16,0},{20,4},{24,8},{28,12},{1,17},{... | collective-permute-start | bytes 393224 | tf_op jit(solution)/shard_map/ppermute | solution.py:33
  66.5 16.7 %collective-permute-start.21 = (f32[128,2,128]{0,2,1:T(8,128)S(1)}, f32[128,2,128]{0,2,1:T(8,128)S(1)}, u32[]{:S(2)}, u32[]{:S(2)}) collective-permute-start(f32[128,2,128]{0,2,1:T(8,128)S(1)} %get-tuple-element.25), channel_id=1, source_target_pairs={{0,20},{4,16},{8,28},{12,24},{16,4},{20,0},{24,12},{28,8},{1,21},{... | collective-permute-start | bytes 393224 | tf_op jit(solution)/shard_map/ppermute | solution.py:33
  68.8 19.0 %collective-permute-start.22 = (f32[128,2,128]{0,2,1:T(8,128)S(1)}, f32[128,2,128]{0,2,1:T(8,128)S(1)}, u32[]{:S(2)}, u32[]{:S(2)}) collective-permute-start(f32[128,2,128]{0,2,1:T(8,128)S(1)} %get-tuple-element.24), channel_id=1, source_target_pairs={{0,24},{4,28},{8,16},{12,20},{16,8},{20,12},{24,0},{28,4},{1,25},{... | collective-permute-start | bytes 393224 | tf_op jit(solution)/shard_map/ppermute | solution.py:33
  69.8 21.0 %collective-permute-start.23 = (f32[128,2,128]{0,2,1:T(8,128)S(1)}, f32[128,2,128]{0,2,1:T(8,128)S(1)}, u32[]{:S(2)}, u32[]{:S(2)}) collective-permute-start(f32[128,2,128]{0,2,1:T(8,128)S(1)} %get-tuple-element.18), channel_id=1, source_target_pairs={{0,28},{4,24},{8,20},{12,16},{16,12},{20,8},{24,4},{28,0},{1,29},{... | collective-permute-start | bytes 393224 | tf_op jit(solution)/shard_map/ppermute | solution.py:33
  90.9 1.0 %copy-start = (bf16[128,1024]{1,0:T(8,128)(2,1)S(1)}, bf16[128,1024]{1,0:T(8,128)(2,1)}, u32[]{:S(2)}) copy-start(bf16[128,1024]{1,0:T(8,128)(2,1)} %param.19) | copy-start | bytes 786436
  90.9 1.0 %copy-start.1 = (bf16[128,1024]{1,0:T(8,128)(2,1)S(1)}, bf16[128,1024]{1,0:T(8,128)(2,1)}, u32[]{:S(2)}) copy-start(bf16[128,1024]{1,0:T(8,128)(2,1)} %param.18) | copy-start | bytes 786436

commit v8 on v5

--- a/solution.py
+++ b/solution.py
@@ -148,6 +148,10 @@
     return value.transpose(1, 0, 2).reshape(rows, groups * chans)
 
 
+def all_to_all_ctx(stacked):
+    return lax.all_to_all(stacked, "ctx", 0, 0, tiled=True)
+
+
 def transpose_ctx(stacked):
     count = lax.axis_size("ctx")
     me = lax.axis_index("ctx")
@@ -171,7 +175,7 @@
     blocks = lax.axis_size("ctx")
     seq = rows * blocks
     gated = (k_proj.astype(jnp.float32) * v_proj.astype(jnp.float32)).astype(jnp.bfloat16)
-    inputs_t = transpose_ctx(
+    inputs_t = all_to_all_ctx(
         jnp.stack([to_groups(gated, blocks), to_groups(filter_taps, blocks)], axis=1)
     )
     d_gated = gather_matmul(out_grad, out_weight)

time: 90.5 us -> 80 us (0.88)
  starting transfers between devices: 31.5 us -> 26 us
  waiting for transfers between devices: 30.6 us -> 26.7 us
    ppermute x21 -> x14, starting transfers between devices: 28.7 us -> 16.8 us  [transpose_ctx(): lax.ppermute(chunk, 'ctx', [(i, (i + shift) % count) for i in range(count)])]
    all_to_all x0 -> x1, starting transfers between devices: none -> 6.44 us  [all_to_all_ctx(): return lax.all_to_all(stacked, 'ctx', 0, 0, tiled=True)]
    ppermute x21 -> x14, waiting for transfers between devices: 30.6 us -> 25.1 us  [transpose_ctx(): lax.ppermute(chunk, 'ctx', [(i, (i + shift) % count) for i in range(count)])]
    ppermute x3, waiting for transfers between devices: 0.01 us -> 1.6 us  [gather_matmul(): lax.ppermute(out_grad, 'tp', [(i, (i + shift) % count) for i in range(cou...]
    unnamed x80 -> x68, local copies, waits for them, and re-layouts: 5.62 us -> 4.88 us
  transfers between devices with their start and end apart: 24 -> 18, of which waited for: 11 -> 9; matrix products, arithmetic and copies ran while one was open for 3% -> 17% of each run, Pallas kernels for 0% -> 0%
where the time goes in v8:
time: 80 us; the launch traced here: 79.5 us
  waiting for transfers between devices  26.7 us (33%)
  starting transfers between devices  26 us (32%)
  matrix products  13.3 us (17%)
  local copies, waits for them, and re-layouts  6.1 us (8%)
  other arithmetic  5.99 us (7%)
  between operations  1.4 us (2%)
    ppermute x14, waiting for transfers between devices, transpose_ctx(): lax.ppermute(chunk, 'ctx', [(i, (i + shift) % count) for i in range(count)])  25.1 us
    ppermute x14, starting transfers between devices, transpose_ctx(): lax.ppermute(chunk, 'ctx', [(i, (i + shift) % count) for i in range(count)])  16.8 us
    all_to_all x1, starting transfers between devices, all_to_all_ctx(): return lax.all_to_all(stacked, 'ctx', 0, 0, tiled=True)  6.44 us
    dot_general x26, matrix products, one(): jnp.einsum('kn,bnc->bkc', left, right, preferred_element_type=jnp.float32)  6.32 us
    dot_general x1, matrix products, gather_matmul(): lax.dot_general(gathered, out_weight, (((1,), (1,)), ((), ())), preferred...  6.3 us
    unnamed x68, local copies, waits for them, and re-layouts  4.88 us
    ppermute x3, starting transfers between devices, gather_matmul(): lax.ppermute(out_grad, 'tp', [(i, (i + shift) % count) for i in range(cou...  2.76 us
    convert_element_type x4, other arithmetic, split_bf16(): upper = lax.optimization_barrier(value.astype(jnp.bfloat16))  1.71 us
  transfers between devices with their start and end apart: 18, of which 9 were waited for; matrix products, arithmetic and copies ran while one was open for 17% of the time, Pallas kernels for 0%

profile of v8, /device:TPU:9, one launch (start us, length us, event | category | flops | bytes accessed | tf_op | source)
XLA Modules:
  0.0 79.5 jit_solution(17033344823713730132)
XLA Ops:
  0.6 2.2 %collective-permute-start.2 = (bf16[128,1024]{1,0:T(8,128)(2,1)}, bf16[128,1024]{1,0:T(8,128)(2,1)S(1)}, u32[]{:S(2)}, u32[]{:S(2)}) collective-permute-start(bf16[128,1024]{1,0:T(8,128)(2,1)} %param.21), channel_id=1, source_target_pairs={{0,3},{1,0},{2,1},{3,2},{4,7},{5,4},{6,5},{7,6},{8,11},{9,8},{10,9... | collective-permute-start | bytes 786440 | tf_op jit(solution)/shard_map/ppermute | solution.py:25
  2.9 0.2 collective-permute-start.1
  3.1 0.3 collective-permute-start
  3.4 1.1 %fusion.22 = bf16[128,1024]{1,0:T(8,128)(2,1)S(1)} fusion(bf16[128,1024]{1,0:T(8,128)(2,1)} %param.19, bf16[128,1024]{1,0:T(8,128)(2,1)} %param.18), kind=kLoop, calls=%fused_computation.88 | loop fusion | flops 524288 | bytes 786432 | tf_op jit(solution)/shard_map/convert_element_type | solution.py:177
  4.5 1.1 %copy.29 = bf16[128,1024]{0,1:T(8,128)(2,1)S(1)} copy(bf16[128,1024]{1,0:T(8,128)(2,1)} %param.23) | data formatting | bytes 524288 | tf_op args[6]
  5.8 0.8 %pad_maximum_fusion.1 = bf16[8,2,128,128]{2,3,1,0:T(8,128)(2,1)} fusion(bf16[8,1,128,128]{2,3,1,0:T(8,128)(2,1)S(1)} %bitcast.320, bf16[8,1,128,128]{2,3,1,0:T(8,128)(2,1)S(1)} %bitcast.321), kind=kLoop, calls=%fused_computation.93 | loop fusion | flops 262144 | bytes 1048576 | tf_op jit(solution)/shard_map/stack | solution.py:179
  6.6 6.4 %all-to-all-start = ((bf16[8,2,128,128]{2,3,1,0:T(8,128)(2,1)}), bf16[8,2,128,128]{2,3,1,0:T(8,128)(2,1)S(1)}, u32[]{:S(2)}, u32[]{:S(2)}) async-start(bf16[8,2,128,128]{2,3,1,0:T(8,128)(2,1)} %pad_maximum_fusion.1), calls=%async_computation | async-start | bytes 1048576 | tf_op jit(solution)/shard_map/all_to_all | solution.py:152
  13.1 1.6 %collective-permute-done = bf16[128,1024]{1,0:T(8,128)(2,1)S(1)} collective-permute-done((bf16[128,1024]{1,0:T(8,128)(2,1)}, bf16[128,1024]{1,0:T(8,128)(2,1)S(1)}, u32[]{:S(2)}, u32[]{:S(2)}) %collective-permute-start) | collective-permute-done | bytes 262176 | tf_op jit(solution)/shard_map/ppermute | solution.py:25
  15.0 0.7 copy-done.6
  15.7 6.3 %fusion.26 = (bf16[128,1024]{1,0:T(8,128)(2,1)S(1)}, f32[128,1024]{1,0:T(8,128)S(1)}) fusion(bf16[128,1024]{1,0:T(8,128)(2,1)S(1)} %copy-done.6, bf16[1024,4096]{1,0:T(8,128)(2,1)} %param.22, bf16[128,1024]{1,0:T(8,128)(2,1)S(1)} %get-tuple-element.31, bf16[128,1024]{1,0:T(8,128)(2,1)S(1)} %get-tuple-element.32, ...), kind=kOutput, calls=%fused_computation.107 | convolution fusion | flops 1078329344 | bytes 10485760 | tf_op jit(solution)/shard_map/dot_general | solution.py:33
  22.2 0.9 %subtract_convert_fusion.4 = (bf16[128,1024]{1,0:T(8,128)(2,1)S(1)}, bf16[128,1024]{1,0:T(8,128)(2,1)}) fusion(bf16[128,1024]{1,0:T(8,128)(2,1)S(1)} %get-tuple-element.98, f32[128,1024]{1,0:T(8,128)S(1)} %get-tuple-element.99, bf16[128,1024]{1,0:T(8,128)(2,1)S(1)} %copy-done.6, bf16[128,1024]{1,0:T(8,128)(2,1)S(1)} %copy-done.7), kind=kLoop, calls=%fused_computation.103 | loop fusion | flops 1048576 | bytes 1835008 | tf_op jit(solution)/shard_map/convert_element_type | solution.py:15
  23.3 3.9 %collective-permute-start.3 = (bf16[2,128,128]{1,2,0:T(8,128)(2,1)S(1)}, bf16[2,128,128]{1,2,0:T(8,128)(2,1)S(1)}, u32[]{:S(2)}, u32[]{:S(2)}) collective-permute-start(bf16[2,128,128]{1,2,0:T(8,128)(2,1)S(1)} %get-tuple-element.70), channel_id=1, source_target_pairs={{0,4},{4,8},{8,12},{12,16},{16,20},{20,24},{24,28},{28,0},{1,5},{5... | collective-permute-start | bytes 196616 | tf_op jit(solution)/shard_map/ppermute | solution.py:162
  27.2 1.3 %collective-permute-start.4 = (bf16[2,128,128]{1,2,0:T(8,128)(2,1)S(1)}, bf16[2,128,128]{1,2,0:T(8,128)(2,1)S(1)}, u32[]{:S(2)}, u32[]{:S(2)}) collective-permute-start(bf16[2,128,128]{1,2,0:T(8,128)(2,1)S(1)} %get-tuple-element.71), channel_id=1, source_target_pairs={{0,8},{4,12},{8,16},{12,20},{16,24},{20,28},{24,0},{28,4},{1,9},{5... | collective-permute-start | bytes 196616 | tf_op jit(solution)/shard_map/ppermute | solution.py:162
  28.5 1.4 %collective-permute-start.6 = (bf16[2,128,128]{1,2,0:T(8,128)(2,1)S(1)}, bf16[2,128,128]{1,2,0:T(8,128)(2,1)S(1)}, u32[]{:S(2)}, u32[]{:S(2)}) collective-permute-start(bf16[2,128,128]{1,2,0:T(8,128)(2,1)S(1)} %get-tuple-element.73), channel_id=1, source_target_pairs={{0,16},{4,20},{8,24},{12,28},{16,0},{20,4},{24,8},{28,12},{1,17},{... | collective-permute-start | bytes 196616 | tf_op jit(solution)/shard_map/ppermute | solution.py:162
  30.0 1.6 %collective-permute-start.7 = (bf16[2,128,128]{1,2,0:T(8,128)(2,1)S(1)}, bf16[2,128,128]{1,2,0:T(8,128)(2,1)S(1)}, u32[]{:S(2)}, u32[]{:S(2)}) collective-permute-start(bf16[2,128,128]{1,2,0:T(8,128)(2,1)S(1)} %get-tuple-element.75), channel_id=1, source_target_pairs={{0,20},{4,24},{8,28},{12,0},{16,4},{20,8},{24,12},{28,16},{1,21},{... | collective-permute-start | bytes 196616 | tf_op jit(solution)/shard_map/ppermute | solution.py:162
  31.6 1.1 %collective-permute-start.8 = (bf16[2,128,128]{1,2,0:T(8,128)(2,1)S(1)}, bf16[2,128,128]{1,2,0:T(8,128)(2,1)S(1)}, u32[]{:S(2)}, u32[]{:S(2)}) collective-permute-start(bf16[2,128,128]{1,2,0:T(8,128)(2,1)S(1)} %get-tuple-element.74), channel_id=1, source_target_pairs={{0,24},{4,28},{8,0},{12,4},{16,8},{20,12},{24,16},{28,20},{1,25},{... | collective-permute-start | bytes 196616 | tf_op jit(solution)/shard_map/ppermute | solution.py:162
  32.7 0.5 collective-permute-start.9
  33.3 3.0 %collective-permute-done.5 = bf16[2,128,128]{1,2,0:T(8,128)(2,1)S(1)} collective-permute-done((bf16[2,128,128]{1,2,0:T(8,128)(2,1)S(1)}, bf16[2,128,128]{1,2,0:T(8,128)(2,1)S(1)}, u32[]{:S(2)}, u32[]{:S(2)}) %collective-permute-start.5) | collective-permute-done | bytes 65568 | tf_op jit(solution)/shard_map/ppermute | solution.py:162
  36.3 2.2 %collective-permute-done.6 = bf16[2,128,128]{1,2,0:T(8,128)(2,1)S(1)} collective-permute-done((bf16[2,128,128]{1,2,0:T(8,128)(2,1)S(1)}, bf16[2,128,128]{1,2,0:T(8,128)(2,1)S(1)}, u32[]{:S(2)}, u32[]{:S(2)}) %collective-permute-start.6) | collective-permute-done | bytes 65568 | tf_op jit(solution)/shard_map/ppermute | solution.py:162
  38.6 1.8 %collective-permute-done.8 = bf16[2,128,128]{1,2,0:T(8,128)(2,1)S(1)} collective-permute-done((bf16[2,128,128]{1,2,0:T(8,128)(2,1)S(1)}, bf16[2,128,128]{1,2,0:T(8,128)(2,1)S(1)}, u32[]{:S(2)}, u32[]{:S(2)}) %collective-permute-start.8) | collective-permute-done | bytes 65568 | tf_op jit(solution)/shard_map/ppermute | solution.py:162
  41.0 0.2 fusion.33
  41.3 0.2 convolution_add_fusion.14
  41.5 0.2 fusion.32
  41.7 0.2 fusion.7
  42.0 0.2 convolution_add_fusion.11
  42.2 0.2 fusion.5
  42.5 0.2 fusion.30
  42.7 0.2 fusion.8
  43.0 0.2 fusion.29
  43.2 0.2 fusion.6
  43.7 0.4 fusion.75
  44.1 0.4 fusion.74
  44.6 0.2 fusion.35
  44.8 0.2 fusion.36
  45.0 0.2 fusion.3
  45.3 0.2 fusion.4
  45.6 0.4 fusion.73
  46.0 0.4 fusion.72
  46.9 0.3 fusion.79
  47.2 0.3 convolution_add_fusion.3
  47.5 0.3 convolution_add_fusion.2
  47.8 0.2 copy-done.10
  48.0 0.3 fusion.80
  48.3 0.3 convolution_add_fusion.1
  48.7 0.3 fusion.2
  49.2 0.6 copy-done.12
  49.8 0.2 fusion.78
  50.0 0.2 convolution_add_fusion.7
  50.3 0.2 convolution_add_fusion.6
  50.5 0.2 fusion.77
  50.8 0.2 convolution_add_fusion.9
  51.0 0.3 fusion.12
  51.4 1.4 %collective-permute-start.11 = (f32[128,2,128]{0,2,1:T(8,128)S(1)}, f32[128,2,128]{0,2,1:T(8,128)S(1)}, u32[]{:S(2)}, u32[]{:S(2)}) collective-permute-start(f32[128,2,128]{0,2,1:T(8,128)S(1)} %get-tuple-element.25), channel_id=1, source_target_pairs={{0,8},{4,12},{8,16},{12,20},{16,24},{20,28},{24,0},{28,4},{1,9},{5... | collective-permute-start | bytes 393224 | tf_op jit(solution)/shard_map/ppermute | solution.py:162
  52.8 0.9 %collective-permute-start.12 = (f32[128,2,128]{0,2,1:T(8,128)S(1)}, f32[128,2,128]{0,2,1:T(8,128)S(1)}, u32[]{:S(2)}, u32[]{:S(2)}) collective-permute-start(f32[128,2,128]{0,2,1:T(8,128)S(1)} %get-tuple-element.26), channel_id=1, source_target_pairs={{0,12},{4,16},{8,20},{12,24},{16,28},{20,0},{24,4},{28,8},{1,13},{... | collective-permute-start | bytes 393224 | tf_op jit(solution)/shard_map/ppermute | solution.py:162
  53.7 0.5 collective-permute-start.13
  54.3 2.1 %collective-permute-start.14 = (f32[128,2,128]{0,2,1:T(8,128)S(1)}, f32[128,2,128]{0,2,1:T(8,128)S(1)}, u32[]{:S(2)}, u32[]{:S(2)}) collective-permute-start(f32[128,2,128]{0,2,1:T(8,128)S(1)} %get-tuple-element.29), channel_id=1, source_target_pairs={{0,20},{4,24},{8,28},{12,0},{16,4},{20,8},{24,12},{28,16},{1,21},{... | collective-permute-start | bytes 393224 | tf_op jit(solution)/shard_map/ppermute | solution.py:162
  56.4 1.1 %collective-permute-start.15 = (f32[128,2,128]{0,2,1:T(8,128)S(1)}, f32[128,2,128]{0,2,1:T(8,128)S(1)}, u32[]{:S(2)}, u32[]{:S(2)}) collective-permute-start(f32[128,2,128]{0,2,1:T(8,128)S(1)} %get-tuple-element.28), channel_id=1, source_target_pairs={{0,24},{4,28},{8,0},{12,4},{16,8},{20,12},{24,16},{28,20},{1,25},{... | collective-permute-start | bytes 393224 | tf_op jit(solution)/shard_map/ppermute | solution.py:162
  57.5 0.8 %collective-permute-start.16 = (f32[128,2,128]{0,2,1:T(8,128)S(1)}, f32[128,2,128]{0,2,1:T(8,128)S(1)}, u32[]{:S(2)}, u32[]{:S(2)}) collective-permute-start(f32[128,2,128]{0,2,1:T(8,128)S(1)} %get-tuple-element.22), channel_id=1, source_target_pairs={{0,28},{4,0},{8,4},{12,8},{16,12},{20,16},{24,20},{28,24},{1,29},{... | collective-permute-start | bytes 393224 | tf_op jit(solution)/shard_map/ppermute | solution.py:162
  58.3 12.6 %collective-permute-done.12 = f32[128,2,128]{0,2,1:T(8,128)S(1)} collective-permute-done((f32[128,2,128]{0,2,1:T(8,128)S(1)}, f32[128,2,128]{0,2,1:T(8,128)S(1)}, u32[]{:S(2)}, u32[]{:S(2)}) %collective-permute-start.12) | collective-permute-done | bytes 131104 | tf_op jit(solution)/shard_map/ppermute | solution.py:162
  70.9 2.8 %collective-permute-done.13 = f32[128,2,128]{0,2,1:T(8,128)S(1)} collective-permute-done((f32[128,2,128]{0,2,1:T(8,128)S(1)}, f32[128,2,128]{0,2,1:T(8,128)S(1)}, u32[]{:S(2)}, u32[]{:S(2)}) %collective-permute-start.13) | collective-permute-done | bytes 131104 | tf_op jit(solution)/shard_map/ppermute | solution.py:162
  73.8 2.5 %collective-permute-done.15 = f32[128,2,128]{0,2,1:T(8,128)S(1)} collective-permute-done((f32[128,2,128]{0,2,1:T(8,128)S(1)}, f32[128,2,128]{0,2,1:T(8,128)S(1)}, u32[]{:S(2)}, u32[]{:S(2)}) %collective-permute-start.15) | collective-permute-done | bytes 131104 | tf_op jit(solution)/shard_map/ppermute | solution.py:162
  76.9 0.5 copy-done
  77.5 0.9 %fusion.21 = (bf16[128,1024]{1,0:T(8,128)(2,1)}, bf16[128,1024]{1,0:T(8,128)(2,1)}) fusion(f32[128,1024]{1,0:T(8,128)S(1)} %copy.34, bf16[128,1024]{1,0:T(8,128)(2,1)S(1)} %copy-done.1, bf16[128,1024]{1,0:T(8,128)(2,1)S(1)} %copy-done), kind=kLoop, calls=%fused_computation.87 | loop fusion | flops 786432 | bytes 1572864 | tf_op jit(solution)/shard_map/convert_element_type | solution.py:198
  78.5 1.0 %copy.36 = f32[128,1024]{1,0:T(8,128)} copy(f32[128,1024]{0,1:T(8,128)S(1)} %bitcast.318) | data formatting | bytes 1048576
  (106 shorter events, 3.4 us)
Async XLA Ops:
  0.6 14.1 %copy-start.8 = (bf16[128,1024]{1,0:T(8,128)(2,1)S(1)}, bf16[128,1024]{1,0:T(8,128)(2,1)}, u32[]{:S(2)}) copy-start(bf16[128,1024]{1,0:T(8,128)(2,1)} %param.21) | copy-start | bytes 786436
  0.6 12.5 %collective-permute-start.2 = (bf16[128,1024]{1,0:T(8,128)(2,1)}, bf16[128,1024]{1,0:T(8,128)(2,1)S(1)}, u32[]{:S(2)}, u32[]{:S(2)}) collective-permute-start(bf16[128,1024]{1,0:T(8,128)(2,1)} %param.21), channel_id=1, source_target_pairs={{0,3},{1,0},{2,1},{3,2},{4,7},{5,4},{6,5},{7,6},{8,11},{9,8},{10,9... | collective-permute-start | bytes 786440 | tf_op jit(solution)/shard_map/ppermute | solution.py:25
  2.9 10.2 %collective-permute-start.1 = (bf16[128,1024]{1,0:T(8,128)(2,1)}, bf16[128,1024]{1,0:T(8,128)(2,1)S(1)}, u32[]{:S(2)}, u32[]{:S(2)}) collective-permute-start(bf16[128,1024]{1,0:T(8,128)(2,1)} %param.21), channel_id=1, source_target_pairs={{0,2},{1,3},{2,0},{3,1},{4,6},{5,7},{6,4},{7,5},{8,10},{9,11},{10,... | collective-permute-start | bytes 786440 | tf_op jit(solution)/shard_map/ppermute | solution.py:25
  3.1 11.6 %collective-permute-start = (bf16[128,1024]{1,0:T(8,128)(2,1)}, bf16[128,1024]{1,0:T(8,128)(2,1)S(1)}, u32[]{:S(2)}, u32[]{:S(2)}) collective-permute-start(bf16[128,1024]{1,0:T(8,128)(2,1)} %param.21), channel_id=1, source_target_pairs={{0,1},{1,2},{2,3},{3,0},{4,5},{5,6},{6,7},{7,4},{8,9},{9,10},{10,1... | collective-permute-start | bytes 786440 | tf_op jit(solution)/shard_map/ppermute | solution.py:25
  6.6 35.8 %all-to-all-start = ((bf16[8,2,128,128]{2,3,1,0:T(8,128)(2,1)}), bf16[8,2,128,128]{2,3,1,0:T(8,128)(2,1)S(1)}, u32[]{:S(2)}, u32[]{:S(2)}) async-start(bf16[8,2,128,128]{2,3,1,0:T(8,128)(2,1)} %pad_maximum_fusion.1), calls=%async_computation | async-start | bytes 1048576 | tf_op jit(solution)/shard_map/all_to_all | solution.py:152
  14.7 1.0 %copy-start.6 = (bf16[128,1024]{1,0:T(8,128)(2,1)S(1)}, bf16[128,1024]{1,0:T(8,128)(2,1)}, u32[]{:S(2)}) copy-start(bf16[128,1024]{1,0:T(8,128)(2,1)} %param.17) | copy-start | bytes 786436
  15.7 6.5 %copy-start.7 = (bf16[128,1024]{1,0:T(8,128)(2,1)S(1)}, bf16[128,1024]{1,0:T(8,128)(2,1)}, u32[]{:S(2)}) copy-start(bf16[128,1024]{1,0:T(8,128)(2,1)} %param.20) | copy-start | bytes 786436
  23.0 17.6 %copy-start.19 = (bf16[128,1,1]{0,1,2:T(2,128)(2,1)S(1)}, bf16[128,1,1]{0,1,2:T(2,128)(2,1)}, u32[]{:S(2)}) copy-start(bf16[128,1,1]{0,1,2:T(2,128)(2,1)} %constant.317) | copy-start | bytes 772
  23.2 17.8 %copy-start.2 = (bf16[128,128,1]{1,0,2:T(8,128)(2,1)S(1)}, bf16[128,128,1]{1,0,2:T(8,128)(2,1)}, u32[]{:S(2)}) copy-start(bf16[128,128,1]{1,0,2:T(8,128)(2,1)} %constant.309) | copy-start | bytes 98308
  23.3 18.0 %copy-start.4 = (bf16[128,128,1]{1,0,2:T(8,128)(2,1)S(1)}, bf16[128,128,1]{1,0,2:T(8,128)(2,1)}, u32[]{:S(2)}) copy-start(bf16[128,128,1]{1,0,2:T(8,128)(2,1)} %constant.310) | copy-start | bytes 98308
  23.3 8.3 %collective-permute-start.3 = (bf16[2,128,128]{1,2,0:T(8,128)(2,1)S(1)}, bf16[2,128,128]{1,2,0:T(8,128)(2,1)S(1)}, u32[]{:S(2)}, u32[]{:S(2)}) collective-permute-start(bf16[2,128,128]{1,2,0:T(8,128)(2,1)S(1)} %get-tuple-element.70), channel_id=1, source_target_pairs={{0,4},{4,8},{8,12},{12,16},{16,20},{20,24},{24,28},{28,0},{1,5},{5... | collective-permute-start | bytes 196616 | tf_op jit(solution)/shard_map/ppermute | solution.py:162
  27.2 5.5 %collective-permute-start.4 = (bf16[2,128,128]{1,2,0:T(8,128)(2,1)S(1)}, bf16[2,128,128]{1,2,0:T(8,128)(2,1)S(1)}, u32[]{:S(2)}, u32[]{:S(2)}) collective-permute-start(bf16[2,128,128]{1,2,0:T(8,128)(2,1)S(1)} %get-tuple-element.71), channel_id=1, source_target_pairs={{0,8},{4,12},{8,16},{12,20},{16,24},{20,28},{24,0},{28,4},{1,9},{5... | collective-permute-start | bytes 196616 | tf_op jit(solution)/shard_map/ppermute | solution.py:162
  28.5 7.7 %collective-permute-start.5 = (bf16[2,128,128]{1,2,0:T(8,128)(2,1)S(1)}, bf16[2,128,128]{1,2,0:T(8,128)(2,1)S(1)}, u32[]{:S(2)}, u32[]{:S(2)}) collective-permute-start(bf16[2,128,128]{1,2,0:T(8,128)(2,1)S(1)} %get-tuple-element.72), channel_id=1, source_target_pairs={{0,12},{4,16},{8,20},{12,24},{16,28},{20,0},{24,4},{28,8},{1,13},{... | collective-permute-start | bytes 196616 | tf_op jit(solution)/shard_map/ppermute | solution.py:162
  28.5 10.0 %collective-permute-start.6 = (bf16[2,128,128]{1,2,0:T(8,128)(2,1)S(1)}, bf16[2,128,128]{1,2,0:T(8,128)(2,1)S(1)}, u32[]{:S(2)}, u32[]{:S(2)}) collective-permute-start(bf16[2,128,128]{1,2,0:T(8,128)(2,1)S(1)} %get-tuple-element.73), channel_id=1, source_target_pairs={{0,16},{4,20},{8,24},{12,28},{16,0},{20,4},{24,8},{28,12},{1,17},{... | collective-permute-start | bytes 196616 | tf_op jit(solution)/shard_map/ppermute | solution.py:162
  30.0 8.6 %collective-permute-start.7 = (bf16[2,128,128]{1,2,0:T(8,128)(2,1)S(1)}, bf16[2,128,128]{1,2,0:T(8,128)(2,1)S(1)}, u32[]{:S(2)}, u32[]{:S(2)}) collective-permute-start(bf16[2,128,128]{1,2,0:T(8,128)(2,1)S(1)} %get-tuple-element.75), channel_id=1, source_target_pairs={{0,20},{4,24},{8,28},{12,0},{16,4},{20,8},{24,12},{28,16},{1,21},{... | collective-permute-start | bytes 196616 | tf_op jit(solution)/shard_map/ppermute | solution.py:162
  31.6 8.7 %collective-permute-start.8 = (bf16[2,128,128]{1,2,0:T(8,128)(2,1)S(1)}, bf16[2,128,128]{1,2,0:T(8,128)(2,1)S(1)}, u32[]{:S(2)}, u32[]{:S(2)}) collective-permute-start(bf16[2,128,128]{1,2,0:T(8,128)(2,1)S(1)} %get-tuple-element.74), channel_id=1, source_target_pairs={{0,24},{4,28},{8,0},{12,4},{16,8},{20,12},{24,16},{28,20},{1,25},{... | collective-permute-start | bytes 196616 | tf_op jit(solution)/shard_map/ppermute | solution.py:162
  32.7 7.7 %collective-permute-start.9 = (bf16[2,128,128]{1,2,0:T(8,128)(2,1)S(1)}, bf16[2,128,128]{1,2,0:T(8,128)(2,1)S(1)}, u32[]{:S(2)}, u32[]{:S(2)}) collective-permute-start(bf16[2,128,128]{1,2,0:T(8,128)(2,1)S(1)} %get-tuple-element.68), channel_id=1, source_target_pairs={{0,28},{4,0},{8,4},{12,8},{16,12},{20,16},{24,20},{28,24},{1,29},{... | collective-permute-start | bytes 196616 | tf_op jit(solution)/shard_map/ppermute | solution.py:162
  38.5 3.0 %copy-start.3 = (bf16[128,128,1]{1,0,2:T(8,128)(2,1)S(1)}, bf16[128,128,1]{1,0,2:T(8,128)(2,1)}, u32[]{:S(2)}) copy-start(bf16[128,128,1]{1,0,2:T(8,128)(2,1)} %constant.311) | copy-start | bytes 98308
  41.0 1.0 %copy-start.5 = (bf16[128,128,1]{1,0,2:T(8,128)(2,1)S(1)}, bf16[128,128,1]{1,0,2:T(8,128)(2,1)}, u32[]{:S(2)}) copy-start(bf16[128,128,1]{1,0,2:T(8,128)(2,1)} %constant.312) | copy-start | bytes 98308
  46.0 0.8 %copy-start.9 = (bf16[256,128,1]{1,0,2:T(8,128)(2,1)S(1)}, bf16[256,128,1]{1,0,2:T(8,128)(2,1)}, u32[]{:S(2)}) copy-start(bf16[256,128,1]{1,0,2:T(8,128)(2,1)} %constant.318) | copy-start | bytes 196612
  46.0 1.1 %copy-start.14 = (bf16[256,128,1]{1,0,2:T(8,128)(2,1)S(1)}, bf16[256,128,1]{1,0,2:T(8,128)(2,1)}, u32[]{:S(2)}) copy-start(bf16[256,128,1]{1,0,2:T(8,128)(2,1)} %constant.319) | copy-start | bytes 196612
  47.2 0.8 %copy-start.10 = (bf16[256,128,1]{1,0,2:T(8,128)(2,1)S(1)}, bf16[256,128,1]{1,0,2:T(8,128)(2,1)}, u32[]{:S(2)}) copy-start(bf16[256,128,1]{1,0,2:T(8,128)(2,1)} %constant.320) | copy-start | bytes 196612
  47.5 0.9 %copy-start.13 = (bf16[256,128,1]{1,0,2:T(8,128)(2,1)S(1)}, bf16[256,128,1]{1,0,2:T(8,128)(2,1)}, u32[]{:S(2)}) copy-start(bf16[256,128,1]{1,0,2:T(8,128)(2,1)} %constant.321) | copy-start | bytes 196612
  48.0 0.7 copy-start.17
  49.0 0.8 copy-start.12
  49.0 1.0 %copy-start.16 = (bf16[128,128,1]{1,0,2:T(8,128)(2,1)S(1)}, bf16[128,128,1]{1,0,2:T(8,128)(2,1)}, u32[]{:S(2)}) copy-start(bf16[128,128,1]{1,0,2:T(8,128)(2,1)} %constant.316) | copy-start | bytes 98308
  49.8 0.8 copy-start.11
  50.0 0.8 copy-start.15
  50.3 0.8 copy-start.18
  51.4 5.0 %collective-permute-start.10 = (f32[128,2,128]{0,2,1:T(8,128)S(1)}, f32[128,2,128]{0,2,1:T(8,128)S(1)}, u32[]{:S(2)}, u32[]{:S(2)}) collective-permute-start(f32[128,2,128]{0,2,1:T(8,128)S(1)} %get-tuple-element.24), channel_id=1, source_target_pairs={{0,4},{4,8},{8,12},{12,16},{16,20},{20,24},{24,28},{28,0},{1,5},{5... | collective-permute-start | bytes 393224 | tf_op jit(solution)/shard_map/ppermute | solution.py:162
  51.4 6.0 %collective-permute-start.11 = (f32[128,2,128]{0,2,1:T(8,128)S(1)}, f32[128,2,128]{0,2,1:T(8,128)S(1)}, u32[]{:S(2)}, u32[]{:S(2)}) collective-permute-start(f32[128,2,128]{0,2,1:T(8,128)S(1)} %get-tuple-element.25), channel_id=1, source_target_pairs={{0,8},{4,12},{8,16},{12,20},{16,24},{20,28},{24,0},{28,4},{1,9},{5... | collective-permute-start | bytes 393224 | tf_op jit(solution)/shard_map/ppermute | solution.py:162
  52.8 18.1 %collective-permute-start.12 = (f32[128,2,128]{0,2,1:T(8,128)S(1)}, f32[128,2,128]{0,2,1:T(8,128)S(1)}, u32[]{:S(2)}, u32[]{:S(2)}) collective-permute-start(f32[128,2,128]{0,2,1:T(8,128)S(1)} %get-tuple-element.26), channel_id=1, source_target_pairs={{0,12},{4,16},{8,20},{12,24},{16,28},{20,0},{24,4},{28,8},{1,13},{... | collective-permute-start | bytes 393224 | tf_op jit(solution)/shard_map/ppermute | solution.py:162
  53.7 20.0 %collective-permute-start.13 = (f32[128,2,128]{0,2,1:T(8,128)S(1)}, f32[128,2,128]{0,2,1:T(8,128)S(1)}, u32[]{:S(2)}, u32[]{:S(2)}) collective-permute-start(f32[128,2,128]{0,2,1:T(8,128)S(1)} %get-tuple-element.27), channel_id=1, source_target_pairs={{0,16},{4,20},{8,24},{12,28},{16,0},{20,4},{24,8},{28,12},{1,17},{... | collective-permute-start | bytes 393224 | tf_op jit(solution)/shard_map/ppermute | solution.py:162
  54.3 19.4 %collective-permute-start.14 = (f32[128,2,128]{0,2,1:T(8,128)S(1)}, f32[128,2,128]{0,2,1:T(8,128)S(1)}, u32[]{:S(2)}, u32[]{:S(2)}) collective-permute-start(f32[128,2,128]{0,2,1:T(8,128)S(1)} %get-tuple-element.29), channel_id=1, source_target_pairs={{0,20},{4,24},{8,28},{12,0},{16,4},{20,8},{24,12},{28,16},{1,21},{... | collective-permute-start | bytes 393224 | tf_op jit(solution)/shard_map/ppermute | solution.py:162
  56.4 19.9 %collective-permute-start.15 = (f32[128,2,128]{0,2,1:T(8,128)S(1)}, f32[128,2,128]{0,2,1:T(8,128)S(1)}, u32[]{:S(2)}, u32[]{:S(2)}) collective-permute-start(f32[128,2,128]{0,2,1:T(8,128)S(1)} %get-tuple-element.28), channel_id=1, source_target_pairs={{0,24},{4,28},{8,0},{12,4},{16,8},{20,12},{24,16},{28,20},{1,25},{... | collective-permute-start | bytes 393224 | tf_op jit(solution)/shard_map/ppermute | solution.py:162
  57.5 18.9 %collective-permute-start.16 = (f32[128,2,128]{0,2,1:T(8,128)S(1)}, f32[128,2,128]{0,2,1:T(8,128)S(1)}, u32[]{:S(2)}, u32[]{:S(2)}) collective-permute-start(f32[128,2,128]{0,2,1:T(8,128)S(1)} %get-tuple-element.22), channel_id=1, source_target_pairs={{0,28},{4,0},{8,4},{12,8},{16,12},{20,16},{24,20},{28,24},{1,29},{... | collective-permute-start | bytes 393224 | tf_op jit(solution)/shard_map/ppermute | solution.py:162
  76.5 1.0 %copy-start = (bf16[128,1024]{1,0:T(8,128)(2,1)S(1)}, bf16[128,1024]{1,0:T(8,128)(2,1)}, u32[]{:S(2)}) copy-start(bf16[128,1024]{1,0:T(8,128)(2,1)} %param.19) | copy-start | bytes 786436
  76.5 1.0 %copy-start.1 = (bf16[128,1024]{1,0:T(8,128)(2,1)S(1)}, bf16[128,1024]{1,0:T(8,128)(2,1)}, u32[]{:S(2)}) copy-start(bf16[128,1024]{1,0:T(8,128)(2,1)} %param.18) | copy-start | bytes 786436

commit v9 on v8

--- a/solution.py
+++ b/solution.py
@@ -4,6 +4,7 @@
 import numpy as np
 import jax.numpy as jnp
 from jax import lax
+from jax.experimental import pallas as pl
 from jax.sharding import PartitionSpec as P
 
 
@@ -16,7 +17,7 @@
     return upper, lower
 
 
-def gather_matmul(out_grad, out_weight):
+def gather_tp(out_grad):
     count = lax.axis_size("tp")
     me = lax.axis_index("tp")
     pieces = [out_grad]
@@ -29,10 +30,40 @@
         lax.dynamic_index_in_dim(stacked, (me - source) % count, 0, keepdims=False)
         for source in range(count)
     ]
-    gathered = jnp.concatenate(ordered, axis=1)
-    return lax.dot_general(
-        gathered, out_weight, (((1,), (1,)), ((), ())), preferred_element_type=jnp.float32
-    )
+    return jnp.concatenate(ordered, axis=1)
+
+
+def gate_kernel(grad_ref, weight_ref, saved_ref, query_ref, dq_ref, dz_ref):
+    product = lax.dot_general(
+        grad_ref[...], weight_ref[...], (((1,), (1,)), ((), ())),
+        preferred_element_type=jnp.float32,
+    )
+    dq_ref[...] = (product * saved_ref[...].astype(jnp.float32)).astype(dq_ref.dtype)
+    dz_ref[...] = product * query_ref[...].astype(jnp.float32)
+
+
+def gate_matmul(gathered, out_weight, saved_conv, q_proj):
+    rows, width = gathered.shape
+    chans = out_weight.shape[0]
+    tile = min(chans, 256)
+    return pl.pallas_call(
+        gate_kernel,
+        grid=(chans // tile,),
+        in_specs=[
+            pl.BlockSpec((rows, width), lambda i: (0, 0)),
+            pl.BlockSpec((tile, width), lambda i: (i, 0)),
+            pl.BlockSpec((rows, tile), lambda i: (0, i)),
+            pl.BlockSpec((rows, tile), lambda i: (0, i)),
+        ],
+        out_specs=[
+            pl.BlockSpec((rows, tile), lambda i: (0, i)),
+            pl.BlockSpec((rows, tile), lambda i: (0, i)),
+        ],
+        out_shape=[
+            jax.ShapeDtypeStruct((rows, chans), jnp.bfloat16),
+            jax.ShapeDtypeStruct((rows, chans), jnp.float32),
+        ],
+    )(gathered, out_weight, saved_conv, q_proj)
 
 
 def split_constant(table):
@@ -178,9 +209,7 @@
     inputs_t = all_to_all_ctx(
         jnp.stack([to_groups(gated, blocks), to_groups(filter_taps, blocks)], axis=1)
     )
-    d_gated = gather_matmul(out_grad, out_weight)
-    dq_grad = (d_gated * saved_conv.astype(jnp.float32)).astype(jnp.bfloat16)
-    dz = d_gated * q_proj.astype(jnp.float32)
+    dq_grad, dz = gate_matmul(gather_tp(out_grad), out_weight, saved_conv, q_proj)
     dz_hi, dz_lo = split_bf16(dz)
     dz_t = transpose_ctx(jnp.stack([to_groups(dz_hi, blocks), to_groups(dz_lo, blocks)], axis=1))
     sub = chans // blocks

time: 80 us -> 83.1 us (1.039)
  Pallas kernels: 0 us -> 7.6 us
  matrix products: 13.3 us -> 7.01 us
  other arithmetic: 5.99 us -> 8.37 us
    pallas_call x0 -> x1, Pallas kernels: none -> 7.6 us  [gate_matmul(): pl.pallas_call(gate_kernel, grid=(chans // tile,), in_specs=[pl.BlockSpec...]
    dot_general x1 -> x0, matrix products: 6.3 us -> none  [gather_matmul(): lax.dot_general(gathered, out_weight, (((1,), (1,)), ((), ())), preferred...]
    convert_element_type x4 -> x5, other arithmetic: 1.71 us -> 2.78 us  [split_bf16(): upper = lax.optimization_barrier(value.astype(jnp.bfloat16))]
    concatenate x0 -> x1, other arithmetic: none -> 1.07 us  [gather_tp(): return jnp.concatenate(ordered, axis=1)]
    unnamed x68 -> x64, local copies, waits for them, and re-layouts: 4.88 us -> 4.18 us
  transfers between devices with their start and end apart: 18 -> 18, of which waited for: 9 -> 9; matrix products, arithmetic and copies ran while one was open for 17% -> 11% of each run, Pallas kernels for 0% -> 9%
where the time goes in v9:
time: 83.1 us; the launch traced here: 82.4 us
  waiting for transfers between devices  26.7 us (32%)
  starting transfers between devices  26 us (31%)
  other arithmetic  8.37 us (10%)
  Pallas kernels  7.6 us (9%)
  matrix products  7.01 us (8%)
  local copies, waits for them, and re-layouts  5.37 us (6%)
  between operations  1.4 us (2%)
    ppermute x14, waiting for transfers between devices, transpose_ctx(): lax.ppermute(chunk, 'ctx', [(i, (i + shift) % count) for i in range(count)])  25.1 us
    ppermute x14, starting transfers between devices, transpose_ctx(): lax.ppermute(chunk, 'ctx', [(i, (i + shift) % count) for i in range(count)])  16.8 us
    pallas_call x1, Pallas kernels, gate_matmul(): pl.pallas_call(gate_kernel, grid=(chans // tile,), in_specs=[pl.BlockSpec...  7.6 us
    all_to_all x1, starting transfers between devices, all_to_all_ctx(): return lax.all_to_all(stacked, 'ctx', 0, 0, tiled=True)  6.44 us
    dot_general x26, matrix products, one(): jnp.einsum('kn,bnc->bkc', left, right, preferred_element_type=jnp.float32)  6.31 us
    unnamed x64, local copies, waits for them, and re-layouts  4.18 us
    convert_element_type x5, other arithmetic, split_bf16(): upper = lax.optimization_barrier(value.astype(jnp.bfloat16))  2.78 us
    ppermute x3, starting transfers between devices, gather_tp(): lax.ppermute(out_grad, 'tp', [(i, (i + shift) % count) for i in range(cou...  2.76 us
  transfers between devices with their start and end apart: 18, of which 9 were waited for; matrix products, arithmetic and copies ran while one was open for 11% of the time, Pallas kernels for 9%

profile of v9, /device:TPU:9, one launch (start us, length us, event | category | flops | bytes accessed | tf_op | source)
XLA Modules:
  0.0 82.4 jit_solution(5442192459769008943)
XLA Ops:
  0.6 2.2 %collective-permute-start.2 = (bf16[128,1024]{1,0:T(8,128)(2,1)}, bf16[128,1024]{1,0:T(8,128)(2,1)S(1)}, u32[]{:S(2)}, u32[]{:S(2)}) collective-permute-start(bf16[128,1024]{1,0:T(8,128)(2,1)} %param.21), channel_id=1, source_target_pairs={{0,3},{1,0},{2,1},{3,2},{4,7},{5,4},{6,5},{7,6},{8,11},{9,8},{10,9... | collective-permute-start | bytes 786440 | tf_op jit(solution)/shard_map/ppermute | solution.py:26
  2.9 0.2 collective-permute-start.1
  3.1 0.3 collective-permute-start
  3.4 1.1 %fusion.14 = bf16[128,1024]{1,0:T(8,128)(2,1)S(1)} fusion(bf16[128,1024]{1,0:T(8,128)(2,1)} %param.19, bf16[128,1024]{1,0:T(8,128)(2,1)} %param.18), kind=kLoop, calls=%fused_computation.81 | loop fusion | flops 524288 | bytes 786432 | tf_op jit(solution)/shard_map/convert_element_type | solution.py:208
  4.5 1.1 %copy.29 = bf16[128,1024]{0,1:T(8,128)(2,1)S(1)} copy(bf16[128,1024]{1,0:T(8,128)(2,1)} %param.23) | data formatting | bytes 524288 | tf_op args[6]
  5.8 0.9 %pad_maximum_fusion.2 = bf16[8,2,128,128]{2,3,1,0:T(8,128)(2,1)} fusion(bf16[8,1,128,128]{2,3,1,0:T(8,128)(2,1)S(1)} %bitcast.319, bf16[8,1,128,128]{2,3,1,0:T(8,128)(2,1)S(1)} %bitcast.320), kind=kLoop, calls=%fused_computation.86 | loop fusion | flops 262144 | bytes 1048576 | tf_op jit(solution)/shard_map/stack | solution.py:210
  6.7 6.4 %all-to-all-start = ((bf16[8,2,128,128]{2,3,1,0:T(8,128)(2,1)}), bf16[8,2,128,128]{2,3,1,0:T(8,128)(2,1)S(1)}, u32[]{:S(2)}, u32[]{:S(2)}) async-start(bf16[8,2,128,128]{2,3,1,0:T(8,128)(2,1)} %pad_maximum_fusion.2), calls=%async_computation | async-start | bytes 1048576 | tf_op jit(solution)/shard_map/all_to_all | solution.py:183
  13.1 1.6 %collective-permute-done = bf16[128,1024]{1,0:T(8,128)(2,1)S(1)} collective-permute-done((bf16[128,1024]{1,0:T(8,128)(2,1)}, bf16[128,1024]{1,0:T(8,128)(2,1)S(1)}, u32[]{:S(2)}, u32[]{:S(2)}) %collective-permute-start) | collective-permute-done | bytes 262176 | tf_op jit(solution)/shard_map/ppermute | solution.py:26
  14.9 1.1 %pad_maximum_fusion.1.grad_ref = bf16[128,4096]{1,0:T(8,128)(2,1)} fusion(bf16[128,1024]{1,0:T(8,128)(2,1)S(1)} %get-tuple-element.35, bf16[128,1024]{1,0:T(8,128)(2,1)S(1)} %get-tuple-element.36, bf16[128,1024]{1,0:T(8,128)(2,1)S(1)} %get-tuple-element.37, bf16[128,1024]{1,0:T(8,128)(2,1)S(1)} %get-tuple-element.34), kind=kLoop, calls=%fused_computation.60 | loop fusion | flops 4194304 | bytes 2097152 | tf_op jit(solution)/shard_map/concatenate | solution.py:33
  16.0 7.6 %shard_map.192 = (bf16[128,1024]{1,0:T(8,128)(2,1)}, f32[128,1024]{1,0:T(8,128)}) custom-call(bf16[128,4096]{1,0:T(8,128)(2,1)} %pad_maximum_fusion.1.grad_ref, bf16[1024,4096]{1,0:T(8,128)(2,1)} %weight_ref.1, bf16[128,1024]{1,0:T(8,128)(2,1)} %saved_ref.1, bf16[128,1024]{1,0:T(8,128)(2,1)} %query_ref.1), custom_call_target="tpu_custom_call" | custom-call | tf_op jit(solution)/shard_map/pallas_call | solution.py:49
  23.6 1.1 %convert_element_type.75 = bf16[128,1024]{1,0:T(8,128)(2,1)S(1)} convert(f32[128,1024]{1,0:T(8,128)} %get-tuple-element.7) | non-fusion elementwise | flops 131072 | bytes 786432 | tf_op jit(solution)/shard_map/convert_element_type | solution.py:15
  24.7 1.1 %subtract_convert_fusion.4 = bf16[128,1024]{1,0:T(8,128)(2,1)S(1)} fusion(f32[128,1024]{1,0:T(8,128)} %get-tuple-element.7, bf16[128,1024]{1,0:T(8,128)(2,1)S(1)} %convert_element_type.75), kind=kLoop, calls=%fused_computation.96 | loop fusion | flops 393216 | bytes 1048576 | tf_op jit(solution)/shard_map/convert_element_type | solution.py:16
  26.2 3.9 %collective-permute-start.3 = (bf16[2,128,128]{1,2,0:T(8,128)(2,1)S(1)}, bf16[2,128,128]{1,2,0:T(8,128)(2,1)S(1)}, u32[]{:S(2)}, u32[]{:S(2)}) collective-permute-start(bf16[2,128,128]{1,2,0:T(8,128)(2,1)S(1)} %get-tuple-element.74), channel_id=1, source_target_pairs={{0,4},{4,8},{8,12},{12,16},{16,20},{20,24},{24,28},{28,0},{1,5},{5... | collective-permute-start | bytes 196616 | tf_op jit(solution)/shard_map/ppermute | solution.py:193
  30.2 1.3 %collective-permute-start.4 = (bf16[2,128,128]{1,2,0:T(8,128)(2,1)S(1)}, bf16[2,128,128]{1,2,0:T(8,128)(2,1)S(1)}, u32[]{:S(2)}, u32[]{:S(2)}) collective-permute-start(bf16[2,128,128]{1,2,0:T(8,128)(2,1)S(1)} %get-tuple-element.75), channel_id=1, source_target_pairs={{0,8},{4,12},{8,16},{12,20},{16,24},{20,28},{24,0},{28,4},{1,9},{5... | collective-permute-start | bytes 196616 | tf_op jit(solution)/shard_map/ppermute | solution.py:193
  31.5 1.4 %collective-permute-start.6 = (bf16[2,128,128]{1,2,0:T(8,128)(2,1)S(1)}, bf16[2,128,128]{1,2,0:T(8,128)(2,1)S(1)}, u32[]{:S(2)}, u32[]{:S(2)}) collective-permute-start(bf16[2,128,128]{1,2,0:T(8,128)(2,1)S(1)} %get-tuple-element.77), channel_id=1, source_target_pairs={{0,16},{4,20},{8,24},{12,28},{16,0},{20,4},{24,8},{28,12},{1,17},{... | collective-permute-start | bytes 196616 | tf_op jit(solution)/shard_map/ppermute | solution.py:193
  32.9 1.6 %collective-permute-start.7 = (bf16[2,128,128]{1,2,0:T(8,128)(2,1)S(1)}, bf16[2,128,128]{1,2,0:T(8,128)(2,1)S(1)}, u32[]{:S(2)}, u32[]{:S(2)}) collective-permute-start(bf16[2,128,128]{1,2,0:T(8,128)(2,1)S(1)} %get-tuple-element.79), channel_id=1, source_target_pairs={{0,20},{4,24},{8,28},{12,0},{16,4},{20,8},{24,12},{28,16},{1,21},{... | collective-permute-start | bytes 196616 | tf_op jit(solution)/shard_map/ppermute | solution.py:193
  34.5 1.1 %collective-permute-start.8 = (bf16[2,128,128]{1,2,0:T(8,128)(2,1)S(1)}, bf16[2,128,128]{1,2,0:T(8,128)(2,1)S(1)}, u32[]{:S(2)}, u32[]{:S(2)}) collective-permute-start(bf16[2,128,128]{1,2,0:T(8,128)(2,1)S(1)} %get-tuple-element.78), channel_id=1, source_target_pairs={{0,24},{4,28},{8,0},{12,4},{16,8},{20,12},{24,16},{28,20},{1,25},{... | collective-permute-start | bytes 196616 | tf_op jit(solution)/shard_map/ppermute | solution.py:193
  35.7 0.5 collective-permute-start.9
  36.2 3.0 %collective-permute-done.5 = bf16[2,128,128]{1,2,0:T(8,128)(2,1)S(1)} collective-permute-done((bf16[2,128,128]{1,2,0:T(8,128)(2,1)S(1)}, bf16[2,128,128]{1,2,0:T(8,128)(2,1)S(1)}, u32[]{:S(2)}, u32[]{:S(2)}) %collective-permute-start.5) | collective-permute-done | bytes 65568 | tf_op jit(solution)/shard_map/ppermute | solution.py:193
  39.2 2.2 %collective-permute-done.6 = bf16[2,128,128]{1,2,0:T(8,128)(2,1)S(1)} collective-permute-done((bf16[2,128,128]{1,2,0:T(8,128)(2,1)S(1)}, bf16[2,128,128]{1,2,0:T(8,128)(2,1)S(1)}, u32[]{:S(2)}, u32[]{:S(2)}) %collective-permute-start.6) | collective-permute-done | bytes 65568 | tf_op jit(solution)/shard_map/ppermute | solution.py:193
  41.5 1.8 %collective-permute-done.8 = bf16[2,128,128]{1,2,0:T(8,128)(2,1)S(1)} collective-permute-done((bf16[2,128,128]{1,2,0:T(8,128)(2,1)S(1)}, bf16[2,128,128]{1,2,0:T(8,128)(2,1)S(1)}, u32[]{:S(2)}, u32[]{:S(2)}) %collective-permute-start.8) | collective-permute-done | bytes 65568 | tf_op jit(solution)/shard_map/ppermute | solution.py:193
  43.9 0.2 fusion.24
  44.2 0.2 convolution_add_fusion.14
  44.4 0.2 fusion.23
  44.7 0.2 fusion.7
  44.9 0.2 convolution_add_fusion.11
  45.2 0.2 fusion.5
  45.4 0.2 fusion.21
  45.6 0.2 fusion.8
  45.9 0.2 fusion.20
  46.1 0.2 fusion.6
  46.6 0.4 fusion.65
  47.1 0.4 fusion.64
  47.5 0.2 fusion.26
  47.7 0.2 fusion.27
  48.0 0.2 fusion.3
  48.2 0.2 fusion.4
  48.5 0.4 fusion.63
  49.0 0.4 fusion.62
  49.8 0.3 fusion.69
  50.1 0.3 convolution_add_fusion.3
  50.4 0.3 convolution_add_fusion.2
  50.9 0.3 fusion.70
  51.3 0.3 convolution_add_fusion.1
  51.6 0.3 fusion.2
  52.1 0.6 copy-done.10
  52.7 0.2 fusion.68
  53.0 0.2 convolution_add_fusion.7
  53.2 0.2 convolution_add_fusion.6
  53.5 0.2 fusion.67
  53.7 0.2 convolution_add_fusion.9
  54.0 0.3 fusion.12
  54.4 1.4 %collective-permute-start.11 = (f32[128,2,128]{0,2,1:T(8,128)S(1)}, f32[128,2,128]{0,2,1:T(8,128)S(1)}, u32[]{:S(2)}, u32[]{:S(2)}) collective-permute-start(f32[128,2,128]{0,2,1:T(8,128)S(1)} %get-tuple-element.29), channel_id=1, source_target_pairs={{0,8},{4,12},{8,16},{12,20},{16,24},{20,28},{24,0},{28,4},{1,9},{5... | collective-permute-start | bytes 393224 | tf_op jit(solution)/shard_map/ppermute | solution.py:193
  55.8 0.9 %collective-permute-start.12 = (f32[128,2,128]{0,2,1:T(8,128)S(1)}, f32[128,2,128]{0,2,1:T(8,128)S(1)}, u32[]{:S(2)}, u32[]{:S(2)}) collective-permute-start(f32[128,2,128]{0,2,1:T(8,128)S(1)} %get-tuple-element.30), channel_id=1, source_target_pairs={{0,12},{4,16},{8,20},{12,24},{16,28},{20,0},{24,4},{28,8},{1,13},{... | collective-permute-start | bytes 393224 | tf_op jit(solution)/shard_map/ppermute | solution.py:193
  56.7 0.5 collective-permute-start.13
  57.2 2.1 %collective-permute-start.14 = (f32[128,2,128]{0,2,1:T(8,128)S(1)}, f32[128,2,128]{0,2,1:T(8,128)S(1)}, u32[]{:S(2)}, u32[]{:S(2)}) collective-permute-start(f32[128,2,128]{0,2,1:T(8,128)S(1)} %get-tuple-element.33), channel_id=1, source_target_pairs={{0,20},{4,24},{8,28},{12,0},{16,4},{20,8},{24,12},{28,16},{1,21},{... | collective-permute-start | bytes 393224 | tf_op jit(solution)/shard_map/ppermute | solution.py:193
  59.3 1.1 %collective-permute-start.15 = (f32[128,2,128]{0,2,1:T(8,128)S(1)}, f32[128,2,128]{0,2,1:T(8,128)S(1)}, u32[]{:S(2)}, u32[]{:S(2)}) collective-permute-start(f32[128,2,128]{0,2,1:T(8,128)S(1)} %get-tuple-element.32), channel_id=1, source_target_pairs={{0,24},{4,28},{8,0},{12,4},{16,8},{20,12},{24,16},{28,20},{1,25},{... | collective-permute-start | bytes 393224 | tf_op jit(solution)/shard_map/ppermute | solution.py:193
  60.4 0.8 %collective-permute-start.16 = (f32[128,2,128]{0,2,1:T(8,128)S(1)}, f32[128,2,128]{0,2,1:T(8,128)S(1)}, u32[]{:S(2)}, u32[]{:S(2)}) collective-permute-start(f32[128,2,128]{0,2,1:T(8,128)S(1)} %get-tuple-element.26), channel_id=1, source_target_pairs={{0,28},{4,0},{8,4},{12,8},{16,12},{20,16},{24,20},{28,24},{1,29},{... | collective-permute-start | bytes 393224 | tf_op jit(solution)/shard_map/ppermute | solution.py:193
  61.3 12.6 %collective-permute-done.12 = f32[128,2,128]{0,2,1:T(8,128)S(1)} collective-permute-done((f32[128,2,128]{0,2,1:T(8,128)S(1)}, f32[128,2,128]{0,2,1:T(8,128)S(1)}, u32[]{:S(2)}, u32[]{:S(2)}) %collective-permute-start.12) | collective-permute-done | bytes 131104 | tf_op jit(solution)/shard_map/ppermute | solution.py:193
  73.9 2.8 %collective-permute-done.13 = f32[128,2,128]{0,2,1:T(8,128)S(1)} collective-permute-done((f32[128,2,128]{0,2,1:T(8,128)S(1)}, f32[128,2,128]{0,2,1:T(8,128)S(1)}, u32[]{:S(2)}, u32[]{:S(2)}) %collective-permute-start.13) | collective-permute-done | bytes 131104 | tf_op jit(solution)/shard_map/ppermute | solution.py:193
  76.7 2.5 %collective-permute-done.15 = f32[128,2,128]{0,2,1:T(8,128)S(1)} collective-permute-done((f32[128,2,128]{0,2,1:T(8,128)S(1)}, f32[128,2,128]{0,2,1:T(8,128)S(1)}, u32[]{:S(2)}, u32[]{:S(2)}) %collective-permute-start.15) | collective-permute-done | bytes 131104 | tf_op jit(solution)/shard_map/ppermute | solution.py:193
  79.9 0.5 copy-done
  80.5 0.9 %fusion.13 = (bf16[128,1024]{1,0:T(8,128)(2,1)}, bf16[128,1024]{1,0:T(8,128)(2,1)}) fusion(f32[128,1024]{1,0:T(8,128)S(1)} %copy.34, bf16[128,1024]{1,0:T(8,128)(2,1)S(1)} %copy-done.1, bf16[128,1024]{1,0:T(8,128)(2,1)S(1)} %copy-done), kind=kLoop, calls=%fused_computation.80 | loop fusion | flops 786432 | bytes 1572864 | tf_op jit(solution)/shard_map/convert_element_type | solution.py:227
  81.4 1.0 %copy.36 = f32[128,1024]{1,0:T(8,128)} copy(f32[128,1024]{0,1:T(8,128)S(1)} %bitcast.317) | data formatting | bytes 1048576
  (104 shorter events, 3.6 us)
Async XLA Ops:
  0.6 14.1 %copy-start.6 = (bf16[128,1024]{1,0:T(8,128)(2,1)S(1)}, bf16[128,1024]{1,0:T(8,128)(2,1)}, u32[]{:S(2)}) copy-start(bf16[128,1024]{1,0:T(8,128)(2,1)} %param.21) | copy-start | bytes 786436
  0.6 12.5 %collective-permute-start.2 = (bf16[128,1024]{1,0:T(8,128)(2,1)}, bf16[128,1024]{1,0:T(8,128)(2,1)S(1)}, u32[]{:S(2)}, u32[]{:S(2)}) collective-permute-start(bf16[128,1024]{1,0:T(8,128)(2,1)} %param.21), channel_id=1, source_target_pairs={{0,3},{1,0},{2,1},{3,2},{4,7},{5,4},{6,5},{7,6},{8,11},{9,8},{10,9... | collective-permute-start | bytes 786440 | tf_op jit(solution)/shard_map/ppermute | solution.py:26
  2.9 10.3 %collective-permute-start.1 = (bf16[128,1024]{1,0:T(8,128)(2,1)}, bf16[128,1024]{1,0:T(8,128)(2,1)S(1)}, u32[]{:S(2)}, u32[]{:S(2)}) collective-permute-start(bf16[128,1024]{1,0:T(8,128)(2,1)} %param.21), channel_id=1, source_target_pairs={{0,2},{1,3},{2,0},{3,1},{4,6},{5,7},{6,4},{7,5},{8,10},{9,11},{10,... | collective-permute-start | bytes 786440 | tf_op jit(solution)/shard_map/ppermute | solution.py:26
  3.1 11.6 %collective-permute-start = (bf16[128,1024]{1,0:T(8,128)(2,1)}, bf16[128,1024]{1,0:T(8,128)(2,1)S(1)}, u32[]{:S(2)}, u32[]{:S(2)}) collective-permute-start(bf16[128,1024]{1,0:T(8,128)(2,1)} %param.21), channel_id=1, source_target_pairs={{0,1},{1,2},{2,3},{3,0},{4,5},{5,6},{6,7},{7,4},{8,9},{9,10},{10,1... | collective-permute-start | bytes 786440 | tf_op jit(solution)/shard_map/ppermute | solution.py:26
  6.7 38.7 %all-to-all-start = ((bf16[8,2,128,128]{2,3,1,0:T(8,128)(2,1)}), bf16[8,2,128,128]{2,3,1,0:T(8,128)(2,1)S(1)}, u32[]{:S(2)}, u32[]{:S(2)}) async-start(bf16[8,2,128,128]{2,3,1,0:T(8,128)(2,1)} %pad_maximum_fusion.2), calls=%async_computation | async-start | bytes 1048576 | tf_op jit(solution)/shard_map/all_to_all | solution.py:183
  26.0 17.6 %copy-start.17 = (bf16[128,1,1]{0,1,2:T(2,128)(2,1)S(1)}, bf16[128,1,1]{0,1,2:T(2,128)(2,1)}, u32[]{:S(2)}) copy-start(bf16[128,1,1]{0,1,2:T(2,128)(2,1)} %constant.317) | copy-start | bytes 772
  26.2 17.8 %copy-start.2 = (bf16[128,128,1]{1,0,2:T(8,128)(2,1)S(1)}, bf16[128,128,1]{1,0,2:T(8,128)(2,1)}, u32[]{:S(2)}) copy-start(bf16[128,128,1]{1,0,2:T(8,128)(2,1)} %constant.309) | copy-start | bytes 98308
  26.2 18.0 %copy-start.4 = (bf16[128,128,1]{1,0,2:T(8,128)(2,1)S(1)}, bf16[128,128,1]{1,0,2:T(8,128)(2,1)}, u32[]{:S(2)}) copy-start(bf16[128,128,1]{1,0,2:T(8,128)(2,1)} %constant.310) | copy-start | bytes 98308
  26.2 8.3 %collective-permute-start.3 = (bf16[2,128,128]{1,2,0:T(8,128)(2,1)S(1)}, bf16[2,128,128]{1,2,0:T(8,128)(2,1)S(1)}, u32[]{:S(2)}, u32[]{:S(2)}) collective-permute-start(bf16[2,128,128]{1,2,0:T(8,128)(2,1)S(1)} %get-tuple-element.74), channel_id=1, source_target_pairs={{0,4},{4,8},{8,12},{12,16},{16,20},{20,24},{24,28},{28,0},{1,5},{5... | collective-permute-start | bytes 196616 | tf_op jit(solution)/shard_map/ppermute | solution.py:193
  30.2 5.5 %collective-permute-start.4 = (bf16[2,128,128]{1,2,0:T(8,128)(2,1)S(1)}, bf16[2,128,128]{1,2,0:T(8,128)(2,1)S(1)}, u32[]{:S(2)}, u32[]{:S(2)}) collective-permute-start(bf16[2,128,128]{1,2,0:T(8,128)(2,1)S(1)} %get-tuple-element.75), channel_id=1, source_target_pairs={{0,8},{4,12},{8,16},{12,20},{16,24},{20,28},{24,0},{28,4},{1,9},{5... | collective-permute-start | bytes 196616 | tf_op jit(solution)/shard_map/ppermute | solution.py:193
  31.5 7.7 %collective-permute-start.5 = (bf16[2,128,128]{1,2,0:T(8,128)(2,1)S(1)}, bf16[2,128,128]{1,2,0:T(8,128)(2,1)S(1)}, u32[]{:S(2)}, u32[]{:S(2)}) collective-permute-start(bf16[2,128,128]{1,2,0:T(8,128)(2,1)S(1)} %get-tuple-element.76), channel_id=1, source_target_pairs={{0,12},{4,16},{8,20},{12,24},{16,28},{20,0},{24,4},{28,8},{1,13},{... | collective-permute-start | bytes 196616 | tf_op jit(solution)/shard_map/ppermute | solution.py:193
  31.5 10.0 %collective-permute-start.6 = (bf16[2,128,128]{1,2,0:T(8,128)(2,1)S(1)}, bf16[2,128,128]{1,2,0:T(8,128)(2,1)S(1)}, u32[]{:S(2)}, u32[]{:S(2)}) collective-permute-start(bf16[2,128,128]{1,2,0:T(8,128)(2,1)S(1)} %get-tuple-element.77), channel_id=1, source_target_pairs={{0,16},{4,20},{8,24},{12,28},{16,0},{20,4},{24,8},{28,12},{1,17},{... | collective-permute-start | bytes 196616 | tf_op jit(solution)/shard_map/ppermute | solution.py:193
  32.9 8.6 %collective-permute-start.7 = (bf16[2,128,128]{1,2,0:T(8,128)(2,1)S(1)}, bf16[2,128,128]{1,2,0:T(8,128)(2,1)S(1)}, u32[]{:S(2)}, u32[]{:S(2)}) collective-permute-start(bf16[2,128,128]{1,2,0:T(8,128)(2,1)S(1)} %get-tuple-element.79), channel_id=1, source_target_pairs={{0,20},{4,24},{8,28},{12,0},{16,4},{20,8},{24,12},{28,16},{1,21},{... | collective-permute-start | bytes 196616 | tf_op jit(solution)/shard_map/ppermute | solution.py:193
  34.5 8.7 %collective-permute-start.8 = (bf16[2,128,128]{1,2,0:T(8,128)(2,1)S(1)}, bf16[2,128,128]{1,2,0:T(8,128)(2,1)S(1)}, u32[]{:S(2)}, u32[]{:S(2)}) collective-permute-start(bf16[2,128,128]{1,2,0:T(8,128)(2,1)S(1)} %get-tuple-element.78), channel_id=1, source_target_pairs={{0,24},{4,28},{8,0},{12,4},{16,8},{20,12},{24,16},{28,20},{1,25},{... | collective-permute-start | bytes 196616 | tf_op jit(solution)/shard_map/ppermute | solution.py:193
  35.7 7.7 %collective-permute-start.9 = (bf16[2,128,128]{1,2,0:T(8,128)(2,1)S(1)}, bf16[2,128,128]{1,2,0:T(8,128)(2,1)S(1)}, u32[]{:S(2)}, u32[]{:S(2)}) collective-permute-start(bf16[2,128,128]{1,2,0:T(8,128)(2,1)S(1)} %get-tuple-element.72), channel_id=1, source_target_pairs={{0,28},{4,0},{8,4},{12,8},{16,12},{20,16},{24,20},{28,24},{1,29},{... | collective-permute-start | bytes 196616 | tf_op jit(solution)/shard_map/ppermute | solution.py:193
  41.5 3.0 %copy-start.3 = (bf16[128,128,1]{1,0,2:T(8,128)(2,1)S(1)}, bf16[128,128,1]{1,0,2:T(8,128)(2,1)}, u32[]{:S(2)}) copy-start(bf16[128,128,1]{1,0,2:T(8,128)(2,1)} %constant.311) | copy-start | bytes 98308
  43.9 1.0 %copy-start.5 = (bf16[128,128,1]{1,0,2:T(8,128)(2,1)S(1)}, bf16[128,128,1]{1,0,2:T(8,128)(2,1)}, u32[]{:S(2)}) copy-start(bf16[128,128,1]{1,0,2:T(8,128)(2,1)} %constant.312) | copy-start | bytes 98308
  48.9 0.8 %copy-start.7 = (bf16[256,128,1]{1,0,2:T(8,128)(2,1)S(1)}, bf16[256,128,1]{1,0,2:T(8,128)(2,1)}, u32[]{:S(2)}) copy-start(bf16[256,128,1]{1,0,2:T(8,128)(2,1)} %constant.318) | copy-start | bytes 196612
  49.0 1.1 %copy-start.12 = (bf16[256,128,1]{1,0,2:T(8,128)(2,1)S(1)}, bf16[256,128,1]{1,0,2:T(8,128)(2,1)}, u32[]{:S(2)}) copy-start(bf16[256,128,1]{1,0,2:T(8,128)(2,1)} %constant.319) | copy-start | bytes 196612
  50.1 0.8 %copy-start.8 = (bf16[256,128,1]{1,0,2:T(8,128)(2,1)S(1)}, bf16[256,128,1]{1,0,2:T(8,128)(2,1)}, u32[]{:S(2)}) copy-start(bf16[256,128,1]{1,0,2:T(8,128)(2,1)} %constant.320) | copy-start | bytes 196612
  50.4 0.9 %copy-start.11 = (bf16[256,128,1]{1,0,2:T(8,128)(2,1)S(1)}, bf16[256,128,1]{1,0,2:T(8,128)(2,1)}, u32[]{:S(2)}) copy-start(bf16[256,128,1]{1,0,2:T(8,128)(2,1)} %constant.321) | copy-start | bytes 196612
  50.9 0.7 copy-start.15
  52.0 0.8 copy-start.10
  52.0 1.0 %copy-start.14 = (bf16[128,128,1]{1,0,2:T(8,128)(2,1)S(1)}, bf16[128,128,1]{1,0,2:T(8,128)(2,1)}, u32[]{:S(2)}) copy-start(bf16[128,128,1]{1,0,2:T(8,128)(2,1)} %constant.316) | copy-start | bytes 98308
  52.7 0.8 copy-start.9
  53.0 0.8 copy-start.13
  53.2 0.8 copy-start.16
  54.3 5.0 %collective-permute-start.10 = (f32[128,2,128]{0,2,1:T(8,128)S(1)}, f32[128,2,128]{0,2,1:T(8,128)S(1)}, u32[]{:S(2)}, u32[]{:S(2)}) collective-permute-start(f32[128,2,128]{0,2,1:T(8,128)S(1)} %get-tuple-element.28), channel_id=1, source_target_pairs={{0,4},{4,8},{8,12},{12,16},{16,20},{20,24},{24,28},{28,0},{1,5},{5... | collective-permute-start | bytes 393224 | tf_op jit(solution)/shard_map/ppermute | solution.py:193
  54.4 6.0 %collective-permute-start.11 = (f32[128,2,128]{0,2,1:T(8,128)S(1)}, f32[128,2,128]{0,2,1:T(8,128)S(1)}, u32[]{:S(2)}, u32[]{:S(2)}) collective-permute-start(f32[128,2,128]{0,2,1:T(8,128)S(1)} %get-tuple-element.29), channel_id=1, source_target_pairs={{0,8},{4,12},{8,16},{12,20},{16,24},{20,28},{24,0},{28,4},{1,9},{5... | collective-permute-start | bytes 393224 | tf_op jit(solution)/shard_map/ppermute | solution.py:193
  55.8 18.1 %collective-permute-start.12 = (f32[128,2,128]{0,2,1:T(8,128)S(1)}, f32[128,2,128]{0,2,1:T(8,128)S(1)}, u32[]{:S(2)}, u32[]{:S(2)}) collective-permute-start(f32[128,2,128]{0,2,1:T(8,128)S(1)} %get-tuple-element.30), channel_id=1, source_target_pairs={{0,12},{4,16},{8,20},{12,24},{16,28},{20,0},{24,4},{28,8},{1,13},{... | collective-permute-start | bytes 393224 | tf_op jit(solution)/shard_map/ppermute | solution.py:193
  56.7 20.0 %collective-permute-start.13 = (f32[128,2,128]{0,2,1:T(8,128)S(1)}, f32[128,2,128]{0,2,1:T(8,128)S(1)}, u32[]{:S(2)}, u32[]{:S(2)}) collective-permute-start(f32[128,2,128]{0,2,1:T(8,128)S(1)} %get-tuple-element.31), channel_id=1, source_target_pairs={{0,16},{4,20},{8,24},{12,28},{16,0},{20,4},{24,8},{28,12},{1,17},{... | collective-permute-start | bytes 393224 | tf_op jit(solution)/shard_map/ppermute | solution.py:193
  57.2 19.4 %collective-permute-start.14 = (f32[128,2,128]{0,2,1:T(8,128)S(1)}, f32[128,2,128]{0,2,1:T(8,128)S(1)}, u32[]{:S(2)}, u32[]{:S(2)}) collective-permute-start(f32[128,2,128]{0,2,1:T(8,128)S(1)} %get-tuple-element.33), channel_id=1, source_target_pairs={{0,20},{4,24},{8,28},{12,0},{16,4},{20,8},{24,12},{28,16},{1,21},{... | collective-permute-start | bytes 393224 | tf_op jit(solution)/shard_map/ppermute | solution.py:193
  59.3 19.9 %collective-permute-start.15 = (f32[128,2,128]{0,2,1:T(8,128)S(1)}, f32[128,2,128]{0,2,1:T(8,128)S(1)}, u32[]{:S(2)}, u32[]{:S(2)}) collective-permute-start(f32[128,2,128]{0,2,1:T(8,128)S(1)} %get-tuple-element.32), channel_id=1, source_target_pairs={{0,24},{4,28},{8,0},{12,4},{16,8},{20,12},{24,16},{28,20},{1,25},{... | collective-permute-start | bytes 393224 | tf_op jit(solution)/shard_map/ppermute | solution.py:193
  60.4 18.9 %collective-permute-start.16 = (f32[128,2,128]{0,2,1:T(8,128)S(1)}, f32[128,2,128]{0,2,1:T(8,128)S(1)}, u32[]{:S(2)}, u32[]{:S(2)}) collective-permute-start(f32[128,2,128]{0,2,1:T(8,128)S(1)} %get-tuple-element.26), channel_id=1, source_target_pairs={{0,28},{4,0},{8,4},{12,8},{16,12},{20,16},{24,20},{28,24},{1,29},{... | collective-permute-start | bytes 393224 | tf_op jit(solution)/shard_map/ppermute | solution.py:193
  79.5 1.0 %copy-start = (bf16[128,1024]{1,0:T(8,128)(2,1)S(1)}, bf16[128,1024]{1,0:T(8,128)(2,1)}, u32[]{:S(2)}) copy-start(bf16[128,1024]{1,0:T(8,128)(2,1)} %param.19) | copy-start | bytes 786436
  79.5 1.0 %copy-start.1 = (bf16[128,1024]{1,0:T(8,128)(2,1)S(1)}, bf16[128,1024]{1,0:T(8,128)(2,1)}, u32[]{:S(2)}) copy-start(bf16[128,1024]{1,0:T(8,128)(2,1)} %param.18) | copy-start | bytes 786436

commit v10 on v8

--- a/solution.py
+++ b/solution.py
@@ -47,50 +47,22 @@
     angle = (index[:, None] * index[None, :] % (2 * size)) * (math.pi / size)
     angle_back = (long_index[:, None] * index[None, :] % (2 * size)) * (math.pi / size)
     weight = np.where(index == 0, 1.0, 2.0) / (2.0 * size)
+    forward = np.concatenate([np.cos(angle), -np.sin(angle)], axis=0)
+    backward = np.concatenate(
+        [np.cos(angle_back) * weight[None, :], -np.sin(angle_back) * weight[None, :]], axis=1
+    )
     alternate = 1.0 - 2.0 * (index % 2)
     alternate_back = (1.0 - 2.0 * (long_index % 2)) / (2.0 * size)
     return {
-        "cos": split_constant(np.cos(angle)),
-        "sin": split_constant(-np.sin(angle)),
+        "fwd": split_constant(forward),
         "alt": jnp.asarray(alternate.astype(jnp.bfloat16)),
-        "icos": split_constant(np.cos(angle_back) * weight[None, :]),
-        "isin": split_constant(-np.sin(angle_back) * weight[None, :]),
+        "inv": split_constant(backward),
         "ialt": jnp.asarray(alternate_back.astype(np.float32)),
     }
 
 
-def apply(table, signal_hi, signal_lo=None):
-    def one(left, right):
-        return jnp.einsum("kn,bnc->bkc", left, right, preferred_element_type=jnp.float32)
-
-    out = one(table[0], signal_hi) + one(table[1], signal_hi)
-    if signal_lo is not None:
-        out = out + one(table[0], signal_lo)
-    return out
-
-
-def forward(tables, signal_hi, signal_lo=None):
-    real = apply(tables["cos"], signal_hi, signal_lo)
-    imag = apply(tables["sin"], signal_hi, signal_lo)
-    nyq = jnp.einsum("n,bnc->bc", tables["alt"], signal_hi, preferred_element_type=jnp.float32)
-    if signal_lo is not None:
-        nyq = nyq + jnp.einsum(
-            "n,bnc->bc", tables["alt"], signal_lo, preferred_element_type=jnp.float32
-        )
-    return real, imag, nyq
-
-
-def inverse(tables, spectrum, start, count):
-    real_hi, real_lo = split_bf16(spectrum[0])
-    imag_hi, imag_lo = split_bf16(spectrum[1])
-    icos = tuple(t[start : start + count] for t in tables["icos"])
-    isin = tuple(t[start : start + count] for t in tables["isin"])
-    ialt = tables["ialt"][start : start + count]
-    return (
-        apply(icos, real_hi, real_lo)
-        + apply(isin, imag_hi, imag_lo)
-        + ialt[None, :, None] * spectrum[2][:, None, :]
-    )
+def table_times(table, signal):
+    return jnp.einsum("kn,snc->skc", table, signal, preferred_element_type=jnp.float32)
 
 
 def conj_times(first, second):
@@ -104,10 +76,18 @@
     size = min(BLOCK, seq)
     blocks = seq // size
     tables = make_tables(size)
-    shape = (blocks, size, chans)
-    dz_spec = forward(tables, dz_hi.reshape(shape), dz_lo.reshape(shape))
-    gated_spec = forward(tables, gated.reshape(shape))
-    taps_spec = forward(tables, taps.reshape(shape))
+    signals = jnp.stack([dz_hi, dz_lo, gated, taps]).reshape(4 * blocks, size, chans)
+    upper = table_times(tables["fwd"][0], signals).reshape(4, blocks, 2 * size, chans)
+    exact = jnp.stack([dz_hi, gated, taps]).reshape(3 * blocks, size, chans)
+    lower = table_times(tables["fwd"][1], exact).reshape(3, blocks, 2 * size, chans)
+    top = jnp.einsum("n,snc->sc", tables["alt"], signals, preferred_element_type=jnp.float32)
+    top = top.reshape(4, blocks, chans)
+    dz_full = upper[0] + upper[1] + lower[0]
+    gated_full = upper[2] + lower[1]
+    taps_full = upper[3] + lower[2]
+    dz_spec = (dz_full[:, :size], dz_full[:, size:], top[0] + top[1])
+    gated_spec = (gated_full[:, :size], gated_full[:, size:], top[2])
+    taps_spec = (taps_full[:, :size], taps_full[:, size:], top[3])
     parity = (1 - 2 * (jnp.arange(size, dtype=jnp.int32) % 2)).astype(jnp.float32)[None, :, None]
     parity_top = float(1 - 2 * (size % 2))
 
@@ -131,8 +111,23 @@
         else:
             du_spec = tuple(a + b for a, b in zip(du_spec, du_term))
             lag_sums = tuple(a + b for a, b in zip(lag_sums, lag_term))
-    du = inverse(tables, du_spec, size, size).reshape(seq, chans)
-    lagged = inverse(tables, lag_sums, 0, 2 * size)
+    spectra = jnp.stack(
+        [
+            jnp.concatenate([du_spec[0], du_spec[1]], axis=1),
+            jnp.concatenate([lag_sums[0], lag_sums[1]], axis=1),
+        ]
+    ).reshape(2 * blocks, 2 * size, chans)
+    spectra_hi, spectra_lo = split_bf16(spectra)
+    inv_hi, inv_lo = tables["inv"]
+    signal = (
+        table_times(inv_hi, spectra_hi)
+        + table_times(inv_hi, spectra_lo)
+        + table_times(inv_lo, spectra_hi)
+    ).reshape(2, blocks, 2 * size, chans)
+    tops = jnp.stack([du_spec[2], lag_sums[2]])
+    signal = signal + tables["ialt"][None, None, :, None] * tops[:, :, None, :]
+    du = signal[0, :, size:].reshape(seq, chans)
+    lagged = signal[1]
     later_half = jnp.concatenate([lagged[1:, size:], jnp.zeros_like(lagged[:1, size:])], axis=0)
     filter_grad = (lagged[:, :size] + later_half).reshape(seq, chans) * seq_scale
     return du, filter_grad

time: 80 us -> 78.8 us (0.985)
  waiting for transfers between devices: 26.7 us -> 15 us
  starting transfers between devices: 26 us -> 36.6 us
  local copies, waits for them, and re-layouts: 6.1 us -> 11 us
  matrix products: 13.3 us -> 9.26 us
  other arithmetic: 5.99 us -> 5.15 us
    ppermute x14, waiting for transfers between devices: 25.1 us -> 14.5 us  [transpose_ctx(): lax.ppermute(chunk, 'ctx', [(i, (i + shift) % count) for i in range(count)])]
    ppermute x14, starting transfers between devices: 16.8 us -> 26.5 us  [transpose_ctx(): lax.ppermute(chunk, 'ctx', [(i, (i + shift) % count) for i in range(count)])]
    dot_general x30 -> x6, matrix products: 7.01 us -> 2.96 us  [the longest x5 2.72 us: table_times(): jnp.einsum('kn,snc->skc', table, signal, preferred_element_type=jnp.float32)]
    unnamed x68 -> x51, local copies, waits for them, and re-layouts: 4.88 us -> 8.22 us
    add x1 -> x4, other arithmetic: 0.01 us -> 1.74 us  [the longest x2 0.82 us: long_correlations(): du_spec = tuple((a + b for a, b in zip(du_spec, du_term)))]
    convert_element_type x4 -> x1, other arithmetic: 1.71 us -> 0.1 us  [split_bf16(): upper = lax.optimization_barrier(value.astype(jnp.bfloat16))]
    ppermute x3, waiting for transfers between devices: 1.6 us -> 0.5 us  [gather_matmul(): lax.ppermute(out_grad, 'tp', [(i, (i + shift) % count) for i in range(cou...]
    convert_element_type x1, other arithmetic: 1.09 us -> 0.07 us  [body(): (k_proj.astype(jnp.float32) * v_proj.astype(jnp.float32)).astype(jnp.bflo...]
  transfers between devices with their start and end apart: 18 -> 18, of which waited for: 9 -> 9; matrix products, arithmetic and copies ran while one was open for 17% -> 16% of each run, Pallas kernels for 0% -> 0%
where the time goes in v10:
time: 78.8 us; the launch traced here: 78.3 us
  starting transfers between devices  36.6 us (46%)
  waiting for transfers between devices  15 us (19%)
  local copies, waits for them, and re-layouts  11 us (14%)
  matrix products  9.26 us (12%)
  other arithmetic  5.15 us (7%)
  between operations  1.26 us (2%)
    ppermute x14, starting transfers between devices, transpose_ctx(): lax.ppermute(chunk, 'ctx', [(i, (i + shift) % count) for i in range(count)])  26.5 us
    ppermute x14, waiting for transfers between devices, transpose_ctx(): lax.ppermute(chunk, 'ctx', [(i, (i + shift) % count) for i in range(count)])  14.5 us
    unnamed x51, local copies, waits for them, and re-layouts  8.22 us
    all_to_all x1, starting transfers between devices, all_to_all_ctx(): return lax.all_to_all(stacked, 'ctx', 0, 0, tiled=True)  6.44 us
    dot_general x1, matrix products, gather_matmul(): lax.dot_general(gathered, out_weight, (((1,), (1,)), ((), ())), preferred...  6.3 us
    ppermute x3, starting transfers between devices, gather_matmul(): lax.ppermute(out_grad, 'tp', [(i, (i + shift) % count) for i in range(cou...  3.66 us
    dot_general x5, matrix products, table_times(): jnp.einsum('kn,snc->skc', table, signal, preferred_element_type=jnp.float32)  2.72 us
  transfers between devices with their start and end apart: 18, of which 9 were waited for; matrix products, arithmetic and copies ran while one was open for 16% of the time, Pallas kernels for 0%

profile of v10, /device:TPU:9, one launch (start us, length us, event | category | flops | bytes accessed | tf_op | source)
XLA Modules:
  0.0 78.3 jit_solution(10964114730626041098)
XLA Ops:
  0.6 1.3 %collective-permute-start = (bf16[128,1024]{1,0:T(8,128)(2,1)}, bf16[128,1024]{1,0:T(8,128)(2,1)S(1)}, u32[]{:S(2)}, u32[]{:S(2)}) collective-permute-start(bf16[128,1024]{1,0:T(8,128)(2,1)} %param.17), channel_id=1, source_target_pairs={{0,1},{1,2},{2,3},{3,0},{4,5},{5,6},{6,7},{7,4},{8,9},{9,10},{10,1... | collective-permute-start | bytes 786440 | tf_op jit(solution)/shard_map/ppermute | solution.py:25
  1.9 1.2 %collective-permute-start.1 = (bf16[128,1024]{1,0:T(8,128)(2,1)}, bf16[128,1024]{1,0:T(8,128)(2,1)S(1)}, u32[]{:S(2)}, u32[]{:S(2)}) collective-permute-start(bf16[128,1024]{1,0:T(8,128)(2,1)} %param.17), channel_id=1, source_target_pairs={{0,2},{1,3},{2,0},{3,1},{4,6},{5,7},{6,4},{7,5},{8,10},{9,11},{10,... | collective-permute-start | bytes 786440 | tf_op jit(solution)/shard_map/ppermute | solution.py:25
  3.1 1.2 %collective-permute-start.2 = (bf16[128,1024]{1,0:T(8,128)(2,1)}, bf16[128,1024]{1,0:T(8,128)(2,1)S(1)}, u32[]{:S(2)}, u32[]{:S(2)}) collective-permute-start(bf16[128,1024]{1,0:T(8,128)(2,1)} %param.17), channel_id=1, source_target_pairs={{0,3},{1,0},{2,1},{3,2},{4,7},{5,4},{6,5},{7,6},{8,11},{9,8},{10,9... | collective-permute-start | bytes 786440 | tf_op jit(solution)/shard_map/ppermute | solution.py:25
  4.3 1.1 %copy.39 = bf16[128,1024]{0,1:T(8,128)(2,1)S(1)} copy(bf16[128,1024]{1,0:T(8,128)(2,1)} %param.14) | data formatting | bytes 524288 | tf_op args[1]
  5.4 1.1 %copy.40 = bf16[128,1024]{0,1:T(8,128)(2,1)S(1)} copy(bf16[128,1024]{1,0:T(8,128)(2,1)} %param.15) | data formatting | bytes 524288 | tf_op args[2]
  6.6 1.2 %copy.41 = bf16[128,1024]{0,1:T(8,128)(2,1)S(1)} copy(bf16[128,1024]{1,0:T(8,128)(2,1)} %param.19) | data formatting | bytes 524288 | tf_op args[6]
  7.9 0.8 %copy.42 = bf16[8,2,128,128]{2,3,1,0:T(8,128)(2,1)} copy(bf16[8,2,128,128]{2,3,0,1:T(8,128)(2,1)S(1)} %pad_maximum_fusion.4) | data formatting | bytes 1048576 | tf_op jit(solution)/shard_map/stack | solution.py:174
  8.7 6.4 %all-to-all-start = ((bf16[8,2,128,128]{2,3,1,0:T(8,128)(2,1)}), bf16[8,2,128,128]{2,3,1,0:T(8,128)(2,1)S(1)}, u32[]{:S(2)}, u32[]{:S(2)}) async-start(bf16[8,2,128,128]{2,3,1,0:T(8,128)(2,1)} %copy.42), calls=%async_computation | async-start | bytes 1048576 | tf_op jit(solution)/shard_map/all_to_all | solution.py:147
  15.1 0.5 collective-permute-done.1
  15.6 0.1 pad_maximum_fusion.1
  15.9 0.7 copy-done.1
  16.6 6.3 %fusion.16 = (bf16[128,1024]{1,0:T(8,128)(2,1)S(1)}, f32[128,1024]{1,0:T(8,128)S(1)}) fusion(bf16[128,1024]{1,0:T(8,128)(2,1)S(1)} %copy-done.1, bf16[1024,4096]{1,0:T(8,128)(2,1)} %param.18, bf16[128,1024]{1,0:T(8,128)(2,1)S(1)} %get-tuple-element.48, bf16[128,1024]{1,0:T(8,128)(2,1)S(1)} %get-tuple-element.49, ...), kind=kOutput, calls=%fused_computation.94 | convolution fusion | flops 1078329344 | bytes 10485760 | tf_op jit(solution)/shard_map/dot_general | solution.py:33
  22.9 0.9 %fusion.17 = (bf16[16,8,8,128]{3,2,1,0:T(8,128)(2,1)S(1)}, bf16[128,1024]{1,0:T(8,128)(2,1)}) fusion(bf16[128,1024]{1,0:T(8,128)(2,1)S(1)} %get-tuple-element.103, f32[128,1024]{1,0:T(8,128)S(1)} %get-tuple-element.104, bf16[128,1024]{1,0:T(8,128)(2,1)S(1)} %copy-done.1, bf16[128,1024]{1,0:T(8,128)(2,1)S(1)} %copy-done.2), kind=kLoop, calls=%fused_computation.95 | loop fusion | flops 1048576 | bytes 1835008
  23.8 0.1 bitcast_bitcast_fusion
  24.0 1.8 %collective-permute-start.3 = (bf16[2,128,128]{2,1,0:T(8,128)(2,1)S(1)}, bf16[2,128,128]{2,1,0:T(8,128)(2,1)S(1)}, u32[]{:S(2)}, u32[]{:S(2)}) collective-permute-start(bf16[2,128,128]{2,1,0:T(8,128)(2,1)S(1)} %get-tuple-element.73), channel_id=1, source_target_pairs={{0,4},{4,8},{8,12},{12,16},{16,20},{20,24},{24,28},{28,0},{1,5},{5... | collective-permute-start | bytes 196616 | tf_op jit(solution)/shard_map/ppermute | solution.py:157
  25.9 1.3 %collective-permute-start.4 = (bf16[2,128,128]{2,1,0:T(8,128)(2,1)S(1)}, bf16[2,128,128]{2,1,0:T(8,128)(2,1)S(1)}, u32[]{:S(2)}, u32[]{:S(2)}) collective-permute-start(bf16[2,128,128]{2,1,0:T(8,128)(2,1)S(1)} %get-tuple-element.74), channel_id=1, source_target_pairs={{0,8},{4,12},{8,16},{12,20},{16,24},{20,28},{24,0},{28,4},{1,9},{5... | collective-permute-start | bytes 196616 | tf_op jit(solution)/shard_map/ppermute | solution.py:157
  27.2 3.8 %collective-permute-start.5 = (bf16[2,128,128]{2,1,0:T(8,128)(2,1)S(1)}, bf16[2,128,128]{2,1,0:T(8,128)(2,1)S(1)}, u32[]{:S(2)}, u32[]{:S(2)}) collective-permute-start(bf16[2,128,128]{2,1,0:T(8,128)(2,1)S(1)} %get-tuple-element.75), channel_id=1, source_target_pairs={{0,12},{4,16},{8,20},{12,24},{16,28},{20,0},{24,4},{28,8},{1,13},{... | collective-permute-start | bytes 196616 | tf_op jit(solution)/shard_map/ppermute | solution.py:157
  31.0 0.2 collective-permute-start.8
  31.3 1.9 %collective-permute-start.9 = (bf16[2,128,128]{2,1,0:T(8,128)(2,1)S(1)}, bf16[2,128,128]{2,1,0:T(8,128)(2,1)S(1)}, u32[]{:S(2)}, u32[]{:S(2)}) collective-permute-start(bf16[2,128,128]{2,1,0:T(8,128)(2,1)S(1)} %get-tuple-element.71), channel_id=1, source_target_pairs={{0,28},{4,0},{8,4},{12,8},{16,12},{20,16},{24,20},{28,24},{1,29},{... | collective-permute-start | bytes 196616 | tf_op jit(solution)/shard_map/ppermute | solution.py:157
  33.2 2.6 %collective-permute-done.5 = bf16[2,128,128]{2,1,0:T(8,128)(2,1)S(1)} collective-permute-done((bf16[2,128,128]{2,1,0:T(8,128)(2,1)S(1)}, bf16[2,128,128]{2,1,0:T(8,128)(2,1)S(1)}, u32[]{:S(2)}, u32[]{:S(2)}) %collective-permute-start.5) | collective-permute-done | bytes 65568 | tf_op jit(solution)/shard_map/ppermute | solution.py:157
  35.8 2.2 %collective-permute-done.6 = bf16[2,128,128]{2,1,0:T(8,128)(2,1)S(1)} collective-permute-done((bf16[2,128,128]{2,1,0:T(8,128)(2,1)S(1)}, bf16[2,128,128]{2,1,0:T(8,128)(2,1)S(1)}, u32[]{:S(2)}, u32[]{:S(2)}) %collective-permute-start.6) | collective-permute-done | bytes 65568 | tf_op jit(solution)/shard_map/ppermute | solution.py:157
  38.0 1.4 %collective-permute-done.8 = bf16[2,128,128]{2,1,0:T(8,128)(2,1)S(1)} collective-permute-done((bf16[2,128,128]{2,1,0:T(8,128)(2,1)S(1)}, bf16[2,128,128]{2,1,0:T(8,128)(2,1)S(1)}, u32[]{:S(2)}, u32[]{:S(2)}) %collective-permute-start.8) | collective-permute-done | bytes 65568 | tf_op jit(solution)/shard_map/ppermute | solution.py:157
  39.5 0.5 collective-permute-done.9
  40.4 0.2 copy.54
  40.5 0.2 copy.55
  40.7 0.1 pad_maximum_fusion.2
  40.9 0.2 fusion.60
  41.2 0.1 pad_maximum_fusion.3
  41.3 0.3 copy-done.6
  41.6 0.7 convolution_bitcast_fusion
  42.3 0.1 copy-done.5
  42.4 0.6 convolution_bitcast_fusion.1
  43.0 0.6 slice_add_fusion.3
  43.6 0.1 fusion.54
  43.7 0.1 fusion.15
  43.9 0.1 fusion.55
  44.0 0.4 add_add_fusion.2
  44.5 0.4 subtract_add_fusion.1
  44.9 0.1 slice_bitcast_fusion.17
  45.0 0.4 add_add_fusion.1
  45.4 0.4 subtract_add_fusion
  46.0 0.1 pad_maximum_fusion
  46.2 0.1 bitcast_convert_fusion
  46.3 0.3 fusion
  46.6 0.6 copy-done
  47.2 0.5 fusion.58
  47.7 0.5 fusion.59
  48.2 0.4 copy-done.4
  48.6 0.5 add_add_fusion
  49.0 0.2 copy-done.7
  49.2 0.3 multiply_add_fusion
  50.0 0.2 collective-permute-start.14
  50.2 1.9 %collective-permute-start.11 = (f32[128,2,128]{0,2,1:T(8,128)S(1)}, f32[128,2,128]{0,2,1:T(8,128)S(1)}, u32[]{:S(2)}, u32[]{:S(2)}) collective-permute-start(f32[128,2,128]{0,2,1:T(8,128)S(1)} %get-tuple-element.22), channel_id=1, source_target_pairs={{0,8},{4,12},{8,16},{12,20},{16,24},{20,28},{24,0},{28,4},{1,9},{5... | collective-permute-start | bytes 393224 | tf_op jit(solution)/shard_map/ppermute | solution.py:157
  52.1 3.8 %collective-permute-start.12 = (f32[128,2,128]{0,2,1:T(8,128)S(1)}, f32[128,2,128]{0,2,1:T(8,128)S(1)}, u32[]{:S(2)}, u32[]{:S(2)}) collective-permute-start(f32[128,2,128]{0,2,1:T(8,128)S(1)} %get-tuple-element.23), channel_id=1, source_target_pairs={{0,12},{4,16},{8,20},{12,24},{16,28},{20,0},{24,4},{28,8},{1,13},{... | collective-permute-start | bytes 393224 | tf_op jit(solution)/shard_map/ppermute | solution.py:157
  55.9 0.4 collective-permute-start.15
  56.2 2.8 %collective-permute-done.11 = f32[128,2,128]{0,2,1:T(8,128)S(1)} collective-permute-done((f32[128,2,128]{0,2,1:T(8,128)S(1)}, f32[128,2,128]{0,2,1:T(8,128)S(1)}, u32[]{:S(2)}, u32[]{:S(2)}) %collective-permute-start.11) | collective-permute-done | bytes 131104 | tf_op jit(solution)/shard_map/ppermute | solution.py:157
  59.0 11.1 %collective-permute-start.16 = (f32[128,2,128]{0,2,1:T(8,128)S(1)}, f32[128,2,128]{0,2,1:T(8,128)S(1)}, u32[]{:S(2)}, u32[]{:S(2)}) collective-permute-start(f32[128,2,128]{0,2,1:T(8,128)S(1)} %get-tuple-element.19), channel_id=1, source_target_pairs={{0,28},{4,0},{8,4},{12,8},{16,12},{20,16},{24,20},{28,24},{1,29},{... | collective-permute-start | bytes 393224 | tf_op jit(solution)/shard_map/ppermute | solution.py:157
  70.2 1.8 %collective-permute-done.13 = f32[128,2,128]{0,2,1:T(8,128)S(1)} collective-permute-done((f32[128,2,128]{0,2,1:T(8,128)S(1)}, f32[128,2,128]{0,2,1:T(8,128)S(1)}, u32[]{:S(2)}, u32[]{:S(2)}) %collective-permute-start.13) | collective-permute-done | bytes 131104 | tf_op jit(solution)/shard_map/ppermute | solution.py:157
  72.0 2.0 %collective-permute-done.15 = f32[128,2,128]{0,2,1:T(8,128)S(1)} collective-permute-done((f32[128,2,128]{0,2,1:T(8,128)S(1)}, f32[128,2,128]{0,2,1:T(8,128)S(1)}, u32[]{:S(2)}, u32[]{:S(2)}) %collective-permute-start.15) | collective-permute-done | bytes 131104 | tf_op jit(solution)/shard_map/ppermute | solution.py:157
  74.1 1.1 %collective-permute-done.16 = f32[128,2,128]{0,2,1:T(8,128)S(1)} collective-permute-done((f32[128,2,128]{0,2,1:T(8,128)S(1)}, f32[128,2,128]{0,2,1:T(8,128)S(1)}, u32[]{:S(2)}, u32[]{:S(2)}) %collective-permute-start.16) | collective-permute-done | bytes 131104 | tf_op jit(solution)/shard_map/ppermute | solution.py:157
  75.5 0.1 fusion.9
  75.6 0.9 %copy.48 = bf16[128,1024]{1,0:T(8,128)(2,1)} copy(bf16[128,1024]{0,1:T(8,128)(2,1)S(1)} %get-tuple-element.52) | data formatting | bytes 524288
  76.5 0.8 %copy.49 = bf16[128,1024]{1,0:T(8,128)(2,1)} copy(bf16[128,1024]{0,1:T(8,128)(2,1)S(1)} %get-tuple-element.51) | data formatting | bytes 524288
  77.3 1.0 %copy.53 = f32[128,1024]{1,0:T(8,128)} copy(f32[128,1024]{0,1:T(8,128)S(1)} %bitcast.265) | data formatting | bytes 1048576 | tf_op jit(solution)/shard_map/reshape | solution.py:143
  (80 shorter events, 1.8 us)
Async XLA Ops:
  0.6 14.5 %collective-permute-start = (bf16[128,1024]{1,0:T(8,128)(2,1)}, bf16[128,1024]{1,0:T(8,128)(2,1)S(1)}, u32[]{:S(2)}, u32[]{:S(2)}) collective-permute-start(bf16[128,1024]{1,0:T(8,128)(2,1)} %param.17), channel_id=1, source_target_pairs={{0,1},{1,2},{2,3},{3,0},{4,5},{5,6},{6,7},{7,4},{8,9},{9,10},{10,1... | collective-permute-start | bytes 786440 | tf_op jit(solution)/shard_map/ppermute | solution.py:25
  1.9 13.7 %collective-permute-start.1 = (bf16[128,1024]{1,0:T(8,128)(2,1)}, bf16[128,1024]{1,0:T(8,128)(2,1)S(1)}, u32[]{:S(2)}, u32[]{:S(2)}) collective-permute-start(bf16[128,1024]{1,0:T(8,128)(2,1)} %param.17), channel_id=1, source_target_pairs={{0,2},{1,3},{2,0},{3,1},{4,6},{5,7},{6,4},{7,5},{8,10},{9,11},{10,... | collective-permute-start | bytes 786440 | tf_op jit(solution)/shard_map/ppermute | solution.py:25
  3.1 12.5 %collective-permute-start.2 = (bf16[128,1024]{1,0:T(8,128)(2,1)}, bf16[128,1024]{1,0:T(8,128)(2,1)S(1)}, u32[]{:S(2)}, u32[]{:S(2)}) collective-permute-start(bf16[128,1024]{1,0:T(8,128)(2,1)} %param.17), channel_id=1, source_target_pairs={{0,3},{1,0},{2,1},{3,2},{4,7},{5,4},{6,5},{7,6},{8,11},{9,8},{10,9... | collective-permute-start | bytes 786440 | tf_op jit(solution)/shard_map/ppermute | solution.py:25
  6.6 9.0 %copy-start.3 = (bf16[128,1024]{1,0:T(8,128)(2,1)S(1)}, bf16[128,1024]{1,0:T(8,128)(2,1)}, u32[]{:S(2)}) copy-start(bf16[128,1024]{1,0:T(8,128)(2,1)} %param.17) | copy-start | bytes 786436
  8.7 31.6 %all-to-all-start = ((bf16[8,2,128,128]{2,3,1,0:T(8,128)(2,1)}), bf16[8,2,128,128]{2,3,1,0:T(8,128)(2,1)S(1)}, u32[]{:S(2)}, u32[]{:S(2)}) async-start(bf16[8,2,128,128]{2,3,1,0:T(8,128)(2,1)} %copy.42), calls=%async_computation | async-start | bytes 1048576 | tf_op jit(solution)/shard_map/all_to_all | solution.py:147
  15.6 1.0 %copy-start.1 = (bf16[128,1024]{1,0:T(8,128)(2,1)S(1)}, bf16[128,1024]{1,0:T(8,128)(2,1)}, u32[]{:S(2)}) copy-start(bf16[128,1024]{1,0:T(8,128)(2,1)} %param.13) | copy-start | bytes 786436
  16.6 6.3 %copy-start.2 = (bf16[128,1024]{1,0:T(8,128)(2,1)S(1)}, bf16[128,1024]{1,0:T(8,128)(2,1)}, u32[]{:S(2)}) copy-start(bf16[128,1024]{1,0:T(8,128)(2,1)} %param.16) | copy-start | bytes 786436
  24.0 7.0 %collective-permute-start.3 = (bf16[2,128,128]{2,1,0:T(8,128)(2,1)S(1)}, bf16[2,128,128]{2,1,0:T(8,128)(2,1)S(1)}, u32[]{:S(2)}, u32[]{:S(2)}) collective-permute-start(bf16[2,128,128]{2,1,0:T(8,128)(2,1)S(1)} %get-tuple-element.73), channel_id=1, source_target_pairs={{0,4},{4,8},{8,12},{12,16},{16,20},{20,24},{24,28},{28,0},{1,5},{5... | collective-permute-start | bytes 196616 | tf_op jit(solution)/shard_map/ppermute | solution.py:157
  25.8 12.2 %collective-permute-start.7 = (bf16[2,128,128]{2,1,0:T(8,128)(2,1)S(1)}, bf16[2,128,128]{2,1,0:T(8,128)(2,1)S(1)}, u32[]{:S(2)}, u32[]{:S(2)}) collective-permute-start(bf16[2,128,128]{2,1,0:T(8,128)(2,1)S(1)} %get-tuple-element.78), channel_id=1, source_target_pairs={{0,20},{4,24},{8,28},{12,0},{16,4},{20,8},{24,12},{28,16},{1,21},{... | collective-permute-start | bytes 196616 | tf_op jit(solution)/shard_map/ppermute | solution.py:157
  25.9 5.4 %collective-permute-start.4 = (bf16[2,128,128]{2,1,0:T(8,128)(2,1)S(1)}, bf16[2,128,128]{2,1,0:T(8,128)(2,1)S(1)}, u32[]{:S(2)}, u32[]{:S(2)}) collective-permute-start(bf16[2,128,128]{2,1,0:T(8,128)(2,1)S(1)} %get-tuple-element.74), channel_id=1, source_target_pairs={{0,8},{4,12},{8,16},{12,20},{16,24},{20,28},{24,0},{28,4},{1,9},{5... | collective-permute-start | bytes 196616 | tf_op jit(solution)/shard_map/ppermute | solution.py:157
  27.2 8.5 %collective-permute-start.5 = (bf16[2,128,128]{2,1,0:T(8,128)(2,1)S(1)}, bf16[2,128,128]{2,1,0:T(8,128)(2,1)S(1)}, u32[]{:S(2)}, u32[]{:S(2)}) collective-permute-start(bf16[2,128,128]{2,1,0:T(8,128)(2,1)S(1)} %get-tuple-element.75), channel_id=1, source_target_pairs={{0,12},{4,16},{8,20},{12,24},{16,28},{20,0},{24,4},{28,8},{1,13},{... | collective-permute-start | bytes 196616 | tf_op jit(solution)/shard_map/ppermute | solution.py:157
  31.0 7.0 %collective-permute-start.6 = (bf16[2,128,128]{2,1,0:T(8,128)(2,1)S(1)}, bf16[2,128,128]{2,1,0:T(8,128)(2,1)S(1)}, u32[]{:S(2)}, u32[]{:S(2)}) collective-permute-start(bf16[2,128,128]{2,1,0:T(8,128)(2,1)S(1)} %get-tuple-element.76), channel_id=1, source_target_pairs={{0,16},{4,20},{8,24},{12,28},{16,0},{20,4},{24,8},{28,12},{1,17},{... | collective-permute-start | bytes 196616 | tf_op jit(solution)/shard_map/ppermute | solution.py:157
  31.0 8.5 %collective-permute-start.8 = (bf16[2,128,128]{2,1,0:T(8,128)(2,1)S(1)}, bf16[2,128,128]{2,1,0:T(8,128)(2,1)S(1)}, u32[]{:S(2)}, u32[]{:S(2)}) collective-permute-start(bf16[2,128,128]{2,1,0:T(8,128)(2,1)S(1)} %get-tuple-element.77), channel_id=1, source_target_pairs={{0,24},{4,28},{8,0},{12,4},{16,8},{20,12},{24,16},{28,20},{1,25},{... | collective-permute-start | bytes 196616 | tf_op jit(solution)/shard_map/ppermute | solution.py:157
  31.3 8.8 %collective-permute-start.9 = (bf16[2,128,128]{2,1,0:T(8,128)(2,1)S(1)}, bf16[2,128,128]{2,1,0:T(8,128)(2,1)S(1)}, u32[]{:S(2)}, u32[]{:S(2)}) collective-permute-start(bf16[2,128,128]{2,1,0:T(8,128)(2,1)S(1)} %get-tuple-element.71), channel_id=1, source_target_pairs={{0,28},{4,0},{8,4},{12,8},{16,12},{20,16},{24,20},{28,24},{1,29},{... | collective-permute-start | bytes 196616 | tf_op jit(solution)/shard_map/ppermute | solution.py:157
  40.3 0.7 copy-start.8
  40.7 0.8 %copy-start.6 = (bf16[256,128,1]{1,0,2:T(8,128)(2,1)S(1)}, bf16[256,128,1]{1,0,2:T(8,128)(2,1)}, u32[]{:S(2)}) copy-start(bf16[256,128,1]{1,0,2:T(8,128)(2,1)} %constant.292) | copy-start | bytes 196612
  41.6 0.8 %copy-start.5 = (bf16[256,128,1]{1,0,2:T(8,128)(2,1)S(1)}, bf16[256,128,1]{1,0,2:T(8,128)(2,1)}, u32[]{:S(2)}) copy-start(bf16[256,128,1]{1,0,2:T(8,128)(2,1)} %constant.293) | copy-start | bytes 196612
  46.3 0.9 %copy-start = (bf16[256,256,1]{1,0,2:T(8,128)(2,1)S(1)}, bf16[256,256,1]{1,0,2:T(8,128)(2,1)}, u32[]{:S(2)}) copy-start(bf16[256,256,1]{1,0,2:T(8,128)(2,1)} %constant.294) | copy-start | bytes 393220
  47.7 0.9 %copy-start.4 = (bf16[256,256,1]{1,0,2:T(8,128)(2,1)S(1)}, bf16[256,256,1]{1,0,2:T(8,128)(2,1)}, u32[]{:S(2)}) copy-start(bf16[256,256,1]{1,0,2:T(8,128)(2,1)} %constant.295) | copy-start | bytes 393220
  48.6 0.7 copy-start.7
  49.9 6.0 %collective-permute-start.10 = (f32[128,2,128]{0,2,1:T(8,128)S(1)}, f32[128,2,128]{0,2,1:T(8,128)S(1)}, u32[]{:S(2)}, u32[]{:S(2)}) collective-permute-start(f32[128,2,128]{0,2,1:T(8,128)S(1)} %get-tuple-element.21), channel_id=1, source_target_pairs={{0,4},{4,8},{8,12},{12,16},{16,20},{20,24},{24,28},{28,0},{1,5},{5... | collective-permute-start | bytes 393224 | tf_op jit(solution)/shard_map/ppermute | solution.py:157
  50.0 22.0 %collective-permute-start.14 = (f32[128,2,128]{0,2,1:T(8,128)S(1)}, f32[128,2,128]{0,2,1:T(8,128)S(1)}, u32[]{:S(2)}, u32[]{:S(2)}) collective-permute-start(f32[128,2,128]{0,2,1:T(8,128)S(1)} %get-tuple-element.26), channel_id=1, source_target_pairs={{0,20},{4,24},{8,28},{12,0},{16,4},{20,8},{24,12},{28,16},{1,21},{... | collective-permute-start | bytes 393224 | tf_op jit(solution)/shard_map/ppermute | solution.py:157
  50.2 8.8 %collective-permute-start.11 = (f32[128,2,128]{0,2,1:T(8,128)S(1)}, f32[128,2,128]{0,2,1:T(8,128)S(1)}, u32[]{:S(2)}, u32[]{:S(2)}) collective-permute-start(f32[128,2,128]{0,2,1:T(8,128)S(1)} %get-tuple-element.22), channel_id=1, source_target_pairs={{0,8},{4,12},{8,16},{12,20},{16,24},{20,28},{24,0},{28,4},{1,9},{5... | collective-permute-start | bytes 393224 | tf_op jit(solution)/shard_map/ppermute | solution.py:157
  52.1 18.1 %collective-permute-start.12 = (f32[128,2,128]{0,2,1:T(8,128)S(1)}, f32[128,2,128]{0,2,1:T(8,128)S(1)}, u32[]{:S(2)}, u32[]{:S(2)}) collective-permute-start(f32[128,2,128]{0,2,1:T(8,128)S(1)} %get-tuple-element.23), channel_id=1, source_target_pairs={{0,12},{4,16},{8,20},{12,24},{16,28},{20,0},{24,4},{28,8},{1,13},{... | collective-permute-start | bytes 393224 | tf_op jit(solution)/shard_map/ppermute | solution.py:157
  55.9 16.1 %collective-permute-start.13 = (f32[128,2,128]{0,2,1:T(8,128)S(1)}, f32[128,2,128]{0,2,1:T(8,128)S(1)}, u32[]{:S(2)}, u32[]{:S(2)}) collective-permute-start(f32[128,2,128]{0,2,1:T(8,128)S(1)} %get-tuple-element.24), channel_id=1, source_target_pairs={{0,16},{4,20},{8,24},{12,28},{16,0},{20,4},{24,8},{28,12},{1,17},{... | collective-permute-start | bytes 393224 | tf_op jit(solution)/shard_map/ppermute | solution.py:157
  55.9 18.2 %collective-permute-start.15 = (f32[128,2,128]{0,2,1:T(8,128)S(1)}, f32[128,2,128]{0,2,1:T(8,128)S(1)}, u32[]{:S(2)}, u32[]{:S(2)}) collective-permute-start(f32[128,2,128]{0,2,1:T(8,128)S(1)} %get-tuple-element.25), channel_id=1, source_target_pairs={{0,24},{4,28},{8,0},{12,4},{16,8},{20,12},{24,16},{28,20},{1,25},{... | collective-permute-start | bytes 393224 | tf_op jit(solution)/shard_map/ppermute | solution.py:157
  59.0 16.1 %collective-permute-start.16 = (f32[128,2,128]{0,2,1:T(8,128)S(1)}, f32[128,2,128]{0,2,1:T(8,128)S(1)}, u32[]{:S(2)}, u32[]{:S(2)}) collective-permute-start(f32[128,2,128]{0,2,1:T(8,128)S(1)} %get-tuple-element.19), channel_id=1, source_target_pairs={{0,28},{4,0},{8,4},{12,8},{16,12},{20,16},{24,20},{28,24},{1,29},{... | collective-permute-start | bytes 393224 | tf_op jit(solution)/shard_map/ppermute | solution.py:157

commit v11 on v10

--- a/solution.py
+++ b/solution.py
@@ -186,9 +186,11 @@
         inputs_t[:, 1].reshape(seq, sub),
         float(seq) ** -0.5,
     )
-    back = transpose_ctx(jnp.stack([du_t, filter_t], axis=1).reshape(blocks, rows, 2, sub))
-    du_local = from_groups(back[:, :, 0])
-    filter_grad = from_groups(back[:, :, 1])
+    du_hi, du_lo = split_bf16(du_t)
+    outgoing = jnp.stack([du_hi, du_lo, filter_t.astype(jnp.bfloat16)], axis=1)
+    back = transpose_ctx(outgoing.reshape(blocks, rows, 3, sub))
+    du_local = from_groups(back[:, :, 0].astype(jnp.float32) + back[:, :, 1].astype(jnp.float32))
+    filter_grad = from_groups(back[:, :, 2].astype(jnp.float32))
     dk_grad = (du_local * v_proj.astype(jnp.float32)).astype(jnp.bfloat16)
     dv_grad = (du_local * k_proj.astype(jnp.float32)).astype(jnp.bfloat16)
     return (dq_grad, dk_grad, dv_grad, filter_grad)

time: 78.8 us -> 77.1 us (0.978)
  starting transfers between devices: 36.6 us -> 25.9 us
  waiting for transfers between devices: 15 us -> 20.2 us
  local copies, waits for them, and re-layouts: 11 us -> 13.1 us
  other arithmetic: 5.15 us -> 6.89 us
    ppermute x14, starting transfers between devices: 26.5 us -> 15.8 us  [transpose_ctx(): lax.ppermute(chunk, 'ctx', [(i, (i + shift) % count) for i in range(count)])]
    ppermute x14, waiting for transfers between devices: 14.5 us -> 19.7 us  [transpose_ctx(): lax.ppermute(chunk, 'ctx', [(i, (i + shift) % count) for i in range(count)])]
    reshape x0 -> x1, local copies, waits for them, and re-layouts: none -> 1.84 us  [long_correlations(): signal = (table_times(inv_hi, spectra_hi) + table_times(inv_hi, spectra_l...]
    add x1, other arithmetic: 0.34 us -> 1.93 us  [long_correlations(): signal = signal + tables['ialt'][None, None, :, None] * tops[:, :, None, :]]
    unnamed x51 -> x52, local copies, waits for them, and re-layouts: 8.22 us -> 9.06 us
    reshape x1, local copies, waits for them, and re-layouts: 0.99 us -> 0.19 us  [from_groups(): return value.transpose(1, 0, 2).reshape(rows, groups * chans)]
where the time goes in v11:
time: 77.1 us; the launch traced here: 76.6 us
  starting transfers between devices  25.9 us (34%)
  waiting for transfers between devices  20.2 us (26%)
  local copies, waits for them, and re-layouts  13.1 us (17%)
  matrix products  9.26 us (12%)
  other arithmetic  6.89 us (9%)
  between operations  1.3 us (2%)
    ppermute x14, waiting for transfers between devices, transpose_ctx(): lax.ppermute(chunk, 'ctx', [(i, (i + shift) % count) for i in range(count)])  19.7 us
    ppermute x14, starting transfers between devices, transpose_ctx(): lax.ppermute(chunk, 'ctx', [(i, (i + shift) % count) for i in range(count)])  15.8 us
    unnamed x52, local copies, waits for them, and re-layouts  9.06 us
    all_to_all x1, starting transfers between devices, all_to_all_ctx(): return lax.all_to_all(stacked, 'ctx', 0, 0, tiled=True)  6.44 us
    dot_general x1, matrix products, gather_matmul(): lax.dot_general(gathered, out_weight, (((1,), (1,)), ((), ())), preferred...  6.3 us
    ppermute x3, starting transfers between devices, gather_matmul(): lax.ppermute(out_grad, 'tp', [(i, (i + shift) % count) for i in range(cou...  3.66 us
    dot_general x5, matrix products, table_times(): jnp.einsum('kn,snc->skc', table, signal, preferred_element_type=jnp.float32)  2.72 us
    add x1, other arithmetic, long_correlations(): signal = signal + tables['ialt'][None, None, :, None] * tops[:, :, None, :]  1.93 us
  transfers between devices with their start and end apart: 18, of which 9 were waited for; matrix products, arithmetic and copies ran while one was open for 16% of the time, Pallas kernels for 0%

profile of v11, /device:TPU:9, one launch (start us, length us, event | category | flops | bytes accessed | tf_op | source)
XLA Modules:
  0.0 76.6 jit_solution(11068876533167619363)
XLA Ops:
  0.6 1.3 %collective-permute-start = (bf16[128,1024]{1,0:T(8,128)(2,1)}, bf16[128,1024]{1,0:T(8,128)(2,1)S(1)}, u32[]{:S(2)}, u32[]{:S(2)}) collective-permute-start(bf16[128,1024]{1,0:T(8,128)(2,1)} %param.17), channel_id=1, source_target_pairs={{0,1},{1,2},{2,3},{3,0},{4,5},{5,6},{6,7},{7,4},{8,9},{9,10},{10,1... | collective-permute-start | bytes 786440 | tf_op jit(solution)/shard_map/ppermute | solution.py:25
  1.9 1.2 %collective-permute-start.1 = (bf16[128,1024]{1,0:T(8,128)(2,1)}, bf16[128,1024]{1,0:T(8,128)(2,1)S(1)}, u32[]{:S(2)}, u32[]{:S(2)}) collective-permute-start(bf16[128,1024]{1,0:T(8,128)(2,1)} %param.17), channel_id=1, source_target_pairs={{0,2},{1,3},{2,0},{3,1},{4,6},{5,7},{6,4},{7,5},{8,10},{9,11},{10,... | collective-permute-start | bytes 786440 | tf_op jit(solution)/shard_map/ppermute | solution.py:25
  3.1 1.2 %collective-permute-start.2 = (bf16[128,1024]{1,0:T(8,128)(2,1)}, bf16[128,1024]{1,0:T(8,128)(2,1)S(1)}, u32[]{:S(2)}, u32[]{:S(2)}) collective-permute-start(bf16[128,1024]{1,0:T(8,128)(2,1)} %param.17), channel_id=1, source_target_pairs={{0,3},{1,0},{2,1},{3,2},{4,7},{5,4},{6,5},{7,6},{8,11},{9,8},{10,9... | collective-permute-start | bytes 786440 | tf_op jit(solution)/shard_map/ppermute | solution.py:25
  4.3 1.1 %copy.41 = bf16[128,1024]{0,1:T(8,128)(2,1)S(1)} copy(bf16[128,1024]{1,0:T(8,128)(2,1)} %param.14) | data formatting | bytes 524288 | tf_op args[1]
  5.4 1.1 %copy.42 = bf16[128,1024]{0,1:T(8,128)(2,1)S(1)} copy(bf16[128,1024]{1,0:T(8,128)(2,1)} %param.15) | data formatting | bytes 524288 | tf_op args[2]
  6.6 1.2 %copy.43 = bf16[128,1024]{0,1:T(8,128)(2,1)S(1)} copy(bf16[128,1024]{1,0:T(8,128)(2,1)} %param.19) | data formatting | bytes 524288 | tf_op args[6]
  7.9 0.8 %copy.44 = bf16[8,2,128,128]{2,3,1,0:T(8,128)(2,1)} copy(bf16[8,2,128,128]{2,3,0,1:T(8,128)(2,1)S(1)} %pad_maximum_fusion.5) | data formatting | bytes 1048576 | tf_op jit(solution)/shard_map/stack | solution.py:174
  8.7 6.4 %all-to-all-start = ((bf16[8,2,128,128]{2,3,1,0:T(8,128)(2,1)}), bf16[8,2,128,128]{2,3,1,0:T(8,128)(2,1)S(1)}, u32[]{:S(2)}, u32[]{:S(2)}) async-start(bf16[8,2,128,128]{2,3,1,0:T(8,128)(2,1)} %copy.44), calls=%async_computation | async-start | bytes 1048576 | tf_op jit(solution)/shard_map/all_to_all | solution.py:147
  15.1 0.5 collective-permute-done.1
  15.6 0.1 pad_maximum_fusion.1
  15.8 0.1 dynamic-slice_bitcast_fusion.3
  15.9 0.7 copy-done.1
  16.6 6.3 %fusion.17 = (bf16[128,1024]{1,0:T(8,128)(2,1)S(1)}, f32[128,1024]{1,0:T(8,128)S(1)}) fusion(bf16[128,1024]{1,0:T(8,128)(2,1)S(1)} %copy-done.1, bf16[1024,4096]{1,0:T(8,128)(2,1)} %param.18, bf16[128,1024]{1,0:T(8,128)(2,1)S(1)} %get-tuple-element.38, bf16[128,1024]{1,0:T(8,128)(2,1)S(1)} %get-tuple-element.39, ...), kind=kOutput, calls=%fused_computation.83 | convolution fusion | flops 1078329344 | bytes 10485760 | tf_op jit(solution)/shard_map/dot_general | solution.py:33
  22.9 0.9 %fusion.18 = (bf16[16,8,8,128]{3,2,1,0:T(8,128)(2,1)S(1)}, bf16[128,1024]{1,0:T(8,128)(2,1)}) fusion(bf16[128,1024]{1,0:T(8,128)(2,1)S(1)} %get-tuple-element.101, f32[128,1024]{1,0:T(8,128)S(1)} %get-tuple-element.102, bf16[128,1024]{1,0:T(8,128)(2,1)S(1)} %copy-done.1, bf16[128,1024]{1,0:T(8,128)(2,1)S(1)} %copy-done.2), kind=kLoop, calls=%fused_computation.84 | loop fusion | flops 1048576 | bytes 1835008
  23.8 0.1 bitcast_bitcast_fusion
  24.0 1.8 %collective-permute-start.3 = (bf16[2,128,128]{2,1,0:T(8,128)(2,1)S(1)}, bf16[2,128,128]{2,1,0:T(8,128)(2,1)S(1)}, u32[]{:S(2)}, u32[]{:S(2)}) collective-permute-start(bf16[2,128,128]{2,1,0:T(8,128)(2,1)S(1)} %get-tuple-element.71), channel_id=1, source_target_pairs={{0,4},{4,8},{8,12},{12,16},{16,20},{20,24},{24,28},{28,0},{1,5},{5... | collective-permute-start | bytes 196616 | tf_op jit(solution)/shard_map/ppermute | solution.py:157
  25.9 1.3 %collective-permute-start.4 = (bf16[2,128,128]{2,1,0:T(8,128)(2,1)S(1)}, bf16[2,128,128]{2,1,0:T(8,128)(2,1)S(1)}, u32[]{:S(2)}, u32[]{:S(2)}) collective-permute-start(bf16[2,128,128]{2,1,0:T(8,128)(2,1)S(1)} %get-tuple-element.72), channel_id=1, source_target_pairs={{0,8},{4,12},{8,16},{12,20},{16,24},{20,28},{24,0},{28,4},{1,9},{5... | collective-permute-start | bytes 196616 | tf_op jit(solution)/shard_map/ppermute | solution.py:157
  27.2 3.8 %collective-permute-start.5 = (bf16[2,128,128]{2,1,0:T(8,128)(2,1)S(1)}, bf16[2,128,128]{2,1,0:T(8,128)(2,1)S(1)}, u32[]{:S(2)}, u32[]{:S(2)}) collective-permute-start(bf16[2,128,128]{2,1,0:T(8,128)(2,1)S(1)} %get-tuple-element.73), channel_id=1, source_target_pairs={{0,12},{4,16},{8,20},{12,24},{16,28},{20,0},{24,4},{28,8},{1,13},{... | collective-permute-start | bytes 196616 | tf_op jit(solution)/shard_map/ppermute | solution.py:157
  31.0 0.2 collective-permute-start.8
  31.3 1.9 %collective-permute-start.9 = (bf16[2,128,128]{2,1,0:T(8,128)(2,1)S(1)}, bf16[2,128,128]{2,1,0:T(8,128)(2,1)S(1)}, u32[]{:S(2)}, u32[]{:S(2)}) collective-permute-start(bf16[2,128,128]{2,1,0:T(8,128)(2,1)S(1)} %get-tuple-element.69), channel_id=1, source_target_pairs={{0,28},{4,0},{8,4},{12,8},{16,12},{20,16},{24,20},{28,24},{1,29},{... | collective-permute-start | bytes 196616 | tf_op jit(solution)/shard_map/ppermute | solution.py:157
  33.2 2.6 %collective-permute-done.5 = bf16[2,128,128]{2,1,0:T(8,128)(2,1)S(1)} collective-permute-done((bf16[2,128,128]{2,1,0:T(8,128)(2,1)S(1)}, bf16[2,128,128]{2,1,0:T(8,128)(2,1)S(1)}, u32[]{:S(2)}, u32[]{:S(2)}) %collective-permute-start.5) | collective-permute-done | bytes 65568 | tf_op jit(solution)/shard_map/ppermute | solution.py:157
  35.8 2.2 %collective-permute-done.6 = bf16[2,128,128]{2,1,0:T(8,128)(2,1)S(1)} collective-permute-done((bf16[2,128,128]{2,1,0:T(8,128)(2,1)S(1)}, bf16[2,128,128]{2,1,0:T(8,128)(2,1)S(1)}, u32[]{:S(2)}, u32[]{:S(2)}) %collective-permute-start.6) | collective-permute-done | bytes 65568 | tf_op jit(solution)/shard_map/ppermute | solution.py:157
  38.0 1.4 %collective-permute-done.8 = bf16[2,128,128]{2,1,0:T(8,128)(2,1)S(1)} collective-permute-done((bf16[2,128,128]{2,1,0:T(8,128)(2,1)S(1)}, bf16[2,128,128]{2,1,0:T(8,128)(2,1)S(1)}, u32[]{:S(2)}, u32[]{:S(2)}) %collective-permute-start.8) | collective-permute-done | bytes 65568 | tf_op jit(solution)/shard_map/ppermute | solution.py:157
  39.5 0.5 collective-permute-done.9
  40.4 0.2 copy.58
  40.5 0.2 copy.59
  40.7 0.1 pad_maximum_fusion.2
  40.9 0.2 fusion.45
  41.3 0.3 copy-done.6
  41.6 0.7 convolution_bitcast_fusion
  42.4 0.6 convolution_bitcast_fusion.1
  43.0 0.6 slice_add_fusion.3
  43.7 0.1 fusion.15
  43.9 0.1 fusion.40
  44.0 0.4 add_add_fusion.2
  44.5 0.4 subtract_add_fusion.1
  44.9 0.1 slice_bitcast_fusion.17
  45.0 0.4 add_add_fusion.1
  45.4 0.4 subtract_add_fusion
  46.0 0.1 pad_maximum_fusion
  46.2 0.1 bitcast_convert_fusion
  46.3 0.3 fusion
  46.6 0.6 copy-done
  47.2 0.5 fusion.43
  47.7 0.5 fusion.44
  48.1 0.4 copy-done.4
  48.6 0.5 add_add_fusion
  49.0 1.8 %copy.49 = f32[2,8,256,128]{3,2,1,0:T(8,128)} copy(f32[2,8,256,128]{2,3,1,0:T(8,128)S(1)} %bitcast.265) | data formatting | bytes 4194304 | tf_op jit(solution)/shard_map/reshape | solution.py:126
  50.9 1.9 %multiply_add_fusion = f32[2,8,256,128]{3,2,1,0:T(8,128)S(1)} fusion(f32[2,8,256,128]{3,2,1,0:T(8,128)} %copy.49, f32[2,8,128]{2,1,0:T(8,128)S(1)} %pad_maximum_fusion.6, f32[256]{0:T(256)S(1)} %copy-done.7), kind=kLoop, calls=%fused_computation.19 | loop fusion | flops 1048576 | bytes 4203520 | tf_op jit(solution)/shard_map/add | solution.py:128
  53.5 2.0 %collective-permute-start.11 = (bf16[128,3,128]{2,0,1:T(8,128)(2,1)S(1)}, bf16[128,3,128]{2,0,1:T(8,128)(2,1)S(1)}, u32[]{:S(2)}, u32[]{:S(2)}) collective-permute-start(bf16[128,3,128]{2,0,1:T(8,128)(2,1)S(1)} %get-tuple-element.46), channel_id=1, source_target_pairs={{0,8},{4,12},{8,16},{12,20},{16,24},{20,28},{24,0},{28,4},{1,9},{5... | collective-permute-start | bytes 294920 | tf_op jit(solution)/shard_map/ppermute | solution.py:157
  55.4 0.5 collective-permute-start.12
  56.0 0.8 %collective-permute-start.13 = (bf16[128,3,128]{2,0,1:T(8,128)(2,1)S(1)}, bf16[128,3,128]{2,0,1:T(8,128)(2,1)S(1)}, u32[]{:S(2)}, u32[]{:S(2)}) collective-permute-start(bf16[128,3,128]{2,0,1:T(8,128)(2,1)S(1)} %get-tuple-element.44), channel_id=1, source_target_pairs={{0,16},{4,20},{8,24},{12,28},{16,0},{20,4},{24,8},{28,12},{1,17},{... | collective-permute-start | bytes 294920 | tf_op jit(solution)/shard_map/ppermute | solution.py:157
  56.8 2.0 %collective-permute-start.14 = (bf16[128,3,128]{2,0,1:T(8,128)(2,1)S(1)}, bf16[128,3,128]{2,0,1:T(8,128)(2,1)S(1)}, u32[]{:S(2)}, u32[]{:S(2)}) collective-permute-start(bf16[128,3,128]{2,0,1:T(8,128)(2,1)S(1)} %get-tuple-element.43), channel_id=1, source_target_pairs={{0,20},{4,24},{8,28},{12,0},{16,4},{20,8},{24,12},{28,16},{1,21},{... | collective-permute-start | bytes 294920 | tf_op jit(solution)/shard_map/ppermute | solution.py:157
  58.8 0.8 %collective-permute-start.15 = (bf16[128,3,128]{2,0,1:T(8,128)(2,1)S(1)}, bf16[128,3,128]{2,0,1:T(8,128)(2,1)S(1)}, u32[]{:S(2)}, u32[]{:S(2)}) collective-permute-start(bf16[128,3,128]{2,0,1:T(8,128)(2,1)S(1)} %get-tuple-element.42), channel_id=1, source_target_pairs={{0,24},{4,28},{8,0},{12,4},{16,8},{20,12},{24,16},{28,20},{1,25},{... | collective-permute-start | bytes 294920 | tf_op jit(solution)/shard_map/ppermute | solution.py:157
  59.7 0.4 collective-permute-start.16
  60.1 7.9 %collective-permute-done.12 = bf16[128,3,128]{2,0,1:T(8,128)(2,1)S(1)} collective-permute-done((bf16[128,3,128]{2,0,1:T(8,128)(2,1)S(1)}, bf16[128,3,128]{2,0,1:T(8,128)(2,1)S(1)}, u32[]{:S(2)}, u32[]{:S(2)}) %collective-permute-start.12) | collective-permute-done | bytes 98336 | tf_op jit(solution)/shard_map/ppermute | solution.py:157
  68.0 2.2 %collective-permute-done.13 = bf16[128,3,128]{2,0,1:T(8,128)(2,1)S(1)} collective-permute-done((bf16[128,3,128]{2,0,1:T(8,128)(2,1)S(1)}, bf16[128,3,128]{2,0,1:T(8,128)(2,1)S(1)}, u32[]{:S(2)}, u32[]{:S(2)}) %collective-permute-start.13) | collective-permute-done | bytes 98336 | tf_op jit(solution)/shard_map/ppermute | solution.py:157
  70.3 2.6 %collective-permute-done.15 = bf16[128,3,128]{2,0,1:T(8,128)(2,1)S(1)} collective-permute-done((bf16[128,3,128]{2,0,1:T(8,128)(2,1)S(1)}, bf16[128,3,128]{2,0,1:T(8,128)(2,1)S(1)}, u32[]{:S(2)}, u32[]{:S(2)}) %collective-permute-start.15) | collective-permute-done | bytes 98336 | tf_op jit(solution)/shard_map/ppermute | solution.py:157
  73.4 0.2 copy.50
  73.6 0.1 fusion.9
  73.7 0.9 %copy.52 = bf16[128,1024]{1,0:T(8,128)(2,1)} copy(bf16[128,1024]{0,1:T(8,128)(2,1)S(1)} %get-tuple-element.50) | data formatting | bytes 524288
  74.6 0.8 %copy.53 = bf16[128,1024]{1,0:T(8,128)(2,1)} copy(bf16[128,1024]{0,1:T(8,128)(2,1)S(1)} %get-tuple-element.49) | data formatting | bytes 524288
  75.4 0.2 copy.51
  75.6 1.0 %copy.54 = f32[128,1024]{1,0:T(8,128)} copy(f32[128,1024]{0,1:T(8,128)S(1)} %bitcast.274) | data formatting | bytes 1048576
  (86 shorter events, 2.3 us)
Async XLA Ops:
  0.6 14.5 %collective-permute-start = (bf16[128,1024]{1,0:T(8,128)(2,1)}, bf16[128,1024]{1,0:T(8,128)(2,1)S(1)}, u32[]{:S(2)}, u32[]{:S(2)}) collective-permute-start(bf16[128,1024]{1,0:T(8,128)(2,1)} %param.17), channel_id=1, source_target_pairs={{0,1},{1,2},{2,3},{3,0},{4,5},{5,6},{6,7},{7,4},{8,9},{9,10},{10,1... | collective-permute-start | bytes 786440 | tf_op jit(solution)/shard_map/ppermute | solution.py:25
  1.9 13.7 %collective-permute-start.1 = (bf16[128,1024]{1,0:T(8,128)(2,1)}, bf16[128,1024]{1,0:T(8,128)(2,1)S(1)}, u32[]{:S(2)}, u32[]{:S(2)}) collective-permute-start(bf16[128,1024]{1,0:T(8,128)(2,1)} %param.17), channel_id=1, source_target_pairs={{0,2},{1,3},{2,0},{3,1},{4,6},{5,7},{6,4},{7,5},{8,10},{9,11},{10,... | collective-permute-start | bytes 786440 | tf_op jit(solution)/shard_map/ppermute | solution.py:25
  3.1 12.5 %collective-permute-start.2 = (bf16[128,1024]{1,0:T(8,128)(2,1)}, bf16[128,1024]{1,0:T(8,128)(2,1)S(1)}, u32[]{:S(2)}, u32[]{:S(2)}) collective-permute-start(bf16[128,1024]{1,0:T(8,128)(2,1)} %param.17), channel_id=1, source_target_pairs={{0,3},{1,0},{2,1},{3,2},{4,7},{5,4},{6,5},{7,6},{8,11},{9,8},{10,9... | collective-permute-start | bytes 786440 | tf_op jit(solution)/shard_map/ppermute | solution.py:25
  6.6 9.0 %copy-start.3 = (bf16[128,1024]{1,0:T(8,128)(2,1)S(1)}, bf16[128,1024]{1,0:T(8,128)(2,1)}, u32[]{:S(2)}) copy-start(bf16[128,1024]{1,0:T(8,128)(2,1)} %param.17) | copy-start | bytes 786436
  8.7 31.6 %all-to-all-start = ((bf16[8,2,128,128]{2,3,1,0:T(8,128)(2,1)}), bf16[8,2,128,128]{2,3,1,0:T(8,128)(2,1)S(1)}, u32[]{:S(2)}, u32[]{:S(2)}) async-start(bf16[8,2,128,128]{2,3,1,0:T(8,128)(2,1)} %copy.44), calls=%async_computation | async-start | bytes 1048576 | tf_op jit(solution)/shard_map/all_to_all | solution.py:147
  15.6 1.0 %copy-start.1 = (bf16[128,1024]{1,0:T(8,128)(2,1)S(1)}, bf16[128,1024]{1,0:T(8,128)(2,1)}, u32[]{:S(2)}) copy-start(bf16[128,1024]{1,0:T(8,128)(2,1)} %param.13) | copy-start | bytes 786436
  16.6 6.3 %copy-start.2 = (bf16[128,1024]{1,0:T(8,128)(2,1)S(1)}, bf16[128,1024]{1,0:T(8,128)(2,1)}, u32[]{:S(2)}) copy-start(bf16[128,1024]{1,0:T(8,128)(2,1)} %param.16) | copy-start | bytes 786436
  24.0 7.0 %collective-permute-start.3 = (bf16[2,128,128]{2,1,0:T(8,128)(2,1)S(1)}, bf16[2,128,128]{2,1,0:T(8,128)(2,1)S(1)}, u32[]{:S(2)}, u32[]{:S(2)}) collective-permute-start(bf16[2,128,128]{2,1,0:T(8,128)(2,1)S(1)} %get-tuple-element.71), channel_id=1, source_target_pairs={{0,4},{4,8},{8,12},{12,16},{16,20},{20,24},{24,28},{28,0},{1,5},{5... | collective-permute-start | bytes 196616 | tf_op jit(solution)/shard_map/ppermute | solution.py:157
  25.8 12.2 %collective-permute-start.7 = (bf16[2,128,128]{2,1,0:T(8,128)(2,1)S(1)}, bf16[2,128,128]{2,1,0:T(8,128)(2,1)S(1)}, u32[]{:S(2)}, u32[]{:S(2)}) collective-permute-start(bf16[2,128,128]{2,1,0:T(8,128)(2,1)S(1)} %get-tuple-element.76), channel_id=1, source_target_pairs={{0,20},{4,24},{8,28},{12,0},{16,4},{20,8},{24,12},{28,16},{1,21},{... | collective-permute-start | bytes 196616 | tf_op jit(solution)/shard_map/ppermute | solution.py:157
  25.9 5.4 %collective-permute-start.4 = (bf16[2,128,128]{2,1,0:T(8,128)(2,1)S(1)}, bf16[2,128,128]{2,1,0:T(8,128)(2,1)S(1)}, u32[]{:S(2)}, u32[]{:S(2)}) collective-permute-start(bf16[2,128,128]{2,1,0:T(8,128)(2,1)S(1)} %get-tuple-element.72), channel_id=1, source_target_pairs={{0,8},{4,12},{8,16},{12,20},{16,24},{20,28},{24,0},{28,4},{1,9},{5... | collective-permute-start | bytes 196616 | tf_op jit(solution)/shard_map/ppermute | solution.py:157
  27.2 8.5 %collective-permute-start.5 = (bf16[2,128,128]{2,1,0:T(8,128)(2,1)S(1)}, bf16[2,128,128]{2,1,0:T(8,128)(2,1)S(1)}, u32[]{:S(2)}, u32[]{:S(2)}) collective-permute-start(bf16[2,128,128]{2,1,0:T(8,128)(2,1)S(1)} %get-tuple-element.73), channel_id=1, source_target_pairs={{0,12},{4,16},{8,20},{12,24},{16,28},{20,0},{24,4},{28,8},{1,13},{... | collective-permute-start | bytes 196616 | tf_op jit(solution)/shard_map/ppermute | solution.py:157
  31.0 7.0 %collective-permute-start.6 = (bf16[2,128,128]{2,1,0:T(8,128)(2,1)S(1)}, bf16[2,128,128]{2,1,0:T(8,128)(2,1)S(1)}, u32[]{:S(2)}, u32[]{:S(2)}) collective-permute-start(bf16[2,128,128]{2,1,0:T(8,128)(2,1)S(1)} %get-tuple-element.74), channel_id=1, source_target_pairs={{0,16},{4,20},{8,24},{12,28},{16,0},{20,4},{24,8},{28,12},{1,17},{... | collective-permute-start | bytes 196616 | tf_op jit(solution)/shard_map/ppermute | solution.py:157
  31.0 8.5 %collective-permute-start.8 = (bf16[2,128,128]{2,1,0:T(8,128)(2,1)S(1)}, bf16[2,128,128]{2,1,0:T(8,128)(2,1)S(1)}, u32[]{:S(2)}, u32[]{:S(2)}) collective-permute-start(bf16[2,128,128]{2,1,0:T(8,128)(2,1)S(1)} %get-tuple-element.75), channel_id=1, source_target_pairs={{0,24},{4,28},{8,0},{12,4},{16,8},{20,12},{24,16},{28,20},{1,25},{... | collective-permute-start | bytes 196616 | tf_op jit(solution)/shard_map/ppermute | solution.py:157
  31.3 8.8 %collective-permute-start.9 = (bf16[2,128,128]{2,1,0:T(8,128)(2,1)S(1)}, bf16[2,128,128]{2,1,0:T(8,128)(2,1)S(1)}, u32[]{:S(2)}, u32[]{:S(2)}) collective-permute-start(bf16[2,128,128]{2,1,0:T(8,128)(2,1)S(1)} %get-tuple-element.69), channel_id=1, source_target_pairs={{0,28},{4,0},{8,4},{12,8},{16,12},{20,16},{24,20},{28,24},{1,29},{... | collective-permute-start | bytes 196616 | tf_op jit(solution)/shard_map/ppermute | solution.py:157
  40.3 0.7 copy-start.8
  40.7 0.8 %copy-start.6 = (bf16[256,128,1]{1,0,2:T(8,128)(2,1)S(1)}, bf16[256,128,1]{1,0,2:T(8,128)(2,1)}, u32[]{:S(2)}) copy-start(bf16[256,128,1]{1,0,2:T(8,128)(2,1)} %constant.292) | copy-start | bytes 196612
  41.6 0.8 %copy-start.5 = (bf16[256,128,1]{1,0,2:T(8,128)(2,1)S(1)}, bf16[256,128,1]{1,0,2:T(8,128)(2,1)}, u32[]{:S(2)}) copy-start(bf16[256,128,1]{1,0,2:T(8,128)(2,1)} %constant.293) | copy-start | bytes 196612
  46.3 0.9 %copy-start = (bf16[256,256,1]{1,0,2:T(8,128)(2,1)S(1)}, bf16[256,256,1]{1,0,2:T(8,128)(2,1)}, u32[]{:S(2)}) copy-start(bf16[256,256,1]{1,0,2:T(8,128)(2,1)} %constant.294) | copy-start | bytes 393220
  47.6 0.9 %copy-start.4 = (bf16[256,256,1]{1,0,2:T(8,128)(2,1)S(1)}, bf16[256,256,1]{1,0,2:T(8,128)(2,1)}, u32[]{:S(2)}) copy-start(bf16[256,256,1]{1,0,2:T(8,128)(2,1)} %constant.295) | copy-start | bytes 393220
  49.0 1.9 %copy-start.7 = (f32[256]{0:T(256)S(1)}, f32[256]{0:T(256)}, u32[]{:S(2)}) copy-start(f32[256]{0:T(256)} %constant.277.clone) | copy-start | bytes 3076
  53.4 5.4 %collective-permute-start.10 = (bf16[128,3,128]{2,0,1:T(8,128)(2,1)S(1)}, bf16[128,3,128]{2,0,1:T(8,128)(2,1)S(1)}, u32[]{:S(2)}, u32[]{:S(2)}) collective-permute-start(bf16[128,3,128]{2,0,1:T(8,128)(2,1)S(1)} %get-tuple-element.47), channel_id=1, source_target_pairs={{0,4},{4,8},{8,12},{12,16},{16,20},{20,24},{24,28},{28,0},{1,5},{5... | collective-permute-start | bytes 294920 | tf_op jit(solution)/shard_map/ppermute | solution.py:157
  53.5 6.2 %collective-permute-start.11 = (bf16[128,3,128]{2,0,1:T(8,128)(2,1)S(1)}, bf16[128,3,128]{2,0,1:T(8,128)(2,1)S(1)}, u32[]{:S(2)}, u32[]{:S(2)}) collective-permute-start(bf16[128,3,128]{2,0,1:T(8,128)(2,1)S(1)} %get-tuple-element.46), channel_id=1, source_target_pairs={{0,8},{4,12},{8,16},{12,20},{16,24},{20,28},{24,0},{28,4},{1,9},{5... | collective-permute-start | bytes 294920 | tf_op jit(solution)/shard_map/ppermute | solution.py:157
  55.4 12.6 %collective-permute-start.12 = (bf16[128,3,128]{2,0,1:T(8,128)(2,1)S(1)}, bf16[128,3,128]{2,0,1:T(8,128)(2,1)S(1)}, u32[]{:S(2)}, u32[]{:S(2)}) collective-permute-start(bf16[128,3,128]{2,0,1:T(8,128)(2,1)S(1)} %get-tuple-element.45), channel_id=1, source_target_pairs={{0,12},{4,16},{8,20},{12,24},{16,28},{20,0},{24,4},{28,8},{1,13},{... | collective-permute-start | bytes 294920 | tf_op jit(solution)/shard_map/ppermute | solution.py:157
  56.0 14.3 %collective-permute-start.13 = (bf16[128,3,128]{2,0,1:T(8,128)(2,1)S(1)}, bf16[128,3,128]{2,0,1:T(8,128)(2,1)S(1)}, u32[]{:S(2)}, u32[]{:S(2)}) collective-permute-start(bf16[128,3,128]{2,0,1:T(8,128)(2,1)S(1)} %get-tuple-element.44), channel_id=1, source_target_pairs={{0,16},{4,20},{8,24},{12,28},{16,0},{20,4},{24,8},{28,12},{1,17},{... | collective-permute-start | bytes 294920 | tf_op jit(solution)/shard_map/ppermute | solution.py:157
  56.8 13.5 %collective-permute-start.14 = (bf16[128,3,128]{2,0,1:T(8,128)(2,1)S(1)}, bf16[128,3,128]{2,0,1:T(8,128)(2,1)S(1)}, u32[]{:S(2)}, u32[]{:S(2)}) collective-permute-start(bf16[128,3,128]{2,0,1:T(8,128)(2,1)S(1)} %get-tuple-element.43), channel_id=1, source_target_pairs={{0,20},{4,24},{8,28},{12,0},{16,4},{20,8},{24,12},{28,16},{1,21},{... | collective-permute-start | bytes 294920 | tf_op jit(solution)/shard_map/ppermute | solution.py:157
  58.8 14.1 %collective-permute-start.15 = (bf16[128,3,128]{2,0,1:T(8,128)(2,1)S(1)}, bf16[128,3,128]{2,0,1:T(8,128)(2,1)S(1)}, u32[]{:S(2)}, u32[]{:S(2)}) collective-permute-start(bf16[128,3,128]{2,0,1:T(8,128)(2,1)S(1)} %get-tuple-element.42), channel_id=1, source_target_pairs={{0,24},{4,28},{8,0},{12,4},{16,8},{20,12},{24,16},{28,20},{1,25},{... | collective-permute-start | bytes 294920 | tf_op jit(solution)/shard_map/ppermute | solution.py:157
  59.7 13.4 %collective-permute-start.16 = (bf16[128,3,128]{2,0,1:T(8,128)(2,1)S(1)}, bf16[128,3,128]{2,0,1:T(8,128)(2,1)S(1)}, u32[]{:S(2)}, u32[]{:S(2)}) collective-permute-start(bf16[128,3,128]{2,0,1:T(8,128)(2,1)S(1)} %get-tuple-element.41), channel_id=1, source_target_pairs={{0,28},{4,0},{8,4},{12,8},{16,12},{20,16},{24,20},{28,24},{1,29},{... | collective-permute-start | bytes 294920 | tf_op jit(solution)/shard_map/ppermute | solution.py:157

commit v12 on v10

--- a/solution.py
+++ b/solution.py
@@ -150,6 +150,39 @@
 def transpose_ctx(stacked):
     count = lax.axis_size("ctx")
     me = lax.axis_index("ctx")
+    if count % 2:
+        return transpose_ring(stacked, count, me)
+    outer = count // 2
+    core = me % 2
+    chip = me // 2
+    paired = stacked.reshape((outer, 2) + stacked.shape[1:])
+    mine = lax.dynamic_index_in_dim(paired, core, 1, keepdims=False)
+    other = lax.dynamic_index_in_dim(paired, 1 - core, 1, keepdims=False)
+    other = lax.ppermute(other, "ctx", [(i, i ^ 1) for i in range(count)])
+    held = jnp.stack([mine, other], axis=1)
+    received = []
+    for shift in range(outer):
+        chunk = lax.dynamic_index_in_dim(held, (chip + shift) % outer, 0, keepdims=False)
+        if shift:
+            chunk = lax.ppermute(
+                chunk,
+                "ctx",
+                [(i, 2 * ((i // 2 + shift) % outer) + i % 2) for i in range(count)],
+            )
+        received.append(chunk)
+    received = jnp.stack(received)
+    ordered = jnp.stack(
+        [
+            lax.dynamic_index_in_dim(received, (chip - source) % outer, 0, keepdims=False)
+            for source in range(outer)
+        ]
+    )
+    first = lax.dynamic_index_in_dim(ordered, core, 1, keepdims=False)
+    second = lax.dynamic_index_in_dim(ordered, 1 - core, 1, keepdims=False)
+    return jnp.stack([first, second], axis=1).reshape(stacked.shape)
+
+
+def transpose_ring(stacked, count, me):
     received = []
     for shift in range(count):
         chunk = lax.dynamic_index_in_dim(stacked, (me + shift) % count, 0, keepdims=False)

time: 78.8 us -> 94.1 us (1.19)
  waiting for transfers between devices: 15 us -> 48.4 us
  starting transfers between devices: 36.6 us -> 20 us
  local copies, waits for them, and re-layouts: 11 us -> 7.21 us
  other arithmetic: 5.15 us -> 6.85 us
    ppermute x14 -> x8, starting transfers between devices: 26.5 us -> 10.7 us  [the longest x6 8.65 us: transpose_ctx(): lax.ppermute(chunk, 'ctx', [(i, 2 * ((i // 2 + shift) % outer) + i % 2) f...]
    ppermute x14 -> x8, waiting for transfers between devices: 14.5 us -> 29.3 us  [the longest x6 27.3 us: transpose_ctx(): lax.ppermute(chunk, 'ctx', [(i, 2 * ((i // 2 + shift) % outer) + i % 2) f...]
    ppermute x3, waiting for transfers between devices: 0.5 us -> 11.4 us  [gather_matmul(): lax.ppermute(out_grad, 'tp', [(i, (i + shift) % count) for i in range(cou...]
    all_to_all x1, waiting for transfers between devices: 0.01 us -> 7.73 us  [all_to_all_ctx(): return lax.all_to_all(stacked, 'ctx', 0, 0, tiled=True)]
    unnamed x51 -> x29, local copies, waits for them, and re-layouts: 8.22 us -> 4.27 us
    another operation x1, other arithmetic: 0.13 us -> 1.13 us  [gather_matmul(): stacked = jnp.stack(pieces)]
  transfers between devices with their start and end apart: 18 -> 12, of which waited for: 9 -> 10; matrix products, arithmetic and copies ran while one was open for 16% -> 2% of each run, Pallas kernels for 0% -> 0%
where the time goes in v12:
time: 94.1 us; the launch traced here: 92.9 us
  waiting for transfers between devices  48.4 us (51%)
  starting transfers between devices  20 us (21%)
  matrix products  9.28 us (10%)
  local copies, waits for them, and re-layouts  7.21 us (8%)
  other arithmetic  6.85 us (7%)
  between operations  1.2 us (1%)
    ppermute x6, waiting for transfers between devices, transpose_ctx(): lax.ppermute(chunk, 'ctx', [(i, 2 * ((i // 2 + shift) % outer) + i % 2) f...  27.3 us
    ppermute x3, waiting for transfers between devices, gather_matmul(): lax.ppermute(out_grad, 'tp', [(i, (i + shift) % count) for i in range(cou...  11.4 us
    ppermute x6, starting transfers between devices, transpose_ctx(): lax.ppermute(chunk, 'ctx', [(i, 2 * ((i // 2 + shift) % outer) + i % 2) f...  8.65 us
    all_to_all x1, waiting for transfers between devices, all_to_all_ctx(): return lax.all_to_all(stacked, 'ctx', 0, 0, tiled=True)  7.73 us
    dot_general x1, matrix products, gather_matmul(): lax.dot_general(gathered, out_weight, (((1,), (1,)), ((), ())), preferred...  6.3 us
    all_to_all x1, starting transfers between devices, all_to_all_ctx(): return lax.all_to_all(stacked, 'ctx', 0, 0, tiled=True)  5.58 us
    unnamed x29, local copies, waits for them, and re-layouts  4.27 us
    ppermute x3, starting transfers between devices, gather_matmul(): lax.ppermute(out_grad, 'tp', [(i, (i + shift) % count) for i in range(cou...  3.66 us
  transfers between devices with their start and end apart: 12, of which 10 were waited for; matrix products, arithmetic and copies ran while one was open for 2% of the time, Pallas kernels for 0%

profile of v12, /device:TPU:9, one launch (start us, length us, event | category | flops | bytes accessed | tf_op | source)
XLA Modules:
  0.0 92.9 jit_solution(12084135618120593000)
XLA Ops:
  0.6 1.3 %collective-permute-start = (bf16[128,1024]{1,0:T(8,128)(2,1)}, bf16[128,1024]{1,0:T(8,128)(2,1)S(1)}, u32[]{:S(2)}, u32[]{:S(2)}) collective-permute-start(bf16[128,1024]{1,0:T(8,128)(2,1)} %param.17), channel_id=1, source_target_pairs={{0,1},{1,2},{2,3},{3,0},{4,5},{5,6},{6,7},{7,4},{8,9},{9,10},{10,1... | collective-permute-start | bytes 786440 | tf_op jit(solution)/shard_map/ppermute | solution.py:25
  1.9 1.2 %collective-permute-start.1 = (bf16[128,1024]{1,0:T(8,128)(2,1)}, bf16[128,1024]{1,0:T(8,128)(2,1)S(1)}, u32[]{:S(2)}, u32[]{:S(2)}) collective-permute-start(bf16[128,1024]{1,0:T(8,128)(2,1)} %param.17), channel_id=1, source_target_pairs={{0,2},{1,3},{2,0},{3,1},{4,6},{5,7},{6,4},{7,5},{8,10},{9,11},{10,... | collective-permute-start | bytes 786440 | tf_op jit(solution)/shard_map/ppermute | solution.py:25
  3.1 1.2 %collective-permute-start.2 = (bf16[128,1024]{1,0:T(8,128)(2,1)}, bf16[128,1024]{1,0:T(8,128)(2,1)S(1)}, u32[]{:S(2)}, u32[]{:S(2)}) collective-permute-start(bf16[128,1024]{1,0:T(8,128)(2,1)} %param.17), channel_id=1, source_target_pairs={{0,3},{1,0},{2,1},{3,2},{4,7},{5,4},{6,5},{7,6},{8,11},{9,8},{10,9... | collective-permute-start | bytes 786440 | tf_op jit(solution)/shard_map/ppermute | solution.py:25
  4.3 4.7 %collective-permute-done = bf16[128,1024]{1,0:T(8,128)(2,1)S(1)} collective-permute-done((bf16[128,1024]{1,0:T(8,128)(2,1)}, bf16[128,1024]{1,0:T(8,128)(2,1)S(1)}, u32[]{:S(2)}, u32[]{:S(2)}) %collective-permute-start) | collective-permute-done | bytes 262176 | tf_op jit(solution)/shard_map/ppermute | solution.py:25
  9.0 6.6 %collective-permute-done.1 = bf16[128,1024]{1,0:T(8,128)(2,1)S(1)} collective-permute-done((bf16[128,1024]{1,0:T(8,128)(2,1)}, bf16[128,1024]{1,0:T(8,128)(2,1)S(1)}, u32[]{:S(2)}, u32[]{:S(2)}) %collective-permute-start.1) | collective-permute-done | bytes 262176 | tf_op jit(solution)/shard_map/ppermute | solution.py:25
  15.6 1.1 %pad_maximum_fusion.1 = bf16[4,128,1024]{2,1,0:T(8,128)(2,1)S(1)} fusion(bf16[1,128,1024]{2,1,0:T(8,128)(2,1)S(1)} %bitcast.251, bf16[1,128,1024]{2,1,0:T(8,128)(2,1)S(1)} %bitcast.250, bf16[1,128,1024]{2,1,0:T(8,128)(2,1)S(1)} %bitcast.249, bf16[1,128,1024]{2,1,0:T(8,128)(2,1)} %bitcast.248), kind=kLoop, calls=%fused_computation.39 | loop fusion | flops 1572864 | bytes 2097152 | tf_op jit(solution)/shard_map/stack | solution.py:27
  16.9 6.3 %fusion.18 = (bf16[128,1024]{1,0:T(8,128)(2,1)S(1)}, f32[128,1024]{1,0:T(8,128)S(1)}) fusion(bf16[128,1024]{1,0:T(8,128)(2,1)S(1)} %copy-done.1, bf16[1024,4096]{1,0:T(8,128)(2,1)} %param.18, bf16[128,1024]{1,0:T(8,128)(2,1)S(1)} %get-tuple-element.52, bf16[128,1024]{1,0:T(8,128)(2,1)S(1)} %get-tuple-element.53, ...), kind=kOutput, calls=%fused_computation.93 | convolution fusion | flops 1078329344 | bytes 10485760 | tf_op jit(solution)/shard_map/dot_general | solution.py:33
  23.3 0.9 fusion.19
  24.3 0.7 collective-permute-start.3
  25.0 0.2 copy.41
  25.1 0.2 copy.42
  25.3 0.2 copy.43
  25.6 0.5 collective-permute-done.3
  26.2 1.4 %collective-permute-start.4 = (bf16[2,2,128,128]{3,2,0,1:T(8,128)(2,1)S(1)}, bf16[2,2,128,128]{3,2,0,1:T(8,128)(2,1)S(1)}, u32[]{:S(2)}, u32[]{:S(2)}) collective-permute-start(bf16[2,2,128,128]{3,2,0,1:T(8,128)(2,1)S(1)} %get-tuple-element.82), channel_id=1, source_target_pairs={{0,8},{4,12},{8,16},{12,20},{16,24},{20,28},{24,0},{28,4},{1,9},{5... | collective-permute-start | bytes 393224 | tf_op jit(solution)/shard_map/ppermute | solution.py:167
  27.5 1.1 %collective-permute-start.5 = (bf16[2,2,128,128]{3,2,0,1:T(8,128)(2,1)S(1)}, bf16[2,2,128,128]{3,2,0,1:T(8,128)(2,1)S(1)}, u32[]{:S(2)}, u32[]{:S(2)}) collective-permute-start(bf16[2,2,128,128]{3,2,0,1:T(8,128)(2,1)S(1)} %get-tuple-element.83), channel_id=1, source_target_pairs={{0,16},{4,20},{8,24},{12,28},{16,0},{20,4},{24,8},{28,12},{1,17},{... | collective-permute-start | bytes 393224 | tf_op jit(solution)/shard_map/ppermute | solution.py:167
  28.6 1.4 %collective-permute-start.6 = (bf16[2,2,128,128]{3,2,0,1:T(8,128)(2,1)S(1)}, bf16[2,2,128,128]{3,2,0,1:T(8,128)(2,1)S(1)}, u32[]{:S(2)}, u32[]{:S(2)}) collective-permute-start(bf16[2,2,128,128]{3,2,0,1:T(8,128)(2,1)S(1)} %get-tuple-element.84), channel_id=1, source_target_pairs={{0,24},{4,28},{8,0},{12,4},{16,8},{20,12},{24,16},{28,20},{1,25},{... | collective-permute-start | bytes 393224 | tf_op jit(solution)/shard_map/ppermute | solution.py:167
  30.1 0.8 copy.44
  30.9 5.6 %all-to-all-start = ((bf16[8,2,128,128]{2,3,1,0:T(8,128)(2,1)}), bf16[8,2,128,128]{2,3,1,0:T(8,128)(2,1)S(1)}, u32[]{:S(2)}, u32[]{:S(2)}) async-start(bf16[8,2,128,128]{2,3,1,0:T(8,128)(2,1)} %copy.44), calls=%async_computation | async-start | bytes 1048576 | tf_op jit(solution)/shard_map/all_to_all | solution.py:147
  36.5 4.0 %collective-permute-done.5 = bf16[2,2,128,128]{3,2,0,1:T(8,128)(2,1)S(1)} collective-permute-done((bf16[2,2,128,128]{3,2,0,1:T(8,128)(2,1)S(1)}, bf16[2,2,128,128]{3,2,0,1:T(8,128)(2,1)S(1)}, u32[]{:S(2)}, u32[]{:S(2)}) %collective-permute-start.5) | collective-permute-done | bytes 131104 | tf_op jit(solution)/shard_map/ppermute | solution.py:167
  40.5 1.1 %collective-permute-done.6 = bf16[2,2,128,128]{3,2,0,1:T(8,128)(2,1)S(1)} collective-permute-done((bf16[2,2,128,128]{3,2,0,1:T(8,128)(2,1)S(1)}, bf16[2,2,128,128]{3,2,0,1:T(8,128)(2,1)S(1)}, u32[]{:S(2)}, u32[]{:S(2)}) %collective-permute-start.6) | collective-permute-done | bytes 131104 | tf_op jit(solution)/shard_map/ppermute | solution.py:167
  42.0 7.7 %all-to-all-done = bf16[8,2,128,128]{2,3,1,0:T(8,128)(2,1)S(1)} async-done(((bf16[8,2,128,128]{2,3,1,0:T(8,128)(2,1)}), bf16[8,2,128,128]{2,3,1,0:T(8,128)(2,1)S(1)}, u32[]{:S(2)}, u32[]{:S(2)}) %all-to-all-start) | async-done | bytes 524320 | tf_op jit(solution)/shard_map/all_to_all | solution.py:147
  49.8 0.2 copy.56
  50.0 0.2 copy.57
  50.2 0.1 pad_maximum_fusion.6
  50.3 0.1 pad_maximum_fusion.2
  50.4 0.4 copy-done.8
  50.8 0.7 convolution_bitcast_fusion
  51.6 0.1 copy-done.7
  51.7 0.6 convolution_bitcast_fusion.1
  52.3 0.6 slice_add_fusion.3
  53.0 0.2 fusion.17
  53.3 0.4 add_add_fusion.2
  53.7 0.4 subtract_add_fusion.1
  54.2 0.1 slice_bitcast_fusion.16
  54.3 0.4 add_add_fusion.1
  54.7 0.4 subtract_add_fusion
  55.1 0.2 fusion.47
  55.6 0.1 pad_maximum_fusion
  55.7 0.1 bitcast_convert_fusion
  55.8 0.3 fusion
  56.2 0.6 copy-done
  56.7 0.5 fusion.45
  57.2 0.5 fusion.46
  57.7 0.4 copy-done.6
  58.1 0.5 add_add_fusion
  58.6 0.2 copy-done.9
  58.8 0.3 multiply_add_fusion
  59.4 0.1 fusion.13
  59.5 1.4 %collective-permute-start.7 = (f32[4,128,2,128]{1,3,0,2:T(8,128)S(1)}, f32[4,128,2,128]{1,3,0,2:T(8,128)S(1)}, u32[]{:S(2)}, u32[]{:S(2)}) collective-permute-start(f32[4,128,2,128]{1,3,0,2:T(8,128)S(1)} %get-tuple-element.29), channel_id=1, source_target_pairs={{0,4},{4,0},{8,12},{12,8},{16,20},{20,16},{24,28},{28,24},{1,5},{5... | collective-permute-start | bytes 1572872 | tf_op jit(solution)/shard_map/ppermute | solution.py:161
  60.9 1.5 %collective-permute-done.7 = f32[4,128,2,128]{1,3,0,2:T(8,128)S(1)} collective-permute-done((f32[4,128,2,128]{1,3,0,2:T(8,128)S(1)}, f32[4,128,2,128]{1,3,0,2:T(8,128)S(1)}, u32[]{:S(2)}, u32[]{:S(2)}) %collective-permute-start.7) | collective-permute-done | bytes 524320 | tf_op jit(solution)/shard_map/ppermute | solution.py:161
  62.6 0.9 collective-permute-start.8
  63.5 3.9 %collective-permute-start.9 = (f32[2,128,2,128]{1,3,0,2:T(8,128)S(1)}, f32[2,128,2,128]{1,3,0,2:T(8,128)S(1)}, u32[]{:S(2)}, u32[]{:S(2)}) collective-permute-start(f32[2,128,2,128]{1,3,0,2:T(8,128)S(1)} %get-tuple-element.27), channel_id=1, source_target_pairs={{0,16},{4,20},{8,24},{12,28},{16,0},{20,4},{24,8},{28,12},{1,17},{... | collective-permute-start | bytes 786440 | tf_op jit(solution)/shard_map/ppermute | solution.py:167
  67.4 4.2 %collective-permute-done.8 = f32[2,128,2,128]{1,3,0,2:T(8,128)S(1)} collective-permute-done((f32[2,128,2,128]{1,3,0,2:T(8,128)S(1)}, f32[2,128,2,128]{1,3,0,2:T(8,128)S(1)}, u32[]{:S(2)}, u32[]{:S(2)}) %collective-permute-start.8) | collective-permute-done | bytes 262176 | tf_op jit(solution)/shard_map/ppermute | solution.py:167
  71.6 14.0 %collective-permute-done.9 = f32[2,128,2,128]{1,3,0,2:T(8,128)S(1)} collective-permute-done((f32[2,128,2,128]{1,3,0,2:T(8,128)S(1)}, f32[2,128,2,128]{1,3,0,2:T(8,128)S(1)}, u32[]{:S(2)}, u32[]{:S(2)}) %collective-permute-start.9) | collective-permute-done | bytes 262176 | tf_op jit(solution)/shard_map/ppermute | solution.py:167
  85.6 3.9 %collective-permute-done.10 = f32[2,128,2,128]{1,3,0,2:T(8,128)S(1)} collective-permute-done((f32[2,128,2,128]{1,3,0,2:T(8,128)S(1)}, f32[2,128,2,128]{1,3,0,2:T(8,128)S(1)}, u32[]{:S(2)}, u32[]{:S(2)}) %collective-permute-start.10) | collective-permute-done | bytes 262176 | tf_op jit(solution)/shard_map/ppermute | solution.py:167
  89.5 0.1 pad_maximum_fusion.3
  89.6 0.1 constant_dynamic-slice_fusion.5
  89.7 0.1 pad_maximum_fusion.4
  89.8 0.1 constant_dynamic-slice_fusion.1
  89.9 0.1 pad_maximum_fusion.5
  90.1 0.1 fusion.9
  90.2 0.9 copy.50
  91.1 0.8 copy.51
  91.9 1.0 %copy.55 = f32[128,1024]{1,0:T(8,128)} copy(f32[128,1024]{0,1:T(8,128)S(1)} %bitcast.239) | data formatting | bytes 1048576 | tf_op jit(solution)/shard_map/reshape | solution.py:143
  (53 shorter events, 1.6 us)
Async XLA Ops:
  0.6 8.4 %collective-permute-start = (bf16[128,1024]{1,0:T(8,128)(2,1)}, bf16[128,1024]{1,0:T(8,128)(2,1)S(1)}, u32[]{:S(2)}, u32[]{:S(2)}) collective-permute-start(bf16[128,1024]{1,0:T(8,128)(2,1)} %param.17), channel_id=1, source_target_pairs={{0,1},{1,2},{2,3},{3,0},{4,5},{5,6},{6,7},{7,4},{8,9},{9,10},{10,1... | collective-permute-start | bytes 786440 | tf_op jit(solution)/shard_map/ppermute | solution.py:25
  1.9 13.7 %collective-permute-start.1 = (bf16[128,1024]{1,0:T(8,128)(2,1)}, bf16[128,1024]{1,0:T(8,128)(2,1)S(1)}, u32[]{:S(2)}, u32[]{:S(2)}) collective-permute-start(bf16[128,1024]{1,0:T(8,128)(2,1)} %param.17), channel_id=1, source_target_pairs={{0,2},{1,3},{2,0},{3,1},{4,6},{5,7},{6,4},{7,5},{8,10},{9,11},{10,... | collective-permute-start | bytes 786440 | tf_op jit(solution)/shard_map/ppermute | solution.py:25
  3.1 12.5 %collective-permute-start.2 = (bf16[128,1024]{1,0:T(8,128)(2,1)}, bf16[128,1024]{1,0:T(8,128)(2,1)S(1)}, u32[]{:S(2)}, u32[]{:S(2)}) collective-permute-start(bf16[128,1024]{1,0:T(8,128)(2,1)} %param.17), channel_id=1, source_target_pairs={{0,3},{1,0},{2,1},{3,2},{4,7},{5,4},{6,5},{7,6},{8,11},{9,8},{10,9... | collective-permute-start | bytes 786440 | tf_op jit(solution)/shard_map/ppermute | solution.py:25
  15.6 1.2 %copy-start.1 = (bf16[128,1024]{1,0:T(8,128)(2,1)S(1)}, bf16[128,1024]{1,0:T(8,128)(2,1)}, u32[]{:S(2)}) copy-start(bf16[128,1024]{1,0:T(8,128)(2,1)} %param.13) | copy-start | bytes 786436
  16.9 6.4 %copy-start.2 = (bf16[128,1024]{1,0:T(8,128)(2,1)S(1)}, bf16[128,1024]{1,0:T(8,128)(2,1)}, u32[]{:S(2)}) copy-start(bf16[128,1024]{1,0:T(8,128)(2,1)} %param.16) | copy-start | bytes 786436
  23.2 1.7 %copy-start.3 = (bf16[128,1024]{1,0:T(8,128)(2,1)S(1)}, bf16[128,1024]{1,0:T(8,128)(2,1)}, u32[]{:S(2)}) copy-start(bf16[128,1024]{1,0:T(8,128)(2,1)} %param.14) | copy-start | bytes 786436
  23.3 1.9 %copy-start.4 = (bf16[128,1024]{1,0:T(8,128)(2,1)S(1)}, bf16[128,1024]{1,0:T(8,128)(2,1)}, u32[]{:S(2)}) copy-start(bf16[128,1024]{1,0:T(8,128)(2,1)} %param.15) | copy-start | bytes 786436
  24.2 1.2 %copy-start.5 = (bf16[128,1024]{1,0:T(8,128)(2,1)S(1)}, bf16[128,1024]{1,0:T(8,128)(2,1)}, u32[]{:S(2)}) copy-start(bf16[128,1024]{1,0:T(8,128)(2,1)} %param.19) | copy-start | bytes 786436
  24.3 1.8 %collective-permute-start.3 = (bf16[4,2,128,128]{3,2,1,0:T(8,128)(2,1)S(1)}, bf16[4,2,128,128]{3,2,1,0:T(8,128)(2,1)S(1)}, u32[]{:S(2)}, u32[]{:S(2)}) collective-permute-start(bf16[4,2,128,128]{3,2,1,0:T(8,128)(2,1)S(1)} %bitcast.247), channel_id=1, source_target_pairs={{0,4},{4,0},{8,12},{12,8},{16,20},{20,16},{24,28},{28,24},{1,5},{5... | collective-permute-start | bytes 786440 | tf_op jit(solution)/shard_map/ppermute | solution.py:161
  26.2 10.3 %collective-permute-start.4 = (bf16[2,2,128,128]{3,2,0,1:T(8,128)(2,1)S(1)}, bf16[2,2,128,128]{3,2,0,1:T(8,128)(2,1)S(1)}, u32[]{:S(2)}, u32[]{:S(2)}) collective-permute-start(bf16[2,2,128,128]{3,2,0,1:T(8,128)(2,1)S(1)} %get-tuple-element.82), channel_id=1, source_target_pairs={{0,8},{4,12},{8,16},{12,20},{16,24},{20,28},{24,0},{28,4},{1,9},{5... | collective-permute-start | bytes 393224 | tf_op jit(solution)/shard_map/ppermute | solution.py:167
  27.5 13.0 %collective-permute-start.5 = (bf16[2,2,128,128]{3,2,0,1:T(8,128)(2,1)S(1)}, bf16[2,2,128,128]{3,2,0,1:T(8,128)(2,1)S(1)}, u32[]{:S(2)}, u32[]{:S(2)}) collective-permute-start(bf16[2,2,128,128]{3,2,0,1:T(8,128)(2,1)S(1)} %get-tuple-element.83), channel_id=1, source_target_pairs={{0,16},{4,20},{8,24},{12,28},{16,0},{20,4},{24,8},{28,12},{1,17},{... | collective-permute-start | bytes 393224 | tf_op jit(solution)/shard_map/ppermute | solution.py:167
  28.6 13.0 %collective-permute-start.6 = (bf16[2,2,128,128]{3,2,0,1:T(8,128)(2,1)S(1)}, bf16[2,2,128,128]{3,2,0,1:T(8,128)(2,1)S(1)}, u32[]{:S(2)}, u32[]{:S(2)}) collective-permute-start(bf16[2,2,128,128]{3,2,0,1:T(8,128)(2,1)S(1)} %get-tuple-element.84), channel_id=1, source_target_pairs={{0,24},{4,28},{8,0},{12,4},{16,8},{20,12},{24,16},{28,20},{1,25},{... | collective-permute-start | bytes 393224 | tf_op jit(solution)/shard_map/ppermute | solution.py:167
  30.9 18.9 %all-to-all-start = ((bf16[8,2,128,128]{2,3,1,0:T(8,128)(2,1)}), bf16[8,2,128,128]{2,3,1,0:T(8,128)(2,1)S(1)}, u32[]{:S(2)}, u32[]{:S(2)}) async-start(bf16[8,2,128,128]{2,3,1,0:T(8,128)(2,1)} %copy.44), calls=%async_computation | async-start | bytes 1048576 | tf_op jit(solution)/shard_map/all_to_all | solution.py:147
  50.0 0.8 copy-start.8
  50.8 0.8 copy-start.7
  54.3 0.8 copy-start.10
  55.8 0.9 copy-start
  57.2 0.9 copy-start.6
  58.1 0.7 copy-start.9
  59.5 3.0 %collective-permute-start.7 = (f32[4,128,2,128]{1,3,0,2:T(8,128)S(1)}, f32[4,128,2,128]{1,3,0,2:T(8,128)S(1)}, u32[]{:S(2)}, u32[]{:S(2)}) collective-permute-start(f32[4,128,2,128]{1,3,0,2:T(8,128)S(1)} %get-tuple-element.29), channel_id=1, source_target_pairs={{0,4},{4,0},{8,12},{12,8},{16,20},{20,16},{24,28},{28,24},{1,5},{5... | collective-permute-start | bytes 1572872 | tf_op jit(solution)/shard_map/ppermute | solution.py:161
  62.6 9.1 %collective-permute-start.8 = (f32[2,128,2,128]{1,3,0,2:T(8,128)S(1)}, f32[2,128,2,128]{1,3,0,2:T(8,128)S(1)}, u32[]{:S(2)}, u32[]{:S(2)}) collective-permute-start(f32[2,128,2,128]{1,3,0,2:T(8,128)S(1)} %get-tuple-element.26), channel_id=1, source_target_pairs={{0,8},{4,12},{8,16},{12,20},{16,24},{20,28},{24,0},{28,4},{1,9},{5... | collective-permute-start | bytes 786440 | tf_op jit(solution)/shard_map/ppermute | solution.py:167
  63.5 22.1 %collective-permute-start.9 = (f32[2,128,2,128]{1,3,0,2:T(8,128)S(1)}, f32[2,128,2,128]{1,3,0,2:T(8,128)S(1)}, u32[]{:S(2)}, u32[]{:S(2)}) collective-permute-start(f32[2,128,2,128]{1,3,0,2:T(8,128)S(1)} %get-tuple-element.27), channel_id=1, source_target_pairs={{0,16},{4,20},{8,24},{12,28},{16,0},{20,4},{24,8},{28,12},{1,17},{... | collective-permute-start | bytes 786440 | tf_op jit(solution)/shard_map/ppermute | solution.py:167
  67.4 22.1 %collective-permute-start.10 = (f32[2,128,2,128]{1,3,0,2:T(8,128)S(1)}, f32[2,128,2,128]{1,3,0,2:T(8,128)S(1)}, u32[]{:S(2)}, u32[]{:S(2)}) collective-permute-start(f32[2,128,2,128]{1,3,0,2:T(8,128)S(1)} %get-tuple-element.28), channel_id=1, source_target_pairs={{0,24},{4,28},{8,0},{12,4},{16,8},{20,12},{24,16},{28,20},{1,25},{... | collective-permute-start | bytes 786440 | tf_op jit(solution)/shard_map/ppermute | solution.py:167

commit v13 on v10

--- a/solution.py
+++ b/solution.py
@@ -165,10 +165,45 @@
     )
 
 
+def scatter_lanes(value, sub):
+    count = lax.axis_size("ctx")
+    me = lax.axis_index("ctx")
+    axis = value.ndim - 1
+    received = []
+    for shift in range(count):
+        chunk = lax.dynamic_slice_in_dim(value, ((me + shift) % count) * sub, sub, axis=axis)
+        if shift:
+            chunk = lax.ppermute(chunk, "ctx", [(i, (i + shift) % count) for i in range(count)])
+        received.append(chunk)
+    received = jnp.stack(received)
+    return jnp.stack(
+        [
+            lax.dynamic_index_in_dim(received, (me - source) % count, 0, keepdims=False)
+            for source in range(count)
+        ]
+    )
+
+
+def gather_lanes(value, chans):
+    count = lax.axis_size("ctx")
+    me = lax.axis_index("ctx")
+    sub = value.shape[-1]
+    result = jnp.zeros(value.shape[1:-1] + (chans,), value.dtype)
+    for shift in range(count):
+        chunk = lax.dynamic_index_in_dim(value, (me + shift) % count, 0, keepdims=False)
+        if shift:
+            chunk = lax.ppermute(chunk, "ctx", [(i, (i + shift) % count) for i in range(count)])
+        result = lax.dynamic_update_slice_in_dim(
+            result, chunk, ((me - shift) % count) * sub, axis=result.ndim - 1
+        )
+    return result
+
+
 def body(q_proj, k_proj, v_proj, saved_conv, out_grad, out_weight, filter_taps):
     rows, chans = q_proj.shape
     blocks = lax.axis_size("ctx")
     seq = rows * blocks
+    sub = chans // blocks
     gated = (k_proj.astype(jnp.float32) * v_proj.astype(jnp.float32)).astype(jnp.bfloat16)
     inputs_t = all_to_all_ctx(
         jnp.stack([to_groups(gated, blocks), to_groups(filter_taps, blocks)], axis=1)
@@ -177,8 +212,7 @@
     dq_grad = (d_gated * saved_conv.astype(jnp.float32)).astype(jnp.bfloat16)
     dz = d_gated * q_proj.astype(jnp.float32)
     dz_hi, dz_lo = split_bf16(dz)
-    dz_t = transpose_ctx(jnp.stack([to_groups(dz_hi, blocks), to_groups(dz_lo, blocks)], axis=1))
-    sub = chans // blocks
+    dz_t = scatter_lanes(jnp.stack([dz_hi, dz_lo]), sub)
     du_t, filter_t = long_correlations(
         dz_t[:, 0].reshape(seq, sub),
         dz_t[:, 1].reshape(seq, sub),
@@ -186,9 +220,10 @@
         inputs_t[:, 1].reshape(seq, sub),
         float(seq) ** -0.5,
     )
-    back = transpose_ctx(jnp.stack([du_t, filter_t], axis=1).reshape(blocks, rows, 2, sub))
-    du_local = from_groups(back[:, :, 0])
-    filter_grad = from_groups(back[:, :, 1])
+    outgoing = jnp.stack([du_t, filter_t]).reshape(2, blocks, rows, sub).transpose(1, 0, 2, 3)
+    back = gather_lanes(outgoing, chans)
+    du_local = back[0]
+    filter_grad = back[1]
     dk_grad = (du_local * v_proj.astype(jnp.float32)).astype(jnp.bfloat16)
     dv_grad = (du_local * k_proj.astype(jnp.float32)).astype(jnp.bfloat16)
     return (dq_grad, dk_grad, dv_grad, filter_grad)

time: 78.8 us -> 78.4 us (level)
  starting transfers between devices: 36.6 us -> 26.1 us
  waiting for transfers between devices: 15 us -> 25.3 us
    ppermute x14, starting transfers between devices: 26.5 us -> 16 us  [the longest x7 8.15 us: gather_lanes(): lax.ppermute(chunk, 'ctx', [(i, (i + shift) % count) for i in range(count)])]
    ppermute x14, waiting for transfers between devices: 14.5 us -> 25 us  [the longest x7 16.7 us: gather_lanes(): lax.ppermute(chunk, 'ctx', [(i, (i + shift) % count) for i in range(count)])]
    another operation x0 -> x3, other arithmetic: none -> 1 us  [body(): dz_t = scatter_lanes(jnp.stack([dz_hi, dz_lo]), sub)]
    reshape x1 -> x0, local copies, waits for them, and re-layouts: 0.99 us -> none  [from_groups(): return value.transpose(1, 0, 2).reshape(rows, groups * chans)]
    unnamed x1, other arithmetic: 0.88 us -> 0.02 us
    unnamed x51 -> x37, local copies, waits for them, and re-layouts: 8.22 us -> 8.91 us
where the time goes in v13:
time: 78.4 us; the launch traced here: 78 us
  starting transfers between devices  26.1 us (33%)
  waiting for transfers between devices  25.3 us (32%)
  local copies, waits for them, and re-layouts  10.7 us (14%)
  matrix products  9.28 us (12%)
  other arithmetic  5.37 us (7%)
  between operations  1.18 us (2%)
    ppermute x7, waiting for transfers between devices, gather_lanes(): lax.ppermute(chunk, 'ctx', [(i, (i + shift) % count) for i in range(count)])  16.7 us
    unnamed x37, local copies, waits for them, and re-layouts  8.91 us
    ppermute x7, waiting for transfers between devices, scatter_lanes(): lax.ppermute(chunk, 'ctx', [(i, (i + shift) % count) for i in range(count)])  8.29 us
    ppermute x7, starting transfers between devices, gather_lanes(): lax.ppermute(chunk, 'ctx', [(i, (i + shift) % count) for i in range(count)])  8.15 us
    ppermute x7, starting transfers between devices, scatter_lanes(): lax.ppermute(chunk, 'ctx', [(i, (i + shift) % count) for i in range(count)])  7.81 us
    all_to_all x1, starting transfers between devices, all_to_all_ctx(): return lax.all_to_all(stacked, 'ctx', 0, 0, tiled=True)  6.44 us
    dot_general x1, matrix products, gather_matmul(): lax.dot_general(gathered, out_weight, (((1,), (1,)), ((), ())), preferred...  6.3 us
    ppermute x3, starting transfers between devices, gather_matmul(): lax.ppermute(out_grad, 'tp', [(i, (i + shift) % count) for i in range(cou...  3.66 us
  transfers between devices with their start and end apart: 18, of which 9 were waited for; matrix products, arithmetic and copies ran while one was open for 16% of the time, Pallas kernels for 0%

profile of v13, /device:TPU:9, one launch (start us, length us, event | category | flops | bytes accessed | tf_op | source)
XLA Modules:
  0.0 78.0 jit_solution(7454425813897225204)
XLA Ops:
  0.6 1.3 %collective-permute-start = (bf16[128,1024]{1,0:T(8,128)(2,1)}, bf16[128,1024]{1,0:T(8,128)(2,1)S(1)}, u32[]{:S(2)}, u32[]{:S(2)}) collective-permute-start(bf16[128,1024]{1,0:T(8,128)(2,1)} %param.17), channel_id=1, source_target_pairs={{0,1},{1,2},{2,3},{3,0},{4,5},{5,6},{6,7},{7,4},{8,9},{9,10},{10,1... | collective-permute-start | bytes 786440 | tf_op jit(solution)/shard_map/ppermute | solution.py:25
  1.9 1.2 %collective-permute-start.1 = (bf16[128,1024]{1,0:T(8,128)(2,1)}, bf16[128,1024]{1,0:T(8,128)(2,1)S(1)}, u32[]{:S(2)}, u32[]{:S(2)}) collective-permute-start(bf16[128,1024]{1,0:T(8,128)(2,1)} %param.17), channel_id=1, source_target_pairs={{0,2},{1,3},{2,0},{3,1},{4,6},{5,7},{6,4},{7,5},{8,10},{9,11},{10,... | collective-permute-start | bytes 786440 | tf_op jit(solution)/shard_map/ppermute | solution.py:25
  3.1 1.2 %collective-permute-start.2 = (bf16[128,1024]{1,0:T(8,128)(2,1)}, bf16[128,1024]{1,0:T(8,128)(2,1)S(1)}, u32[]{:S(2)}, u32[]{:S(2)}) collective-permute-start(bf16[128,1024]{1,0:T(8,128)(2,1)} %param.17), channel_id=1, source_target_pairs={{0,3},{1,0},{2,1},{3,2},{4,7},{5,4},{6,5},{7,6},{8,11},{9,8},{10,9... | collective-permute-start | bytes 786440 | tf_op jit(solution)/shard_map/ppermute | solution.py:25
  4.3 1.1 %copy.49 = bf16[128,1024]{0,1:T(8,128)(2,1)S(1)} copy(bf16[128,1024]{1,0:T(8,128)(2,1)} %param.14) | data formatting | bytes 524288 | tf_op args[1]
  5.4 1.1 %copy.50 = bf16[128,1024]{0,1:T(8,128)(2,1)S(1)} copy(bf16[128,1024]{1,0:T(8,128)(2,1)} %param.15) | data formatting | bytes 524288 | tf_op args[2]
  6.6 1.2 %copy.51 = bf16[128,1024]{0,1:T(8,128)(2,1)S(1)} copy(bf16[128,1024]{1,0:T(8,128)(2,1)} %param.19) | data formatting | bytes 524288 | tf_op args[6]
  7.9 1.0 %copy.52 = bf16[8,2,128,128]{3,2,1,0:T(8,128)(2,1)} copy(bf16[8,2,128,128]{2,3,0,1:T(8,128)(2,1)S(1)} %pad_maximum_fusion.4) | data formatting | bytes 1048576 | tf_op jit(solution)/shard_map/stack | solution.py:209
  8.9 6.4 %all-to-all-start = ((bf16[8,2,128,128]{3,2,1,0:T(8,128)(2,1)}), bf16[8,2,128,128]{3,2,1,0:T(8,128)(2,1)S(1)}, u32[]{:S(2)}, u32[]{:S(2)}) async-start(bf16[8,2,128,128]{3,2,1,0:T(8,128)(2,1)} %copy.52), calls=%async_computation | async-start | bytes 1048576 | tf_op jit(solution)/shard_map/all_to_all | solution.py:147
  15.3 0.3 collective-permute-done.1
  15.6 0.1 pad_maximum_fusion.1
  15.8 0.1 dynamic-slice_bitcast_fusion.3
  15.9 0.7 copy-done.1
  16.6 6.3 %fusion.16 = (bf16[128,1024]{1,0:T(8,128)(2,1)S(1)}, f32[128,1024]{1,0:T(8,128)S(1)}) fusion(bf16[128,1024]{1,0:T(8,128)(2,1)S(1)} %copy-done.1, bf16[1024,4096]{1,0:T(8,128)(2,1)} %param.18, bf16[128,1024]{1,0:T(8,128)(2,1)S(1)} %get-tuple-element.42, bf16[128,1024]{1,0:T(8,128)(2,1)S(1)} %get-tuple-element.43, ...), kind=kOutput, calls=%fused_computation.95 | convolution fusion | flops 1078329344 | bytes 10485760 | tf_op jit(solution)/shard_map/dot_general | solution.py:33
  22.9 0.9 %fusion.17 = (bf16[1,128,1024]{2,1,0:T(8,128)(2,1)S(1)}, bf16[128,1024]{1,0:T(8,128)(2,1)}) fusion(bf16[128,1024]{1,0:T(8,128)(2,1)S(1)} %get-tuple-element.93, f32[128,1024]{1,0:T(8,128)S(1)} %get-tuple-element.94, bf16[128,1024]{1,0:T(8,128)(2,1)S(1)} %copy-done.1, bf16[128,1024]{1,0:T(8,128)(2,1)S(1)} %copy-done.2), kind=kLoop, calls=%fused_computation.96 | loop fusion | flops 1048576 | bytes 1835008 | tf_op jit(solution)/shard_map/stack | solution.py:215
  23.8 0.1 fusion.35
  23.9 1.8 %collective-permute-start.3 = (bf16[2,128,128]{2,1,0:T(8,128)(2,1)S(1)}, bf16[2,128,128]{2,1,0:T(8,128)(2,1)S(1)}, u32[]{:S(2)}, u32[]{:S(2)}) collective-permute-start(bf16[2,128,128]{2,1,0:T(8,128)(2,1)S(1)} %get-tuple-element.64), channel_id=1, source_target_pairs={{0,4},{4,8},{8,12},{12,16},{16,20},{20,24},{24,28},{28,0},{1,5},{5... | collective-permute-start | bytes 196616 | tf_op jit(solution)/shard_map/ppermute | solution.py:176
  25.8 1.4 %collective-permute-start.4 = (bf16[2,128,128]{2,1,0:T(8,128)(2,1)S(1)}, bf16[2,128,128]{2,1,0:T(8,128)(2,1)S(1)}, u32[]{:S(2)}, u32[]{:S(2)}) collective-permute-start(bf16[2,128,128]{2,1,0:T(8,128)(2,1)S(1)} %get-tuple-element.65), channel_id=1, source_target_pairs={{0,8},{4,12},{8,16},{12,20},{16,24},{20,28},{24,0},{28,4},{1,9},{5... | collective-permute-start | bytes 196616 | tf_op jit(solution)/shard_map/ppermute | solution.py:176
  27.1 1.4 %collective-permute-start.6 = (bf16[2,128,128]{2,1,0:T(8,128)(2,1)S(1)}, bf16[2,128,128]{2,1,0:T(8,128)(2,1)S(1)}, u32[]{:S(2)}, u32[]{:S(2)}) collective-permute-start(bf16[2,128,128]{2,1,0:T(8,128)(2,1)S(1)} %get-tuple-element.67), channel_id=1, source_target_pairs={{0,16},{4,20},{8,24},{12,28},{16,0},{20,4},{24,8},{28,12},{1,17},{... | collective-permute-start | bytes 196616 | tf_op jit(solution)/shard_map/ppermute | solution.py:176
  28.5 1.6 %collective-permute-start.7 = (bf16[2,128,128]{2,1,0:T(8,128)(2,1)S(1)}, bf16[2,128,128]{2,1,0:T(8,128)(2,1)S(1)}, u32[]{:S(2)}, u32[]{:S(2)}) collective-permute-start(bf16[2,128,128]{2,1,0:T(8,128)(2,1)S(1)} %get-tuple-element.68), channel_id=1, source_target_pairs={{0,20},{4,24},{8,28},{12,0},{16,4},{20,8},{24,12},{28,16},{1,21},{... | collective-permute-start | bytes 196616 | tf_op jit(solution)/shard_map/ppermute | solution.py:176
  30.1 1.2 %collective-permute-start.8 = (bf16[2,128,128]{2,1,0:T(8,128)(2,1)S(1)}, bf16[2,128,128]{2,1,0:T(8,128)(2,1)S(1)}, u32[]{:S(2)}, u32[]{:S(2)}) collective-permute-start(bf16[2,128,128]{2,1,0:T(8,128)(2,1)S(1)} %fusion.42), channel_id=1, source_target_pairs={{0,24},{4,28},{8,0},{12,4},{16,8},{20,12},{24,16},{28,20},{1,25},{... | collective-permute-start | bytes 196616 | tf_op jit(solution)/shard_map/ppermute | solution.py:176
  31.4 0.4 collective-permute-start.9
  31.8 5.1 %collective-permute-done.5 = bf16[2,128,128]{2,1,0:T(8,128)(2,1)S(1)} collective-permute-done((bf16[2,128,128]{2,1,0:T(8,128)(2,1)S(1)}, bf16[2,128,128]{2,1,0:T(8,128)(2,1)S(1)}, u32[]{:S(2)}, u32[]{:S(2)}) %collective-permute-start.5) | collective-permute-done | bytes 65568 | tf_op jit(solution)/shard_map/ppermute | solution.py:176
  36.9 1.4 %collective-permute-done.6 = bf16[2,128,128]{2,1,0:T(8,128)(2,1)S(1)} collective-permute-done((bf16[2,128,128]{2,1,0:T(8,128)(2,1)S(1)}, bf16[2,128,128]{2,1,0:T(8,128)(2,1)S(1)}, u32[]{:S(2)}, u32[]{:S(2)}) %collective-permute-start.6) | collective-permute-done | bytes 65568 | tf_op jit(solution)/shard_map/ppermute | solution.py:176
  38.3 1.3 %collective-permute-done.8 = bf16[2,128,128]{2,1,0:T(8,128)(2,1)S(1)} collective-permute-done((bf16[2,128,128]{2,1,0:T(8,128)(2,1)S(1)}, bf16[2,128,128]{2,1,0:T(8,128)(2,1)S(1)}, u32[]{:S(2)}, u32[]{:S(2)}) %collective-permute-start.8) | collective-permute-done | bytes 65568 | tf_op jit(solution)/shard_map/ppermute | solution.py:176
  39.6 0.5 collective-permute-done.9
  40.5 0.1 pad_maximum_fusion.3
  40.6 0.1 pad_maximum_fusion.2
  40.7 0.6 copy-done.6
  41.3 0.7 convolution_bitcast_fusion
  42.1 0.1 copy-done.5
  42.2 0.6 convolution_bitcast_fusion.1
  42.8 0.6 slice_add_fusion.3
  43.4 0.1 fusion.47
  43.5 0.2 fusion.15
  43.8 0.4 add_add_fusion.2
  44.2 0.4 subtract_add_fusion.1
  44.6 0.1 slice_bitcast_fusion.18
  44.8 0.4 add_add_fusion.1
  45.2 0.4 subtract_add_fusion
  45.6 0.2 fusion.53
  46.1 0.1 pad_maximum_fusion
  46.2 0.1 bitcast_convert_fusion
  46.3 0.3 fusion
  46.7 0.6 copy-done
  47.2 0.5 fusion.51
  47.7 0.5 fusion.52
  48.2 0.4 copy-done.4
  48.6 0.5 add_add_fusion
  49.1 0.2 copy-done.7
  49.3 0.3 multiply_add_fusion
  49.8 0.1 fusion.13
  50.1 1.3 %collective-permute-start.15 = (f32[2,128,128]{1,2,0:T(8,128)S(1)}, f32[2,128,128]{1,2,0:T(8,128)S(1)}, u32[]{:S(2)}, u32[]{:S(2)}) collective-permute-start(f32[2,128,128]{1,2,0:T(8,128)S(1)} %fusion.34), channel_id=1, source_target_pairs={{0,24},{4,28},{8,0},{12,4},{16,8},{20,12},{24,16},{28,20},{1,25},{... | collective-permute-start | bytes 393224 | tf_op jit(solution)/shard_map/ppermute | solution.py:195
  51.3 0.3 collective-permute-start.11
  51.7 3.8 %collective-permute-start.12 = (f32[2,128,128]{1,2,0:T(8,128)S(1)}, f32[2,128,128]{1,2,0:T(8,128)S(1)}, u32[]{:S(2)}, u32[]{:S(2)}) collective-permute-start(f32[2,128,128]{1,2,0:T(8,128)S(1)} %get-tuple-element.18), channel_id=1, source_target_pairs={{0,12},{4,16},{8,20},{12,24},{16,28},{20,0},{24,4},{28,8},{1,13},{... | collective-permute-start | bytes 393224 | tf_op jit(solution)/shard_map/ppermute | solution.py:195
  55.5 1.7 %collective-permute-start.14 = (f32[2,128,128]{1,2,0:T(8,128)S(1)}, f32[2,128,128]{1,2,0:T(8,128)S(1)}, u32[]{:S(2)}, u32[]{:S(2)}) collective-permute-start(f32[2,128,128]{1,2,0:T(8,128)S(1)} %get-tuple-element.20), channel_id=1, source_target_pairs={{0,20},{4,24},{8,28},{12,0},{16,4},{20,8},{24,12},{28,16},{1,21},{... | collective-permute-start | bytes 393224 | tf_op jit(solution)/shard_map/ppermute | solution.py:195
  57.2 2.3 %collective-permute-done.11 = f32[2,128,128]{1,2,0:T(8,128)S(1)} collective-permute-done((f32[2,128,128]{1,2,0:T(8,128)S(1)}, f32[2,128,128]{1,2,0:T(8,128)S(1)}, u32[]{:S(2)}, u32[]{:S(2)}) %collective-permute-start.11) | collective-permute-done | bytes 131104 | tf_op jit(solution)/shard_map/ppermute | solution.py:195
  59.5 1.1 %collective-permute-start.16 = (f32[2,128,128]{1,2,0:T(8,128)S(1)}, f32[2,128,128]{1,2,0:T(8,128)S(1)}, u32[]{:S(2)}, u32[]{:S(2)}) collective-permute-start(f32[2,128,128]{1,2,0:T(8,128)S(1)} %get-tuple-element.15), channel_id=1, source_target_pairs={{0,28},{4,0},{8,4},{12,8},{16,12},{20,16},{24,20},{28,24},{1,29},{... | collective-permute-start | bytes 393224 | tf_op jit(solution)/shard_map/ppermute | solution.py:195
  60.6 2.4 %collective-permute-done.12 = f32[2,128,128]{1,2,0:T(8,128)S(1)} collective-permute-done((f32[2,128,128]{1,2,0:T(8,128)S(1)}, f32[2,128,128]{1,2,0:T(8,128)S(1)}, u32[]{:S(2)}, u32[]{:S(2)}) %collective-permute-start.12) | collective-permute-done | bytes 131104 | tf_op jit(solution)/shard_map/ppermute | solution.py:195
  63.0 7.6 %collective-permute-done.13 = f32[2,128,128]{1,2,0:T(8,128)S(1)} collective-permute-done((f32[2,128,128]{1,2,0:T(8,128)S(1)}, f32[2,128,128]{1,2,0:T(8,128)S(1)}, u32[]{:S(2)}, u32[]{:S(2)}) %collective-permute-start.13) | collective-permute-done | bytes 131104 | tf_op jit(solution)/shard_map/ppermute | solution.py:195
  70.7 4.4 %collective-permute-done.16 = f32[2,128,128]{1,2,0:T(8,128)S(1)} collective-permute-done((f32[2,128,128]{1,2,0:T(8,128)S(1)}, f32[2,128,128]{1,2,0:T(8,128)S(1)}, u32[]{:S(2)}, u32[]{:S(2)}) %collective-permute-start.16) | collective-permute-done | bytes 131104 | tf_op jit(solution)/shard_map/ppermute | solution.py:195
  75.2 0.1 fusion.9
  75.3 1.0 %copy.57 = f32[128,1024]{1,0:T(8,128)} copy(f32[128,1024]{0,1:T(8,128)S(1)} %slice_bitcast_fusion.1) | data formatting | bytes 1048576
  76.3 0.8 %copy.55 = bf16[128,1024]{1,0:T(8,128)(2,1)} copy(bf16[128,1024]{0,1:T(8,128)(2,1)S(1)} %get-tuple-element.14) | data formatting | bytes 524288
  77.1 0.8 %copy.56 = bf16[128,1024]{1,0:T(8,128)(2,1)} copy(bf16[128,1024]{0,1:T(8,128)(2,1)S(1)} %get-tuple-element.13) | data formatting | bytes 524288
  (70 shorter events, 1.3 us)
Async XLA Ops:
  0.6 14.7 %collective-permute-start = (bf16[128,1024]{1,0:T(8,128)(2,1)}, bf16[128,1024]{1,0:T(8,128)(2,1)S(1)}, u32[]{:S(2)}, u32[]{:S(2)}) collective-permute-start(bf16[128,1024]{1,0:T(8,128)(2,1)} %param.17), channel_id=1, source_target_pairs={{0,1},{1,2},{2,3},{3,0},{4,5},{5,6},{6,7},{7,4},{8,9},{9,10},{10,1... | collective-permute-start | bytes 786440 | tf_op jit(solution)/shard_map/ppermute | solution.py:25
  1.9 13.7 %collective-permute-start.1 = (bf16[128,1024]{1,0:T(8,128)(2,1)}, bf16[128,1024]{1,0:T(8,128)(2,1)S(1)}, u32[]{:S(2)}, u32[]{:S(2)}) collective-permute-start(bf16[128,1024]{1,0:T(8,128)(2,1)} %param.17), channel_id=1, source_target_pairs={{0,2},{1,3},{2,0},{3,1},{4,6},{5,7},{6,4},{7,5},{8,10},{9,11},{10,... | collective-permute-start | bytes 786440 | tf_op jit(solution)/shard_map/ppermute | solution.py:25
  3.1 12.5 %collective-permute-start.2 = (bf16[128,1024]{1,0:T(8,128)(2,1)}, bf16[128,1024]{1,0:T(8,128)(2,1)S(1)}, u32[]{:S(2)}, u32[]{:S(2)}) collective-permute-start(bf16[128,1024]{1,0:T(8,128)(2,1)} %param.17), channel_id=1, source_target_pairs={{0,3},{1,0},{2,1},{3,2},{4,7},{5,4},{6,5},{7,6},{8,11},{9,8},{10,9... | collective-permute-start | bytes 786440 | tf_op jit(solution)/shard_map/ppermute | solution.py:25
  6.6 9.0 %copy-start.3 = (bf16[128,1024]{1,0:T(8,128)(2,1)S(1)}, bf16[128,1024]{1,0:T(8,128)(2,1)}, u32[]{:S(2)}) copy-start(bf16[128,1024]{1,0:T(8,128)(2,1)} %param.17) | copy-start | bytes 786436
  8.9 31.6 %all-to-all-start = ((bf16[8,2,128,128]{3,2,1,0:T(8,128)(2,1)}), bf16[8,2,128,128]{3,2,1,0:T(8,128)(2,1)S(1)}, u32[]{:S(2)}, u32[]{:S(2)}) async-start(bf16[8,2,128,128]{3,2,1,0:T(8,128)(2,1)} %copy.52), calls=%async_computation | async-start | bytes 1048576 | tf_op jit(solution)/shard_map/all_to_all | solution.py:147
  15.6 1.0 %copy-start.1 = (bf16[128,1024]{1,0:T(8,128)(2,1)S(1)}, bf16[128,1024]{1,0:T(8,128)(2,1)}, u32[]{:S(2)}) copy-start(bf16[128,1024]{1,0:T(8,128)(2,1)} %param.13) | copy-start | bytes 786436
  16.6 6.3 %copy-start.2 = (bf16[128,1024]{1,0:T(8,128)(2,1)S(1)}, bf16[128,1024]{1,0:T(8,128)(2,1)}, u32[]{:S(2)}) copy-start(bf16[128,1024]{1,0:T(8,128)(2,1)} %param.16) | copy-start | bytes 786436
  23.9 6.2 %collective-permute-start.3 = (bf16[2,128,128]{2,1,0:T(8,128)(2,1)S(1)}, bf16[2,128,128]{2,1,0:T(8,128)(2,1)S(1)}, u32[]{:S(2)}, u32[]{:S(2)}) collective-permute-start(bf16[2,128,128]{2,1,0:T(8,128)(2,1)S(1)} %get-tuple-element.64), channel_id=1, source_target_pairs={{0,4},{4,8},{8,12},{12,16},{16,20},{20,24},{24,28},{28,0},{1,5},{5... | collective-permute-start | bytes 196616 | tf_op jit(solution)/shard_map/ppermute | solution.py:176
  25.8 5.6 %collective-permute-start.4 = (bf16[2,128,128]{2,1,0:T(8,128)(2,1)S(1)}, bf16[2,128,128]{2,1,0:T(8,128)(2,1)S(1)}, u32[]{:S(2)}, u32[]{:S(2)}) collective-permute-start(bf16[2,128,128]{2,1,0:T(8,128)(2,1)S(1)} %get-tuple-element.65), channel_id=1, source_target_pairs={{0,8},{4,12},{8,16},{12,20},{16,24},{20,28},{24,0},{28,4},{1,9},{5... | collective-permute-start | bytes 196616 | tf_op jit(solution)/shard_map/ppermute | solution.py:176
  27.1 9.8 %collective-permute-start.5 = (bf16[2,128,128]{2,1,0:T(8,128)(2,1)S(1)}, bf16[2,128,128]{2,1,0:T(8,128)(2,1)S(1)}, u32[]{:S(2)}, u32[]{:S(2)}) collective-permute-start(bf16[2,128,128]{2,1,0:T(8,128)(2,1)S(1)} %get-tuple-element.66), channel_id=1, source_target_pairs={{0,12},{4,16},{8,20},{12,24},{16,28},{20,0},{24,4},{28,8},{1,13},{... | collective-permute-start | bytes 196616 | tf_op jit(solution)/shard_map/ppermute | solution.py:176
  27.1 11.2 %collective-permute-start.6 = (bf16[2,128,128]{2,1,0:T(8,128)(2,1)S(1)}, bf16[2,128,128]{2,1,0:T(8,128)(2,1)S(1)}, u32[]{:S(2)}, u32[]{:S(2)}) collective-permute-start(bf16[2,128,128]{2,1,0:T(8,128)(2,1)S(1)} %get-tuple-element.67), channel_id=1, source_target_pairs={{0,16},{4,20},{8,24},{12,28},{16,0},{20,4},{24,8},{28,12},{1,17},{... | collective-permute-start | bytes 196616 | tf_op jit(solution)/shard_map/ppermute | solution.py:176
  28.5 9.8 %collective-permute-start.7 = (bf16[2,128,128]{2,1,0:T(8,128)(2,1)S(1)}, bf16[2,128,128]{2,1,0:T(8,128)(2,1)S(1)}, u32[]{:S(2)}, u32[]{:S(2)}) collective-permute-start(bf16[2,128,128]{2,1,0:T(8,128)(2,1)S(1)} %get-tuple-element.68), channel_id=1, source_target_pairs={{0,20},{4,24},{8,28},{12,0},{16,4},{20,8},{24,12},{28,16},{1,21},{... | collective-permute-start | bytes 196616 | tf_op jit(solution)/shard_map/ppermute | solution.py:176
  30.1 9.5 %collective-permute-start.8 = (bf16[2,128,128]{2,1,0:T(8,128)(2,1)S(1)}, bf16[2,128,128]{2,1,0:T(8,128)(2,1)S(1)}, u32[]{:S(2)}, u32[]{:S(2)}) collective-permute-start(bf16[2,128,128]{2,1,0:T(8,128)(2,1)S(1)} %fusion.42), channel_id=1, source_target_pairs={{0,24},{4,28},{8,0},{12,4},{16,8},{20,12},{24,16},{28,20},{1,25},{... | collective-permute-start | bytes 196616 | tf_op jit(solution)/shard_map/ppermute | solution.py:176
  31.4 8.8 %collective-permute-start.9 = (bf16[2,128,128]{2,1,0:T(8,128)(2,1)S(1)}, bf16[2,128,128]{2,1,0:T(8,128)(2,1)S(1)}, u32[]{:S(2)}, u32[]{:S(2)}) collective-permute-start(bf16[2,128,128]{2,1,0:T(8,128)(2,1)S(1)} %get-tuple-element.63), channel_id=1, source_target_pairs={{0,28},{4,0},{8,4},{12,8},{16,12},{20,16},{24,20},{28,24},{1,29},{... | collective-permute-start | bytes 196616 | tf_op jit(solution)/shard_map/ppermute | solution.py:176
  40.5 0.8 %copy-start.6 = (bf16[256,128,1]{1,0,2:T(8,128)(2,1)S(1)}, bf16[256,128,1]{1,0,2:T(8,128)(2,1)}, u32[]{:S(2)}) copy-start(bf16[256,128,1]{1,0,2:T(8,128)(2,1)} %constant.266) | copy-start | bytes 196612
  41.3 0.8 %copy-start.5 = (bf16[256,128,1]{1,0,2:T(8,128)(2,1)S(1)}, bf16[256,128,1]{1,0,2:T(8,128)(2,1)}, u32[]{:S(2)}) copy-start(bf16[256,128,1]{1,0,2:T(8,128)(2,1)} %constant.267) | copy-start | bytes 196612
  44.8 0.8 %copy-start.8 = (bf16[128,1,1]{0,1,2:T(2,128)(2,1)S(1)}, bf16[128,1,1]{0,1,2:T(2,128)(2,1)}, u32[]{:S(2)}) copy-start(bf16[128,1,1]{0,1,2:T(2,128)(2,1)} %constant.270) | copy-start | bytes 772
  46.3 0.9 %copy-start = (bf16[256,256,1]{1,0,2:T(8,128)(2,1)S(1)}, bf16[256,256,1]{1,0,2:T(8,128)(2,1)}, u32[]{:S(2)}) copy-start(bf16[256,256,1]{1,0,2:T(8,128)(2,1)} %constant.268) | copy-start | bytes 393220
  47.7 0.9 %copy-start.4 = (bf16[256,256,1]{1,0,2:T(8,128)(2,1)S(1)}, bf16[256,256,1]{1,0,2:T(8,128)(2,1)}, u32[]{:S(2)}) copy-start(bf16[256,256,1]{1,0,2:T(8,128)(2,1)} %constant.269) | copy-start | bytes 393220
  48.6 0.7 copy-start.7
  50.0 5.5 %collective-permute-start.10 = (f32[2,128,128]{1,2,0:T(8,128)S(1)}, f32[2,128,128]{1,2,0:T(8,128)S(1)}, u32[]{:S(2)}, u32[]{:S(2)}) collective-permute-start(f32[2,128,128]{1,2,0:T(8,128)S(1)} %get-tuple-element.16), channel_id=1, source_target_pairs={{0,4},{4,8},{8,12},{12,16},{16,20},{20,24},{24,28},{28,0},{1,5},{5... | collective-permute-start | bytes 393224 | tf_op jit(solution)/shard_map/ppermute | solution.py:195
  50.1 20.6 %collective-permute-start.15 = (f32[2,128,128]{1,2,0:T(8,128)S(1)}, f32[2,128,128]{1,2,0:T(8,128)S(1)}, u32[]{:S(2)}, u32[]{:S(2)}) collective-permute-start(f32[2,128,128]{1,2,0:T(8,128)S(1)} %fusion.34), channel_id=1, source_target_pairs={{0,24},{4,28},{8,0},{12,4},{16,8},{20,12},{24,16},{28,20},{1,25},{... | collective-permute-start | bytes 393224 | tf_op jit(solution)/shard_map/ppermute | solution.py:195
  51.3 8.2 %collective-permute-start.11 = (f32[2,128,128]{1,2,0:T(8,128)S(1)}, f32[2,128,128]{1,2,0:T(8,128)S(1)}, u32[]{:S(2)}, u32[]{:S(2)}) collective-permute-start(f32[2,128,128]{1,2,0:T(8,128)S(1)} %get-tuple-element.17), channel_id=1, source_target_pairs={{0,8},{4,12},{8,16},{12,20},{16,24},{20,28},{24,0},{28,4},{1,9},{5... | collective-permute-start | bytes 393224 | tf_op jit(solution)/shard_map/ppermute | solution.py:195
  51.7 11.3 %collective-permute-start.12 = (f32[2,128,128]{1,2,0:T(8,128)S(1)}, f32[2,128,128]{1,2,0:T(8,128)S(1)}, u32[]{:S(2)}, u32[]{:S(2)}) collective-permute-start(f32[2,128,128]{1,2,0:T(8,128)S(1)} %get-tuple-element.18), channel_id=1, source_target_pairs={{0,12},{4,16},{8,20},{12,24},{16,28},{20,0},{24,4},{28,8},{1,13},{... | collective-permute-start | bytes 393224 | tf_op jit(solution)/shard_map/ppermute | solution.py:195
  55.5 15.1 %collective-permute-start.13 = (f32[2,128,128]{1,2,0:T(8,128)S(1)}, f32[2,128,128]{1,2,0:T(8,128)S(1)}, u32[]{:S(2)}, u32[]{:S(2)}) collective-permute-start(f32[2,128,128]{1,2,0:T(8,128)S(1)} %get-tuple-element.19), channel_id=1, source_target_pairs={{0,16},{4,20},{8,24},{12,28},{16,0},{20,4},{24,8},{28,12},{1,17},{... | collective-permute-start | bytes 393224 | tf_op jit(solution)/shard_map/ppermute | solution.py:195
  55.5 15.1 %collective-permute-start.14 = (f32[2,128,128]{1,2,0:T(8,128)S(1)}, f32[2,128,128]{1,2,0:T(8,128)S(1)}, u32[]{:S(2)}, u32[]{:S(2)}) collective-permute-start(f32[2,128,128]{1,2,0:T(8,128)S(1)} %get-tuple-element.20), channel_id=1, source_target_pairs={{0,20},{4,24},{8,28},{12,0},{16,4},{20,8},{24,12},{28,16},{1,21},{... | collective-permute-start | bytes 393224 | tf_op jit(solution)/shard_map/ppermute | solution.py:195
  59.5 15.6 %collective-permute-start.16 = (f32[2,128,128]{1,2,0:T(8,128)S(1)}, f32[2,128,128]{1,2,0:T(8,128)S(1)}, u32[]{:S(2)}, u32[]{:S(2)}) collective-permute-start(f32[2,128,128]{1,2,0:T(8,128)S(1)} %get-tuple-element.15), channel_id=1, source_target_pairs={{0,28},{4,0},{8,4},{12,8},{16,12},{20,16},{24,20},{28,24},{1,29},{... | collective-permute-start | bytes 393224 | tf_op jit(solution)/shard_map/ppermute | solution.py:195

commit v14 on v13

--- a/solution.py
+++ b/solution.py
@@ -187,16 +187,18 @@
 def gather_lanes(value, chans):
     count = lax.axis_size("ctx")
     me = lax.axis_index("ctx")
-    sub = value.shape[-1]
-    result = jnp.zeros(value.shape[1:-1] + (chans,), value.dtype)
+    parts, rows, sub = value.shape[1:]
+    results = [jnp.zeros((rows, chans), value.dtype) for _ in range(parts)]
     for shift in range(count):
         chunk = lax.dynamic_index_in_dim(value, (me + shift) % count, 0, keepdims=False)
         if shift:
             chunk = lax.ppermute(chunk, "ctx", [(i, (i + shift) % count) for i in range(count)])
-        result = lax.dynamic_update_slice_in_dim(
-            result, chunk, ((me - shift) % count) * sub, axis=result.ndim - 1
-        )
-    return result
+        offset = ((me - shift) % count) * sub
+        results = [
+            lax.dynamic_update_slice_in_dim(result, chunk[part], offset, axis=1)
+            for part, result in enumerate(results)
+        ]
+    return results
 
 
 def body(q_proj, k_proj, v_proj, saved_conv, out_grad, out_weight, filter_taps):
@@ -221,11 +223,10 @@
         float(seq) ** -0.5,
     )
     outgoing = jnp.stack([du_t, filter_t]).reshape(2, blocks, rows, sub).transpose(1, 0, 2, 3)
-    back = gather_lanes(outgoing, chans)
-    du_local = back[0]
-    filter_grad = back[1]
-    dk_grad = (du_local * v_proj.astype(jnp.float32)).astype(jnp.bfloat16)
-    dv_grad = (du_local * k_proj.astype(jnp.float32)).astype(jnp.bfloat16)
+    du_local, filter_grad = gather_lanes(outgoing, chans)
+    k_late, v_late = lax.optimization_barrier((k_proj, v_proj))
+    dk_grad = (du_local * v_late.astype(jnp.float32)).astype(jnp.bfloat16)
+    dv_grad = (du_local * k_late.astype(jnp.float32)).astype(jnp.bfloat16)
     return (dq_grad, dk_grad, dv_grad, filter_grad)
 
 

time: 78.4 us -> 76.7 us (0.978)
  starting transfers between devices: 26.1 us -> 23.9 us
  local copies, waits for them, and re-layouts: 10.7 us -> 8.82 us
  waiting for transfers between devices: 25.3 us -> 26.3 us
  other arithmetic: 5.37 us -> 6.19 us
    unnamed x37 -> x40, local copies, waits for them, and re-layouts: 8.91 us -> 6.23 us
    ppermute x7, starting transfers between devices: 8.15 us -> 6.01 us  [gather_lanes(): lax.ppermute(chunk, 'ctx', [(i, (i + shift) % count) for i in range(count)])]
    ppermute x7, waiting for transfers between devices: 16.7 us -> 17.7 us  [gather_lanes(): lax.ppermute(chunk, 'ctx', [(i, (i + shift) % count) for i in range(count)])]
    another operation x0 -> x10, local copies, waits for them, and re-layouts: none -> 0.84 us
    convert_element_type x1, other arithmetic: 0.11 us -> 0.93 us  [body(): dv_grad = (du_local * k_late.astype(jnp.float32)).astype(jnp.bfloat16)]
  transfers between devices with their start and end apart: 18 -> 18, of which waited for: 9 -> 11; matrix products, arithmetic and copies ran while one was open for 16% -> 18% of each run, Pallas kernels for 0% -> 0%
where the time goes in v14:
time: 76.7 us; the launch traced here: 75.8 us
  waiting for transfers between devices  26.3 us (34%)
  starting transfers between devices  23.9 us (31%)
  matrix products  9.28 us (12%)
  local copies, waits for them, and re-layouts  8.82 us (11%)
  other arithmetic  6.19 us (8%)
  between operations  1.26 us (2%)
    ppermute x7, waiting for transfers between devices, gather_lanes(): lax.ppermute(chunk, 'ctx', [(i, (i + shift) % count) for i in range(count)])  17.7 us
    ppermute x7, waiting for transfers between devices, scatter_lanes(): lax.ppermute(chunk, 'ctx', [(i, (i + shift) % count) for i in range(count)])  8.29 us
    ppermute x7, starting transfers between devices, scatter_lanes(): lax.ppermute(chunk, 'ctx', [(i, (i + shift) % count) for i in range(count)])  7.81 us
    all_to_all x1, starting transfers between devices, all_to_all_ctx(): return lax.all_to_all(stacked, 'ctx', 0, 0, tiled=True)  6.44 us
    dot_general x1, matrix products, gather_matmul(): lax.dot_general(gathered, out_weight, (((1,), (1,)), ((), ())), preferred...  6.3 us
    unnamed x40, local copies, waits for them, and re-layouts  6.23 us
    ppermute x7, starting transfers between devices, gather_lanes(): lax.ppermute(chunk, 'ctx', [(i, (i + shift) % count) for i in range(count)])  6.01 us
    ppermute x3, starting transfers between devices, gather_matmul(): lax.ppermute(out_grad, 'tp', [(i, (i + shift) % count) for i in range(cou...  3.66 us
  transfers between devices with their start and end apart: 18, of which 11 were waited for; matrix products, arithmetic and copies ran while one was open for 18% of the time, Pallas kernels for 0%

profile of v14, /device:TPU:9, one launch (start us, length us, event | category | flops | bytes accessed | tf_op | source)
XLA Modules:
  0.0 75.8 jit_solution(13385491834731737220)
XLA Ops:
  0.6 1.3 %collective-permute-start = (bf16[128,1024]{1,0:T(8,128)(2,1)}, bf16[128,1024]{1,0:T(8,128)(2,1)S(1)}, u32[]{:S(2)}, u32[]{:S(2)}) collective-permute-start(bf16[128,1024]{1,0:T(8,128)(2,1)} %param.17), channel_id=1, source_target_pairs={{0,1},{1,2},{2,3},{3,0},{4,5},{5,6},{6,7},{7,4},{8,9},{9,10},{10,1... | collective-permute-start | bytes 786440 | tf_op jit(solution)/shard_map/ppermute | solution.py:25
  1.9 1.2 %collective-permute-start.1 = (bf16[128,1024]{1,0:T(8,128)(2,1)}, bf16[128,1024]{1,0:T(8,128)(2,1)S(1)}, u32[]{:S(2)}, u32[]{:S(2)}) collective-permute-start(bf16[128,1024]{1,0:T(8,128)(2,1)} %param.17), channel_id=1, source_target_pairs={{0,2},{1,3},{2,0},{3,1},{4,6},{5,7},{6,4},{7,5},{8,10},{9,11},{10,... | collective-permute-start | bytes 786440 | tf_op jit(solution)/shard_map/ppermute | solution.py:25
  3.1 1.2 %collective-permute-start.2 = (bf16[128,1024]{1,0:T(8,128)(2,1)}, bf16[128,1024]{1,0:T(8,128)(2,1)S(1)}, u32[]{:S(2)}, u32[]{:S(2)}) collective-permute-start(bf16[128,1024]{1,0:T(8,128)(2,1)} %param.17), channel_id=1, source_target_pairs={{0,3},{1,0},{2,1},{3,2},{4,7},{5,4},{6,5},{7,6},{8,11},{9,8},{10,9... | collective-permute-start | bytes 786440 | tf_op jit(solution)/shard_map/ppermute | solution.py:25
  4.3 1.1 %copy.49 = bf16[128,1024]{0,1:T(8,128)(2,1)S(1)} copy(bf16[128,1024]{1,0:T(8,128)(2,1)} %param.14) | data formatting | bytes 524288 | tf_op args[1]
  5.4 1.1 %copy.50 = bf16[128,1024]{0,1:T(8,128)(2,1)S(1)} copy(bf16[128,1024]{1,0:T(8,128)(2,1)} %param.15) | data formatting | bytes 524288 | tf_op args[2]
  6.6 1.2 %copy.51 = bf16[128,1024]{0,1:T(8,128)(2,1)S(1)} copy(bf16[128,1024]{1,0:T(8,128)(2,1)} %param.19) | data formatting | bytes 524288 | tf_op args[6]
  7.9 1.0 %copy.52 = bf16[8,2,128,128]{3,2,1,0:T(8,128)(2,1)} copy(bf16[8,2,128,128]{2,3,0,1:T(8,128)(2,1)S(1)} %pad_maximum_fusion.4) | data formatting | bytes 1048576 | tf_op jit(solution)/shard_map/stack | solution.py:211
  8.9 6.4 %all-to-all-start = ((bf16[8,2,128,128]{3,2,1,0:T(8,128)(2,1)}), bf16[8,2,128,128]{3,2,1,0:T(8,128)(2,1)S(1)}, u32[]{:S(2)}, u32[]{:S(2)}) async-start(bf16[8,2,128,128]{3,2,1,0:T(8,128)(2,1)} %copy.52), calls=%async_computation | async-start | bytes 1048576 | tf_op jit(solution)/shard_map/all_to_all | solution.py:147
  15.3 0.3 collective-permute-done.1
  15.6 0.1 pad_maximum_fusion.1
  15.9 0.7 copy-done.4
  16.6 6.3 %fusion.13 = (bf16[128,1024]{1,0:T(8,128)(2,1)S(1)}, f32[128,1024]{1,0:T(8,128)S(1)}) fusion(bf16[128,1024]{1,0:T(8,128)(2,1)S(1)} %copy-done.4, bf16[1024,4096]{1,0:T(8,128)(2,1)} %param.18, bf16[128,1024]{1,0:T(8,128)(2,1)S(1)} %get-tuple-element.42, bf16[128,1024]{1,0:T(8,128)(2,1)S(1)} %get-tuple-element.43, ...), kind=kOutput, calls=%fused_computation.90 | convolution fusion | flops 1078329344 | bytes 10485760 | tf_op jit(solution)/shard_map/dot_general | solution.py:33
  22.9 0.9 %fusion.14 = (bf16[1,128,1024]{2,1,0:T(8,128)(2,1)S(1)}, bf16[128,1024]{1,0:T(8,128)(2,1)}) fusion(bf16[128,1024]{1,0:T(8,128)(2,1)S(1)} %get-tuple-element.109, f32[128,1024]{1,0:T(8,128)S(1)} %get-tuple-element.110, bf16[128,1024]{1,0:T(8,128)(2,1)S(1)} %copy-done.4, bf16[128,1024]{1,0:T(8,128)(2,1)S(1)} %copy-done.5), kind=kLoop, calls=%fused_computation.91 | loop fusion | flops 1048576 | bytes 1835008 | tf_op jit(solution)/shard_map/stack | solution.py:217
  23.8 0.1 fusion.23
  23.9 1.8 %collective-permute-start.3 = (bf16[2,128,128]{2,1,0:T(8,128)(2,1)S(1)}, bf16[2,128,128]{2,1,0:T(8,128)(2,1)S(1)}, u32[]{:S(2)}, u32[]{:S(2)}) collective-permute-start(bf16[2,128,128]{2,1,0:T(8,128)(2,1)S(1)} %get-tuple-element.66), channel_id=1, source_target_pairs={{0,4},{4,8},{8,12},{12,16},{16,20},{20,24},{24,28},{28,0},{1,5},{5... | collective-permute-start | bytes 196616 | tf_op jit(solution)/shard_map/ppermute | solution.py:176
  25.8 1.4 %collective-permute-start.4 = (bf16[2,128,128]{2,1,0:T(8,128)(2,1)S(1)}, bf16[2,128,128]{2,1,0:T(8,128)(2,1)S(1)}, u32[]{:S(2)}, u32[]{:S(2)}) collective-permute-start(bf16[2,128,128]{2,1,0:T(8,128)(2,1)S(1)} %get-tuple-element.67), channel_id=1, source_target_pairs={{0,8},{4,12},{8,16},{12,20},{16,24},{20,28},{24,0},{28,4},{1,9},{5... | collective-permute-start | bytes 196616 | tf_op jit(solution)/shard_map/ppermute | solution.py:176
  27.1 1.4 %collective-permute-start.6 = (bf16[2,128,128]{2,1,0:T(8,128)(2,1)S(1)}, bf16[2,128,128]{2,1,0:T(8,128)(2,1)S(1)}, u32[]{:S(2)}, u32[]{:S(2)}) collective-permute-start(bf16[2,128,128]{2,1,0:T(8,128)(2,1)S(1)} %get-tuple-element.69), channel_id=1, source_target_pairs={{0,16},{4,20},{8,24},{12,28},{16,0},{20,4},{24,8},{28,12},{1,17},{... | collective-permute-start | bytes 196616 | tf_op jit(solution)/shard_map/ppermute | solution.py:176
  28.5 1.6 %collective-permute-start.7 = (bf16[2,128,128]{2,1,0:T(8,128)(2,1)S(1)}, bf16[2,128,128]{2,1,0:T(8,128)(2,1)S(1)}, u32[]{:S(2)}, u32[]{:S(2)}) collective-permute-start(bf16[2,128,128]{2,1,0:T(8,128)(2,1)S(1)} %get-tuple-element.70), channel_id=1, source_target_pairs={{0,20},{4,24},{8,28},{12,0},{16,4},{20,8},{24,12},{28,16},{1,21},{... | collective-permute-start | bytes 196616 | tf_op jit(solution)/shard_map/ppermute | solution.py:176
  30.1 1.2 %collective-permute-start.8 = (bf16[2,128,128]{2,1,0:T(8,128)(2,1)S(1)}, bf16[2,128,128]{2,1,0:T(8,128)(2,1)S(1)}, u32[]{:S(2)}, u32[]{:S(2)}) collective-permute-start(bf16[2,128,128]{2,1,0:T(8,128)(2,1)S(1)} %fusion.30), channel_id=1, source_target_pairs={{0,24},{4,28},{8,0},{12,4},{16,8},{20,12},{24,16},{28,20},{1,25},{... | collective-permute-start | bytes 196616 | tf_op jit(solution)/shard_map/ppermute | solution.py:176
  31.4 0.4 collective-permute-start.9
  31.8 5.1 %collective-permute-done.5 = bf16[2,128,128]{2,1,0:T(8,128)(2,1)S(1)} collective-permute-done((bf16[2,128,128]{2,1,0:T(8,128)(2,1)S(1)}, bf16[2,128,128]{2,1,0:T(8,128)(2,1)S(1)}, u32[]{:S(2)}, u32[]{:S(2)}) %collective-permute-start.5) | collective-permute-done | bytes 65568 | tf_op jit(solution)/shard_map/ppermute | solution.py:176
  36.9 1.4 %collective-permute-done.6 = bf16[2,128,128]{2,1,0:T(8,128)(2,1)S(1)} collective-permute-done((bf16[2,128,128]{2,1,0:T(8,128)(2,1)S(1)}, bf16[2,128,128]{2,1,0:T(8,128)(2,1)S(1)}, u32[]{:S(2)}, u32[]{:S(2)}) %collective-permute-start.6) | collective-permute-done | bytes 65568 | tf_op jit(solution)/shard_map/ppermute | solution.py:176
  38.3 1.3 %collective-permute-done.8 = bf16[2,128,128]{2,1,0:T(8,128)(2,1)S(1)} collective-permute-done((bf16[2,128,128]{2,1,0:T(8,128)(2,1)S(1)}, bf16[2,128,128]{2,1,0:T(8,128)(2,1)S(1)}, u32[]{:S(2)}, u32[]{:S(2)}) %collective-permute-start.8) | collective-permute-done | bytes 65568 | tf_op jit(solution)/shard_map/ppermute | solution.py:176
  39.6 0.5 collective-permute-done.9
  40.6 0.1 pad_maximum_fusion.2
  40.7 0.6 copy-done.9
  41.3 0.7 convolution_bitcast_fusion
  42.1 0.1 copy-done.8
  42.2 0.6 convolution_bitcast_fusion.1
  42.8 0.6 slice_add_fusion.3
  43.5 0.2 fusion.12
  43.8 0.4 add_add_fusion.2
  44.2 0.4 subtract_add_fusion.1
  44.6 0.1 slice_bitcast_fusion.32
  44.8 0.4 add_add_fusion.1
  45.2 0.4 subtract_add_fusion
  45.6 0.2 fusion.57
  46.1 0.1 pad_maximum_fusion
  46.2 0.1 bitcast_convert_fusion
  46.3 0.3 fusion
  46.7 0.6 copy-done.2
  47.2 0.5 fusion.55
  47.7 0.5 fusion.56
  48.2 0.4 copy-done.7
  48.6 0.5 add_add_fusion
  49.1 0.2 copy-done.10
  49.3 0.3 multiply_add_fusion
  49.9 0.1 copy.60
  50.2 0.1 copy.55
  50.3 0.1 copy.56
  50.4 1.1 %collective-permute-start.10 = (f32[2,128,128]{2,1,0:T(8,128)S(1)}, f32[2,128,128]{2,1,0:T(8,128)S(1)}, u32[]{:S(2)}, u32[]{:S(2)}) collective-permute-start(f32[2,128,128]{2,1,0:T(8,128)S(1)} %bitcast.287), channel_id=1, source_target_pairs={{0,4},{4,8},{8,12},{12,16},{16,20},{20,24},{24,28},{28,0},{1,5},{5... | collective-permute-start | bytes 393224 | tf_op jit(solution)/shard_map/ppermute | solution.py:195
  51.5 0.1 copy.57
  51.6 1.9 %collective-permute-start.11 = (f32[2,128,128]{2,1,0:T(8,128)S(1)}, f32[2,128,128]{2,1,0:T(8,128)S(1)}, u32[]{:S(2)}, u32[]{:S(2)}) collective-permute-start(f32[2,128,128]{2,1,0:T(8,128)S(1)} %bitcast.286), channel_id=1, source_target_pairs={{0,8},{4,12},{8,16},{12,20},{16,24},{20,28},{24,0},{28,4},{1,9},{5... | collective-permute-start | bytes 393224 | tf_op jit(solution)/shard_map/ppermute | solution.py:195
  53.6 1.9 %collective-permute-start.12 = (f32[2,128,128]{2,1,0:T(8,128)S(1)}, f32[2,128,128]{2,1,0:T(8,128)S(1)}, u32[]{:S(2)}, u32[]{:S(2)}) collective-permute-start(f32[2,128,128]{2,1,0:T(8,128)S(1)} %bitcast.285), channel_id=1, source_target_pairs={{0,12},{4,16},{8,20},{12,24},{16,28},{20,0},{24,4},{28,8},{1,13},{... | collective-permute-start | bytes 393224 | tf_op jit(solution)/shard_map/ppermute | solution.py:195
  55.5 0.2 collective-permute-start.13
  55.8 0.1 copy.62
  56.1 1.4 %collective-permute-done.10 = f32[2,128,128]{2,1,0:T(8,128)S(1)} collective-permute-done((f32[2,128,128]{2,1,0:T(8,128)S(1)}, f32[2,128,128]{2,1,0:T(8,128)S(1)}, u32[]{:S(2)}, u32[]{:S(2)}) %collective-permute-start.10) | collective-permute-done | bytes 131104 | tf_op jit(solution)/shard_map/ppermute | solution.py:195
  57.5 3.1 %collective-permute-done.11 = f32[2,128,128]{2,1,0:T(8,128)S(1)} collective-permute-done((f32[2,128,128]{2,1,0:T(8,128)S(1)}, f32[2,128,128]{2,1,0:T(8,128)S(1)}, u32[]{:S(2)}, u32[]{:S(2)}) %collective-permute-start.11) | collective-permute-done | bytes 131104 | tf_op jit(solution)/shard_map/ppermute | solution.py:195
  60.6 0.9 %collective-permute-start.16 = (f32[2,128,128]{2,1,0:T(8,128)S(1)}, f32[2,128,128]{2,1,0:T(8,128)S(1)}, u32[]{:S(2)}, u32[]{:S(2)}) collective-permute-start(f32[2,128,128]{2,1,0:T(8,128)S(1)} %bitcast.282), channel_id=1, source_target_pairs={{0,28},{4,0},{8,4},{12,8},{16,12},{20,16},{24,20},{28,24},{1,29},{... | collective-permute-start | bytes 393224 | tf_op jit(solution)/shard_map/ppermute | solution.py:195
  61.6 10.0 %collective-permute-done.12 = f32[2,128,128]{2,1,0:T(8,128)S(1)} collective-permute-done((f32[2,128,128]{2,1,0:T(8,128)S(1)}, f32[2,128,128]{2,1,0:T(8,128)S(1)}, u32[]{:S(2)}, u32[]{:S(2)}) %collective-permute-start.12) | collective-permute-done | bytes 131104 | tf_op jit(solution)/shard_map/ppermute | solution.py:195
  71.6 2.8 %collective-permute-done.13 = f32[2,128,128]{2,1,0:T(8,128)S(1)} collective-permute-done((f32[2,128,128]{2,1,0:T(8,128)S(1)}, f32[2,128,128]{2,1,0:T(8,128)S(1)}, u32[]{:S(2)}, u32[]{:S(2)}) %collective-permute-start.13) | collective-permute-done | bytes 131104 | tf_op jit(solution)/shard_map/ppermute | solution.py:195
  74.4 0.1 collective-permute-done.15
  74.6 0.2 collective-permute-done.16
  74.8 0.9 %multiply_convert_fusion = (bf16[128,1024]{1,0:T(8,128)(2,1)}, bf16[128,1024]{1,0:T(8,128)(2,1)}) fusion(f32[128,1024]{1,0:T(8,128)S(1)} %get-tuple-element.76, bf16[128,1024]{1,0:T(8,128)(2,1)S(1)} %copy-done.1, bf16[128,1024]{1,0:T(8,128)(2,1)S(1)} %copy-done), kind=kLoop, calls=%fused_computation.80 | loop fusion | flops 786432 | bytes 1572864 | tf_op jit(solution)/shard_map/convert_element_type | solution.py:229
  (82 shorter events, 2.0 us)
Async XLA Ops:
  0.6 14.7 %collective-permute-start = (bf16[128,1024]{1,0:T(8,128)(2,1)}, bf16[128,1024]{1,0:T(8,128)(2,1)S(1)}, u32[]{:S(2)}, u32[]{:S(2)}) collective-permute-start(bf16[128,1024]{1,0:T(8,128)(2,1)} %param.17), channel_id=1, source_target_pairs={{0,1},{1,2},{2,3},{3,0},{4,5},{5,6},{6,7},{7,4},{8,9},{9,10},{10,1... | collective-permute-start | bytes 786440 | tf_op jit(solution)/shard_map/ppermute | solution.py:25
  1.9 13.7 %collective-permute-start.1 = (bf16[128,1024]{1,0:T(8,128)(2,1)}, bf16[128,1024]{1,0:T(8,128)(2,1)S(1)}, u32[]{:S(2)}, u32[]{:S(2)}) collective-permute-start(bf16[128,1024]{1,0:T(8,128)(2,1)} %param.17), channel_id=1, source_target_pairs={{0,2},{1,3},{2,0},{3,1},{4,6},{5,7},{6,4},{7,5},{8,10},{9,11},{10,... | collective-permute-start | bytes 786440 | tf_op jit(solution)/shard_map/ppermute | solution.py:25
  3.1 12.5 %collective-permute-start.2 = (bf16[128,1024]{1,0:T(8,128)(2,1)}, bf16[128,1024]{1,0:T(8,128)(2,1)S(1)}, u32[]{:S(2)}, u32[]{:S(2)}) collective-permute-start(bf16[128,1024]{1,0:T(8,128)(2,1)} %param.17), channel_id=1, source_target_pairs={{0,3},{1,0},{2,1},{3,2},{4,7},{5,4},{6,5},{7,6},{8,11},{9,8},{10,9... | collective-permute-start | bytes 786440 | tf_op jit(solution)/shard_map/ppermute | solution.py:25
  6.6 9.0 %copy-start.6 = (bf16[128,1024]{1,0:T(8,128)(2,1)S(1)}, bf16[128,1024]{1,0:T(8,128)(2,1)}, u32[]{:S(2)}) copy-start(bf16[128,1024]{1,0:T(8,128)(2,1)} %param.17) | copy-start | bytes 786436
  8.9 31.6 %all-to-all-start = ((bf16[8,2,128,128]{3,2,1,0:T(8,128)(2,1)}), bf16[8,2,128,128]{3,2,1,0:T(8,128)(2,1)S(1)}, u32[]{:S(2)}, u32[]{:S(2)}) async-start(bf16[8,2,128,128]{3,2,1,0:T(8,128)(2,1)} %copy.52), calls=%async_computation | async-start | bytes 1048576 | tf_op jit(solution)/shard_map/all_to_all | solution.py:147
  15.6 1.0 %copy-start.4 = (bf16[128,1024]{1,0:T(8,128)(2,1)S(1)}, bf16[128,1024]{1,0:T(8,128)(2,1)}, u32[]{:S(2)}) copy-start(bf16[128,1024]{1,0:T(8,128)(2,1)} %param.13) | copy-start | bytes 786436
  16.6 6.3 %copy-start.5 = (bf16[128,1024]{1,0:T(8,128)(2,1)S(1)}, bf16[128,1024]{1,0:T(8,128)(2,1)}, u32[]{:S(2)}) copy-start(bf16[128,1024]{1,0:T(8,128)(2,1)} %param.16) | copy-start | bytes 786436
  23.9 6.2 %collective-permute-start.3 = (bf16[2,128,128]{2,1,0:T(8,128)(2,1)S(1)}, bf16[2,128,128]{2,1,0:T(8,128)(2,1)S(1)}, u32[]{:S(2)}, u32[]{:S(2)}) collective-permute-start(bf16[2,128,128]{2,1,0:T(8,128)(2,1)S(1)} %get-tuple-element.66), channel_id=1, source_target_pairs={{0,4},{4,8},{8,12},{12,16},{16,20},{20,24},{24,28},{28,0},{1,5},{5... | collective-permute-start | bytes 196616 | tf_op jit(solution)/shard_map/ppermute | solution.py:176
  25.8 5.6 %collective-permute-start.4 = (bf16[2,128,128]{2,1,0:T(8,128)(2,1)S(1)}, bf16[2,128,128]{2,1,0:T(8,128)(2,1)S(1)}, u32[]{:S(2)}, u32[]{:S(2)}) collective-permute-start(bf16[2,128,128]{2,1,0:T(8,128)(2,1)S(1)} %get-tuple-element.67), channel_id=1, source_target_pairs={{0,8},{4,12},{8,16},{12,20},{16,24},{20,28},{24,0},{28,4},{1,9},{5... | collective-permute-start | bytes 196616 | tf_op jit(solution)/shard_map/ppermute | solution.py:176
  27.1 9.8 %collective-permute-start.5 = (bf16[2,128,128]{2,1,0:T(8,128)(2,1)S(1)}, bf16[2,128,128]{2,1,0:T(8,128)(2,1)S(1)}, u32[]{:S(2)}, u32[]{:S(2)}) collective-permute-start(bf16[2,128,128]{2,1,0:T(8,128)(2,1)S(1)} %get-tuple-element.68), channel_id=1, source_target_pairs={{0,12},{4,16},{8,20},{12,24},{16,28},{20,0},{24,4},{28,8},{1,13},{... | collective-permute-start | bytes 196616 | tf_op jit(solution)/shard_map/ppermute | solution.py:176
  27.1 11.2 %collective-permute-start.6 = (bf16[2,128,128]{2,1,0:T(8,128)(2,1)S(1)}, bf16[2,128,128]{2,1,0:T(8,128)(2,1)S(1)}, u32[]{:S(2)}, u32[]{:S(2)}) collective-permute-start(bf16[2,128,128]{2,1,0:T(8,128)(2,1)S(1)} %get-tuple-element.69), channel_id=1, source_target_pairs={{0,16},{4,20},{8,24},{12,28},{16,0},{20,4},{24,8},{28,12},{1,17},{... | collective-permute-start | bytes 196616 | tf_op jit(solution)/shard_map/ppermute | solution.py:176
  28.5 9.8 %collective-permute-start.7 = (bf16[2,128,128]{2,1,0:T(8,128)(2,1)S(1)}, bf16[2,128,128]{2,1,0:T(8,128)(2,1)S(1)}, u32[]{:S(2)}, u32[]{:S(2)}) collective-permute-start(bf16[2,128,128]{2,1,0:T(8,128)(2,1)S(1)} %get-tuple-element.70), channel_id=1, source_target_pairs={{0,20},{4,24},{8,28},{12,0},{16,4},{20,8},{24,12},{28,16},{1,21},{... | collective-permute-start | bytes 196616 | tf_op jit(solution)/shard_map/ppermute | solution.py:176
  30.1 9.5 %collective-permute-start.8 = (bf16[2,128,128]{2,1,0:T(8,128)(2,1)S(1)}, bf16[2,128,128]{2,1,0:T(8,128)(2,1)S(1)}, u32[]{:S(2)}, u32[]{:S(2)}) collective-permute-start(bf16[2,128,128]{2,1,0:T(8,128)(2,1)S(1)} %fusion.30), channel_id=1, source_target_pairs={{0,24},{4,28},{8,0},{12,4},{16,8},{20,12},{24,16},{28,20},{1,25},{... | collective-permute-start | bytes 196616 | tf_op jit(solution)/shard_map/ppermute | solution.py:176
  31.4 8.8 %collective-permute-start.9 = (bf16[2,128,128]{2,1,0:T(8,128)(2,1)S(1)}, bf16[2,128,128]{2,1,0:T(8,128)(2,1)S(1)}, u32[]{:S(2)}, u32[]{:S(2)}) collective-permute-start(bf16[2,128,128]{2,1,0:T(8,128)(2,1)S(1)} %get-tuple-element.65), channel_id=1, source_target_pairs={{0,28},{4,0},{8,4},{12,8},{16,12},{20,16},{24,20},{28,24},{1,29},{... | collective-permute-start | bytes 196616 | tf_op jit(solution)/shard_map/ppermute | solution.py:176
  40.5 0.8 %copy-start.9 = (bf16[256,128,1]{1,0,2:T(8,128)(2,1)S(1)}, bf16[256,128,1]{1,0,2:T(8,128)(2,1)}, u32[]{:S(2)}) copy-start(bf16[256,128,1]{1,0,2:T(8,128)(2,1)} %constant.266) | copy-start | bytes 196612
  41.3 0.8 %copy-start.8 = (bf16[256,128,1]{1,0,2:T(8,128)(2,1)S(1)}, bf16[256,128,1]{1,0,2:T(8,128)(2,1)}, u32[]{:S(2)}) copy-start(bf16[256,128,1]{1,0,2:T(8,128)(2,1)} %constant.267) | copy-start | bytes 196612
  44.8 0.8 %copy-start.11 = (bf16[128,1,1]{0,1,2:T(2,128)(2,1)S(1)}, bf16[128,1,1]{0,1,2:T(2,128)(2,1)}, u32[]{:S(2)}) copy-start(bf16[128,1,1]{0,1,2:T(2,128)(2,1)} %constant.270) | copy-start | bytes 772
  46.3 0.9 %copy-start.2 = (bf16[256,256,1]{1,0,2:T(8,128)(2,1)S(1)}, bf16[256,256,1]{1,0,2:T(8,128)(2,1)}, u32[]{:S(2)}) copy-start(bf16[256,256,1]{1,0,2:T(8,128)(2,1)} %constant.268) | copy-start | bytes 393220
  47.7 0.9 %copy-start.7 = (bf16[256,256,1]{1,0,2:T(8,128)(2,1)S(1)}, bf16[256,256,1]{1,0,2:T(8,128)(2,1)}, u32[]{:S(2)}) copy-start(bf16[256,256,1]{1,0,2:T(8,128)(2,1)} %constant.269) | copy-start | bytes 393220
  48.6 0.7 copy-start.10
  50.0 24.4 %collective-permute-start.14 = (f32[2,128,128]{2,1,0:T(8,128)S(1)}, f32[2,128,128]{2,1,0:T(8,128)S(1)}, u32[]{:S(2)}, u32[]{:S(2)}) collective-permute-start(f32[2,128,128]{2,1,0:T(8,128)S(1)} %bitcast.281), channel_id=1, source_target_pairs={{0,20},{4,24},{8,28},{12,0},{16,4},{20,8},{24,12},{28,16},{1,21},{... | collective-permute-start | bytes 393224 | tf_op jit(solution)/shard_map/ppermute | solution.py:195
  50.4 7.2 %collective-permute-start.10 = (f32[2,128,128]{2,1,0:T(8,128)S(1)}, f32[2,128,128]{2,1,0:T(8,128)S(1)}, u32[]{:S(2)}, u32[]{:S(2)}) collective-permute-start(f32[2,128,128]{2,1,0:T(8,128)S(1)} %bitcast.287), channel_id=1, source_target_pairs={{0,4},{4,8},{8,12},{12,16},{16,20},{20,24},{24,28},{28,0},{1,5},{5... | collective-permute-start | bytes 393224 | tf_op jit(solution)/shard_map/ppermute | solution.py:195
  51.6 9.0 %collective-permute-start.11 = (f32[2,128,128]{2,1,0:T(8,128)S(1)}, f32[2,128,128]{2,1,0:T(8,128)S(1)}, u32[]{:S(2)}, u32[]{:S(2)}) collective-permute-start(f32[2,128,128]{2,1,0:T(8,128)S(1)} %bitcast.286), channel_id=1, source_target_pairs={{0,8},{4,12},{8,16},{12,20},{16,24},{20,28},{24,0},{28,4},{1,9},{5... | collective-permute-start | bytes 393224 | tf_op jit(solution)/shard_map/ppermute | solution.py:195
  53.5 21.3 %copy-start = (bf16[128,1024]{1,0:T(8,128)(2,1)S(1)}, bf16[128,1024]{1,0:T(8,128)(2,1)}, u32[]{:S(2)}) copy-start(bf16[128,1024]{1,0:T(8,128)(2,1)} %param.15) | copy-start | bytes 786436
  53.5 21.3 %copy-start.1 = (bf16[128,1024]{1,0:T(8,128)(2,1)S(1)}, bf16[128,1024]{1,0:T(8,128)(2,1)}, u32[]{:S(2)}) copy-start(bf16[128,1024]{1,0:T(8,128)(2,1)} %param.14) | copy-start | bytes 786436
  53.6 18.0 %collective-permute-start.12 = (f32[2,128,128]{2,1,0:T(8,128)S(1)}, f32[2,128,128]{2,1,0:T(8,128)S(1)}, u32[]{:S(2)}, u32[]{:S(2)}) collective-permute-start(f32[2,128,128]{2,1,0:T(8,128)S(1)} %bitcast.285), channel_id=1, source_target_pairs={{0,12},{4,16},{8,20},{12,24},{16,28},{20,0},{24,4},{28,8},{1,13},{... | collective-permute-start | bytes 393224 | tf_op jit(solution)/shard_map/ppermute | solution.py:195
  55.5 18.8 %collective-permute-start.13 = (f32[2,128,128]{2,1,0:T(8,128)S(1)}, f32[2,128,128]{2,1,0:T(8,128)S(1)}, u32[]{:S(2)}, u32[]{:S(2)}) collective-permute-start(f32[2,128,128]{2,1,0:T(8,128)S(1)} %bitcast.284), channel_id=1, source_target_pairs={{0,16},{4,20},{8,24},{12,28},{16,0},{20,4},{24,8},{28,12},{1,17},{... | collective-permute-start | bytes 393224 | tf_op jit(solution)/shard_map/ppermute | solution.py:195
  57.5 17.0 %collective-permute-start.15 = (f32[2,128,128]{2,1,0:T(8,128)S(1)}, f32[2,128,128]{2,1,0:T(8,128)S(1)}, u32[]{:S(2)}, u32[]{:S(2)}) collective-permute-start(f32[2,128,128]{2,1,0:T(8,128)S(1)} %bitcast.283), channel_id=1, source_target_pairs={{0,24},{4,28},{8,0},{12,4},{16,8},{20,12},{24,16},{28,20},{1,25},{... | collective-permute-start | bytes 393224 | tf_op jit(solution)/shard_map/ppermute | solution.py:195
  60.6 14.1 %collective-permute-start.16 = (f32[2,128,128]{2,1,0:T(8,128)S(1)}, f32[2,128,128]{2,1,0:T(8,128)S(1)}, u32[]{:S(2)}, u32[]{:S(2)}) collective-permute-start(f32[2,128,128]{2,1,0:T(8,128)S(1)} %bitcast.282), channel_id=1, source_target_pairs={{0,28},{4,0},{8,4},{12,8},{16,12},{20,16},{24,20},{28,24},{1,29},{... | collective-permute-start | bytes 393224 | tf_op jit(solution)/shard_map/ppermute | solution.py:195
  74.8 1.0 %copy-start.3 = (f32[128,1024]{1,0:T(8,128)}, f32[128,1024]{1,0:T(8,128)S(1)}, u32[]{:S(2)}) copy-start(f32[128,1024]{1,0:T(8,128)S(1)} %get-tuple-element.75) | copy-start | bytes 1572868

commit v15 on v14

--- a/solution.py
+++ b/solution.py
@@ -222,8 +222,12 @@
         inputs_t[:, 1].reshape(seq, sub),
         float(seq) ** -0.5,
     )
-    outgoing = jnp.stack([du_t, filter_t]).reshape(2, blocks, rows, sub).transpose(1, 0, 2, 3)
-    du_local, filter_grad = gather_lanes(outgoing, chans)
+    du_hi, du_lo = split_bf16(du_t)
+    outgoing = jnp.stack([du_hi, du_lo, filter_t.astype(jnp.bfloat16)])
+    outgoing = outgoing.reshape(3, blocks, rows, sub).transpose(1, 0, 2, 3)
+    du_hi, du_lo, filter_low = gather_lanes(outgoing, chans)
+    du_local = du_hi.astype(jnp.float32) + du_lo.astype(jnp.float32)
+    filter_grad = filter_low.astype(jnp.float32)
     k_late, v_late = lax.optimization_barrier((k_proj, v_proj))
     dk_grad = (du_local * v_late.astype(jnp.float32)).astype(jnp.bfloat16)
     dv_grad = (du_local * k_late.astype(jnp.float32)).astype(jnp.bfloat16)

time: 76.7 us -> 75.5 us (0.984)
  waiting for transfers between devices: 26.3 us -> 21.4 us
  other arithmetic: 6.19 us -> 8.73 us
  local copies, waits for them, and re-layouts: 8.82 us -> 9.92 us
    ppermute x7, waiting for transfers between devices: 17.7 us -> 13 us  [gather_lanes(): lax.ppermute(chunk, 'ctx', [(i, (i + shift) % count) for i in range(count)])]
    reshape x0 -> x1, local copies, waits for them, and re-layouts: none -> 1.83 us  [long_correlations(): signal = (table_times(inv_hi, spectra_hi) + table_times(inv_hi, spectra_l...]
    add x1, other arithmetic: 0.34 us -> 1.93 us  [long_correlations(): signal = signal + tables['ialt'][None, None, :, None] * tops[:, :, None, :]]
    convert_element_type x0 -> x2, other arithmetic: none -> 0.92 us  [the longest x1 0.84 us: body(): filter_grad = filter_low.astype(jnp.float32)]
    another operation x10 -> x3, local copies, waits for them, and re-layouts: 0.84 us -> 0.07 us
    unnamed x40 -> x38, local copies, waits for them, and re-layouts: 6.23 us -> 6.08 us
  transfers between devices with their start and end apart: 18 -> 18, of which waited for: 11 -> 9; matrix products, arithmetic and copies ran while one was open for 18% -> 17% of each run, Pallas kernels for 0% -> 0%
where the time goes in v15:
time: 75.5 us; the launch traced here: 75 us
  starting transfers between devices  24.4 us (32%)
  waiting for transfers between devices  21.4 us (28%)
  local copies, waits for them, and re-layouts  9.92 us (13%)
  matrix products  9.26 us (12%)
  other arithmetic  8.73 us (12%)
  between operations  1.24 us (2%)
    ppermute x7, waiting for transfers between devices, gather_lanes(): lax.ppermute(chunk, 'ctx', [(i, (i + shift) % count) for i in range(count)])  13 us
    ppermute x7, waiting for transfers between devices, scatter_lanes(): lax.ppermute(chunk, 'ctx', [(i, (i + shift) % count) for i in range(count)])  8.12 us
    ppermute x7, starting transfers between devices, scatter_lanes(): lax.ppermute(chunk, 'ctx', [(i, (i + shift) % count) for i in range(count)])  7.99 us
    all_to_all x1, starting transfers between devices, all_to_all_ctx(): return lax.all_to_all(stacked, 'ctx', 0, 0, tiled=True)  6.44 us
    ppermute x7, starting transfers between devices, gather_lanes(): lax.ppermute(chunk, 'ctx', [(i, (i + shift) % count) for i in range(count)])  6.35 us
    dot_general x1, matrix products, gather_matmul(): lax.dot_general(gathered, out_weight, (((1,), (1,)), ((), ())), preferred...  6.3 us
    unnamed x38, local copies, waits for them, and re-layouts  6.08 us
    ppermute x3, starting transfers between devices, gather_matmul(): lax.ppermute(out_grad, 'tp', [(i, (i + shift) % count) for i in range(cou...  3.66 us
  transfers between devices with their start and end apart: 18, of which 9 were waited for; matrix products, arithmetic and copies ran while one was open for 17% of the time, Pallas kernels for 0%

profile of v15, /device:TPU:9, one launch (start us, length us, event | category | flops | bytes accessed | tf_op | source)
XLA Modules:
  0.0 75.0 jit_solution(11939140562655327835)
XLA Ops:
  0.6 1.3 %collective-permute-start = (bf16[128,1024]{1,0:T(8,128)(2,1)}, bf16[128,1024]{1,0:T(8,128)(2,1)S(1)}, u32[]{:S(2)}, u32[]{:S(2)}) collective-permute-start(bf16[128,1024]{1,0:T(8,128)(2,1)} %param.17), channel_id=1, source_target_pairs={{0,1},{1,2},{2,3},{3,0},{4,5},{5,6},{6,7},{7,4},{8,9},{9,10},{10,1... | collective-permute-start | bytes 786440 | tf_op jit(solution)/shard_map/ppermute | solution.py:25
  1.9 1.2 %collective-permute-start.1 = (bf16[128,1024]{1,0:T(8,128)(2,1)}, bf16[128,1024]{1,0:T(8,128)(2,1)S(1)}, u32[]{:S(2)}, u32[]{:S(2)}) collective-permute-start(bf16[128,1024]{1,0:T(8,128)(2,1)} %param.17), channel_id=1, source_target_pairs={{0,2},{1,3},{2,0},{3,1},{4,6},{5,7},{6,4},{7,5},{8,10},{9,11},{10,... | collective-permute-start | bytes 786440 | tf_op jit(solution)/shard_map/ppermute | solution.py:25
  3.1 1.2 %collective-permute-start.2 = (bf16[128,1024]{1,0:T(8,128)(2,1)}, bf16[128,1024]{1,0:T(8,128)(2,1)S(1)}, u32[]{:S(2)}, u32[]{:S(2)}) collective-permute-start(bf16[128,1024]{1,0:T(8,128)(2,1)} %param.17), channel_id=1, source_target_pairs={{0,3},{1,0},{2,1},{3,2},{4,7},{5,4},{6,5},{7,6},{8,11},{9,8},{10,9... | collective-permute-start | bytes 786440 | tf_op jit(solution)/shard_map/ppermute | solution.py:25
  4.3 1.1 %copy.35 = bf16[128,1024]{0,1:T(8,128)(2,1)S(1)} copy(bf16[128,1024]{1,0:T(8,128)(2,1)} %param.14) | data formatting | bytes 524288 | tf_op args[1]
  5.4 1.1 %copy.36 = bf16[128,1024]{0,1:T(8,128)(2,1)S(1)} copy(bf16[128,1024]{1,0:T(8,128)(2,1)} %param.15) | data formatting | bytes 524288 | tf_op args[2]
  6.6 1.2 %copy.37 = bf16[128,1024]{0,1:T(8,128)(2,1)S(1)} copy(bf16[128,1024]{1,0:T(8,128)(2,1)} %param.19) | data formatting | bytes 524288 | tf_op args[6]
  7.9 1.0 %copy.38 = bf16[8,2,128,128]{3,2,1,0:T(8,128)(2,1)} copy(bf16[8,2,128,128]{2,3,0,1:T(8,128)(2,1)S(1)} %pad_maximum_fusion.5) | data formatting | bytes 1048576 | tf_op jit(solution)/shard_map/stack | solution.py:211
  8.9 6.4 %all-to-all-start = ((bf16[8,2,128,128]{3,2,1,0:T(8,128)(2,1)}), bf16[8,2,128,128]{3,2,1,0:T(8,128)(2,1)S(1)}, u32[]{:S(2)}, u32[]{:S(2)}) async-start(bf16[8,2,128,128]{3,2,1,0:T(8,128)(2,1)} %copy.38), calls=%async_computation | async-start | bytes 1048576 | tf_op jit(solution)/shard_map/all_to_all | solution.py:147
  15.3 0.3 collective-permute-done.1
  15.6 0.1 pad_maximum_fusion.1
  15.8 0.1 dynamic-slice_bitcast_fusion.3
  15.9 0.7 copy-done.3
  16.6 6.3 %fusion.14 = (bf16[128,1024]{1,0:T(8,128)(2,1)S(1)}, f32[128,1024]{1,0:T(8,128)S(1)}) fusion(bf16[128,1024]{1,0:T(8,128)(2,1)S(1)} %copy-done.3, bf16[1024,4096]{1,0:T(8,128)(2,1)} %param.18, bf16[128,1024]{1,0:T(8,128)(2,1)S(1)} %get-tuple-element.34, bf16[128,1024]{1,0:T(8,128)(2,1)S(1)} %get-tuple-element.35, ...), kind=kOutput, calls=%fused_computation.79 | convolution fusion | flops 1078329344 | bytes 10485760 | tf_op jit(solution)/shard_map/dot_general | solution.py:33
  22.9 0.9 %fusion.15 = (bf16[1,128,1024]{2,1,0:T(8,128)(2,1)S(1)}, bf16[128,1024]{1,0:T(8,128)(2,1)}) fusion(bf16[128,1024]{1,0:T(8,128)(2,1)S(1)} %get-tuple-element.116, f32[128,1024]{1,0:T(8,128)S(1)} %get-tuple-element.117, bf16[128,1024]{1,0:T(8,128)(2,1)S(1)} %copy-done.3, bf16[128,1024]{1,0:T(8,128)(2,1)S(1)} %copy-done.4), kind=kLoop, calls=%fused_computation.80 | loop fusion | flops 1048576 | bytes 1835008 | tf_op jit(solution)/shard_map/stack | solution.py:217
  23.8 0.1 fusion.17
  23.9 1.8 %collective-permute-start.3 = (bf16[2,128,128]{2,1,0:T(8,128)(2,1)S(1)}, bf16[2,128,128]{2,1,0:T(8,128)(2,1)S(1)}, u32[]{:S(2)}, u32[]{:S(2)}) collective-permute-start(bf16[2,128,128]{2,1,0:T(8,128)(2,1)S(1)} %get-tuple-element.66), channel_id=1, source_target_pairs={{0,4},{4,8},{8,12},{12,16},{16,20},{20,24},{24,28},{28,0},{1,5},{5... | collective-permute-start | bytes 196616 | tf_op jit(solution)/shard_map/ppermute | solution.py:176
  25.8 1.4 %collective-permute-start.4 = (bf16[2,128,128]{2,1,0:T(8,128)(2,1)S(1)}, bf16[2,128,128]{2,1,0:T(8,128)(2,1)S(1)}, u32[]{:S(2)}, u32[]{:S(2)}) collective-permute-start(bf16[2,128,128]{2,1,0:T(8,128)(2,1)S(1)} %get-tuple-element.67), channel_id=1, source_target_pairs={{0,8},{4,12},{8,16},{12,20},{16,24},{20,28},{24,0},{28,4},{1,9},{5... | collective-permute-start | bytes 196616 | tf_op jit(solution)/shard_map/ppermute | solution.py:176
  27.1 1.4 %collective-permute-start.6 = (bf16[2,128,128]{2,1,0:T(8,128)(2,1)S(1)}, bf16[2,128,128]{2,1,0:T(8,128)(2,1)S(1)}, u32[]{:S(2)}, u32[]{:S(2)}) collective-permute-start(bf16[2,128,128]{2,1,0:T(8,128)(2,1)S(1)} %get-tuple-element.69), channel_id=1, source_target_pairs={{0,16},{4,20},{8,24},{12,28},{16,0},{20,4},{24,8},{28,12},{1,17},{... | collective-permute-start | bytes 196616 | tf_op jit(solution)/shard_map/ppermute | solution.py:176
  28.5 1.6 %collective-permute-start.7 = (bf16[2,128,128]{2,1,0:T(8,128)(2,1)S(1)}, bf16[2,128,128]{2,1,0:T(8,128)(2,1)S(1)}, u32[]{:S(2)}, u32[]{:S(2)}) collective-permute-start(bf16[2,128,128]{2,1,0:T(8,128)(2,1)S(1)} %get-tuple-element.70), channel_id=1, source_target_pairs={{0,20},{4,24},{8,28},{12,0},{16,4},{20,8},{24,12},{28,16},{1,21},{... | collective-permute-start | bytes 196616 | tf_op jit(solution)/shard_map/ppermute | solution.py:176
  30.1 1.2 %collective-permute-start.8 = (bf16[2,128,128]{2,1,0:T(8,128)(2,1)S(1)}, bf16[2,128,128]{2,1,0:T(8,128)(2,1)S(1)}, u32[]{:S(2)}, u32[]{:S(2)}) collective-permute-start(bf16[2,128,128]{2,1,0:T(8,128)(2,1)S(1)} %fusion.24), channel_id=1, source_target_pairs={{0,24},{4,28},{8,0},{12,4},{16,8},{20,12},{24,16},{28,20},{1,25},{... | collective-permute-start | bytes 196616 | tf_op jit(solution)/shard_map/ppermute | solution.py:176
  31.4 0.6 collective-permute-start.9
  32.0 4.9 %collective-permute-done.5 = bf16[2,128,128]{2,1,0:T(8,128)(2,1)S(1)} collective-permute-done((bf16[2,128,128]{2,1,0:T(8,128)(2,1)S(1)}, bf16[2,128,128]{2,1,0:T(8,128)(2,1)S(1)}, u32[]{:S(2)}, u32[]{:S(2)}) %collective-permute-start.5) | collective-permute-done | bytes 65568 | tf_op jit(solution)/shard_map/ppermute | solution.py:176
  36.9 1.4 %collective-permute-done.6 = bf16[2,128,128]{2,1,0:T(8,128)(2,1)S(1)} collective-permute-done((bf16[2,128,128]{2,1,0:T(8,128)(2,1)S(1)}, bf16[2,128,128]{2,1,0:T(8,128)(2,1)S(1)}, u32[]{:S(2)}, u32[]{:S(2)}) %collective-permute-start.6) | collective-permute-done | bytes 65568 | tf_op jit(solution)/shard_map/ppermute | solution.py:176
  38.3 1.3 %collective-permute-done.8 = bf16[2,128,128]{2,1,0:T(8,128)(2,1)S(1)} collective-permute-done((bf16[2,128,128]{2,1,0:T(8,128)(2,1)S(1)}, bf16[2,128,128]{2,1,0:T(8,128)(2,1)S(1)}, u32[]{:S(2)}, u32[]{:S(2)}) %collective-permute-start.8) | collective-permute-done | bytes 65568 | tf_op jit(solution)/shard_map/ppermute | solution.py:176
  39.6 0.5 collective-permute-done.9
  40.5 0.1 pad_maximum_fusion.3
  40.6 0.1 pad_maximum_fusion.2
  40.7 0.6 copy-done.8
  41.3 0.7 convolution_bitcast_fusion
  42.1 0.1 copy-done.7
  42.2 0.6 convolution_bitcast_fusion.1
  42.8 0.6 slice_add_fusion.3
  43.4 0.1 fusion.53
  43.5 0.2 fusion.12
  43.8 0.4 add_add_fusion.2
  44.2 0.4 subtract_add_fusion.1
  44.6 0.1 slice_bitcast_fusion.16
  44.8 0.4 add_add_fusion.1
  45.2 0.4 subtract_add_fusion
  45.6 0.2 fusion.59
  46.1 0.1 pad_maximum_fusion
  46.2 0.1 bitcast_convert_fusion
  46.3 0.3 fusion
  46.7 0.6 copy-done.2
  47.2 0.5 fusion.57
  47.7 0.5 fusion.58
  48.2 0.4 copy-done.6
  48.6 0.5 add_add_fusion
  49.1 1.8 %copy.41 = f32[2,8,256,128]{3,2,1,0:T(8,128)} copy(f32[2,8,256,128]{2,3,1,0:T(8,128)S(1)} %bitcast.308) | data formatting | bytes 4194304 | tf_op jit(solution)/shard_map/reshape | solution.py:126
  50.9 1.9 %multiply_add_fusion = f32[2,8,256,128]{3,2,1,0:T(8,128)S(1)} fusion(f32[2,8,256,128]{3,2,1,0:T(8,128)} %copy.41, f32[2,8,128]{2,1,0:T(8,128)S(1)} %pad_maximum_fusion.6, f32[256]{0:T(256)S(1)} %copy-done.9), kind=kLoop, calls=%fused_computation.19 | loop fusion | flops 1048576 | bytes 4203520 | tf_op jit(solution)/shard_map/add | solution.py:128
  53.1 0.1 fusion.16
  53.2 0.1 pad_maximum_fusion.4
  53.3 0.1 dynamic-slice_bitcast_fusion.4
  53.7 0.6 collective-permute-start.11
  54.3 1.9 %collective-permute-start.12 = (bf16[3,128,128]{2,1,0:T(8,128)(2,1)S(1)}, bf16[3,128,128]{2,1,0:T(8,128)(2,1)S(1)}, u32[]{:S(2)}, u32[]{:S(2)}) collective-permute-start(bf16[3,128,128]{2,1,0:T(8,128)(2,1)S(1)} %get-tuple-element.41), channel_id=1, source_target_pairs={{0,12},{4,16},{8,20},{12,24},{16,28},{20,0},{24,4},{28,8},{1,13},{... | collective-permute-start | bytes 294920 | tf_op jit(solution)/shard_map/ppermute | solution.py:195
  56.1 0.9 %collective-permute-start.13 = (bf16[3,128,128]{2,1,0:T(8,128)(2,1)S(1)}, bf16[3,128,128]{2,1,0:T(8,128)(2,1)S(1)}, u32[]{:S(2)}, u32[]{:S(2)}) collective-permute-start(bf16[3,128,128]{2,1,0:T(8,128)(2,1)S(1)} %get-tuple-element.40), channel_id=1, source_target_pairs={{0,16},{4,20},{8,24},{12,28},{16,0},{20,4},{24,8},{28,12},{1,17},{... | collective-permute-start | bytes 294920 | tf_op jit(solution)/shard_map/ppermute | solution.py:195
  57.0 2.0 %collective-permute-start.14 = (bf16[3,128,128]{2,1,0:T(8,128)(2,1)S(1)}, bf16[3,128,128]{2,1,0:T(8,128)(2,1)S(1)}, u32[]{:S(2)}, u32[]{:S(2)}) collective-permute-start(bf16[3,128,128]{2,1,0:T(8,128)(2,1)S(1)} %get-tuple-element.39), channel_id=1, source_target_pairs={{0,20},{4,24},{8,28},{12,0},{16,4},{20,8},{24,12},{28,16},{1,21},{... | collective-permute-start | bytes 294920 | tf_op jit(solution)/shard_map/ppermute | solution.py:195
  59.1 0.7 collective-permute-start.15
  59.8 0.2 collective-permute-start.16
  60.0 1.6 %collective-permute-done.12 = bf16[3,128,128]{2,1,0:T(8,128)(2,1)S(1)} collective-permute-done((bf16[3,128,128]{2,1,0:T(8,128)(2,1)S(1)}, bf16[3,128,128]{2,1,0:T(8,128)(2,1)S(1)}, u32[]{:S(2)}, u32[]{:S(2)}) %collective-permute-start.12) | collective-permute-done | bytes 98336 | tf_op jit(solution)/shard_map/ppermute | solution.py:195
  61.6 8.1 %collective-permute-done.13 = bf16[3,128,128]{2,1,0:T(8,128)(2,1)S(1)} collective-permute-done((bf16[3,128,128]{2,1,0:T(8,128)(2,1)S(1)}, bf16[3,128,128]{2,1,0:T(8,128)(2,1)S(1)}, u32[]{:S(2)}, u32[]{:S(2)}) %collective-permute-start.13) | collective-permute-done | bytes 98336 | tf_op jit(solution)/shard_map/ppermute | solution.py:195
  69.8 3.3 %collective-permute-done.15 = bf16[3,128,128]{2,1,0:T(8,128)(2,1)S(1)} collective-permute-done((bf16[3,128,128]{2,1,0:T(8,128)(2,1)S(1)}, bf16[3,128,128]{2,1,0:T(8,128)(2,1)S(1)}, u32[]{:S(2)}, u32[]{:S(2)}) %collective-permute-start.15) | collective-permute-done | bytes 98336 | tf_op jit(solution)/shard_map/ppermute | solution.py:195
  73.2 0.8 %convert_element_type.107 = f32[128,1024]{1,0:T(8,128)} convert(bf16[128,1024]{1,0:T(8,128)(2,1)S(1)} %get-tuple-element.75) | non-fusion elementwise | flops 131072 | bytes 786432 | tf_op jit(solution)/shard_map/convert_element_type | solution.py:230
  74.0 1.0 %multiply_convert_fusion = (bf16[128,1024]{1,0:T(8,128)(2,1)}, bf16[128,1024]{1,0:T(8,128)(2,1)}) fusion(bf16[128,1024]{1,0:T(8,128)(2,1)S(1)} %copy-done, bf16[128,1024]{1,0:T(8,128)(2,1)S(1)} %get-tuple-element.76, bf16[128,1024]{1,0:T(8,128)(2,1)S(1)} %get-tuple-element.77, bf16[128,1024]{1,0:T(8,128)(2,1)S(1)} %copy-done.1), kind=kLoop, calls=%fused_computation.68 | loop fusion | flops 1179648 | bytes 1572864 | tf_op jit(solution)/shard_map/convert_element_type | solution.py:233
  (78 shorter events, 1.5 us)
Async XLA Ops:
  0.6 14.7 %collective-permute-start = (bf16[128,1024]{1,0:T(8,128)(2,1)}, bf16[128,1024]{1,0:T(8,128)(2,1)S(1)}, u32[]{:S(2)}, u32[]{:S(2)}) collective-permute-start(bf16[128,1024]{1,0:T(8,128)(2,1)} %param.17), channel_id=1, source_target_pairs={{0,1},{1,2},{2,3},{3,0},{4,5},{5,6},{6,7},{7,4},{8,9},{9,10},{10,1... | collective-permute-start | bytes 786440 | tf_op jit(solution)/shard_map/ppermute | solution.py:25
  1.9 13.7 %collective-permute-start.1 = (bf16[128,1024]{1,0:T(8,128)(2,1)}, bf16[128,1024]{1,0:T(8,128)(2,1)S(1)}, u32[]{:S(2)}, u32[]{:S(2)}) collective-permute-start(bf16[128,1024]{1,0:T(8,128)(2,1)} %param.17), channel_id=1, source_target_pairs={{0,2},{1,3},{2,0},{3,1},{4,6},{5,7},{6,4},{7,5},{8,10},{9,11},{10,... | collective-permute-start | bytes 786440 | tf_op jit(solution)/shard_map/ppermute | solution.py:25
  3.1 12.5 %collective-permute-start.2 = (bf16[128,1024]{1,0:T(8,128)(2,1)}, bf16[128,1024]{1,0:T(8,128)(2,1)S(1)}, u32[]{:S(2)}, u32[]{:S(2)}) collective-permute-start(bf16[128,1024]{1,0:T(8,128)(2,1)} %param.17), channel_id=1, source_target_pairs={{0,3},{1,0},{2,1},{3,2},{4,7},{5,4},{6,5},{7,6},{8,11},{9,8},{10,9... | collective-permute-start | bytes 786440 | tf_op jit(solution)/shard_map/ppermute | solution.py:25
  6.6 9.0 %copy-start.5 = (bf16[128,1024]{1,0:T(8,128)(2,1)S(1)}, bf16[128,1024]{1,0:T(8,128)(2,1)}, u32[]{:S(2)}) copy-start(bf16[128,1024]{1,0:T(8,128)(2,1)} %param.17) | copy-start | bytes 786436
  8.9 31.6 %all-to-all-start = ((bf16[8,2,128,128]{3,2,1,0:T(8,128)(2,1)}), bf16[8,2,128,128]{3,2,1,0:T(8,128)(2,1)S(1)}, u32[]{:S(2)}, u32[]{:S(2)}) async-start(bf16[8,2,128,128]{3,2,1,0:T(8,128)(2,1)} %copy.38), calls=%async_computation | async-start | bytes 1048576 | tf_op jit(solution)/shard_map/all_to_all | solution.py:147
  15.6 1.0 %copy-start.3 = (bf16[128,1024]{1,0:T(8,128)(2,1)S(1)}, bf16[128,1024]{1,0:T(8,128)(2,1)}, u32[]{:S(2)}) copy-start(bf16[128,1024]{1,0:T(8,128)(2,1)} %param.13) | copy-start | bytes 786436
  16.6 6.3 %copy-start.4 = (bf16[128,1024]{1,0:T(8,128)(2,1)S(1)}, bf16[128,1024]{1,0:T(8,128)(2,1)}, u32[]{:S(2)}) copy-start(bf16[128,1024]{1,0:T(8,128)(2,1)} %param.16) | copy-start | bytes 786436
  23.9 6.2 %collective-permute-start.3 = (bf16[2,128,128]{2,1,0:T(8,128)(2,1)S(1)}, bf16[2,128,128]{2,1,0:T(8,128)(2,1)S(1)}, u32[]{:S(2)}, u32[]{:S(2)}) collective-permute-start(bf16[2,128,128]{2,1,0:T(8,128)(2,1)S(1)} %get-tuple-element.66), channel_id=1, source_target_pairs={{0,4},{4,8},{8,12},{12,16},{16,20},{20,24},{24,28},{28,0},{1,5},{5... | collective-permute-start | bytes 196616 | tf_op jit(solution)/shard_map/ppermute | solution.py:176
  25.8 5.6 %collective-permute-start.4 = (bf16[2,128,128]{2,1,0:T(8,128)(2,1)S(1)}, bf16[2,128,128]{2,1,0:T(8,128)(2,1)S(1)}, u32[]{:S(2)}, u32[]{:S(2)}) collective-permute-start(bf16[2,128,128]{2,1,0:T(8,128)(2,1)S(1)} %get-tuple-element.67), channel_id=1, source_target_pairs={{0,8},{4,12},{8,16},{12,20},{16,24},{20,28},{24,0},{28,4},{1,9},{5... | collective-permute-start | bytes 196616 | tf_op jit(solution)/shard_map/ppermute | solution.py:176
  27.1 9.8 %collective-permute-start.5 = (bf16[2,128,128]{2,1,0:T(8,128)(2,1)S(1)}, bf16[2,128,128]{2,1,0:T(8,128)(2,1)S(1)}, u32[]{:S(2)}, u32[]{:S(2)}) collective-permute-start(bf16[2,128,128]{2,1,0:T(8,128)(2,1)S(1)} %get-tuple-element.68), channel_id=1, source_target_pairs={{0,12},{4,16},{8,20},{12,24},{16,28},{20,0},{24,4},{28,8},{1,13},{... | collective-permute-start | bytes 196616 | tf_op jit(solution)/shard_map/ppermute | solution.py:176
  27.1 11.2 %collective-permute-start.6 = (bf16[2,128,128]{2,1,0:T(8,128)(2,1)S(1)}, bf16[2,128,128]{2,1,0:T(8,128)(2,1)S(1)}, u32[]{:S(2)}, u32[]{:S(2)}) collective-permute-start(bf16[2,128,128]{2,1,0:T(8,128)(2,1)S(1)} %get-tuple-element.69), channel_id=1, source_target_pairs={{0,16},{4,20},{8,24},{12,28},{16,0},{20,4},{24,8},{28,12},{1,17},{... | collective-permute-start | bytes 196616 | tf_op jit(solution)/shard_map/ppermute | solution.py:176
  28.5 9.8 %collective-permute-start.7 = (bf16[2,128,128]{2,1,0:T(8,128)(2,1)S(1)}, bf16[2,128,128]{2,1,0:T(8,128)(2,1)S(1)}, u32[]{:S(2)}, u32[]{:S(2)}) collective-permute-start(bf16[2,128,128]{2,1,0:T(8,128)(2,1)S(1)} %get-tuple-element.70), channel_id=1, source_target_pairs={{0,20},{4,24},{8,28},{12,0},{16,4},{20,8},{24,12},{28,16},{1,21},{... | collective-permute-start | bytes 196616 | tf_op jit(solution)/shard_map/ppermute | solution.py:176
  30.1 9.5 %collective-permute-start.8 = (bf16[2,128,128]{2,1,0:T(8,128)(2,1)S(1)}, bf16[2,128,128]{2,1,0:T(8,128)(2,1)S(1)}, u32[]{:S(2)}, u32[]{:S(2)}) collective-permute-start(bf16[2,128,128]{2,1,0:T(8,128)(2,1)S(1)} %fusion.24), channel_id=1, source_target_pairs={{0,24},{4,28},{8,0},{12,4},{16,8},{20,12},{24,16},{28,20},{1,25},{... | collective-permute-start | bytes 196616 | tf_op jit(solution)/shard_map/ppermute | solution.py:176
  31.4 8.8 %collective-permute-start.9 = (bf16[2,128,128]{2,1,0:T(8,128)(2,1)S(1)}, bf16[2,128,128]{2,1,0:T(8,128)(2,1)S(1)}, u32[]{:S(2)}, u32[]{:S(2)}) collective-permute-start(bf16[2,128,128]{2,1,0:T(8,128)(2,1)S(1)} %get-tuple-element.65), channel_id=1, source_target_pairs={{0,28},{4,0},{8,4},{12,8},{16,12},{20,16},{24,20},{28,24},{1,29},{... | collective-permute-start | bytes 196616 | tf_op jit(solution)/shard_map/ppermute | solution.py:176
  40.5 0.8 %copy-start.8 = (bf16[256,128,1]{1,0,2:T(8,128)(2,1)S(1)}, bf16[256,128,1]{1,0,2:T(8,128)(2,1)}, u32[]{:S(2)}) copy-start(bf16[256,128,1]{1,0,2:T(8,128)(2,1)} %constant.267) | copy-start | bytes 196612
  41.3 0.8 %copy-start.7 = (bf16[256,128,1]{1,0,2:T(8,128)(2,1)S(1)}, bf16[256,128,1]{1,0,2:T(8,128)(2,1)}, u32[]{:S(2)}) copy-start(bf16[256,128,1]{1,0,2:T(8,128)(2,1)} %constant.268) | copy-start | bytes 196612
  44.8 0.8 %copy-start.10 = (bf16[128,1,1]{0,1,2:T(2,128)(2,1)S(1)}, bf16[128,1,1]{0,1,2:T(2,128)(2,1)}, u32[]{:S(2)}) copy-start(bf16[128,1,1]{0,1,2:T(2,128)(2,1)} %constant.271) | copy-start | bytes 772
  46.3 0.9 %copy-start.2 = (bf16[256,256,1]{1,0,2:T(8,128)(2,1)S(1)}, bf16[256,256,1]{1,0,2:T(8,128)(2,1)}, u32[]{:S(2)}) copy-start(bf16[256,256,1]{1,0,2:T(8,128)(2,1)} %constant.269) | copy-start | bytes 393220
  47.7 0.9 %copy-start.6 = (bf16[256,256,1]{1,0,2:T(8,128)(2,1)S(1)}, bf16[256,256,1]{1,0,2:T(8,128)(2,1)}, u32[]{:S(2)}) copy-start(bf16[256,256,1]{1,0,2:T(8,128)(2,1)} %constant.270) | copy-start | bytes 393220
  49.1 1.9 %copy-start.9 = (f32[256]{0:T(256)S(1)}, f32[256]{0:T(256)}, u32[]{:S(2)}) copy-start(f32[256]{0:T(256)} %constant.252.clone) | copy-start | bytes 3076
  53.3 20.7 %copy-start = (bf16[128,1024]{1,0:T(8,128)(2,1)S(1)}, bf16[128,1024]{1,0:T(8,128)(2,1)}, u32[]{:S(2)}) copy-start(bf16[128,1024]{1,0:T(8,128)(2,1)} %param.14) | copy-start | bytes 786436
  53.3 20.7 %copy-start.1 = (bf16[128,1024]{1,0:T(8,128)(2,1)S(1)}, bf16[128,1024]{1,0:T(8,128)(2,1)}, u32[]{:S(2)}) copy-start(bf16[128,1024]{1,0:T(8,128)(2,1)} %param.15) | copy-start | bytes 786436
  53.5 5.5 %collective-permute-start.10 = (bf16[3,128,128]{2,1,0:T(8,128)(2,1)S(1)}, bf16[3,128,128]{2,1,0:T(8,128)(2,1)S(1)}, u32[]{:S(2)}, u32[]{:S(2)}) collective-permute-start(bf16[3,128,128]{2,1,0:T(8,128)(2,1)S(1)} %get-tuple-element.43), channel_id=1, source_target_pairs={{0,4},{4,8},{8,12},{12,16},{16,20},{20,24},{24,28},{28,0},{1,5},{5... | collective-permute-start | bytes 294920 | tf_op jit(solution)/shard_map/ppermute | solution.py:195
  53.7 6.1 %collective-permute-start.11 = (bf16[3,128,128]{2,1,0:T(8,128)(2,1)S(1)}, bf16[3,128,128]{2,1,0:T(8,128)(2,1)S(1)}, u32[]{:S(2)}, u32[]{:S(2)}) collective-permute-start(bf16[3,128,128]{2,1,0:T(8,128)(2,1)S(1)} %get-tuple-element.42), channel_id=1, source_target_pairs={{0,8},{4,12},{8,16},{12,20},{16,24},{20,28},{24,0},{28,4},{1,9},{5... | collective-permute-start | bytes 294920 | tf_op jit(solution)/shard_map/ppermute | solution.py:195
  54.3 7.3 %collective-permute-start.12 = (bf16[3,128,128]{2,1,0:T(8,128)(2,1)S(1)}, bf16[3,128,128]{2,1,0:T(8,128)(2,1)S(1)}, u32[]{:S(2)}, u32[]{:S(2)}) collective-permute-start(bf16[3,128,128]{2,1,0:T(8,128)(2,1)S(1)} %get-tuple-element.41), channel_id=1, source_target_pairs={{0,12},{4,16},{8,20},{12,24},{16,28},{20,0},{24,4},{28,8},{1,13},{... | collective-permute-start | bytes 294920 | tf_op jit(solution)/shard_map/ppermute | solution.py:195
  56.1 13.6 %collective-permute-start.13 = (bf16[3,128,128]{2,1,0:T(8,128)(2,1)S(1)}, bf16[3,128,128]{2,1,0:T(8,128)(2,1)S(1)}, u32[]{:S(2)}, u32[]{:S(2)}) collective-permute-start(bf16[3,128,128]{2,1,0:T(8,128)(2,1)S(1)} %get-tuple-element.40), channel_id=1, source_target_pairs={{0,16},{4,20},{8,24},{12,28},{16,0},{20,4},{24,8},{28,12},{1,17},{... | collective-permute-start | bytes 294920 | tf_op jit(solution)/shard_map/ppermute | solution.py:195
  57.0 12.7 %collective-permute-start.14 = (bf16[3,128,128]{2,1,0:T(8,128)(2,1)S(1)}, bf16[3,128,128]{2,1,0:T(8,128)(2,1)S(1)}, u32[]{:S(2)}, u32[]{:S(2)}) collective-permute-start(bf16[3,128,128]{2,1,0:T(8,128)(2,1)S(1)} %get-tuple-element.39), channel_id=1, source_target_pairs={{0,20},{4,24},{8,28},{12,0},{16,4},{20,8},{24,12},{28,16},{1,21},{... | collective-permute-start | bytes 294920 | tf_op jit(solution)/shard_map/ppermute | solution.py:195
  59.1 14.0 %collective-permute-start.15 = (bf16[3,128,128]{2,1,0:T(8,128)(2,1)S(1)}, bf16[3,128,128]{2,1,0:T(8,128)(2,1)S(1)}, u32[]{:S(2)}, u32[]{:S(2)}) collective-permute-start(bf16[3,128,128]{2,1,0:T(8,128)(2,1)S(1)} %get-tuple-element.38), channel_id=1, source_target_pairs={{0,24},{4,28},{8,0},{12,4},{16,8},{20,12},{24,16},{28,20},{1,25},{... | collective-permute-start | bytes 294920 | tf_op jit(solution)/shard_map/ppermute | solution.py:195
  59.8 13.4 %collective-permute-start.16 = (bf16[3,128,128]{2,1,0:T(8,128)(2,1)S(1)}, bf16[3,128,128]{2,1,0:T(8,128)(2,1)S(1)}, u32[]{:S(2)}, u32[]{:S(2)}) collective-permute-start(bf16[3,128,128]{2,1,0:T(8,128)(2,1)S(1)} %get-tuple-element.37), channel_id=1, source_target_pairs={{0,28},{4,0},{8,4},{12,8},{16,12},{20,16},{24,20},{28,24},{1,29},{... | collective-permute-start | bytes 294920 | tf_op jit(solution)/shard_map/ppermute | solution.py:195

commit v16 on v14

--- a/solution.py
+++ b/solution.py
@@ -7,7 +7,7 @@
 from jax.sharding import PartitionSpec as P
 
 
-BLOCK = 128
+BLOCK = 256
 
 
 def split_bf16(value):

time: 76.7 us -> 79.9 us (1.042)
  matrix products: 9.28 us -> 11.5 us
  waiting for transfers between devices: 26.3 us -> 27.9 us
  starting transfers between devices: 23.9 us -> 23 us
  local copies, waits for them, and re-layouts: 8.82 us -> 9.65 us
    dot_general x5, matrix products: 2.73 us -> 4.95 us  [table_times(): jnp.einsum('kn,snc->skc', table, signal, preferred_element_type=jnp.float32)]
    reshape x0 -> x1, local copies, waits for them, and re-layouts: none -> 1.92 us  [long_correlations(): signal = (table_times(inv_hi, spectra_hi) + table_times(inv_hi, spectra_l...]
    ppermute x7, waiting for transfers between devices: 17.7 us -> 19.4 us  [gather_lanes(): lax.ppermute(chunk, 'ctx', [(i, (i + shift) % count) for i in range(count)])]
    ppermute x7, starting transfers between devices: 6.01 us -> 4.95 us  [gather_lanes(): lax.ppermute(chunk, 'ctx', [(i, (i + shift) % count) for i in range(count)])]
  transfers between devices with their start and end apart: 18 -> 18, of which waited for: 11 -> 11; matrix products, arithmetic and copies ran while one was open for 18% -> 16% of each run, Pallas kernels for 0% -> 0%
where the time goes in v16:
time: 79.9 us; the launch traced here: 79.1 us
  waiting for transfers between devices  27.9 us (35%)
  starting transfers between devices  23 us (29%)
  matrix products  11.5 us (14%)
  local copies, waits for them, and re-layouts  9.65 us (12%)
  other arithmetic  5.76 us (7%)
  between operations  1.22 us (2%)
    ppermute x7, waiting for transfers between devices, gather_lanes(): lax.ppermute(chunk, 'ctx', [(i, (i + shift) % count) for i in range(count)])  19.4 us
    ppermute x7, waiting for transfers between devices, scatter_lanes(): lax.ppermute(chunk, 'ctx', [(i, (i + shift) % count) for i in range(count)])  8.12 us
    ppermute x7, starting transfers between devices, scatter_lanes(): lax.ppermute(chunk, 'ctx', [(i, (i + shift) % count) for i in range(count)])  7.99 us
    all_to_all x1, starting transfers between devices, all_to_all_ctx(): return lax.all_to_all(stacked, 'ctx', 0, 0, tiled=True)  6.44 us
    dot_general x1, matrix products, gather_matmul(): lax.dot_general(gathered, out_weight, (((1,), (1,)), ((), ())), preferred...  6.3 us
    unnamed x40, local copies, waits for them, and re-layouts  5.95 us
    dot_general x5, matrix products, table_times(): jnp.einsum('kn,snc->skc', table, signal, preferred_element_type=jnp.float32)  4.95 us
    ppermute x7, starting transfers between devices, gather_lanes(): lax.ppermute(chunk, 'ctx', [(i, (i + shift) % count) for i in range(count)])  4.95 us
  transfers between devices with their start and end apart: 18, of which 11 were waited for; matrix products, arithmetic and copies ran while one was open for 16% of the time, Pallas kernels for 0%

profile of v16, /device:TPU:9, one launch (start us, length us, event | category | flops | bytes accessed | tf_op | source)
XLA Modules:
  0.0 79.1 jit_solution(3142128851475950287)
XLA Ops:
  0.6 1.3 %collective-permute-start = (bf16[128,1024]{1,0:T(8,128)(2,1)}, bf16[128,1024]{1,0:T(8,128)(2,1)S(1)}, u32[]{:S(2)}, u32[]{:S(2)}) collective-permute-start(bf16[128,1024]{1,0:T(8,128)(2,1)} %param.17), channel_id=1, source_target_pairs={{0,1},{1,2},{2,3},{3,0},{4,5},{5,6},{6,7},{7,4},{8,9},{9,10},{10,1... | collective-permute-start | bytes 786440 | tf_op jit(solution)/shard_map/ppermute | solution.py:25
  1.9 1.2 %collective-permute-start.1 = (bf16[128,1024]{1,0:T(8,128)(2,1)}, bf16[128,1024]{1,0:T(8,128)(2,1)S(1)}, u32[]{:S(2)}, u32[]{:S(2)}) collective-permute-start(bf16[128,1024]{1,0:T(8,128)(2,1)} %param.17), channel_id=1, source_target_pairs={{0,2},{1,3},{2,0},{3,1},{4,6},{5,7},{6,4},{7,5},{8,10},{9,11},{10,... | collective-permute-start | bytes 786440 | tf_op jit(solution)/shard_map/ppermute | solution.py:25
  3.1 1.2 %collective-permute-start.2 = (bf16[128,1024]{1,0:T(8,128)(2,1)}, bf16[128,1024]{1,0:T(8,128)(2,1)S(1)}, u32[]{:S(2)}, u32[]{:S(2)}) collective-permute-start(bf16[128,1024]{1,0:T(8,128)(2,1)} %param.17), channel_id=1, source_target_pairs={{0,3},{1,0},{2,1},{3,2},{4,7},{5,4},{6,5},{7,6},{8,11},{9,8},{10,9... | collective-permute-start | bytes 786440 | tf_op jit(solution)/shard_map/ppermute | solution.py:25
  4.3 1.1 %copy.27 = bf16[128,1024]{0,1:T(8,128)(2,1)S(1)} copy(bf16[128,1024]{1,0:T(8,128)(2,1)} %param.14) | data formatting | bytes 524288 | tf_op args[1]
  5.4 1.1 %copy.28 = bf16[128,1024]{0,1:T(8,128)(2,1)S(1)} copy(bf16[128,1024]{1,0:T(8,128)(2,1)} %param.15) | data formatting | bytes 524288 | tf_op args[2]
  6.5 0.1 multiply_convert_fusion.2
  6.6 1.2 %copy.29 = bf16[128,1024]{0,1:T(8,128)(2,1)S(1)} copy(bf16[128,1024]{1,0:T(8,128)(2,1)} %param.19) | data formatting | bytes 524288 | tf_op args[6]
  7.9 1.0 %copy.30 = bf16[8,2,128,128]{3,2,1,0:T(8,128)(2,1)} copy(bf16[8,2,128,128]{2,3,0,1:T(8,128)(2,1)S(1)} %pad_maximum_fusion.4) | data formatting | bytes 1048576 | tf_op jit(solution)/shard_map/stack | solution.py:211
  8.9 6.4 %all-to-all-start = ((bf16[8,2,128,128]{3,2,1,0:T(8,128)(2,1)}), bf16[8,2,128,128]{3,2,1,0:T(8,128)(2,1)S(1)}, u32[]{:S(2)}, u32[]{:S(2)}) async-start(bf16[8,2,128,128]{3,2,1,0:T(8,128)(2,1)} %copy.30), calls=%async_computation | async-start | bytes 1048576 | tf_op jit(solution)/shard_map/all_to_all | solution.py:147
  15.3 0.3 collective-permute-done.1
  15.6 0.1 pad_maximum_fusion.1
  15.8 0.1 dynamic-slice_bitcast_fusion.3
  15.9 0.7 copy-done.5
  16.6 6.3 %fusion.12 = (bf16[128,1024]{1,0:T(8,128)(2,1)S(1)}, f32[128,1024]{1,0:T(8,128)S(1)}) fusion(bf16[128,1024]{1,0:T(8,128)(2,1)S(1)} %copy-done.5, bf16[1024,4096]{1,0:T(8,128)(2,1)} %param.18, bf16[128,1024]{1,0:T(8,128)(2,1)S(1)} %get-tuple-element.38, bf16[128,1024]{1,0:T(8,128)(2,1)S(1)} %get-tuple-element.39, ...), kind=kOutput, calls=%fused_computation.81 | convolution fusion | flops 1078329344 | bytes 10485760 | tf_op jit(solution)/shard_map/dot_general | solution.py:33
  22.9 0.9 %fusion.13 = (bf16[1,128,1024]{2,1,0:T(8,128)(2,1)S(1)}, bf16[128,1024]{1,0:T(8,128)(2,1)}) fusion(bf16[128,1024]{1,0:T(8,128)(2,1)S(1)} %get-tuple-element.89, f32[128,1024]{1,0:T(8,128)S(1)} %get-tuple-element.90, bf16[128,1024]{1,0:T(8,128)(2,1)S(1)} %copy-done.5, bf16[128,1024]{1,0:T(8,128)(2,1)S(1)} %copy-done.6), kind=kLoop, calls=%fused_computation.82 | loop fusion | flops 1048576 | bytes 1835008 | tf_op jit(solution)/shard_map/stack | solution.py:217
  23.8 0.1 fusion.30
  23.9 1.8 %collective-permute-start.3 = (bf16[2,128,128]{2,1,0:T(8,128)(2,1)S(1)}, bf16[2,128,128]{2,1,0:T(8,128)(2,1)S(1)}, u32[]{:S(2)}, u32[]{:S(2)}) collective-permute-start(bf16[2,128,128]{2,1,0:T(8,128)(2,1)S(1)} %get-tuple-element.54), channel_id=1, source_target_pairs={{0,4},{4,8},{8,12},{12,16},{16,20},{20,24},{24,28},{28,0},{1,5},{5... | collective-permute-start | bytes 196616 | tf_op jit(solution)/shard_map/ppermute | solution.py:176
  25.8 1.4 %collective-permute-start.4 = (bf16[2,128,128]{2,1,0:T(8,128)(2,1)S(1)}, bf16[2,128,128]{2,1,0:T(8,128)(2,1)S(1)}, u32[]{:S(2)}, u32[]{:S(2)}) collective-permute-start(bf16[2,128,128]{2,1,0:T(8,128)(2,1)S(1)} %get-tuple-element.55), channel_id=1, source_target_pairs={{0,8},{4,12},{8,16},{12,20},{16,24},{20,28},{24,0},{28,4},{1,9},{5... | collective-permute-start | bytes 196616 | tf_op jit(solution)/shard_map/ppermute | solution.py:176
  27.1 1.4 %collective-permute-start.6 = (bf16[2,128,128]{2,1,0:T(8,128)(2,1)S(1)}, bf16[2,128,128]{2,1,0:T(8,128)(2,1)S(1)}, u32[]{:S(2)}, u32[]{:S(2)}) collective-permute-start(bf16[2,128,128]{2,1,0:T(8,128)(2,1)S(1)} %get-tuple-element.57), channel_id=1, source_target_pairs={{0,16},{4,20},{8,24},{12,28},{16,0},{20,4},{24,8},{28,12},{1,17},{... | collective-permute-start | bytes 196616 | tf_op jit(solution)/shard_map/ppermute | solution.py:176
  28.5 1.6 %collective-permute-start.7 = (bf16[2,128,128]{2,1,0:T(8,128)(2,1)S(1)}, bf16[2,128,128]{2,1,0:T(8,128)(2,1)S(1)}, u32[]{:S(2)}, u32[]{:S(2)}) collective-permute-start(bf16[2,128,128]{2,1,0:T(8,128)(2,1)S(1)} %get-tuple-element.58), channel_id=1, source_target_pairs={{0,20},{4,24},{8,28},{12,0},{16,4},{20,8},{24,12},{28,16},{1,21},{... | collective-permute-start | bytes 196616 | tf_op jit(solution)/shard_map/ppermute | solution.py:176
  30.1 1.2 %collective-permute-start.8 = (bf16[2,128,128]{2,1,0:T(8,128)(2,1)S(1)}, bf16[2,128,128]{2,1,0:T(8,128)(2,1)S(1)}, u32[]{:S(2)}, u32[]{:S(2)}) collective-permute-start(bf16[2,128,128]{2,1,0:T(8,128)(2,1)S(1)} %fusion.37), channel_id=1, source_target_pairs={{0,24},{4,28},{8,0},{12,4},{16,8},{20,12},{24,16},{28,20},{1,25},{... | collective-permute-start | bytes 196616 | tf_op jit(solution)/shard_map/ppermute | solution.py:176
  31.4 0.6 collective-permute-start.9
  32.0 4.9 %collective-permute-done.5 = bf16[2,128,128]{2,1,0:T(8,128)(2,1)S(1)} collective-permute-done((bf16[2,128,128]{2,1,0:T(8,128)(2,1)S(1)}, bf16[2,128,128]{2,1,0:T(8,128)(2,1)S(1)}, u32[]{:S(2)}, u32[]{:S(2)}) %collective-permute-start.5) | collective-permute-done | bytes 65568 | tf_op jit(solution)/shard_map/ppermute | solution.py:176
  36.9 1.4 %collective-permute-done.6 = bf16[2,128,128]{2,1,0:T(8,128)(2,1)S(1)} collective-permute-done((bf16[2,128,128]{2,1,0:T(8,128)(2,1)S(1)}, bf16[2,128,128]{2,1,0:T(8,128)(2,1)S(1)}, u32[]{:S(2)}, u32[]{:S(2)}) %collective-permute-start.6) | collective-permute-done | bytes 65568 | tf_op jit(solution)/shard_map/ppermute | solution.py:176
  38.3 1.3 %collective-permute-done.8 = bf16[2,128,128]{2,1,0:T(8,128)(2,1)S(1)} collective-permute-done((bf16[2,128,128]{2,1,0:T(8,128)(2,1)S(1)}, bf16[2,128,128]{2,1,0:T(8,128)(2,1)S(1)}, u32[]{:S(2)}, u32[]{:S(2)}) %collective-permute-start.8) | collective-permute-done | bytes 65568 | tf_op jit(solution)/shard_map/ppermute | solution.py:176
  39.6 0.5 collective-permute-done.9
  40.5 0.1 pad_maximum_fusion.3
  40.6 0.1 pad_maximum_fusion.2
  40.8 0.4 copy-done.11
  41.2 0.2 fusion.64
  41.5 0.8 convolution_bitcast_fusion
  42.2 0.2 copy-done.7
  42.4 0.6 convolution_bitcast_fusion.1
  43.0 0.9 %slice_add_fusion.3 = (f32[4,512,128]{1,2,0:T(8,128)S(1)}, f32[4,512,128]{1,2,0:T(8,128)S(1)}, f32[4,512,128]{1,2,0:T(8,128)S(1)}) fusion(f32[12,512,128]{1,2,0:T(8,128)S(1)} %convolution_bitcast_fusion.1, f32[16,512,128]{1,2,0:T(8,128)S(1)} %convolution_bitcast_fusion), kind=kLoop, calls=%fused_computation.34 | loop fusion | flops 1048576 | bytes 10485760 | tf_op jit(solution)/shard_map/add | solution.py:87
  44.0 0.2 fusion.11
  44.3 0.1 slice_bitcast_fusion.8
  44.4 0.4 add_add_fusion.2
  44.8 0.1 maximum_bitcast_fusion
  45.0 0.4 add_add_fusion.1
  45.4 0.1 maximum_bitcast_fusion.1
  45.5 0.2 pad_maximum_fusion
  45.8 0.1 bitcast_convert_fusion
  45.9 0.4 fusion
  46.3 0.7 copy-done
  46.9 0.7 fusion.62
  47.7 0.7 fusion.63
  48.4 0.3 copy-done.4
  48.7 2.1 %add_add_fusion = f32[8,128,512]{2,1,0:T(8,128)} fusion(f32[8,128,512]{2,1,0:T(8,128)S(1)} %fusion.62, f32[8,128,512]{2,1,0:T(8,128)S(1)} %fusion.63, bf16[8,512,128]{1,2,0:T(8,128)(2,1)S(1)} %bitcast_convert_fusion, bf16[512,512,1]{1,0,2:T(8,128)(2,1)S(1)} %copy-done.4), kind=kOutput, calls=%fused_computation.22 | convolution fusion | flops 537919488 | bytes 7864320 | tf_op jit(solution)/shard_map/kn,snc->skc/dot_general | solution.py:65
  50.8 1.9 %copy.33 = f32[2,4,512,128]{3,2,1,0:T(8,128)S(1)} copy(f32[2,4,512,128]{2,3,1,0:T(8,128)} %bitcast.220) | data formatting | bytes 4194304 | tf_op jit(solution)/shard_map/reshape | solution.py:126
  52.8 0.2 multiply_add_fusion
  53.0 0.1 slice_bitcast_fusion
  53.2 0.1 fusion.9
  53.4 0.1 fusion.15
  53.5 1.1 %collective-permute-start.10 = (f32[2,128,128]{2,1,0:T(8,128)S(1)}, f32[2,128,128]{2,1,0:T(8,128)S(1)}, u32[]{:S(2)}, u32[]{:S(2)}) collective-permute-start(f32[2,128,128]{2,1,0:T(8,128)S(1)} %get-tuple-element.19), channel_id=1, source_target_pairs={{0,4},{4,8},{8,12},{12,16},{16,20},{20,24},{24,28},{28,0},{1,5},{5... | collective-permute-start | bytes 393224 | tf_op jit(solution)/shard_map/ppermute | solution.py:195
  54.6 1.8 %collective-permute-start.11 = (f32[2,128,128]{2,1,0:T(8,128)S(1)}, f32[2,128,128]{2,1,0:T(8,128)S(1)}, u32[]{:S(2)}, u32[]{:S(2)}) collective-permute-start(f32[2,128,128]{2,1,0:T(8,128)S(1)} %get-tuple-element.20), channel_id=1, source_target_pairs={{0,8},{4,12},{8,16},{12,20},{16,24},{20,28},{24,0},{28,4},{1,9},{5... | collective-permute-start | bytes 393224 | tf_op jit(solution)/shard_map/ppermute | solution.py:195
  56.4 1.3 %collective-permute-start.12 = (f32[2,128,128]{2,1,0:T(8,128)S(1)}, f32[2,128,128]{2,1,0:T(8,128)S(1)}, u32[]{:S(2)}, u32[]{:S(2)}) collective-permute-start(f32[2,128,128]{2,1,0:T(8,128)S(1)} %get-tuple-element.21), channel_id=1, source_target_pairs={{0,12},{4,16},{8,20},{12,24},{16,28},{20,0},{24,4},{28,8},{1,13},{... | collective-permute-start | bytes 393224 | tf_op jit(solution)/shard_map/ppermute | solution.py:195
  57.7 0.6 collective-permute-start.13
  58.5 2.2 %collective-permute-done.10 = f32[2,128,128]{2,1,0:T(8,128)S(1)} collective-permute-done((f32[2,128,128]{2,1,0:T(8,128)S(1)}, f32[2,128,128]{2,1,0:T(8,128)S(1)}, u32[]{:S(2)}, u32[]{:S(2)}) %collective-permute-start.10) | collective-permute-done | bytes 131104 | tf_op jit(solution)/shard_map/ppermute | solution.py:195
  60.7 3.4 %collective-permute-done.11 = f32[2,128,128]{2,1,0:T(8,128)S(1)} collective-permute-done((f32[2,128,128]{2,1,0:T(8,128)S(1)}, f32[2,128,128]{2,1,0:T(8,128)S(1)}, u32[]{:S(2)}, u32[]{:S(2)}) %collective-permute-start.11) | collective-permute-done | bytes 131104 | tf_op jit(solution)/shard_map/ppermute | solution.py:195
  64.1 10.6 %collective-permute-done.12 = f32[2,128,128]{2,1,0:T(8,128)S(1)} collective-permute-done((f32[2,128,128]{2,1,0:T(8,128)S(1)}, f32[2,128,128]{2,1,0:T(8,128)S(1)}, u32[]{:S(2)}, u32[]{:S(2)}) %collective-permute-start.12) | collective-permute-done | bytes 131104 | tf_op jit(solution)/shard_map/ppermute | solution.py:195
  74.7 2.8 %collective-permute-done.13 = f32[2,128,128]{2,1,0:T(8,128)S(1)} collective-permute-done((f32[2,128,128]{2,1,0:T(8,128)S(1)}, f32[2,128,128]{2,1,0:T(8,128)S(1)}, u32[]{:S(2)}, u32[]{:S(2)}) %collective-permute-start.13) | collective-permute-done | bytes 131104 | tf_op jit(solution)/shard_map/ppermute | solution.py:195
  77.5 0.3 collective-permute-done.15
  77.9 0.2 collective-permute-done.16
  78.1 0.9 %multiply_convert_fusion = (bf16[128,1024]{1,0:T(8,128)(2,1)}, bf16[128,1024]{1,0:T(8,128)(2,1)}) fusion(f32[128,1024]{1,0:T(8,128)S(1)} %get-tuple-element.64, bf16[128,1024]{1,0:T(8,128)(2,1)S(1)} %copy-done.2, bf16[128,1024]{1,0:T(8,128)(2,1)S(1)} %copy-done.1), kind=kLoop, calls=%fused_computation.71 | loop fusion | flops 786432 | bytes 1572864 | tf_op jit(solution)/shard_map/convert_element_type | solution.py:229
  (73 shorter events, 1.1 us)
Async XLA Ops:
  0.6 14.7 %collective-permute-start = (bf16[128,1024]{1,0:T(8,128)(2,1)}, bf16[128,1024]{1,0:T(8,128)(2,1)S(1)}, u32[]{:S(2)}, u32[]{:S(2)}) collective-permute-start(bf16[128,1024]{1,0:T(8,128)(2,1)} %param.17), channel_id=1, source_target_pairs={{0,1},{1,2},{2,3},{3,0},{4,5},{5,6},{6,7},{7,4},{8,9},{9,10},{10,1... | collective-permute-start | bytes 786440 | tf_op jit(solution)/shard_map/ppermute | solution.py:25
  1.9 13.7 %collective-permute-start.1 = (bf16[128,1024]{1,0:T(8,128)(2,1)}, bf16[128,1024]{1,0:T(8,128)(2,1)S(1)}, u32[]{:S(2)}, u32[]{:S(2)}) collective-permute-start(bf16[128,1024]{1,0:T(8,128)(2,1)} %param.17), channel_id=1, source_target_pairs={{0,2},{1,3},{2,0},{3,1},{4,6},{5,7},{6,4},{7,5},{8,10},{9,11},{10,... | collective-permute-start | bytes 786440 | tf_op jit(solution)/shard_map/ppermute | solution.py:25
  3.1 12.5 %collective-permute-start.2 = (bf16[128,1024]{1,0:T(8,128)(2,1)}, bf16[128,1024]{1,0:T(8,128)(2,1)S(1)}, u32[]{:S(2)}, u32[]{:S(2)}) collective-permute-start(bf16[128,1024]{1,0:T(8,128)(2,1)} %param.17), channel_id=1, source_target_pairs={{0,3},{1,0},{2,1},{3,2},{4,7},{5,4},{6,5},{7,6},{8,11},{9,8},{10,9... | collective-permute-start | bytes 786440 | tf_op jit(solution)/shard_map/ppermute | solution.py:25
  6.6 9.0 %copy-start.8 = (bf16[128,1024]{1,0:T(8,128)(2,1)S(1)}, bf16[128,1024]{1,0:T(8,128)(2,1)}, u32[]{:S(2)}) copy-start(bf16[128,1024]{1,0:T(8,128)(2,1)} %param.17) | copy-start | bytes 786436
  8.9 31.6 %all-to-all-start = ((bf16[8,2,128,128]{3,2,1,0:T(8,128)(2,1)}), bf16[8,2,128,128]{3,2,1,0:T(8,128)(2,1)S(1)}, u32[]{:S(2)}, u32[]{:S(2)}) async-start(bf16[8,2,128,128]{3,2,1,0:T(8,128)(2,1)} %copy.30), calls=%async_computation | async-start | bytes 1048576 | tf_op jit(solution)/shard_map/all_to_all | solution.py:147
  15.6 1.0 %copy-start.5 = (bf16[128,1024]{1,0:T(8,128)(2,1)S(1)}, bf16[128,1024]{1,0:T(8,128)(2,1)}, u32[]{:S(2)}) copy-start(bf16[128,1024]{1,0:T(8,128)(2,1)} %param.13) | copy-start | bytes 786436
  16.6 6.3 %copy-start.6 = (bf16[128,1024]{1,0:T(8,128)(2,1)S(1)}, bf16[128,1024]{1,0:T(8,128)(2,1)}, u32[]{:S(2)}) copy-start(bf16[128,1024]{1,0:T(8,128)(2,1)} %param.16) | copy-start | bytes 786436
  23.9 6.2 %collective-permute-start.3 = (bf16[2,128,128]{2,1,0:T(8,128)(2,1)S(1)}, bf16[2,128,128]{2,1,0:T(8,128)(2,1)S(1)}, u32[]{:S(2)}, u32[]{:S(2)}) collective-permute-start(bf16[2,128,128]{2,1,0:T(8,128)(2,1)S(1)} %get-tuple-element.54), channel_id=1, source_target_pairs={{0,4},{4,8},{8,12},{12,16},{16,20},{20,24},{24,28},{28,0},{1,5},{5... | collective-permute-start | bytes 196616 | tf_op jit(solution)/shard_map/ppermute | solution.py:176
  25.8 5.6 %collective-permute-start.4 = (bf16[2,128,128]{2,1,0:T(8,128)(2,1)S(1)}, bf16[2,128,128]{2,1,0:T(8,128)(2,1)S(1)}, u32[]{:S(2)}, u32[]{:S(2)}) collective-permute-start(bf16[2,128,128]{2,1,0:T(8,128)(2,1)S(1)} %get-tuple-element.55), channel_id=1, source_target_pairs={{0,8},{4,12},{8,16},{12,20},{16,24},{20,28},{24,0},{28,4},{1,9},{5... | collective-permute-start | bytes 196616 | tf_op jit(solution)/shard_map/ppermute | solution.py:176
  27.1 9.8 %collective-permute-start.5 = (bf16[2,128,128]{2,1,0:T(8,128)(2,1)S(1)}, bf16[2,128,128]{2,1,0:T(8,128)(2,1)S(1)}, u32[]{:S(2)}, u32[]{:S(2)}) collective-permute-start(bf16[2,128,128]{2,1,0:T(8,128)(2,1)S(1)} %get-tuple-element.56), channel_id=1, source_target_pairs={{0,12},{4,16},{8,20},{12,24},{16,28},{20,0},{24,4},{28,8},{1,13},{... | collective-permute-start | bytes 196616 | tf_op jit(solution)/shard_map/ppermute | solution.py:176
  27.1 11.2 %collective-permute-start.6 = (bf16[2,128,128]{2,1,0:T(8,128)(2,1)S(1)}, bf16[2,128,128]{2,1,0:T(8,128)(2,1)S(1)}, u32[]{:S(2)}, u32[]{:S(2)}) collective-permute-start(bf16[2,128,128]{2,1,0:T(8,128)(2,1)S(1)} %get-tuple-element.57), channel_id=1, source_target_pairs={{0,16},{4,20},{8,24},{12,28},{16,0},{20,4},{24,8},{28,12},{1,17},{... | collective-permute-start | bytes 196616 | tf_op jit(solution)/shard_map/ppermute | solution.py:176
  28.5 9.8 %collective-permute-start.7 = (bf16[2,128,128]{2,1,0:T(8,128)(2,1)S(1)}, bf16[2,128,128]{2,1,0:T(8,128)(2,1)S(1)}, u32[]{:S(2)}, u32[]{:S(2)}) collective-permute-start(bf16[2,128,128]{2,1,0:T(8,128)(2,1)S(1)} %get-tuple-element.58), channel_id=1, source_target_pairs={{0,20},{4,24},{8,28},{12,0},{16,4},{20,8},{24,12},{28,16},{1,21},{... | collective-permute-start | bytes 196616 | tf_op jit(solution)/shard_map/ppermute | solution.py:176
  30.1 9.5 %collective-permute-start.8 = (bf16[2,128,128]{2,1,0:T(8,128)(2,1)S(1)}, bf16[2,128,128]{2,1,0:T(8,128)(2,1)S(1)}, u32[]{:S(2)}, u32[]{:S(2)}) collective-permute-start(bf16[2,128,128]{2,1,0:T(8,128)(2,1)S(1)} %fusion.37), channel_id=1, source_target_pairs={{0,24},{4,28},{8,0},{12,4},{16,8},{20,12},{24,16},{28,20},{1,25},{... | collective-permute-start | bytes 196616 | tf_op jit(solution)/shard_map/ppermute | solution.py:176
  31.4 8.8 %collective-permute-start.9 = (bf16[2,128,128]{2,1,0:T(8,128)(2,1)S(1)}, bf16[2,128,128]{2,1,0:T(8,128)(2,1)S(1)}, u32[]{:S(2)}, u32[]{:S(2)}) collective-permute-start(bf16[2,128,128]{2,1,0:T(8,128)(2,1)S(1)} %get-tuple-element.53), channel_id=1, source_target_pairs={{0,28},{4,0},{8,4},{12,8},{16,12},{20,16},{24,20},{28,24},{1,29},{... | collective-permute-start | bytes 196616 | tf_op jit(solution)/shard_map/ppermute | solution.py:176
  40.5 0.7 copy-start.11
  40.5 1.0 %copy-start.9 = (bf16[512,256,1]{1,0,2:T(8,128)(2,1)S(1)}, bf16[512,256,1]{1,0,2:T(8,128)(2,1)}, u32[]{:S(2)}) copy-start(bf16[512,256,1]{1,0,2:T(8,128)(2,1)} %constant.266) | copy-start | bytes 786436
  41.5 1.0 %copy-start.7 = (bf16[512,256,1]{1,0,2:T(8,128)(2,1)S(1)}, bf16[512,256,1]{1,0,2:T(8,128)(2,1)}, u32[]{:S(2)}) copy-start(bf16[512,256,1]{1,0,2:T(8,128)(2,1)} %constant.267) | copy-start | bytes 786436
  45.9 1.0 %copy-start = (bf16[512,512,1]{1,0,2:T(8,128)(2,1)S(1)}, bf16[512,512,1]{1,0,2:T(8,128)(2,1)}, u32[]{:S(2)}) copy-start(bf16[512,512,1]{1,0,2:T(8,128)(2,1)} %constant.268) | copy-start | bytes 1572868
  47.7 1.0 %copy-start.4 = (bf16[512,512,1]{1,0,2:T(8,128)(2,1)S(1)}, bf16[512,512,1]{1,0,2:T(8,128)(2,1)}, u32[]{:S(2)}) copy-start(bf16[512,512,1]{1,0,2:T(8,128)(2,1)} %constant.269) | copy-start | bytes 1572868
  50.8 2.0 %copy-start.10 = (f32[512]{0:T(512)S(1)}, f32[512]{0:T(512)}, u32[]{:S(2)}) copy-start(f32[512]{0:T(512)} %constant.251.clone) | copy-start | bytes 6148
  53.3 24.8 %copy-start.1 = (bf16[128,1024]{1,0:T(8,128)(2,1)S(1)}, bf16[128,1024]{1,0:T(8,128)(2,1)}, u32[]{:S(2)}) copy-start(bf16[128,1024]{1,0:T(8,128)(2,1)} %param.15) | copy-start | bytes 786436
  53.3 24.8 %copy-start.2 = (bf16[128,1024]{1,0:T(8,128)(2,1)S(1)}, bf16[128,1024]{1,0:T(8,128)(2,1)}, u32[]{:S(2)}) copy-start(bf16[128,1024]{1,0:T(8,128)(2,1)} %param.14) | copy-start | bytes 786436
  53.3 24.2 %collective-permute-start.14 = (f32[2,128,128]{2,1,0:T(8,128)S(1)}, f32[2,128,128]{2,1,0:T(8,128)S(1)}, u32[]{:S(2)}, u32[]{:S(2)}) collective-permute-start(f32[2,128,128]{2,1,0:T(8,128)S(1)} %get-tuple-element.24), channel_id=1, source_target_pairs={{0,20},{4,24},{8,28},{12,0},{16,4},{20,8},{24,12},{28,16},{1,21},{... | collective-permute-start | bytes 393224 | tf_op jit(solution)/shard_map/ppermute | solution.py:195
  53.5 7.2 %collective-permute-start.10 = (f32[2,128,128]{2,1,0:T(8,128)S(1)}, f32[2,128,128]{2,1,0:T(8,128)S(1)}, u32[]{:S(2)}, u32[]{:S(2)}) collective-permute-start(f32[2,128,128]{2,1,0:T(8,128)S(1)} %get-tuple-element.19), channel_id=1, source_target_pairs={{0,4},{4,8},{8,12},{12,16},{16,20},{20,24},{24,28},{28,0},{1,5},{5... | collective-permute-start | bytes 393224 | tf_op jit(solution)/shard_map/ppermute | solution.py:195
  54.6 9.4 %collective-permute-start.11 = (f32[2,128,128]{2,1,0:T(8,128)S(1)}, f32[2,128,128]{2,1,0:T(8,128)S(1)}, u32[]{:S(2)}, u32[]{:S(2)}) collective-permute-start(f32[2,128,128]{2,1,0:T(8,128)S(1)} %get-tuple-element.20), channel_id=1, source_target_pairs={{0,8},{4,12},{8,16},{12,20},{16,24},{20,28},{24,0},{28,4},{1,9},{5... | collective-permute-start | bytes 393224 | tf_op jit(solution)/shard_map/ppermute | solution.py:195
  56.4 18.3 %collective-permute-start.12 = (f32[2,128,128]{2,1,0:T(8,128)S(1)}, f32[2,128,128]{2,1,0:T(8,128)S(1)}, u32[]{:S(2)}, u32[]{:S(2)}) collective-permute-start(f32[2,128,128]{2,1,0:T(8,128)S(1)} %get-tuple-element.21), channel_id=1, source_target_pairs={{0,12},{4,16},{8,20},{12,24},{16,28},{20,0},{24,4},{28,8},{1,13},{... | collective-permute-start | bytes 393224 | tf_op jit(solution)/shard_map/ppermute | solution.py:195
  57.7 19.8 %collective-permute-start.13 = (f32[2,128,128]{2,1,0:T(8,128)S(1)}, f32[2,128,128]{2,1,0:T(8,128)S(1)}, u32[]{:S(2)}, u32[]{:S(2)}) collective-permute-start(f32[2,128,128]{2,1,0:T(8,128)S(1)} %get-tuple-element.22), channel_id=1, source_target_pairs={{0,16},{4,20},{8,24},{12,28},{16,0},{20,4},{24,8},{28,12},{1,17},{... | collective-permute-start | bytes 393224 | tf_op jit(solution)/shard_map/ppermute | solution.py:195
  60.6 17.2 %collective-permute-start.15 = (f32[2,128,128]{2,1,0:T(8,128)S(1)}, f32[2,128,128]{2,1,0:T(8,128)S(1)}, u32[]{:S(2)}, u32[]{:S(2)}) collective-permute-start(f32[2,128,128]{2,1,0:T(8,128)S(1)} %get-tuple-element.23), channel_id=1, source_target_pairs={{0,24},{4,28},{8,0},{12,4},{16,8},{20,12},{24,16},{28,20},{1,25},{... | collective-permute-start | bytes 393224 | tf_op jit(solution)/shard_map/ppermute | solution.py:195
  64.1 14.0 %collective-permute-start.16 = (f32[2,128,128]{2,1,0:T(8,128)S(1)}, f32[2,128,128]{2,1,0:T(8,128)S(1)}, u32[]{:S(2)}, u32[]{:S(2)}) collective-permute-start(f32[2,128,128]{2,1,0:T(8,128)S(1)} %get-tuple-element.17), channel_id=1, source_target_pairs={{0,28},{4,0},{8,4},{12,8},{16,12},{20,16},{24,20},{28,24},{1,29},{... | collective-permute-start | bytes 393224 | tf_op jit(solution)/shard_map/ppermute | solution.py:195
  78.1 1.0 %copy-start.3 = (f32[128,1024]{1,0:T(8,128)}, f32[128,1024]{1,0:T(8,128)S(1)}, u32[]{:S(2)}) copy-start(f32[128,1024]{1,0:T(8,128)S(1)} %get-tuple-element.63) | copy-start | bytes 1572868

commit v17 on v14

--- a/solution.py
+++ b/solution.py
@@ -222,8 +222,8 @@
         inputs_t[:, 1].reshape(seq, sub),
         float(seq) ** -0.5,
     )
-    outgoing = jnp.stack([du_t, filter_t]).reshape(2, blocks, rows, sub).transpose(1, 0, 2, 3)
-    du_local, filter_grad = gather_lanes(outgoing, chans)
+    filter_grad = from_groups(all_to_all_ctx(filter_t.reshape(blocks, rows, sub)))
+    (du_local,) = gather_lanes(du_t.reshape(blocks, 1, rows, sub), chans)
     k_late, v_late = lax.optimization_barrier((k_proj, v_proj))
     dk_grad = (du_local * v_late.astype(jnp.float32)).astype(jnp.bfloat16)
     dv_grad = (du_local * k_late.astype(jnp.float32)).astype(jnp.bfloat16)

time: 76.7 us -> 82.2 us (1.072)
  starting transfers between devices: 23.9 us -> 27.8 us
  local copies, waits for them, and re-layouts: 8.82 us -> 9.71 us
    all_to_all x1 -> x2, starting transfers between devices: 6.44 us -> 10.2 us  [all_to_all_ctx(): return lax.all_to_all(stacked, 'ctx', 0, 0, tiled=True)]
    reshape x0 -> x1, local copies, waits for them, and re-layouts: none -> 1 us  [from_groups(): return value.transpose(1, 0, 2).reshape(rows, groups * chans)]
    another operation x10 -> x0, local copies, waits for them, and re-layouts: 0.84 us -> none
    unnamed x40 -> x38, local copies, waits for them, and re-layouts: 6.23 us -> 6.22 us
  transfers between devices with their start and end apart: 18 -> 19, of which waited for: 11 -> 11; matrix products, arithmetic and copies ran while one was open for 18% -> 17% of each run, Pallas kernels for 0% -> 0%
where the time goes in v17:
time: 82.2 us; the launch traced here: 81.2 us
  starting transfers between devices  27.8 us (34%)
  waiting for transfers between devices  26.4 us (32%)
  local copies, waits for them, and re-layouts  9.71 us (12%)
  matrix products  9.28 us (11%)
  other arithmetic  6.88 us (8%)
  between operations  1.21 us (1%)
    ppermute x7, waiting for transfers between devices, gather_lanes(): lax.ppermute(chunk, 'ctx', [(i, (i + shift) % count) for i in range(count)])  17.8 us
    all_to_all x2, starting transfers between devices, all_to_all_ctx(): return lax.all_to_all(stacked, 'ctx', 0, 0, tiled=True)  10.2 us
    ppermute x7, waiting for transfers between devices, scatter_lanes(): lax.ppermute(chunk, 'ctx', [(i, (i + shift) % count) for i in range(count)])  8.29 us
    ppermute x7, starting transfers between devices, scatter_lanes(): lax.ppermute(chunk, 'ctx', [(i, (i + shift) % count) for i in range(count)])  7.81 us
    dot_general x1, matrix products, gather_matmul(): lax.dot_general(gathered, out_weight, (((1,), (1,)), ((), ())), preferred...  6.3 us
    unnamed x38, local copies, waits for them, and re-layouts  6.22 us
    ppermute x7, starting transfers between devices, gather_lanes(): lax.ppermute(chunk, 'ctx', [(i, (i + shift) % count) for i in range(count)])  6.13 us
    ppermute x3, starting transfers between devices, gather_matmul(): lax.ppermute(out_grad, 'tp', [(i, (i + shift) % count) for i in range(cou...  3.66 us
  transfers between devices with their start and end apart: 19, of which 11 were waited for; matrix products, arithmetic and copies ran while one was open for 17% of the time, Pallas kernels for 0%

profile of v17, /device:TPU:9, one launch (start us, length us, event | category | flops | bytes accessed | tf_op | source)
XLA Modules:
  0.0 81.2 jit_solution(17207124212820562494)
XLA Ops:
  0.6 1.3 %collective-permute-start = (bf16[128,1024]{1,0:T(8,128)(2,1)}, bf16[128,1024]{1,0:T(8,128)(2,1)S(1)}, u32[]{:S(2)}, u32[]{:S(2)}) collective-permute-start(bf16[128,1024]{1,0:T(8,128)(2,1)} %param.17), channel_id=1, source_target_pairs={{0,1},{1,2},{2,3},{3,0},{4,5},{5,6},{6,7},{7,4},{8,9},{9,10},{10,1... | collective-permute-start | bytes 786440 | tf_op jit(solution)/shard_map/ppermute | solution.py:25
  1.9 1.2 %collective-permute-start.1 = (bf16[128,1024]{1,0:T(8,128)(2,1)}, bf16[128,1024]{1,0:T(8,128)(2,1)S(1)}, u32[]{:S(2)}, u32[]{:S(2)}) collective-permute-start(bf16[128,1024]{1,0:T(8,128)(2,1)} %param.17), channel_id=1, source_target_pairs={{0,2},{1,3},{2,0},{3,1},{4,6},{5,7},{6,4},{7,5},{8,10},{9,11},{10,... | collective-permute-start | bytes 786440 | tf_op jit(solution)/shard_map/ppermute | solution.py:25
  3.1 1.2 %collective-permute-start.2 = (bf16[128,1024]{1,0:T(8,128)(2,1)}, bf16[128,1024]{1,0:T(8,128)(2,1)S(1)}, u32[]{:S(2)}, u32[]{:S(2)}) collective-permute-start(bf16[128,1024]{1,0:T(8,128)(2,1)} %param.17), channel_id=1, source_target_pairs={{0,3},{1,0},{2,1},{3,2},{4,7},{5,4},{6,5},{7,6},{8,11},{9,8},{10,9... | collective-permute-start | bytes 786440 | tf_op jit(solution)/shard_map/ppermute | solution.py:25
  4.3 1.1 %copy.52 = bf16[128,1024]{0,1:T(8,128)(2,1)S(1)} copy(bf16[128,1024]{1,0:T(8,128)(2,1)} %param.14) | data formatting | bytes 524288 | tf_op args[1]
  5.4 1.1 %copy.53 = bf16[128,1024]{0,1:T(8,128)(2,1)S(1)} copy(bf16[128,1024]{1,0:T(8,128)(2,1)} %param.15) | data formatting | bytes 524288 | tf_op args[2]
  6.6 1.2 %copy.54 = bf16[128,1024]{0,1:T(8,128)(2,1)S(1)} copy(bf16[128,1024]{1,0:T(8,128)(2,1)} %param.19) | data formatting | bytes 524288 | tf_op args[6]
  7.9 1.0 %copy.55 = bf16[8,2,128,128]{3,2,1,0:T(8,128)(2,1)} copy(bf16[8,2,128,128]{2,3,0,1:T(8,128)(2,1)S(1)} %pad_maximum_fusion.4) | data formatting | bytes 1048576 | tf_op jit(solution)/shard_map/stack | solution.py:211
  8.9 6.4 %all-to-all-start = ((bf16[8,2,128,128]{3,2,1,0:T(8,128)(2,1)}), bf16[8,2,128,128]{3,2,1,0:T(8,128)(2,1)S(1)}, u32[]{:S(2)}, u32[]{:S(2)}) async-start(bf16[8,2,128,128]{3,2,1,0:T(8,128)(2,1)} %copy.55), calls=%async_computation | async-start | bytes 1048576 | tf_op jit(solution)/shard_map/all_to_all | solution.py:147
  15.3 0.3 collective-permute-done.1
  15.6 0.1 pad_maximum_fusion.1
  15.9 0.7 copy-done.3
  16.6 6.3 %fusion.12 = (bf16[128,1024]{1,0:T(8,128)(2,1)S(1)}, f32[128,1024]{1,0:T(8,128)S(1)}) fusion(bf16[128,1024]{1,0:T(8,128)(2,1)S(1)} %copy-done.3, bf16[1024,4096]{1,0:T(8,128)(2,1)} %param.18, bf16[128,1024]{1,0:T(8,128)(2,1)S(1)} %get-tuple-element.34, bf16[128,1024]{1,0:T(8,128)(2,1)S(1)} %get-tuple-element.35, ...), kind=kOutput, calls=%fused_computation.73 | convolution fusion | flops 1078329344 | bytes 10485760 | tf_op jit(solution)/shard_map/dot_general | solution.py:33
  22.9 0.9 %fusion.13 = (bf16[1,128,1024]{2,1,0:T(8,128)(2,1)S(1)}, bf16[128,1024]{1,0:T(8,128)(2,1)}) fusion(bf16[128,1024]{1,0:T(8,128)(2,1)S(1)} %get-tuple-element.95, f32[128,1024]{1,0:T(8,128)S(1)} %get-tuple-element.96, bf16[128,1024]{1,0:T(8,128)(2,1)S(1)} %copy-done.3, bf16[128,1024]{1,0:T(8,128)(2,1)S(1)} %copy-done.4), kind=kLoop, calls=%fused_computation.74 | loop fusion | flops 1048576 | bytes 1835008 | tf_op jit(solution)/shard_map/stack | solution.py:217
  23.8 0.1 fusion.14
  23.9 1.8 %collective-permute-start.3 = (bf16[2,128,128]{2,1,0:T(8,128)(2,1)S(1)}, bf16[2,128,128]{2,1,0:T(8,128)(2,1)S(1)}, u32[]{:S(2)}, u32[]{:S(2)}) collective-permute-start(bf16[2,128,128]{2,1,0:T(8,128)(2,1)S(1)} %get-tuple-element.66), channel_id=1, source_target_pairs={{0,4},{4,8},{8,12},{12,16},{16,20},{20,24},{24,28},{28,0},{1,5},{5... | collective-permute-start | bytes 196616 | tf_op jit(solution)/shard_map/ppermute | solution.py:176
  25.8 1.4 %collective-permute-start.4 = (bf16[2,128,128]{2,1,0:T(8,128)(2,1)S(1)}, bf16[2,128,128]{2,1,0:T(8,128)(2,1)S(1)}, u32[]{:S(2)}, u32[]{:S(2)}) collective-permute-start(bf16[2,128,128]{2,1,0:T(8,128)(2,1)S(1)} %get-tuple-element.67), channel_id=1, source_target_pairs={{0,8},{4,12},{8,16},{12,20},{16,24},{20,28},{24,0},{28,4},{1,9},{5... | collective-permute-start | bytes 196616 | tf_op jit(solution)/shard_map/ppermute | solution.py:176
  27.1 1.4 %collective-permute-start.6 = (bf16[2,128,128]{2,1,0:T(8,128)(2,1)S(1)}, bf16[2,128,128]{2,1,0:T(8,128)(2,1)S(1)}, u32[]{:S(2)}, u32[]{:S(2)}) collective-permute-start(bf16[2,128,128]{2,1,0:T(8,128)(2,1)S(1)} %get-tuple-element.69), channel_id=1, source_target_pairs={{0,16},{4,20},{8,24},{12,28},{16,0},{20,4},{24,8},{28,12},{1,17},{... | collective-permute-start | bytes 196616 | tf_op jit(solution)/shard_map/ppermute | solution.py:176
  28.5 1.6 %collective-permute-start.7 = (bf16[2,128,128]{2,1,0:T(8,128)(2,1)S(1)}, bf16[2,128,128]{2,1,0:T(8,128)(2,1)S(1)}, u32[]{:S(2)}, u32[]{:S(2)}) collective-permute-start(bf16[2,128,128]{2,1,0:T(8,128)(2,1)S(1)} %get-tuple-element.70), channel_id=1, source_target_pairs={{0,20},{4,24},{8,28},{12,0},{16,4},{20,8},{24,12},{28,16},{1,21},{... | collective-permute-start | bytes 196616 | tf_op jit(solution)/shard_map/ppermute | solution.py:176
  30.1 1.2 %collective-permute-start.8 = (bf16[2,128,128]{2,1,0:T(8,128)(2,1)S(1)}, bf16[2,128,128]{2,1,0:T(8,128)(2,1)S(1)}, u32[]{:S(2)}, u32[]{:S(2)}) collective-permute-start(bf16[2,128,128]{2,1,0:T(8,128)(2,1)S(1)} %fusion.21), channel_id=1, source_target_pairs={{0,24},{4,28},{8,0},{12,4},{16,8},{20,12},{24,16},{28,20},{1,25},{... | collective-permute-start | bytes 196616 | tf_op jit(solution)/shard_map/ppermute | solution.py:176
  31.4 0.4 collective-permute-start.9
  31.8 5.1 %collective-permute-done.5 = bf16[2,128,128]{2,1,0:T(8,128)(2,1)S(1)} collective-permute-done((bf16[2,128,128]{2,1,0:T(8,128)(2,1)S(1)}, bf16[2,128,128]{2,1,0:T(8,128)(2,1)S(1)}, u32[]{:S(2)}, u32[]{:S(2)}) %collective-permute-start.5) | collective-permute-done | bytes 65568 | tf_op jit(solution)/shard_map/ppermute | solution.py:176
  36.9 1.4 %collective-permute-done.6 = bf16[2,128,128]{2,1,0:T(8,128)(2,1)S(1)} collective-permute-done((bf16[2,128,128]{2,1,0:T(8,128)(2,1)S(1)}, bf16[2,128,128]{2,1,0:T(8,128)(2,1)S(1)}, u32[]{:S(2)}, u32[]{:S(2)}) %collective-permute-start.6) | collective-permute-done | bytes 65568 | tf_op jit(solution)/shard_map/ppermute | solution.py:176
  38.3 1.3 %collective-permute-done.8 = bf16[2,128,128]{2,1,0:T(8,128)(2,1)S(1)} collective-permute-done((bf16[2,128,128]{2,1,0:T(8,128)(2,1)S(1)}, bf16[2,128,128]{2,1,0:T(8,128)(2,1)S(1)}, u32[]{:S(2)}, u32[]{:S(2)}) %collective-permute-start.8) | collective-permute-done | bytes 65568 | tf_op jit(solution)/shard_map/ppermute | solution.py:176
  39.6 0.5 collective-permute-done.9
  40.6 0.1 pad_maximum_fusion.2
  40.7 0.6 copy-done.8
  41.3 0.7 convolution_bitcast_fusion
  42.1 0.1 copy-done.7
  42.2 0.6 convolution_bitcast_fusion.1
  42.8 0.6 slice_add_fusion.3
  43.5 0.2 fusion.11
  43.8 0.4 add_add_fusion.2
  44.2 0.4 subtract_add_fusion.1
  44.6 0.1 slice_bitcast_fusion.16
  44.8 0.4 add_add_fusion.1
  45.2 0.4 subtract_add_fusion
  45.6 0.2 fusion.32
  46.1 0.1 pad_maximum_fusion
  46.2 0.1 bitcast_convert_fusion
  46.3 0.3 fusion
  46.7 0.6 copy-done.2
  47.2 0.5 fusion.30
  47.7 0.5 fusion.31
  48.2 0.4 copy-done.6
  48.6 0.5 add_add_fusion
  49.1 0.2 copy-done.9
  49.3 0.3 multiply_add_fusion
  49.8 0.9 %fusion.9 = f32[8,128,128]{1,2,0:T(8,128)} fusion(f32[8,256,128]{1,2,0:T(8,128)S(1)} %slice_bitcast_fusion, f32[7,128,128]{1,2,0:T(8,128)S(1)} %slice.483), kind=kLoop, calls=%fused_computation.57 | loop fusion | flops 262144 | bytes 1507328 | tf_op jit(solution)/shard_map/mul | solution.py:132
  50.7 3.8 %all-to-all-start.1 = ((f32[8,128,128]{1,2,0:T(8,128)}), f32[8,128,128]{1,2,0:T(8,128)S(1)}, u32[]{:S(2)}, u32[]{:S(2)}) async-start(f32[8,128,128]{1,2,0:T(8,128)} %fusion.9), calls=%async_computation.1 | async-start | bytes 1048576 | tf_op jit(solution)/shard_map/all_to_all | solution.py:147
  54.6 0.1 copy.59
  54.7 1.5 %collective-permute-start.10 = (f32[1,128,128]{2,1,0:T(8,128)S(1)}, f32[1,128,128]{2,1,0:T(8,128)S(1)}, u32[]{:S(2)}, u32[]{:S(2)}) collective-permute-start(f32[1,128,128]{2,1,0:T(8,128)S(1)} %bitcast.241), channel_id=1, source_target_pairs={{0,4},{4,8},{8,12},{12,16},{16,20},{20,24},{24,28},{28,0},{1,5},{5... | collective-permute-start | bytes 196616 | tf_op jit(solution)/shard_map/ppermute | solution.py:195
  56.3 1.2 %collective-permute-start.11 = (f32[1,128,128]{2,1,0:T(8,128)S(1)}, f32[1,128,128]{2,1,0:T(8,128)S(1)}, u32[]{:S(2)}, u32[]{:S(2)}) collective-permute-start(f32[1,128,128]{2,1,0:T(8,128)S(1)} %bitcast.240), channel_id=1, source_target_pairs={{0,8},{4,12},{8,16},{12,20},{16,24},{20,28},{24,0},{28,4},{1,9},{5... | collective-permute-start | bytes 196616 | tf_op jit(solution)/shard_map/ppermute | solution.py:195
  57.6 0.3 collective-permute-start.12
  58.0 1.4 %collective-permute-start.13 = (f32[1,128,128]{2,1,0:T(8,128)S(1)}, f32[1,128,128]{2,1,0:T(8,128)S(1)}, u32[]{:S(2)}, u32[]{:S(2)}) collective-permute-start(f32[1,128,128]{2,1,0:T(8,128)S(1)} %bitcast.237), channel_id=1, source_target_pairs={{0,16},{4,20},{8,24},{12,28},{16,0},{20,4},{24,8},{28,12},{1,17},{... | collective-permute-start | bytes 196616 | tf_op jit(solution)/shard_map/ppermute | solution.py:195
  59.5 1.7 %collective-permute-start.14 = (f32[1,128,128]{2,1,0:T(8,128)S(1)}, f32[1,128,128]{2,1,0:T(8,128)S(1)}, u32[]{:S(2)}, u32[]{:S(2)}) collective-permute-start(f32[1,128,128]{2,1,0:T(8,128)S(1)} %bitcast.236), channel_id=1, source_target_pairs={{0,20},{4,24},{8,28},{12,0},{16,4},{20,8},{24,12},{28,16},{1,21},{... | collective-permute-start | bytes 196616 | tf_op jit(solution)/shard_map/ppermute | solution.py:195
  61.3 0.1 copy.65
  61.4 11.8 %collective-permute-done.10 = f32[1,128,128]{2,1,0:T(8,128)S(1)} collective-permute-done((f32[1,128,128]{2,1,0:T(8,128)S(1)}, f32[1,128,128]{2,1,0:T(8,128)S(1)}, u32[]{:S(2)}, u32[]{:S(2)}) %collective-permute-start.10) | collective-permute-done | bytes 65568 | tf_op jit(solution)/shard_map/ppermute | solution.py:195
  73.2 1.4 %collective-permute-done.11 = f32[1,128,128]{2,1,0:T(8,128)S(1)} collective-permute-done((f32[1,128,128]{2,1,0:T(8,128)S(1)}, f32[1,128,128]{2,1,0:T(8,128)S(1)}, u32[]{:S(2)}, u32[]{:S(2)}) %collective-permute-start.11) | collective-permute-done | bytes 65568 | tf_op jit(solution)/shard_map/ppermute | solution.py:195
  74.6 1.4 %collective-permute-done.12 = f32[1,128,128]{2,1,0:T(8,128)S(1)} collective-permute-done((f32[1,128,128]{2,1,0:T(8,128)S(1)}, f32[1,128,128]{2,1,0:T(8,128)S(1)}, u32[]{:S(2)}, u32[]{:S(2)}) %collective-permute-start.12) | collective-permute-done | bytes 65568 | tf_op jit(solution)/shard_map/ppermute | solution.py:195
  76.0 1.4 %collective-permute-done.13 = f32[1,128,128]{2,1,0:T(8,128)S(1)} collective-permute-done((f32[1,128,128]{2,1,0:T(8,128)S(1)}, f32[1,128,128]{2,1,0:T(8,128)S(1)}, u32[]{:S(2)}, u32[]{:S(2)}) %collective-permute-start.13) | collective-permute-done | bytes 65568 | tf_op jit(solution)/shard_map/ppermute | solution.py:195
  77.5 1.3 %collective-permute-done.15 = f32[1,128,128]{2,1,0:T(8,128)S(1)} collective-permute-done((f32[1,128,128]{2,1,0:T(8,128)S(1)}, f32[1,128,128]{2,1,0:T(8,128)S(1)}, u32[]{:S(2)}, u32[]{:S(2)}) %collective-permute-start.15) | collective-permute-done | bytes 65568 | tf_op jit(solution)/shard_map/ppermute | solution.py:195
  78.8 0.5 collective-permute-done.16
  79.3 0.9 %multiply_convert_fusion = (bf16[128,1024]{1,0:T(8,128)(2,1)}, bf16[128,1024]{1,0:T(8,128)(2,1)}) fusion(f32[128,1024]{1,0:T(8,128)S(1)} %bitcast_dynamic-update-slice_fusion, bf16[128,1024]{1,0:T(8,128)(2,1)S(1)} %copy-done.1, bf16[128,1024]{1,0:T(8,128)(2,1)S(1)} %copy-done), kind=kLoop, calls=%fused_computation.63 | loop fusion | flops 786432 | bytes 1572864 | tf_op jit(solution)/shard_map/convert_element_type | solution.py:229
  80.2 1.0 %copy.70 = f32[128,1024]{1,0:T(8,128)} copy(f32[128,1024]{0,1:T(8,128)S(1)} %bitcast.224) | data formatting | bytes 1048576 | tf_op jit(solution)/shard_map/reshape | solution.py:143
  (80 shorter events, 1.9 us)
Async XLA Ops:
  0.6 14.7 %collective-permute-start = (bf16[128,1024]{1,0:T(8,128)(2,1)}, bf16[128,1024]{1,0:T(8,128)(2,1)S(1)}, u32[]{:S(2)}, u32[]{:S(2)}) collective-permute-start(bf16[128,1024]{1,0:T(8,128)(2,1)} %param.17), channel_id=1, source_target_pairs={{0,1},{1,2},{2,3},{3,0},{4,5},{5,6},{6,7},{7,4},{8,9},{9,10},{10,1... | collective-permute-start | bytes 786440 | tf_op jit(solution)/shard_map/ppermute | solution.py:25
  1.9 13.7 %collective-permute-start.1 = (bf16[128,1024]{1,0:T(8,128)(2,1)}, bf16[128,1024]{1,0:T(8,128)(2,1)S(1)}, u32[]{:S(2)}, u32[]{:S(2)}) collective-permute-start(bf16[128,1024]{1,0:T(8,128)(2,1)} %param.17), channel_id=1, source_target_pairs={{0,2},{1,3},{2,0},{3,1},{4,6},{5,7},{6,4},{7,5},{8,10},{9,11},{10,... | collective-permute-start | bytes 786440 | tf_op jit(solution)/shard_map/ppermute | solution.py:25
  3.1 12.5 %collective-permute-start.2 = (bf16[128,1024]{1,0:T(8,128)(2,1)}, bf16[128,1024]{1,0:T(8,128)(2,1)S(1)}, u32[]{:S(2)}, u32[]{:S(2)}) collective-permute-start(bf16[128,1024]{1,0:T(8,128)(2,1)} %param.17), channel_id=1, source_target_pairs={{0,3},{1,0},{2,1},{3,2},{4,7},{5,4},{6,5},{7,6},{8,11},{9,8},{10,9... | collective-permute-start | bytes 786440 | tf_op jit(solution)/shard_map/ppermute | solution.py:25
  6.6 9.0 %copy-start.5 = (bf16[128,1024]{1,0:T(8,128)(2,1)S(1)}, bf16[128,1024]{1,0:T(8,128)(2,1)}, u32[]{:S(2)}) copy-start(bf16[128,1024]{1,0:T(8,128)(2,1)} %param.17) | copy-start | bytes 786436
  8.9 31.6 %all-to-all-start = ((bf16[8,2,128,128]{3,2,1,0:T(8,128)(2,1)}), bf16[8,2,128,128]{3,2,1,0:T(8,128)(2,1)S(1)}, u32[]{:S(2)}, u32[]{:S(2)}) async-start(bf16[8,2,128,128]{3,2,1,0:T(8,128)(2,1)} %copy.55), calls=%async_computation | async-start | bytes 1048576 | tf_op jit(solution)/shard_map/all_to_all | solution.py:147
  15.6 1.0 %copy-start.3 = (bf16[128,1024]{1,0:T(8,128)(2,1)S(1)}, bf16[128,1024]{1,0:T(8,128)(2,1)}, u32[]{:S(2)}) copy-start(bf16[128,1024]{1,0:T(8,128)(2,1)} %param.13) | copy-start | bytes 786436
  16.6 6.3 %copy-start.4 = (bf16[128,1024]{1,0:T(8,128)(2,1)S(1)}, bf16[128,1024]{1,0:T(8,128)(2,1)}, u32[]{:S(2)}) copy-start(bf16[128,1024]{1,0:T(8,128)(2,1)} %param.16) | copy-start | bytes 786436
  23.9 6.2 %collective-permute-start.3 = (bf16[2,128,128]{2,1,0:T(8,128)(2,1)S(1)}, bf16[2,128,128]{2,1,0:T(8,128)(2,1)S(1)}, u32[]{:S(2)}, u32[]{:S(2)}) collective-permute-start(bf16[2,128,128]{2,1,0:T(8,128)(2,1)S(1)} %get-tuple-element.66), channel_id=1, source_target_pairs={{0,4},{4,8},{8,12},{12,16},{16,20},{20,24},{24,28},{28,0},{1,5},{5... | collective-permute-start | bytes 196616 | tf_op jit(solution)/shard_map/ppermute | solution.py:176
  25.8 5.6 %collective-permute-start.4 = (bf16[2,128,128]{2,1,0:T(8,128)(2,1)S(1)}, bf16[2,128,128]{2,1,0:T(8,128)(2,1)S(1)}, u32[]{:S(2)}, u32[]{:S(2)}) collective-permute-start(bf16[2,128,128]{2,1,0:T(8,128)(2,1)S(1)} %get-tuple-element.67), channel_id=1, source_target_pairs={{0,8},{4,12},{8,16},{12,20},{16,24},{20,28},{24,0},{28,4},{1,9},{5... | collective-permute-start | bytes 196616 | tf_op jit(solution)/shard_map/ppermute | solution.py:176
  27.1 9.8 %collective-permute-start.5 = (bf16[2,128,128]{2,1,0:T(8,128)(2,1)S(1)}, bf16[2,128,128]{2,1,0:T(8,128)(2,1)S(1)}, u32[]{:S(2)}, u32[]{:S(2)}) collective-permute-start(bf16[2,128,128]{2,1,0:T(8,128)(2,1)S(1)} %get-tuple-element.68), channel_id=1, source_target_pairs={{0,12},{4,16},{8,20},{12,24},{16,28},{20,0},{24,4},{28,8},{1,13},{... | collective-permute-start | bytes 196616 | tf_op jit(solution)/shard_map/ppermute | solution.py:176
  27.1 11.2 %collective-permute-start.6 = (bf16[2,128,128]{2,1,0:T(8,128)(2,1)S(1)}, bf16[2,128,128]{2,1,0:T(8,128)(2,1)S(1)}, u32[]{:S(2)}, u32[]{:S(2)}) collective-permute-start(bf16[2,128,128]{2,1,0:T(8,128)(2,1)S(1)} %get-tuple-element.69), channel_id=1, source_target_pairs={{0,16},{4,20},{8,24},{12,28},{16,0},{20,4},{24,8},{28,12},{1,17},{... | collective-permute-start | bytes 196616 | tf_op jit(solution)/shard_map/ppermute | solution.py:176
  28.5 9.8 %collective-permute-start.7 = (bf16[2,128,128]{2,1,0:T(8,128)(2,1)S(1)}, bf16[2,128,128]{2,1,0:T(8,128)(2,1)S(1)}, u32[]{:S(2)}, u32[]{:S(2)}) collective-permute-start(bf16[2,128,128]{2,1,0:T(8,128)(2,1)S(1)} %get-tuple-element.70), channel_id=1, source_target_pairs={{0,20},{4,24},{8,28},{12,0},{16,4},{20,8},{24,12},{28,16},{1,21},{... | collective-permute-start | bytes 196616 | tf_op jit(solution)/shard_map/ppermute | solution.py:176
  30.1 9.5 %collective-permute-start.8 = (bf16[2,128,128]{2,1,0:T(8,128)(2,1)S(1)}, bf16[2,128,128]{2,1,0:T(8,128)(2,1)S(1)}, u32[]{:S(2)}, u32[]{:S(2)}) collective-permute-start(bf16[2,128,128]{2,1,0:T(8,128)(2,1)S(1)} %fusion.21), channel_id=1, source_target_pairs={{0,24},{4,28},{8,0},{12,4},{16,8},{20,12},{24,16},{28,20},{1,25},{... | collective-permute-start | bytes 196616 | tf_op jit(solution)/shard_map/ppermute | solution.py:176
  31.4 8.8 %collective-permute-start.9 = (bf16[2,128,128]{2,1,0:T(8,128)(2,1)S(1)}, bf16[2,128,128]{2,1,0:T(8,128)(2,1)S(1)}, u32[]{:S(2)}, u32[]{:S(2)}) collective-permute-start(bf16[2,128,128]{2,1,0:T(8,128)(2,1)S(1)} %get-tuple-element.65), channel_id=1, source_target_pairs={{0,28},{4,0},{8,4},{12,8},{16,12},{20,16},{24,20},{28,24},{1,29},{... | collective-permute-start | bytes 196616 | tf_op jit(solution)/shard_map/ppermute | solution.py:176
  40.5 0.8 %copy-start.8 = (bf16[256,128,1]{1,0,2:T(8,128)(2,1)S(1)}, bf16[256,128,1]{1,0,2:T(8,128)(2,1)}, u32[]{:S(2)}) copy-start(bf16[256,128,1]{1,0,2:T(8,128)(2,1)} %constant.274) | copy-start | bytes 196612
  41.3 0.8 %copy-start.7 = (bf16[256,128,1]{1,0,2:T(8,128)(2,1)S(1)}, bf16[256,128,1]{1,0,2:T(8,128)(2,1)}, u32[]{:S(2)}) copy-start(bf16[256,128,1]{1,0,2:T(8,128)(2,1)} %constant.275) | copy-start | bytes 196612
  44.8 0.8 %copy-start.10 = (bf16[128,1,1]{0,1,2:T(2,128)(2,1)S(1)}, bf16[128,1,1]{0,1,2:T(2,128)(2,1)}, u32[]{:S(2)}) copy-start(bf16[128,1,1]{0,1,2:T(2,128)(2,1)} %constant.278) | copy-start | bytes 772
  46.3 0.9 %copy-start.2 = (bf16[256,256,1]{1,0,2:T(8,128)(2,1)S(1)}, bf16[256,256,1]{1,0,2:T(8,128)(2,1)}, u32[]{:S(2)}) copy-start(bf16[256,256,1]{1,0,2:T(8,128)(2,1)} %constant.276) | copy-start | bytes 393220
  47.7 0.9 %copy-start.6 = (bf16[256,256,1]{1,0,2:T(8,128)(2,1)S(1)}, bf16[256,256,1]{1,0,2:T(8,128)(2,1)}, u32[]{:S(2)}) copy-start(bf16[256,256,1]{1,0,2:T(8,128)(2,1)} %constant.277) | copy-start | bytes 393220
  48.6 0.7 copy-start.9
  50.7 29.6 %all-to-all-start.1 = ((f32[8,128,128]{1,2,0:T(8,128)}), f32[8,128,128]{1,2,0:T(8,128)S(1)}, u32[]{:S(2)}, u32[]{:S(2)}) async-start(f32[8,128,128]{1,2,0:T(8,128)} %fusion.9), calls=%async_computation.1 | async-start | bytes 1048576 | tf_op jit(solution)/shard_map/all_to_all | solution.py:147
  54.4 24.9 %copy-start = (bf16[128,1024]{1,0:T(8,128)(2,1)S(1)}, bf16[128,1024]{1,0:T(8,128)(2,1)}, u32[]{:S(2)}) copy-start(bf16[128,1024]{1,0:T(8,128)(2,1)} %param.15) | copy-start | bytes 786436
  54.4 24.9 %copy-start.1 = (bf16[128,1024]{1,0:T(8,128)(2,1)S(1)}, bf16[128,1024]{1,0:T(8,128)(2,1)}, u32[]{:S(2)}) copy-start(bf16[128,1024]{1,0:T(8,128)(2,1)} %param.14) | copy-start | bytes 786436
  54.7 18.6 %collective-permute-start.10 = (f32[1,128,128]{2,1,0:T(8,128)S(1)}, f32[1,128,128]{2,1,0:T(8,128)S(1)}, u32[]{:S(2)}, u32[]{:S(2)}) collective-permute-start(f32[1,128,128]{2,1,0:T(8,128)S(1)} %bitcast.241), channel_id=1, source_target_pairs={{0,4},{4,8},{8,12},{12,16},{16,20},{20,24},{24,28},{28,0},{1,5},{5... | collective-permute-start | bytes 196616 | tf_op jit(solution)/shard_map/ppermute | solution.py:195
  56.3 18.3 %collective-permute-start.11 = (f32[1,128,128]{2,1,0:T(8,128)S(1)}, f32[1,128,128]{2,1,0:T(8,128)S(1)}, u32[]{:S(2)}, u32[]{:S(2)}) collective-permute-start(f32[1,128,128]{2,1,0:T(8,128)S(1)} %bitcast.240), channel_id=1, source_target_pairs={{0,8},{4,12},{8,16},{12,20},{16,24},{20,28},{24,0},{28,4},{1,9},{5... | collective-permute-start | bytes 196616 | tf_op jit(solution)/shard_map/ppermute | solution.py:195
  57.6 18.4 %collective-permute-start.12 = (f32[1,128,128]{2,1,0:T(8,128)S(1)}, f32[1,128,128]{2,1,0:T(8,128)S(1)}, u32[]{:S(2)}, u32[]{:S(2)}) collective-permute-start(f32[1,128,128]{2,1,0:T(8,128)S(1)} %bitcast.238), channel_id=1, source_target_pairs={{0,12},{4,16},{8,20},{12,24},{16,28},{20,0},{24,4},{28,8},{1,13},{... | collective-permute-start | bytes 196616 | tf_op jit(solution)/shard_map/ppermute | solution.py:195
  58.0 19.5 %collective-permute-start.13 = (f32[1,128,128]{2,1,0:T(8,128)S(1)}, f32[1,128,128]{2,1,0:T(8,128)S(1)}, u32[]{:S(2)}, u32[]{:S(2)}) collective-permute-start(f32[1,128,128]{2,1,0:T(8,128)S(1)} %bitcast.237), channel_id=1, source_target_pairs={{0,16},{4,20},{8,24},{12,28},{16,0},{20,4},{24,8},{28,12},{1,17},{... | collective-permute-start | bytes 196616 | tf_op jit(solution)/shard_map/ppermute | solution.py:195
  59.5 17.9 %collective-permute-start.14 = (f32[1,128,128]{2,1,0:T(8,128)S(1)}, f32[1,128,128]{2,1,0:T(8,128)S(1)}, u32[]{:S(2)}, u32[]{:S(2)}) collective-permute-start(f32[1,128,128]{2,1,0:T(8,128)S(1)} %bitcast.236), channel_id=1, source_target_pairs={{0,20},{4,24},{8,28},{12,0},{16,4},{20,8},{24,12},{28,16},{1,21},{... | collective-permute-start | bytes 196616 | tf_op jit(solution)/shard_map/ppermute | solution.py:195
  73.2 5.5 %collective-permute-start.15 = (f32[1,128,128]{2,1,0:T(8,128)S(1)}, f32[1,128,128]{2,1,0:T(8,128)S(1)}, u32[]{:S(2)}, u32[]{:S(2)}) collective-permute-start(f32[1,128,128]{2,1,0:T(8,128)S(1)} %bitcast.239), channel_id=1, source_target_pairs={{0,24},{4,28},{8,0},{12,4},{16,8},{20,12},{24,16},{28,20},{1,25},{... | collective-permute-start | bytes 196616 | tf_op jit(solution)/shard_map/ppermute | solution.py:195
  74.6 4.7 %collective-permute-start.16 = (f32[1,128,128]{2,1,0:T(8,128)S(1)}, f32[1,128,128]{2,1,0:T(8,128)S(1)}, u32[]{:S(2)}, u32[]{:S(2)}) collective-permute-start(f32[1,128,128]{2,1,0:T(8,128)S(1)} %bitcast.235), channel_id=1, source_target_pairs={{0,28},{4,0},{8,4},{12,8},{16,12},{20,16},{24,20},{28,24},{1,29},{... | collective-permute-start | bytes 196616 | tf_op jit(solution)/shard_map/ppermute | solution.py:195

commit v18 on v14

--- a/solution.py
+++ b/solution.py
@@ -19,14 +19,16 @@
 def gather_matmul(out_grad, out_weight):
     count = lax.axis_size("tp")
     me = lax.axis_index("tp")
+    paired = count & (count - 1) == 0
     pieces = [out_grad]
-    for shift in range(1, count):
-        pieces.append(
-            lax.ppermute(out_grad, "tp", [(i, (i + shift) % count) for i in range(count)])
-        )
+    for step in range(1, count):
+        pairs = [(i, i ^ step if paired else (i + step) % count) for i in range(count)]
+        pieces.append(lax.ppermute(out_grad, "tp", pairs))
     stacked = jnp.stack(pieces)
     ordered = [
-        lax.dynamic_index_in_dim(stacked, (me - source) % count, 0, keepdims=False)
+        lax.dynamic_index_in_dim(
+            stacked, me ^ source if paired else (me - source) % count, 0, keepdims=False
+        )
         for source in range(count)
     ]
     gathered = jnp.concatenate(ordered, axis=1)

time: 76.7 us -> 75.6 us (0.986)
  waiting for transfers between devices: 26.3 us -> 24.7 us
    ppermute x7, waiting for transfers between devices: 8.29 us -> 7.11 us  [scatter_lanes(): lax.ppermute(chunk, 'ctx', [(i, (i + shift) % count) for i in range(count)])]
    ppermute x7, starting transfers between devices: 7.81 us -> 8.96 us  [scatter_lanes(): lax.ppermute(chunk, 'ctx', [(i, (i + shift) % count) for i in range(count)])]
    ppermute x3, starting transfers between devices: 3.66 us -> 2.71 us  [gather_matmul(): pieces.append(lax.ppermute(out_grad, 'tp', pairs))]
  transfers between devices with their start and end apart: 18 -> 18, of which waited for: 11 -> 7; matrix products, arithmetic and copies ran while one was open for 18% -> 18% of each run, Pallas kernels for 0% -> 0%
where the time goes in v18:
time: 75.6 us; the launch traced here: 74.2 us
  waiting for transfers between devices  24.7 us (33%)
  starting transfers between devices  23.9 us (32%)
  matrix products  9.26 us (12%)
  local copies, waits for them, and re-layouts  8.84 us (12%)
  other arithmetic  6.18 us (8%)
  between operations  1.3 us (2%)
    ppermute x7, waiting for transfers between devices, gather_lanes(): lax.ppermute(chunk, 'ctx', [(i, (i + shift) % count) for i in range(count)])  17.2 us
    ppermute x7, starting transfers between devices, scatter_lanes(): lax.ppermute(chunk, 'ctx', [(i, (i + shift) % count) for i in range(count)])  8.96 us
    ppermute x7, waiting for transfers between devices, scatter_lanes(): lax.ppermute(chunk, 'ctx', [(i, (i + shift) % count) for i in range(count)])  7.11 us
    all_to_all x1, starting transfers between devices, all_to_all_ctx(): return lax.all_to_all(stacked, 'ctx', 0, 0, tiled=True)  6.44 us
    dot_general x1, matrix products, gather_matmul(): lax.dot_general(gathered, out_weight, (((1,), (1,)), ((), ())), preferred...  6.3 us
    unnamed x40, local copies, waits for them, and re-layouts  6.25 us
    ppermute x7, starting transfers between devices, gather_lanes(): lax.ppermute(chunk, 'ctx', [(i, (i + shift) % count) for i in range(count)])  5.83 us
    dot_general x5, matrix products, table_times(): jnp.einsum('kn,snc->skc', table, signal, preferred_element_type=jnp.float32)  2.72 us
  transfers between devices with their start and end apart: 18, of which 7 were waited for; matrix products, arithmetic and copies ran while one was open for 18% of the time, Pallas kernels for 0%

profile of v18, /device:TPU:9, one launch (start us, length us, event | category | flops | bytes accessed | tf_op | source)
XLA Modules:
  0.0 74.2 jit_solution(2892585929893397121)
XLA Ops:
  0.6 1.3 %collective-permute-start = (bf16[128,1024]{1,0:T(8,128)(2,1)}, bf16[128,1024]{1,0:T(8,128)(2,1)S(1)}, u32[]{:S(2)}, u32[]{:S(2)}) collective-permute-start(bf16[128,1024]{1,0:T(8,128)(2,1)} %param.17), channel_id=1, source_target_pairs={{0,1},{1,0},{2,3},{3,2},{4,5},{5,4},{6,7},{7,6},{8,9},{9,8},{10,11... | collective-permute-start | bytes 786440 | tf_op jit(solution)/shard_map/ppermute | solution.py:26
  1.9 1.2 %collective-permute-start.1 = (bf16[128,1024]{1,0:T(8,128)(2,1)}, bf16[128,1024]{1,0:T(8,128)(2,1)S(1)}, u32[]{:S(2)}, u32[]{:S(2)}) collective-permute-start(bf16[128,1024]{1,0:T(8,128)(2,1)} %param.17), channel_id=1, source_target_pairs={{0,2},{1,3},{2,0},{3,1},{4,6},{5,7},{6,4},{7,5},{8,10},{9,11},{10,... | collective-permute-start | bytes 786440 | tf_op jit(solution)/shard_map/ppermute | solution.py:26
  3.1 0.2 collective-permute-start.2
  3.3 1.1 %copy.49 = bf16[128,1024]{0,1:T(8,128)(2,1)S(1)} copy(bf16[128,1024]{1,0:T(8,128)(2,1)} %param.14) | data formatting | bytes 524288 | tf_op args[1]
  4.5 1.1 %copy.50 = bf16[128,1024]{0,1:T(8,128)(2,1)S(1)} copy(bf16[128,1024]{1,0:T(8,128)(2,1)} %param.15) | data formatting | bytes 524288 | tf_op args[2]
  5.7 1.2 %copy.51 = bf16[128,1024]{0,1:T(8,128)(2,1)S(1)} copy(bf16[128,1024]{1,0:T(8,128)(2,1)} %param.19) | data formatting | bytes 524288 | tf_op args[6]
  6.9 1.0 %copy.52 = bf16[8,2,128,128]{3,2,1,0:T(8,128)(2,1)} copy(bf16[8,2,128,128]{2,3,0,1:T(8,128)(2,1)S(1)} %pad_maximum_fusion.4) | data formatting | bytes 1048576 | tf_op jit(solution)/shard_map/stack | solution.py:213
  7.9 6.4 %all-to-all-start = ((bf16[8,2,128,128]{3,2,1,0:T(8,128)(2,1)}), bf16[8,2,128,128]{3,2,1,0:T(8,128)(2,1)S(1)}, u32[]{:S(2)}, u32[]{:S(2)}) async-start(bf16[8,2,128,128]{3,2,1,0:T(8,128)(2,1)} %copy.52), calls=%async_computation | async-start | bytes 1048576 | tf_op jit(solution)/shard_map/all_to_all | solution.py:149
  14.4 0.3 collective-permute-done.2
  14.7 0.1 pad_maximum_fusion.1
  14.9 0.7 copy-done.4
  15.7 6.3 %fusion.13 = (bf16[128,1024]{1,0:T(8,128)(2,1)S(1)}, f32[128,1024]{1,0:T(8,128)S(1)}) fusion(bf16[128,1024]{1,0:T(8,128)(2,1)S(1)} %copy-done.4, bf16[1024,4096]{1,0:T(8,128)(2,1)} %param.18, bf16[128,1024]{1,0:T(8,128)(2,1)S(1)} %get-tuple-element.42, bf16[128,1024]{1,0:T(8,128)(2,1)S(1)} %get-tuple-element.43, ...), kind=kOutput, calls=%fused_computation.90 | convolution fusion | flops 1078329344 | bytes 10485760 | tf_op jit(solution)/shard_map/dot_general | solution.py:35
  22.0 0.9 %fusion.14 = (bf16[1,128,1024]{2,1,0:T(8,128)(2,1)S(1)}, bf16[128,1024]{1,0:T(8,128)(2,1)}) fusion(bf16[128,1024]{1,0:T(8,128)(2,1)S(1)} %get-tuple-element.109, f32[128,1024]{1,0:T(8,128)S(1)} %get-tuple-element.110, bf16[128,1024]{1,0:T(8,128)(2,1)S(1)} %copy-done.4, bf16[128,1024]{1,0:T(8,128)(2,1)S(1)} %copy-done.5), kind=kLoop, calls=%fused_computation.91 | loop fusion | flops 1048576 | bytes 1835008 | tf_op jit(solution)/shard_map/stack | solution.py:219
  22.9 0.1 fusion.23
  23.0 3.0 %collective-permute-start.3 = (bf16[2,128,128]{2,1,0:T(8,128)(2,1)S(1)}, bf16[2,128,128]{2,1,0:T(8,128)(2,1)S(1)}, u32[]{:S(2)}, u32[]{:S(2)}) collective-permute-start(bf16[2,128,128]{2,1,0:T(8,128)(2,1)S(1)} %get-tuple-element.66), channel_id=1, source_target_pairs={{0,4},{4,8},{8,12},{12,16},{16,20},{20,24},{24,28},{28,0},{1,5},{5... | collective-permute-start | bytes 196616 | tf_op jit(solution)/shard_map/ppermute | solution.py:178
  26.0 1.4 %collective-permute-start.4 = (bf16[2,128,128]{2,1,0:T(8,128)(2,1)S(1)}, bf16[2,128,128]{2,1,0:T(8,128)(2,1)S(1)}, u32[]{:S(2)}, u32[]{:S(2)}) collective-permute-start(bf16[2,128,128]{2,1,0:T(8,128)(2,1)S(1)} %get-tuple-element.67), channel_id=1, source_target_pairs={{0,8},{4,12},{8,16},{12,20},{16,24},{20,28},{24,0},{28,4},{1,9},{5... | collective-permute-start | bytes 196616 | tf_op jit(solution)/shard_map/ppermute | solution.py:178
  27.3 1.4 %collective-permute-start.6 = (bf16[2,128,128]{2,1,0:T(8,128)(2,1)S(1)}, bf16[2,128,128]{2,1,0:T(8,128)(2,1)S(1)}, u32[]{:S(2)}, u32[]{:S(2)}) collective-permute-start(bf16[2,128,128]{2,1,0:T(8,128)(2,1)S(1)} %get-tuple-element.69), channel_id=1, source_target_pairs={{0,16},{4,20},{8,24},{12,28},{16,0},{20,4},{24,8},{28,12},{1,17},{... | collective-permute-start | bytes 196616 | tf_op jit(solution)/shard_map/ppermute | solution.py:178
  28.7 1.6 %collective-permute-start.7 = (bf16[2,128,128]{2,1,0:T(8,128)(2,1)S(1)}, bf16[2,128,128]{2,1,0:T(8,128)(2,1)S(1)}, u32[]{:S(2)}, u32[]{:S(2)}) collective-permute-start(bf16[2,128,128]{2,1,0:T(8,128)(2,1)S(1)} %get-tuple-element.70), channel_id=1, source_target_pairs={{0,20},{4,24},{8,28},{12,0},{16,4},{20,8},{24,12},{28,16},{1,21},{... | collective-permute-start | bytes 196616 | tf_op jit(solution)/shard_map/ppermute | solution.py:178
  30.3 1.2 %collective-permute-start.8 = (bf16[2,128,128]{2,1,0:T(8,128)(2,1)S(1)}, bf16[2,128,128]{2,1,0:T(8,128)(2,1)S(1)}, u32[]{:S(2)}, u32[]{:S(2)}) collective-permute-start(bf16[2,128,128]{2,1,0:T(8,128)(2,1)S(1)} %fusion.30), channel_id=1, source_target_pairs={{0,24},{4,28},{8,0},{12,4},{16,8},{20,12},{24,16},{28,20},{1,25},{... | collective-permute-start | bytes 196616 | tf_op jit(solution)/shard_map/ppermute | solution.py:178
  31.6 0.4 collective-permute-start.9
  32.1 5.0 %collective-permute-done.6 = bf16[2,128,128]{2,1,0:T(8,128)(2,1)S(1)} collective-permute-done((bf16[2,128,128]{2,1,0:T(8,128)(2,1)S(1)}, bf16[2,128,128]{2,1,0:T(8,128)(2,1)S(1)}, u32[]{:S(2)}, u32[]{:S(2)}) %collective-permute-start.6) | collective-permute-done | bytes 65568 | tf_op jit(solution)/shard_map/ppermute | solution.py:178
  37.1 2.1 %collective-permute-done.8 = bf16[2,128,128]{2,1,0:T(8,128)(2,1)S(1)} collective-permute-done((bf16[2,128,128]{2,1,0:T(8,128)(2,1)S(1)}, bf16[2,128,128]{2,1,0:T(8,128)(2,1)S(1)}, u32[]{:S(2)}, u32[]{:S(2)}) %collective-permute-start.8) | collective-permute-done | bytes 65568 | tf_op jit(solution)/shard_map/ppermute | solution.py:178
  39.6 0.1 pad_maximum_fusion.3
  39.7 0.1 pad_maximum_fusion.2
  39.8 0.6 copy-done.9
  40.4 0.7 convolution_bitcast_fusion
  41.1 0.1 copy-done.8
  41.2 0.6 convolution_bitcast_fusion.1
  41.8 0.6 slice_add_fusion.3
  42.5 0.2 fusion.12
  42.9 0.4 add_add_fusion.2
  43.3 0.4 subtract_add_fusion.1
  43.7 0.1 slice_bitcast_fusion.32
  43.8 0.4 add_add_fusion.1
  44.3 0.4 subtract_add_fusion
  44.7 0.2 fusion.57
  45.1 0.1 pad_maximum_fusion
  45.3 0.1 bitcast_convert_fusion
  45.4 0.3 fusion
  45.7 0.6 copy-done.2
  46.3 0.5 fusion.55
  46.8 0.5 fusion.56
  47.3 0.4 copy-done.7
  47.7 0.5 add_add_fusion
  48.1 0.2 copy-done.10
  48.4 0.3 multiply_add_fusion
  49.0 0.1 copy.60
  49.2 0.1 copy.55
  49.3 0.1 copy.56
  49.4 1.1 %collective-permute-start.10 = (f32[2,128,128]{2,1,0:T(8,128)S(1)}, f32[2,128,128]{2,1,0:T(8,128)S(1)}, u32[]{:S(2)}, u32[]{:S(2)}) collective-permute-start(f32[2,128,128]{2,1,0:T(8,128)S(1)} %bitcast.287), channel_id=1, source_target_pairs={{0,4},{4,8},{8,12},{12,16},{16,20},{20,24},{24,28},{28,0},{1,5},{5... | collective-permute-start | bytes 393224 | tf_op jit(solution)/shard_map/ppermute | solution.py:197
  50.6 0.1 copy.57
  50.7 1.9 %collective-permute-start.11 = (f32[2,128,128]{2,1,0:T(8,128)S(1)}, f32[2,128,128]{2,1,0:T(8,128)S(1)}, u32[]{:S(2)}, u32[]{:S(2)}) collective-permute-start(f32[2,128,128]{2,1,0:T(8,128)S(1)} %bitcast.286), channel_id=1, source_target_pairs={{0,8},{4,12},{8,16},{12,20},{16,24},{20,28},{24,0},{28,4},{1,9},{5... | collective-permute-start | bytes 393224 | tf_op jit(solution)/shard_map/ppermute | solution.py:197
  52.5 0.1 copy.58
  52.6 2.2 %collective-permute-start.12 = (f32[2,128,128]{2,1,0:T(8,128)S(1)}, f32[2,128,128]{2,1,0:T(8,128)S(1)}, u32[]{:S(2)}, u32[]{:S(2)}) collective-permute-start(f32[2,128,128]{2,1,0:T(8,128)S(1)} %bitcast.285), channel_id=1, source_target_pairs={{0,12},{4,16},{8,20},{12,24},{16,28},{20,0},{24,4},{28,8},{1,13},{... | collective-permute-start | bytes 393224 | tf_op jit(solution)/shard_map/ppermute | solution.py:197
  54.8 0.1 copy.59
  54.9 0.2 collective-permute-start.13
  55.1 0.1 copy.61
  55.2 0.1 copy.62
  55.5 0.8 %collective-permute-done.10 = f32[2,128,128]{2,1,0:T(8,128)S(1)} collective-permute-done((f32[2,128,128]{2,1,0:T(8,128)S(1)}, f32[2,128,128]{2,1,0:T(8,128)S(1)}, u32[]{:S(2)}, u32[]{:S(2)}) %collective-permute-start.10) | collective-permute-done | bytes 131104 | tf_op jit(solution)/shard_map/ppermute | solution.py:197
  56.3 0.4 collective-permute-start.15
  56.7 3.5 %collective-permute-done.11 = f32[2,128,128]{2,1,0:T(8,128)S(1)} collective-permute-done((f32[2,128,128]{2,1,0:T(8,128)S(1)}, f32[2,128,128]{2,1,0:T(8,128)S(1)}, u32[]{:S(2)}, u32[]{:S(2)}) %collective-permute-start.11) | collective-permute-done | bytes 131104 | tf_op jit(solution)/shard_map/ppermute | solution.py:197
  60.2 10.1 %collective-permute-done.12 = f32[2,128,128]{2,1,0:T(8,128)S(1)} collective-permute-done((f32[2,128,128]{2,1,0:T(8,128)S(1)}, f32[2,128,128]{2,1,0:T(8,128)S(1)}, u32[]{:S(2)}, u32[]{:S(2)}) %collective-permute-start.12) | collective-permute-done | bytes 131104 | tf_op jit(solution)/shard_map/ppermute | solution.py:197
  70.3 2.8 %collective-permute-done.13 = f32[2,128,128]{2,1,0:T(8,128)S(1)} collective-permute-done((f32[2,128,128]{2,1,0:T(8,128)S(1)}, f32[2,128,128]{2,1,0:T(8,128)S(1)}, u32[]{:S(2)}, u32[]{:S(2)}) %collective-permute-start.13) | collective-permute-done | bytes 131104 | tf_op jit(solution)/shard_map/ppermute | solution.py:197
  73.3 0.9 %multiply_convert_fusion = (bf16[128,1024]{1,0:T(8,128)(2,1)}, bf16[128,1024]{1,0:T(8,128)(2,1)}) fusion(f32[128,1024]{1,0:T(8,128)S(1)} %get-tuple-element.76, bf16[128,1024]{1,0:T(8,128)(2,1)S(1)} %copy-done.1, bf16[128,1024]{1,0:T(8,128)(2,1)S(1)} %copy-done), kind=kLoop, calls=%fused_computation.80 | loop fusion | flops 786432 | bytes 1572864 | tf_op jit(solution)/shard_map/convert_element_type | solution.py:231
  (82 shorter events, 1.6 us)
Async XLA Ops:
  0.6 13.7 %collective-permute-start = (bf16[128,1024]{1,0:T(8,128)(2,1)}, bf16[128,1024]{1,0:T(8,128)(2,1)S(1)}, u32[]{:S(2)}, u32[]{:S(2)}) collective-permute-start(bf16[128,1024]{1,0:T(8,128)(2,1)} %param.17), channel_id=1, source_target_pairs={{0,1},{1,0},{2,3},{3,2},{4,5},{5,4},{6,7},{7,6},{8,9},{9,8},{10,11... | collective-permute-start | bytes 786440 | tf_op jit(solution)/shard_map/ppermute | solution.py:26
  1.9 12.5 %collective-permute-start.1 = (bf16[128,1024]{1,0:T(8,128)(2,1)}, bf16[128,1024]{1,0:T(8,128)(2,1)S(1)}, u32[]{:S(2)}, u32[]{:S(2)}) collective-permute-start(bf16[128,1024]{1,0:T(8,128)(2,1)} %param.17), channel_id=1, source_target_pairs={{0,2},{1,3},{2,0},{3,1},{4,6},{5,7},{6,4},{7,5},{8,10},{9,11},{10,... | collective-permute-start | bytes 786440 | tf_op jit(solution)/shard_map/ppermute | solution.py:26
  3.1 11.6 %collective-permute-start.2 = (bf16[128,1024]{1,0:T(8,128)(2,1)}, bf16[128,1024]{1,0:T(8,128)(2,1)S(1)}, u32[]{:S(2)}, u32[]{:S(2)}) collective-permute-start(bf16[128,1024]{1,0:T(8,128)(2,1)} %param.17), channel_id=1, source_target_pairs={{0,3},{1,2},{2,1},{3,0},{4,7},{5,6},{6,5},{7,4},{8,11},{9,10},{10,... | collective-permute-start | bytes 786440 | tf_op jit(solution)/shard_map/ppermute | solution.py:26
  5.7 9.0 %copy-start.6 = (bf16[128,1024]{1,0:T(8,128)(2,1)S(1)}, bf16[128,1024]{1,0:T(8,128)(2,1)}, u32[]{:S(2)}) copy-start(bf16[128,1024]{1,0:T(8,128)(2,1)} %param.17) | copy-start | bytes 786436
  7.9 31.6 %all-to-all-start = ((bf16[8,2,128,128]{3,2,1,0:T(8,128)(2,1)}), bf16[8,2,128,128]{3,2,1,0:T(8,128)(2,1)S(1)}, u32[]{:S(2)}, u32[]{:S(2)}) async-start(bf16[8,2,128,128]{3,2,1,0:T(8,128)(2,1)} %copy.52), calls=%async_computation | async-start | bytes 1048576 | tf_op jit(solution)/shard_map/all_to_all | solution.py:149
  14.7 1.0 %copy-start.4 = (bf16[128,1024]{1,0:T(8,128)(2,1)S(1)}, bf16[128,1024]{1,0:T(8,128)(2,1)}, u32[]{:S(2)}) copy-start(bf16[128,1024]{1,0:T(8,128)(2,1)} %param.13) | copy-start | bytes 786436
  15.7 6.3 %copy-start.5 = (bf16[128,1024]{1,0:T(8,128)(2,1)S(1)}, bf16[128,1024]{1,0:T(8,128)(2,1)}, u32[]{:S(2)}) copy-start(bf16[128,1024]{1,0:T(8,128)(2,1)} %param.16) | copy-start | bytes 786436
  23.0 7.4 %collective-permute-start.3 = (bf16[2,128,128]{2,1,0:T(8,128)(2,1)S(1)}, bf16[2,128,128]{2,1,0:T(8,128)(2,1)S(1)}, u32[]{:S(2)}, u32[]{:S(2)}) collective-permute-start(bf16[2,128,128]{2,1,0:T(8,128)(2,1)S(1)} %get-tuple-element.66), channel_id=1, source_target_pairs={{0,4},{4,8},{8,12},{12,16},{16,20},{20,24},{24,28},{28,0},{1,5},{5... | collective-permute-start | bytes 196616 | tf_op jit(solution)/shard_map/ppermute | solution.py:178
  26.0 5.6 %collective-permute-start.4 = (bf16[2,128,128]{2,1,0:T(8,128)(2,1)S(1)}, bf16[2,128,128]{2,1,0:T(8,128)(2,1)S(1)}, u32[]{:S(2)}, u32[]{:S(2)}) collective-permute-start(bf16[2,128,128]{2,1,0:T(8,128)(2,1)S(1)} %get-tuple-element.67), channel_id=1, source_target_pairs={{0,8},{4,12},{8,16},{12,20},{16,24},{20,28},{24,0},{28,4},{1,9},{5... | collective-permute-start | bytes 196616 | tf_op jit(solution)/shard_map/ppermute | solution.py:178
  27.3 4.7 %collective-permute-start.5 = (bf16[2,128,128]{2,1,0:T(8,128)(2,1)S(1)}, bf16[2,128,128]{2,1,0:T(8,128)(2,1)S(1)}, u32[]{:S(2)}, u32[]{:S(2)}) collective-permute-start(bf16[2,128,128]{2,1,0:T(8,128)(2,1)S(1)} %get-tuple-element.68), channel_id=1, source_target_pairs={{0,12},{4,16},{8,20},{12,24},{16,28},{20,0},{24,4},{28,8},{1,13},{... | collective-permute-start | bytes 196616 | tf_op jit(solution)/shard_map/ppermute | solution.py:178
  27.3 9.8 %collective-permute-start.6 = (bf16[2,128,128]{2,1,0:T(8,128)(2,1)S(1)}, bf16[2,128,128]{2,1,0:T(8,128)(2,1)S(1)}, u32[]{:S(2)}, u32[]{:S(2)}) collective-permute-start(bf16[2,128,128]{2,1,0:T(8,128)(2,1)S(1)} %get-tuple-element.69), channel_id=1, source_target_pairs={{0,16},{4,20},{8,24},{12,28},{16,0},{20,4},{24,8},{28,12},{1,17},{... | collective-permute-start | bytes 196616 | tf_op jit(solution)/shard_map/ppermute | solution.py:178
  28.7 8.4 %collective-permute-start.7 = (bf16[2,128,128]{2,1,0:T(8,128)(2,1)S(1)}, bf16[2,128,128]{2,1,0:T(8,128)(2,1)S(1)}, u32[]{:S(2)}, u32[]{:S(2)}) collective-permute-start(bf16[2,128,128]{2,1,0:T(8,128)(2,1)S(1)} %get-tuple-element.70), channel_id=1, source_target_pairs={{0,20},{4,24},{8,28},{12,0},{16,4},{20,8},{24,12},{28,16},{1,21},{... | collective-permute-start | bytes 196616 | tf_op jit(solution)/shard_map/ppermute | solution.py:178
  30.3 8.9 %collective-permute-start.8 = (bf16[2,128,128]{2,1,0:T(8,128)(2,1)S(1)}, bf16[2,128,128]{2,1,0:T(8,128)(2,1)S(1)}, u32[]{:S(2)}, u32[]{:S(2)}) collective-permute-start(bf16[2,128,128]{2,1,0:T(8,128)(2,1)S(1)} %fusion.30), channel_id=1, source_target_pairs={{0,24},{4,28},{8,0},{12,4},{16,8},{20,12},{24,16},{28,20},{1,25},{... | collective-permute-start | bytes 196616 | tf_op jit(solution)/shard_map/ppermute | solution.py:178
  31.6 7.6 %collective-permute-start.9 = (bf16[2,128,128]{2,1,0:T(8,128)(2,1)S(1)}, bf16[2,128,128]{2,1,0:T(8,128)(2,1)S(1)}, u32[]{:S(2)}, u32[]{:S(2)}) collective-permute-start(bf16[2,128,128]{2,1,0:T(8,128)(2,1)S(1)} %get-tuple-element.65), channel_id=1, source_target_pairs={{0,28},{4,0},{8,4},{12,8},{16,12},{20,16},{24,20},{28,24},{1,29},{... | collective-permute-start | bytes 196616 | tf_op jit(solution)/shard_map/ppermute | solution.py:178
  39.6 0.8 %copy-start.9 = (bf16[256,128,1]{1,0,2:T(8,128)(2,1)S(1)}, bf16[256,128,1]{1,0,2:T(8,128)(2,1)}, u32[]{:S(2)}) copy-start(bf16[256,128,1]{1,0,2:T(8,128)(2,1)} %constant.244) | copy-start | bytes 196612
  40.4 0.8 %copy-start.8 = (bf16[256,128,1]{1,0,2:T(8,128)(2,1)S(1)}, bf16[256,128,1]{1,0,2:T(8,128)(2,1)}, u32[]{:S(2)}) copy-start(bf16[256,128,1]{1,0,2:T(8,128)(2,1)} %constant.245) | copy-start | bytes 196612
  43.8 0.8 %copy-start.11 = (bf16[128,1,1]{0,1,2:T(2,128)(2,1)S(1)}, bf16[128,1,1]{0,1,2:T(2,128)(2,1)}, u32[]{:S(2)}) copy-start(bf16[128,1,1]{0,1,2:T(2,128)(2,1)} %constant.248) | copy-start | bytes 772
  45.4 0.9 %copy-start.2 = (bf16[256,256,1]{1,0,2:T(8,128)(2,1)S(1)}, bf16[256,256,1]{1,0,2:T(8,128)(2,1)}, u32[]{:S(2)}) copy-start(bf16[256,256,1]{1,0,2:T(8,128)(2,1)} %constant.246) | copy-start | bytes 393220
  46.8 0.9 %copy-start.7 = (bf16[256,256,1]{1,0,2:T(8,128)(2,1)S(1)}, bf16[256,256,1]{1,0,2:T(8,128)(2,1)}, u32[]{:S(2)}) copy-start(bf16[256,256,1]{1,0,2:T(8,128)(2,1)} %constant.247) | copy-start | bytes 393220
  47.7 0.7 copy-start.10
  49.1 24.0 %collective-permute-start.14 = (f32[2,128,128]{2,1,0:T(8,128)S(1)}, f32[2,128,128]{2,1,0:T(8,128)S(1)}, u32[]{:S(2)}, u32[]{:S(2)}) collective-permute-start(f32[2,128,128]{2,1,0:T(8,128)S(1)} %bitcast.281), channel_id=1, source_target_pairs={{0,20},{4,24},{8,28},{12,0},{16,4},{20,8},{24,12},{28,16},{1,21},{... | collective-permute-start | bytes 393224 | tf_op jit(solution)/shard_map/ppermute | solution.py:197
  49.4 6.8 %collective-permute-start.10 = (f32[2,128,128]{2,1,0:T(8,128)S(1)}, f32[2,128,128]{2,1,0:T(8,128)S(1)}, u32[]{:S(2)}, u32[]{:S(2)}) collective-permute-start(f32[2,128,128]{2,1,0:T(8,128)S(1)} %bitcast.287), channel_id=1, source_target_pairs={{0,4},{4,8},{8,12},{12,16},{16,20},{20,24},{24,28},{28,0},{1,5},{5... | collective-permute-start | bytes 393224 | tf_op jit(solution)/shard_map/ppermute | solution.py:197
  50.7 9.5 %collective-permute-start.11 = (f32[2,128,128]{2,1,0:T(8,128)S(1)}, f32[2,128,128]{2,1,0:T(8,128)S(1)}, u32[]{:S(2)}, u32[]{:S(2)}) collective-permute-start(f32[2,128,128]{2,1,0:T(8,128)S(1)} %bitcast.286), channel_id=1, source_target_pairs={{0,8},{4,12},{8,16},{12,20},{16,24},{20,28},{24,0},{28,4},{1,9},{5... | collective-permute-start | bytes 393224 | tf_op jit(solution)/shard_map/ppermute | solution.py:197
  52.5 20.7 %copy-start = (bf16[128,1024]{1,0:T(8,128)(2,1)S(1)}, bf16[128,1024]{1,0:T(8,128)(2,1)}, u32[]{:S(2)}) copy-start(bf16[128,1024]{1,0:T(8,128)(2,1)} %param.15) | copy-start | bytes 786436
  52.5 20.7 %copy-start.1 = (bf16[128,1024]{1,0:T(8,128)(2,1)S(1)}, bf16[128,1024]{1,0:T(8,128)(2,1)}, u32[]{:S(2)}) copy-start(bf16[128,1024]{1,0:T(8,128)(2,1)} %param.14) | copy-start | bytes 786436
  52.6 17.7 %collective-permute-start.12 = (f32[2,128,128]{2,1,0:T(8,128)S(1)}, f32[2,128,128]{2,1,0:T(8,128)S(1)}, u32[]{:S(2)}, u32[]{:S(2)}) collective-permute-start(f32[2,128,128]{2,1,0:T(8,128)S(1)} %bitcast.285), channel_id=1, source_target_pairs={{0,12},{4,16},{8,20},{12,24},{16,28},{20,0},{24,4},{28,8},{1,13},{... | collective-permute-start | bytes 393224 | tf_op jit(solution)/shard_map/ppermute | solution.py:197
  54.9 18.2 %collective-permute-start.13 = (f32[2,128,128]{2,1,0:T(8,128)S(1)}, f32[2,128,128]{2,1,0:T(8,128)S(1)}, u32[]{:S(2)}, u32[]{:S(2)}) collective-permute-start(f32[2,128,128]{2,1,0:T(8,128)S(1)} %bitcast.284), channel_id=1, source_target_pairs={{0,16},{4,20},{8,24},{12,28},{16,0},{20,4},{24,8},{28,12},{1,17},{... | collective-permute-start | bytes 393224 | tf_op jit(solution)/shard_map/ppermute | solution.py:197
  56.3 16.9 %collective-permute-start.15 = (f32[2,128,128]{2,1,0:T(8,128)S(1)}, f32[2,128,128]{2,1,0:T(8,128)S(1)}, u32[]{:S(2)}, u32[]{:S(2)}) collective-permute-start(f32[2,128,128]{2,1,0:T(8,128)S(1)} %bitcast.283), channel_id=1, source_target_pairs={{0,24},{4,28},{8,0},{12,4},{16,8},{20,12},{24,16},{28,20},{1,25},{... | collective-permute-start | bytes 393224 | tf_op jit(solution)/shard_map/ppermute | solution.py:197
  60.2 13.0 %collective-permute-start.16 = (f32[2,128,128]{2,1,0:T(8,128)S(1)}, f32[2,128,128]{2,1,0:T(8,128)S(1)}, u32[]{:S(2)}, u32[]{:S(2)}) collective-permute-start(f32[2,128,128]{2,1,0:T(8,128)S(1)} %bitcast.282), channel_id=1, source_target_pairs={{0,28},{4,0},{8,4},{12,8},{16,12},{20,16},{24,20},{28,24},{1,29},{... | collective-permute-start | bytes 393224 | tf_op jit(solution)/shard_map/ppermute | solution.py:197
  73.2 1.0 %copy-start.3 = (f32[128,1024]{1,0:T(8,128)}, f32[128,1024]{1,0:T(8,128)S(1)}, u32[]{:S(2)}) copy-start(f32[128,1024]{1,0:T(8,128)S(1)} %get-tuple-element.75) | copy-start | bytes 1572868

commit v19 on v18

--- a/solution.py
+++ b/solution.py
@@ -32,9 +32,18 @@
         for source in range(count)
     ]
     gathered = jnp.concatenate(ordered, axis=1)
-    return lax.dot_general(
-        gathered, out_weight, (((1,), (1,)), ((), ())), preferred_element_type=jnp.float32
-    )
+    halves = 2 if out_weight.shape[0] % 256 == 0 else 1
+    width = out_weight.shape[0] // halves
+    parts = [
+        lax.dot_general(
+            gathered,
+            out_weight[half * width : (half + 1) * width],
+            (((1,), (1,)), ((), ())),
+            preferred_element_type=jnp.float32,
+        )
+        for half in range(halves)
+    ]
+    return jnp.concatenate(parts, axis=1)
 
 
 def split_constant(table):

time: 75.6 us -> 75.8 us (level)
  matrix products: 9.26 us -> 10.5 us
  local copies, waits for them, and re-layouts: 8.84 us -> 8.04 us
    dot_general x1 -> x2, matrix products: 6.3 us -> 7.48 us  [gather_matmul(): lax.dot_general(gathered, out_weight[half * width:(half + 1) * width], ((...]
    unnamed x40, local copies, waits for them, and re-layouts: 6.25 us -> 5.45 us
  transfers between devices with their start and end apart: 18 -> 18, of which waited for: 7 -> 9; matrix products, arithmetic and copies ran while one was open for 18% -> 19% of each run, Pallas kernels for 0% -> 0%
where the time goes in v19:
time: 75.8 us; the launch traced here: 74.7 us
  waiting for transfers between devices  24.8 us (33%)
  starting transfers between devices  23.9 us (32%)
  matrix products  10.5 us (14%)
  local copies, waits for them, and re-layouts  8.04 us (11%)
  other arithmetic  6.24 us (8%)
  between operations  1.33 us (2%)
    ppermute x7, waiting for transfers between devices, gather_lanes(): lax.ppermute(chunk, 'ctx', [(i, (i + shift) % count) for i in range(count)])  17.4 us
    ppermute x7, starting transfers between devices, scatter_lanes(): lax.ppermute(chunk, 'ctx', [(i, (i + shift) % count) for i in range(count)])  8.96 us
    dot_general x2, matrix products, gather_matmul(): lax.dot_general(gathered, out_weight[half * width:(half + 1) * width], ((...  7.48 us
    ppermute x7, waiting for transfers between devices, scatter_lanes(): lax.ppermute(chunk, 'ctx', [(i, (i + shift) % count) for i in range(count)])  7.03 us
    all_to_all x1, starting transfers between devices, all_to_all_ctx(): return lax.all_to_all(stacked, 'ctx', 0, 0, tiled=True)  6.44 us
    ppermute x7, starting transfers between devices, gather_lanes(): lax.ppermute(chunk, 'ctx', [(i, (i + shift) % count) for i in range(count)])  5.75 us
    unnamed x40, local copies, waits for them, and re-layouts  5.45 us
    dot_general x5, matrix products, table_times(): jnp.einsum('kn,snc->skc', table, signal, preferred_element_type=jnp.float32)  2.78 us
  transfers between devices with their start and end apart: 18, of which 9 were waited for; matrix products, arithmetic and copies ran while one was open for 19% of the time, Pallas kernels for 0%

profile of v19, /device:TPU:9, one launch (start us, length us, event | category | flops | bytes accessed | tf_op | source)
XLA Modules:
  0.0 74.7 jit_solution(17878838271237239679)
XLA Ops:
  0.6 1.3 %collective-permute-start = (bf16[128,1024]{1,0:T(8,128)(2,1)}, bf16[128,1024]{1,0:T(8,128)(2,1)S(1)}, u32[]{:S(2)}, u32[]{:S(2)}) collective-permute-start(bf16[128,1024]{1,0:T(8,128)(2,1)} %param.17), channel_id=1, source_target_pairs={{0,1},{1,0},{2,3},{3,2},{4,5},{5,4},{6,7},{7,6},{8,9},{9,8},{10,11... | collective-permute-start | bytes 786440 | tf_op jit(solution)/shard_map/ppermute | solution.py:26
  1.9 1.2 %collective-permute-start.1 = (bf16[128,1024]{1,0:T(8,128)(2,1)}, bf16[128,1024]{1,0:T(8,128)(2,1)S(1)}, u32[]{:S(2)}, u32[]{:S(2)}) collective-permute-start(bf16[128,1024]{1,0:T(8,128)(2,1)} %param.17), channel_id=1, source_target_pairs={{0,2},{1,3},{2,0},{3,1},{4,6},{5,7},{6,4},{7,5},{8,10},{9,11},{10,... | collective-permute-start | bytes 786440 | tf_op jit(solution)/shard_map/ppermute | solution.py:26
  3.1 0.2 collective-permute-start.2
  3.3 1.1 %copy.49 = bf16[128,1024]{0,1:T(8,128)(2,1)S(1)} copy(bf16[128,1024]{1,0:T(8,128)(2,1)} %param.14) | data formatting | bytes 524288 | tf_op args[1]
  4.5 1.1 %copy.50 = bf16[128,1024]{0,1:T(8,128)(2,1)S(1)} copy(bf16[128,1024]{1,0:T(8,128)(2,1)} %param.15) | data formatting | bytes 524288 | tf_op args[2]
  5.7 1.2 %copy.51 = bf16[128,1024]{0,1:T(8,128)(2,1)S(1)} copy(bf16[128,1024]{1,0:T(8,128)(2,1)} %param.19) | data formatting | bytes 524288 | tf_op args[6]
  6.9 1.0 %copy.52 = bf16[8,2,128,128]{3,2,1,0:T(8,128)(2,1)} copy(bf16[8,2,128,128]{2,3,0,1:T(8,128)(2,1)S(1)} %pad_maximum_fusion.6) | data formatting | bytes 1048576 | tf_op jit(solution)/shard_map/stack | solution.py:222
  7.9 6.4 %all-to-all-start = ((bf16[8,2,128,128]{3,2,1,0:T(8,128)(2,1)}), bf16[8,2,128,128]{3,2,1,0:T(8,128)(2,1)S(1)}, u32[]{:S(2)}, u32[]{:S(2)}) async-start(bf16[8,2,128,128]{3,2,1,0:T(8,128)(2,1)} %copy.52), calls=%async_computation | async-start | bytes 1048576 | tf_op jit(solution)/shard_map/all_to_all | solution.py:158
  14.4 0.3 collective-permute-done.2
  14.7 0.1 pad_maximum_fusion.1
  14.9 3.7 %fusion.2 = f32[128,512]{1,0:T(8,128)S(1)} fusion(bf16[1024,4096]{1,0:T(8,128)(2,1)} %param.18, bf16[128,1024]{1,0:T(8,128)(2,1)S(1)} %get-tuple-element.42, bf16[128,1024]{1,0:T(8,128)(2,1)S(1)} %get-tuple-element.43, bf16[128,1024]{1,0:T(8,128)(2,1)S(1)} %get-tuple-element.44, bf16[128,1024]{1,0:T(8,128)(2,1)S(1)} %get-tuple-element.41), kind=kOutput, calls=%fused_computation.2 | convolution fusion | flops 541065216 | bytes 5505024 | tf_op jit(solution)/shard_map/dot_general | solution.py:38
  18.7 3.8 %fusion = f32[128,512]{1,0:T(8,128)S(1)} fusion(bf16[1024,4096]{1,0:T(8,128)(2,1)} %param.18, bf16[128,1024]{1,0:T(8,128)(2,1)S(1)} %get-tuple-element.42, bf16[128,1024]{1,0:T(8,128)(2,1)S(1)} %get-tuple-element.43, bf16[128,1024]{1,0:T(8,128)(2,1)S(1)} %get-tuple-element.44, bf16[128,1024]{1,0:T(8,128)(2,1)S(1)} %get-tuple-element.41), kind=kOutput, calls=%fused_computation | convolution fusion | flops 541065216 | bytes 5505024 | tf_op jit(solution)/shard_map/dot_general | solution.py:38
  22.6 0.9 %fusion.10 = (bf16[1,128,1024]{2,1,0:T(8,128)(2,1)S(1)}, bf16[128,1024]{1,0:T(8,128)(2,1)}) fusion(bf16[128,1024]{1,0:T(8,128)(2,1)S(1)} %fusion.9, bf16[128,1024]{1,0:T(8,128)(2,1)S(1)} %copy-done, f32[128,512]{1,0:T(8,128)S(1)} %fusion, f32[128,512]{1,0:T(8,128)S(1)} %fusion.2, bf16[128,1024]{1,0:T(8,128)(2,1)S(1)} %copy-done.5), kind=kLoop, calls=%fused_computation.89 | loop fusion | flops 1179648 | bytes 1835008 | tf_op jit(solution)/shard_map/stack | solution.py:228
  23.4 0.1 fusion.19
  23.5 3.0 %collective-permute-start.3 = (bf16[2,128,128]{2,1,0:T(8,128)(2,1)S(1)}, bf16[2,128,128]{2,1,0:T(8,128)(2,1)S(1)}, u32[]{:S(2)}, u32[]{:S(2)}) collective-permute-start(bf16[2,128,128]{2,1,0:T(8,128)(2,1)S(1)} %get-tuple-element.66), channel_id=1, source_target_pairs={{0,4},{4,8},{8,12},{12,16},{16,20},{20,24},{24,28},{28,0},{1,5},{5... | collective-permute-start | bytes 196616 | tf_op jit(solution)/shard_map/ppermute | solution.py:187
  26.5 1.4 %collective-permute-start.4 = (bf16[2,128,128]{2,1,0:T(8,128)(2,1)S(1)}, bf16[2,128,128]{2,1,0:T(8,128)(2,1)S(1)}, u32[]{:S(2)}, u32[]{:S(2)}) collective-permute-start(bf16[2,128,128]{2,1,0:T(8,128)(2,1)S(1)} %get-tuple-element.67), channel_id=1, source_target_pairs={{0,8},{4,12},{8,16},{12,20},{16,24},{20,28},{24,0},{28,4},{1,9},{5... | collective-permute-start | bytes 196616 | tf_op jit(solution)/shard_map/ppermute | solution.py:187
  27.9 1.4 %collective-permute-start.6 = (bf16[2,128,128]{2,1,0:T(8,128)(2,1)S(1)}, bf16[2,128,128]{2,1,0:T(8,128)(2,1)S(1)}, u32[]{:S(2)}, u32[]{:S(2)}) collective-permute-start(bf16[2,128,128]{2,1,0:T(8,128)(2,1)S(1)} %get-tuple-element.69), channel_id=1, source_target_pairs={{0,16},{4,20},{8,24},{12,28},{16,0},{20,4},{24,8},{28,12},{1,17},{... | collective-permute-start | bytes 196616 | tf_op jit(solution)/shard_map/ppermute | solution.py:187
  29.3 1.6 %collective-permute-start.7 = (bf16[2,128,128]{2,1,0:T(8,128)(2,1)S(1)}, bf16[2,128,128]{2,1,0:T(8,128)(2,1)S(1)}, u32[]{:S(2)}, u32[]{:S(2)}) collective-permute-start(bf16[2,128,128]{2,1,0:T(8,128)(2,1)S(1)} %get-tuple-element.70), channel_id=1, source_target_pairs={{0,20},{4,24},{8,28},{12,0},{16,4},{20,8},{24,12},{28,16},{1,21},{... | collective-permute-start | bytes 196616 | tf_op jit(solution)/shard_map/ppermute | solution.py:187
  30.9 1.2 %collective-permute-start.8 = (bf16[2,128,128]{2,1,0:T(8,128)(2,1)S(1)}, bf16[2,128,128]{2,1,0:T(8,128)(2,1)S(1)}, u32[]{:S(2)}, u32[]{:S(2)}) collective-permute-start(bf16[2,128,128]{2,1,0:T(8,128)(2,1)S(1)} %fusion.26), channel_id=1, source_target_pairs={{0,24},{4,28},{8,0},{12,4},{16,8},{20,12},{24,16},{28,20},{1,25},{... | collective-permute-start | bytes 196616 | tf_op jit(solution)/shard_map/ppermute | solution.py:187
  32.2 0.4 collective-permute-start.9
  32.6 5.0 %collective-permute-done.6 = bf16[2,128,128]{2,1,0:T(8,128)(2,1)S(1)} collective-permute-done((bf16[2,128,128]{2,1,0:T(8,128)(2,1)S(1)}, bf16[2,128,128]{2,1,0:T(8,128)(2,1)S(1)}, u32[]{:S(2)}, u32[]{:S(2)}) %collective-permute-start.6) | collective-permute-done | bytes 65568 | tf_op jit(solution)/shard_map/ppermute | solution.py:187
  37.7 1.9 %collective-permute-done.8 = bf16[2,128,128]{2,1,0:T(8,128)(2,1)S(1)} collective-permute-done((bf16[2,128,128]{2,1,0:T(8,128)(2,1)S(1)}, bf16[2,128,128]{2,1,0:T(8,128)(2,1)S(1)}, u32[]{:S(2)}, u32[]{:S(2)}) %collective-permute-start.8) | collective-permute-done | bytes 65568 | tf_op jit(solution)/shard_map/ppermute | solution.py:187
  40.1 0.1 pad_maximum_fusion.3
  40.3 0.6 copy-done.9
  40.9 0.7 convolution_bitcast_fusion
  41.6 0.1 copy-done.8
  41.7 0.6 convolution_bitcast_fusion.1
  42.3 0.6 slice_add_fusion.3
  43.0 0.2 fusion.8
  43.3 0.4 add_add_fusion.2
  43.7 0.4 subtract_add_fusion.1
  44.2 0.1 slice_bitcast_fusion.32
  44.3 0.4 add_add_fusion.1
  44.7 0.4 subtract_add_fusion
  45.1 0.2 fusion.54
  45.6 0.1 pad_maximum_fusion
  45.7 0.1 bitcast_convert_fusion
  45.9 0.3 fusion.4
  46.2 0.5 copy-done.3
  46.7 0.5 fusion.52
  47.2 0.5 fusion.53
  47.7 0.4 copy-done.7
  48.1 0.5 add_add_fusion
  48.7 0.2 copy-done.10
  48.8 0.3 multiply_add_fusion
  49.4 0.1 copy.60
  49.7 0.1 copy.55
  49.8 0.1 copy.56
  49.9 1.1 %collective-permute-start.10 = (f32[2,128,128]{2,1,0:T(8,128)S(1)}, f32[2,128,128]{2,1,0:T(8,128)S(1)}, u32[]{:S(2)}, u32[]{:S(2)}) collective-permute-start(f32[2,128,128]{2,1,0:T(8,128)S(1)} %bitcast.286), channel_id=1, source_target_pairs={{0,4},{4,8},{8,12},{12,16},{16,20},{20,24},{24,28},{28,0},{1,5},{5... | collective-permute-start | bytes 393224 | tf_op jit(solution)/shard_map/ppermute | solution.py:206
  51.0 0.1 copy.57
  51.1 1.9 %collective-permute-start.11 = (f32[2,128,128]{2,1,0:T(8,128)S(1)}, f32[2,128,128]{2,1,0:T(8,128)S(1)}, u32[]{:S(2)}, u32[]{:S(2)}) collective-permute-start(f32[2,128,128]{2,1,0:T(8,128)S(1)} %bitcast.285), channel_id=1, source_target_pairs={{0,8},{4,12},{8,16},{12,20},{16,24},{20,28},{24,0},{28,4},{1,9},{5... | collective-permute-start | bytes 393224 | tf_op jit(solution)/shard_map/ppermute | solution.py:206
  53.0 0.1 copy.58
  53.1 2.3 %collective-permute-start.12 = (f32[2,128,128]{2,1,0:T(8,128)S(1)}, f32[2,128,128]{2,1,0:T(8,128)S(1)}, u32[]{:S(2)}, u32[]{:S(2)}) collective-permute-start(f32[2,128,128]{2,1,0:T(8,128)S(1)} %bitcast.284), channel_id=1, source_target_pairs={{0,12},{4,16},{8,20},{12,24},{16,28},{20,0},{24,4},{28,8},{1,13},{... | collective-permute-start | bytes 393224 | tf_op jit(solution)/shard_map/ppermute | solution.py:206
  55.4 0.1 copy.59
  55.5 0.2 collective-permute-start.13
  55.6 0.1 copy.61
  55.7 0.1 copy.62
  56.0 0.6 collective-permute-done.10
  56.6 0.2 collective-permute-start.15
  56.9 3.5 %collective-permute-done.11 = f32[2,128,128]{2,1,0:T(8,128)S(1)} collective-permute-done((f32[2,128,128]{2,1,0:T(8,128)S(1)}, f32[2,128,128]{2,1,0:T(8,128)S(1)}, u32[]{:S(2)}, u32[]{:S(2)}) %collective-permute-start.11) | collective-permute-done | bytes 131104 | tf_op jit(solution)/shard_map/ppermute | solution.py:206
  60.4 10.2 %collective-permute-done.12 = f32[2,128,128]{2,1,0:T(8,128)S(1)} collective-permute-done((f32[2,128,128]{2,1,0:T(8,128)S(1)}, f32[2,128,128]{2,1,0:T(8,128)S(1)}, u32[]{:S(2)}, u32[]{:S(2)}) %collective-permute-start.12) | collective-permute-done | bytes 131104 | tf_op jit(solution)/shard_map/ppermute | solution.py:206
  70.7 2.8 %collective-permute-done.13 = f32[2,128,128]{2,1,0:T(8,128)S(1)} collective-permute-done((f32[2,128,128]{2,1,0:T(8,128)S(1)}, f32[2,128,128]{2,1,0:T(8,128)S(1)}, u32[]{:S(2)}, u32[]{:S(2)}) %collective-permute-start.13) | collective-permute-done | bytes 131104 | tf_op jit(solution)/shard_map/ppermute | solution.py:206
  73.6 0.2 collective-permute-done.16
  73.8 0.9 %multiply_convert_fusion = (bf16[128,1024]{1,0:T(8,128)(2,1)}, bf16[128,1024]{1,0:T(8,128)(2,1)}) fusion(f32[128,1024]{1,0:T(8,128)S(1)} %get-tuple-element.76, bf16[128,1024]{1,0:T(8,128)(2,1)S(1)} %copy-done.2, bf16[128,1024]{1,0:T(8,128)(2,1)S(1)} %copy-done.1), kind=kLoop, calls=%fused_computation.78 | loop fusion | flops 786432 | bytes 1572864 | tf_op jit(solution)/shard_map/convert_element_type | solution.py:240
  (84 shorter events, 1.8 us)
Async XLA Ops:
  0.6 13.7 %collective-permute-start = (bf16[128,1024]{1,0:T(8,128)(2,1)}, bf16[128,1024]{1,0:T(8,128)(2,1)S(1)}, u32[]{:S(2)}, u32[]{:S(2)}) collective-permute-start(bf16[128,1024]{1,0:T(8,128)(2,1)} %param.17), channel_id=1, source_target_pairs={{0,1},{1,0},{2,3},{3,2},{4,5},{5,4},{6,7},{7,6},{8,9},{9,8},{10,11... | collective-permute-start | bytes 786440 | tf_op jit(solution)/shard_map/ppermute | solution.py:26
  1.9 12.5 %collective-permute-start.1 = (bf16[128,1024]{1,0:T(8,128)(2,1)}, bf16[128,1024]{1,0:T(8,128)(2,1)S(1)}, u32[]{:S(2)}, u32[]{:S(2)}) collective-permute-start(bf16[128,1024]{1,0:T(8,128)(2,1)} %param.17), channel_id=1, source_target_pairs={{0,2},{1,3},{2,0},{3,1},{4,6},{5,7},{6,4},{7,5},{8,10},{9,11},{10,... | collective-permute-start | bytes 786440 | tf_op jit(solution)/shard_map/ppermute | solution.py:26
  3.1 11.6 %collective-permute-start.2 = (bf16[128,1024]{1,0:T(8,128)(2,1)}, bf16[128,1024]{1,0:T(8,128)(2,1)S(1)}, u32[]{:S(2)}, u32[]{:S(2)}) collective-permute-start(bf16[128,1024]{1,0:T(8,128)(2,1)} %param.17), channel_id=1, source_target_pairs={{0,3},{1,2},{2,1},{3,0},{4,7},{5,6},{6,5},{7,4},{8,11},{9,10},{10,... | collective-permute-start | bytes 786440 | tf_op jit(solution)/shard_map/ppermute | solution.py:26
  5.7 9.0 %copy-start.6 = (bf16[128,1024]{1,0:T(8,128)(2,1)S(1)}, bf16[128,1024]{1,0:T(8,128)(2,1)}, u32[]{:S(2)}) copy-start(bf16[128,1024]{1,0:T(8,128)(2,1)} %param.17) | copy-start | bytes 786436
  7.9 32.0 %all-to-all-start = ((bf16[8,2,128,128]{3,2,1,0:T(8,128)(2,1)}), bf16[8,2,128,128]{3,2,1,0:T(8,128)(2,1)S(1)}, u32[]{:S(2)}, u32[]{:S(2)}) async-start(bf16[8,2,128,128]{3,2,1,0:T(8,128)(2,1)} %copy.52), calls=%async_computation | async-start | bytes 1048576 | tf_op jit(solution)/shard_map/all_to_all | solution.py:158
  18.7 3.8 %copy-start = (bf16[128,1024]{1,0:T(8,128)(2,1)S(1)}, bf16[128,1024]{1,0:T(8,128)(2,1)}, u32[]{:S(2)}) copy-start(bf16[128,1024]{1,0:T(8,128)(2,1)} %param.13) | copy-start | bytes 786436
  18.7 3.9 %copy-start.5 = (bf16[128,1024]{1,0:T(8,128)(2,1)S(1)}, bf16[128,1024]{1,0:T(8,128)(2,1)}, u32[]{:S(2)}) copy-start(bf16[128,1024]{1,0:T(8,128)(2,1)} %param.16) | copy-start | bytes 786436
  23.5 7.4 %collective-permute-start.3 = (bf16[2,128,128]{2,1,0:T(8,128)(2,1)S(1)}, bf16[2,128,128]{2,1,0:T(8,128)(2,1)S(1)}, u32[]{:S(2)}, u32[]{:S(2)}) collective-permute-start(bf16[2,128,128]{2,1,0:T(8,128)(2,1)S(1)} %get-tuple-element.66), channel_id=1, source_target_pairs={{0,4},{4,8},{8,12},{12,16},{16,20},{20,24},{24,28},{28,0},{1,5},{5... | collective-permute-start | bytes 196616 | tf_op jit(solution)/shard_map/ppermute | solution.py:187
  26.5 5.6 %collective-permute-start.4 = (bf16[2,128,128]{2,1,0:T(8,128)(2,1)S(1)}, bf16[2,128,128]{2,1,0:T(8,128)(2,1)S(1)}, u32[]{:S(2)}, u32[]{:S(2)}) collective-permute-start(bf16[2,128,128]{2,1,0:T(8,128)(2,1)S(1)} %get-tuple-element.67), channel_id=1, source_target_pairs={{0,8},{4,12},{8,16},{12,20},{16,24},{20,28},{24,0},{28,4},{1,9},{5... | collective-permute-start | bytes 196616 | tf_op jit(solution)/shard_map/ppermute | solution.py:187
  27.9 4.7 %collective-permute-start.5 = (bf16[2,128,128]{2,1,0:T(8,128)(2,1)S(1)}, bf16[2,128,128]{2,1,0:T(8,128)(2,1)S(1)}, u32[]{:S(2)}, u32[]{:S(2)}) collective-permute-start(bf16[2,128,128]{2,1,0:T(8,128)(2,1)S(1)} %get-tuple-element.68), channel_id=1, source_target_pairs={{0,12},{4,16},{8,20},{12,24},{16,28},{20,0},{24,4},{28,8},{1,13},{... | collective-permute-start | bytes 196616 | tf_op jit(solution)/shard_map/ppermute | solution.py:187
  27.9 9.8 %collective-permute-start.6 = (bf16[2,128,128]{2,1,0:T(8,128)(2,1)S(1)}, bf16[2,128,128]{2,1,0:T(8,128)(2,1)S(1)}, u32[]{:S(2)}, u32[]{:S(2)}) collective-permute-start(bf16[2,128,128]{2,1,0:T(8,128)(2,1)S(1)} %get-tuple-element.69), channel_id=1, source_target_pairs={{0,16},{4,20},{8,24},{12,28},{16,0},{20,4},{24,8},{28,12},{1,17},{... | collective-permute-start | bytes 196616 | tf_op jit(solution)/shard_map/ppermute | solution.py:187
  29.3 8.4 %collective-permute-start.7 = (bf16[2,128,128]{2,1,0:T(8,128)(2,1)S(1)}, bf16[2,128,128]{2,1,0:T(8,128)(2,1)S(1)}, u32[]{:S(2)}, u32[]{:S(2)}) collective-permute-start(bf16[2,128,128]{2,1,0:T(8,128)(2,1)S(1)} %get-tuple-element.70), channel_id=1, source_target_pairs={{0,20},{4,24},{8,28},{12,0},{16,4},{20,8},{24,12},{28,16},{1,21},{... | collective-permute-start | bytes 196616 | tf_op jit(solution)/shard_map/ppermute | solution.py:187
  30.9 8.7 %collective-permute-start.8 = (bf16[2,128,128]{2,1,0:T(8,128)(2,1)S(1)}, bf16[2,128,128]{2,1,0:T(8,128)(2,1)S(1)}, u32[]{:S(2)}, u32[]{:S(2)}) collective-permute-start(bf16[2,128,128]{2,1,0:T(8,128)(2,1)S(1)} %fusion.26), channel_id=1, source_target_pairs={{0,24},{4,28},{8,0},{12,4},{16,8},{20,12},{24,16},{28,20},{1,25},{... | collective-permute-start | bytes 196616 | tf_op jit(solution)/shard_map/ppermute | solution.py:187
  32.2 7.5 %collective-permute-start.9 = (bf16[2,128,128]{2,1,0:T(8,128)(2,1)S(1)}, bf16[2,128,128]{2,1,0:T(8,128)(2,1)S(1)}, u32[]{:S(2)}, u32[]{:S(2)}) collective-permute-start(bf16[2,128,128]{2,1,0:T(8,128)(2,1)S(1)} %get-tuple-element.65), channel_id=1, source_target_pairs={{0,28},{4,0},{8,4},{12,8},{16,12},{20,16},{24,20},{28,24},{1,29},{... | collective-permute-start | bytes 196616 | tf_op jit(solution)/shard_map/ppermute | solution.py:187
  40.0 0.8 %copy-start.9 = (bf16[256,128,1]{1,0,2:T(8,128)(2,1)S(1)}, bf16[256,128,1]{1,0,2:T(8,128)(2,1)}, u32[]{:S(2)}) copy-start(bf16[256,128,1]{1,0,2:T(8,128)(2,1)} %constant.244) | copy-start | bytes 196612
  40.9 0.8 %copy-start.8 = (bf16[256,128,1]{1,0,2:T(8,128)(2,1)S(1)}, bf16[256,128,1]{1,0,2:T(8,128)(2,1)}, u32[]{:S(2)}) copy-start(bf16[256,128,1]{1,0,2:T(8,128)(2,1)} %constant.245) | copy-start | bytes 196612
  44.3 0.8 %copy-start.11 = (bf16[128,1,1]{0,1,2:T(2,128)(2,1)S(1)}, bf16[128,1,1]{0,1,2:T(2,128)(2,1)}, u32[]{:S(2)}) copy-start(bf16[128,1,1]{0,1,2:T(2,128)(2,1)} %constant.248) | copy-start | bytes 772
  45.8 0.9 %copy-start.3 = (bf16[256,256,1]{1,0,2:T(8,128)(2,1)S(1)}, bf16[256,256,1]{1,0,2:T(8,128)(2,1)}, u32[]{:S(2)}) copy-start(bf16[256,256,1]{1,0,2:T(8,128)(2,1)} %constant.246) | copy-start | bytes 393220
  47.2 0.9 %copy-start.7 = (bf16[256,256,1]{1,0,2:T(8,128)(2,1)S(1)}, bf16[256,256,1]{1,0,2:T(8,128)(2,1)}, u32[]{:S(2)}) copy-start(bf16[256,256,1]{1,0,2:T(8,128)(2,1)} %constant.247) | copy-start | bytes 393220
  48.1 0.7 copy-start.10
  49.5 24.0 %collective-permute-start.14 = (f32[2,128,128]{2,1,0:T(8,128)S(1)}, f32[2,128,128]{2,1,0:T(8,128)S(1)}, u32[]{:S(2)}, u32[]{:S(2)}) collective-permute-start(f32[2,128,128]{2,1,0:T(8,128)S(1)} %bitcast.280), channel_id=1, source_target_pairs={{0,20},{4,24},{8,28},{12,0},{16,4},{20,8},{24,12},{28,16},{1,21},{... | collective-permute-start | bytes 393224 | tf_op jit(solution)/shard_map/ppermute | solution.py:206
  49.9 6.7 %collective-permute-start.10 = (f32[2,128,128]{2,1,0:T(8,128)S(1)}, f32[2,128,128]{2,1,0:T(8,128)S(1)}, u32[]{:S(2)}, u32[]{:S(2)}) collective-permute-start(f32[2,128,128]{2,1,0:T(8,128)S(1)} %bitcast.286), channel_id=1, source_target_pairs={{0,4},{4,8},{8,12},{12,16},{16,20},{20,24},{24,28},{28,0},{1,5},{5... | collective-permute-start | bytes 393224 | tf_op jit(solution)/shard_map/ppermute | solution.py:206
  51.1 9.3 %collective-permute-start.11 = (f32[2,128,128]{2,1,0:T(8,128)S(1)}, f32[2,128,128]{2,1,0:T(8,128)S(1)}, u32[]{:S(2)}, u32[]{:S(2)}) collective-permute-start(f32[2,128,128]{2,1,0:T(8,128)S(1)} %bitcast.285), channel_id=1, source_target_pairs={{0,8},{4,12},{8,16},{12,20},{16,24},{20,28},{24,0},{28,4},{1,9},{5... | collective-permute-start | bytes 393224 | tf_op jit(solution)/shard_map/ppermute | solution.py:206
  53.0 20.8 %copy-start.1 = (bf16[128,1024]{1,0:T(8,128)(2,1)S(1)}, bf16[128,1024]{1,0:T(8,128)(2,1)}, u32[]{:S(2)}) copy-start(bf16[128,1024]{1,0:T(8,128)(2,1)} %param.15) | copy-start | bytes 786436
  53.0 20.8 %copy-start.2 = (bf16[128,1024]{1,0:T(8,128)(2,1)S(1)}, bf16[128,1024]{1,0:T(8,128)(2,1)}, u32[]{:S(2)}) copy-start(bf16[128,1024]{1,0:T(8,128)(2,1)} %param.14) | copy-start | bytes 786436
  53.1 17.6 %collective-permute-start.12 = (f32[2,128,128]{2,1,0:T(8,128)S(1)}, f32[2,128,128]{2,1,0:T(8,128)S(1)}, u32[]{:S(2)}, u32[]{:S(2)}) collective-permute-start(f32[2,128,128]{2,1,0:T(8,128)S(1)} %bitcast.284), channel_id=1, source_target_pairs={{0,12},{4,16},{8,20},{12,24},{16,28},{20,0},{24,4},{28,8},{1,13},{... | collective-permute-start | bytes 393224 | tf_op jit(solution)/shard_map/ppermute | solution.py:206
  55.5 18.0 %collective-permute-start.13 = (f32[2,128,128]{2,1,0:T(8,128)S(1)}, f32[2,128,128]{2,1,0:T(8,128)S(1)}, u32[]{:S(2)}, u32[]{:S(2)}) collective-permute-start(f32[2,128,128]{2,1,0:T(8,128)S(1)} %bitcast.283), channel_id=1, source_target_pairs={{0,16},{4,20},{8,24},{12,28},{16,0},{20,4},{24,8},{28,12},{1,17},{... | collective-permute-start | bytes 393224 | tf_op jit(solution)/shard_map/ppermute | solution.py:206
  56.6 16.9 %collective-permute-start.15 = (f32[2,128,128]{2,1,0:T(8,128)S(1)}, f32[2,128,128]{2,1,0:T(8,128)S(1)}, u32[]{:S(2)}, u32[]{:S(2)}) collective-permute-start(f32[2,128,128]{2,1,0:T(8,128)S(1)} %bitcast.282), channel_id=1, source_target_pairs={{0,24},{4,28},{8,0},{12,4},{16,8},{20,12},{24,16},{28,20},{1,25},{... | collective-permute-start | bytes 393224 | tf_op jit(solution)/shard_map/ppermute | solution.py:206
  60.4 13.3 %collective-permute-start.16 = (f32[2,128,128]{2,1,0:T(8,128)S(1)}, f32[2,128,128]{2,1,0:T(8,128)S(1)}, u32[]{:S(2)}, u32[]{:S(2)}) collective-permute-start(f32[2,128,128]{2,1,0:T(8,128)S(1)} %bitcast.281), channel_id=1, source_target_pairs={{0,28},{4,0},{8,4},{12,8},{16,12},{20,16},{24,20},{28,24},{1,29},{... | collective-permute-start | bytes 393224 | tf_op jit(solution)/shard_map/ppermute | solution.py:206
  73.8 1.0 %copy-start.4 = (f32[128,1024]{1,0:T(8,128)}, f32[128,1024]{1,0:T(8,128)S(1)}, u32[]{:S(2)}) copy-start(f32[128,1024]{1,0:T(8,128)S(1)} %get-tuple-element.75) | copy-start | bytes 1572868

commit v20 on v18

--- a/solution.py
+++ b/solution.py
@@ -186,10 +186,11 @@
     )
 
 
-def gather_lanes(value, chans):
+def gather_lanes(value, chans, parts):
     count = lax.axis_size("ctx")
     me = lax.axis_index("ctx")
-    parts, rows, sub = value.shape[1:]
+    rows, width = value.shape[1:]
+    sub = width // parts
     results = [jnp.zeros((rows, chans), value.dtype) for _ in range(parts)]
     for shift in range(count):
         chunk = lax.dynamic_index_in_dim(value, (me + shift) % count, 0, keepdims=False)
@@ -197,7 +198,9 @@
             chunk = lax.ppermute(chunk, "ctx", [(i, (i + shift) % count) for i in range(count)])
         offset = ((me - shift) % count) * sub
         results = [
-            lax.dynamic_update_slice_in_dim(result, chunk[part], offset, axis=1)
+            lax.dynamic_update_slice_in_dim(
+                result, chunk[:, part * sub : (part + 1) * sub], offset, axis=1
+            )
             for part, result in enumerate(results)
         ]
     return results
@@ -224,8 +227,10 @@
         inputs_t[:, 1].reshape(seq, sub),
         float(seq) ** -0.5,
     )
-    outgoing = jnp.stack([du_t, filter_t]).reshape(2, blocks, rows, sub).transpose(1, 0, 2, 3)
-    du_local, filter_grad = gather_lanes(outgoing, chans)
+    outgoing = jnp.concatenate(
+        [du_t.reshape(blocks, rows, sub), filter_t.reshape(blocks, rows, sub)], axis=2
+    )
+    du_local, filter_grad = gather_lanes(outgoing, chans, 2)
     k_late, v_late = lax.optimization_barrier((k_proj, v_proj))
     dk_grad = (du_local * v_late.astype(jnp.float32)).astype(jnp.bfloat16)
     dv_grad = (du_local * k_late.astype(jnp.float32)).astype(jnp.bfloat16)

time: 75.6 us -> 75.6 us (level)
  no operation moved by 1% of the time
where the time goes in v20:
time: 75.6 us; the launch traced here: 74.2 us
  waiting for transfers between devices  24.7 us (33%)
  starting transfers between devices  24 us (32%)
  matrix products  9.26 us (12%)
  local copies, waits for them, and re-layouts  8.84 us (12%)
  other arithmetic  6.18 us (8%)
  between operations  1.3 us (2%)
    ppermute x7, waiting for transfers between devices, gather_lanes(): lax.ppermute(chunk, 'ctx', [(i, (i + shift) % count) for i in range(count)])  17.2 us
    ppermute x7, starting transfers between devices, scatter_lanes(): lax.ppermute(chunk, 'ctx', [(i, (i + shift) % count) for i in range(count)])  8.96 us
    ppermute x7, waiting for transfers between devices, scatter_lanes(): lax.ppermute(chunk, 'ctx', [(i, (i + shift) % count) for i in range(count)])  7.11 us
    all_to_all x1, starting transfers between devices, all_to_all_ctx(): return lax.all_to_all(stacked, 'ctx', 0, 0, tiled=True)  6.44 us
    dot_general x1, matrix products, gather_matmul(): lax.dot_general(gathered, out_weight, (((1,), (1,)), ((), ())), preferred...  6.3 us
    unnamed x40, local copies, waits for them, and re-layouts  6.25 us
    ppermute x7, starting transfers between devices, gather_lanes(): lax.ppermute(chunk, 'ctx', [(i, (i + shift) % count) for i in range(count)])  5.84 us
    dot_general x5, matrix products, table_times(): jnp.einsum('kn,snc->skc', table, signal, preferred_element_type=jnp.float32)  2.72 us
  transfers between devices with their start and end apart: 18, of which 7 were waited for; matrix products, arithmetic and copies ran while one was open for 18% of the time, Pallas kernels for 0%

profile of v20, /device:TPU:9, one launch (start us, length us, event | category | flops | bytes accessed | tf_op | source)
XLA Modules:
  0.0 74.2 jit_solution(17304296449602764030)
XLA Ops:
  0.6 1.3 %collective-permute-start = (bf16[128,1024]{1,0:T(8,128)(2,1)}, bf16[128,1024]{1,0:T(8,128)(2,1)S(1)}, u32[]{:S(2)}, u32[]{:S(2)}) collective-permute-start(bf16[128,1024]{1,0:T(8,128)(2,1)} %param.17), channel_id=1, source_target_pairs={{0,1},{1,0},{2,3},{3,2},{4,5},{5,4},{6,7},{7,6},{8,9},{9,8},{10,11... | collective-permute-start | bytes 786440 | tf_op jit(solution)/shard_map/ppermute | solution.py:26
  1.9 1.2 %collective-permute-start.1 = (bf16[128,1024]{1,0:T(8,128)(2,1)}, bf16[128,1024]{1,0:T(8,128)(2,1)S(1)}, u32[]{:S(2)}, u32[]{:S(2)}) collective-permute-start(bf16[128,1024]{1,0:T(8,128)(2,1)} %param.17), channel_id=1, source_target_pairs={{0,2},{1,3},{2,0},{3,1},{4,6},{5,7},{6,4},{7,5},{8,10},{9,11},{10,... | collective-permute-start | bytes 786440 | tf_op jit(solution)/shard_map/ppermute | solution.py:26
  3.1 0.2 collective-permute-start.2
  3.3 1.1 %copy.49 = bf16[128,1024]{0,1:T(8,128)(2,1)S(1)} copy(bf16[128,1024]{1,0:T(8,128)(2,1)} %param.14) | data formatting | bytes 524288 | tf_op args[1]
  4.5 1.1 %copy.50 = bf16[128,1024]{0,1:T(8,128)(2,1)S(1)} copy(bf16[128,1024]{1,0:T(8,128)(2,1)} %param.15) | data formatting | bytes 524288 | tf_op args[2]
  5.7 1.2 %copy.51 = bf16[128,1024]{0,1:T(8,128)(2,1)S(1)} copy(bf16[128,1024]{1,0:T(8,128)(2,1)} %param.19) | data formatting | bytes 524288 | tf_op args[6]
  6.9 1.0 %copy.52 = bf16[8,2,128,128]{3,2,1,0:T(8,128)(2,1)} copy(bf16[8,2,128,128]{2,3,0,1:T(8,128)(2,1)S(1)} %pad_maximum_fusion.4) | data formatting | bytes 1048576 | tf_op jit(solution)/shard_map/stack | solution.py:216
  7.9 6.4 %all-to-all-start = ((bf16[8,2,128,128]{3,2,1,0:T(8,128)(2,1)}), bf16[8,2,128,128]{3,2,1,0:T(8,128)(2,1)S(1)}, u32[]{:S(2)}, u32[]{:S(2)}) async-start(bf16[8,2,128,128]{3,2,1,0:T(8,128)(2,1)} %copy.52), calls=%async_computation | async-start | bytes 1048576 | tf_op jit(solution)/shard_map/all_to_all | solution.py:149
  14.4 0.3 collective-permute-done.2
  14.7 0.1 pad_maximum_fusion.1
  14.9 0.7 copy-done.4
  15.7 6.3 %fusion.12 = (bf16[128,1024]{1,0:T(8,128)(2,1)S(1)}, f32[128,1024]{1,0:T(8,128)S(1)}) fusion(bf16[128,1024]{1,0:T(8,128)(2,1)S(1)} %copy-done.4, bf16[1024,4096]{1,0:T(8,128)(2,1)} %param.18, bf16[128,1024]{1,0:T(8,128)(2,1)S(1)} %get-tuple-element.42, bf16[128,1024]{1,0:T(8,128)(2,1)S(1)} %get-tuple-element.43, ...), kind=kOutput, calls=%fused_computation.90 | convolution fusion | flops 1078329344 | bytes 10485760 | tf_op jit(solution)/shard_map/dot_general | solution.py:35
  22.0 0.9 %fusion.13 = (bf16[1,128,1024]{2,1,0:T(8,128)(2,1)S(1)}, bf16[128,1024]{1,0:T(8,128)(2,1)}) fusion(bf16[128,1024]{1,0:T(8,128)(2,1)S(1)} %get-tuple-element.109, f32[128,1024]{1,0:T(8,128)S(1)} %get-tuple-element.110, bf16[128,1024]{1,0:T(8,128)(2,1)S(1)} %copy-done.4, bf16[128,1024]{1,0:T(8,128)(2,1)S(1)} %copy-done.5), kind=kLoop, calls=%fused_computation.91 | loop fusion | flops 1048576 | bytes 1835008 | tf_op jit(solution)/shard_map/stack | solution.py:222
  22.9 0.1 fusion.22
  23.0 3.0 %collective-permute-start.3 = (bf16[2,128,128]{2,1,0:T(8,128)(2,1)S(1)}, bf16[2,128,128]{2,1,0:T(8,128)(2,1)S(1)}, u32[]{:S(2)}, u32[]{:S(2)}) collective-permute-start(bf16[2,128,128]{2,1,0:T(8,128)(2,1)S(1)} %get-tuple-element.66), channel_id=1, source_target_pairs={{0,4},{4,8},{8,12},{12,16},{16,20},{20,24},{24,28},{28,0},{1,5},{5... | collective-permute-start | bytes 196616 | tf_op jit(solution)/shard_map/ppermute | solution.py:178
  26.0 1.4 %collective-permute-start.4 = (bf16[2,128,128]{2,1,0:T(8,128)(2,1)S(1)}, bf16[2,128,128]{2,1,0:T(8,128)(2,1)S(1)}, u32[]{:S(2)}, u32[]{:S(2)}) collective-permute-start(bf16[2,128,128]{2,1,0:T(8,128)(2,1)S(1)} %get-tuple-element.67), channel_id=1, source_target_pairs={{0,8},{4,12},{8,16},{12,20},{16,24},{20,28},{24,0},{28,4},{1,9},{5... | collective-permute-start | bytes 196616 | tf_op jit(solution)/shard_map/ppermute | solution.py:178
  27.3 1.4 %collective-permute-start.6 = (bf16[2,128,128]{2,1,0:T(8,128)(2,1)S(1)}, bf16[2,128,128]{2,1,0:T(8,128)(2,1)S(1)}, u32[]{:S(2)}, u32[]{:S(2)}) collective-permute-start(bf16[2,128,128]{2,1,0:T(8,128)(2,1)S(1)} %get-tuple-element.69), channel_id=1, source_target_pairs={{0,16},{4,20},{8,24},{12,28},{16,0},{20,4},{24,8},{28,12},{1,17},{... | collective-permute-start | bytes 196616 | tf_op jit(solution)/shard_map/ppermute | solution.py:178
  28.7 1.6 %collective-permute-start.7 = (bf16[2,128,128]{2,1,0:T(8,128)(2,1)S(1)}, bf16[2,128,128]{2,1,0:T(8,128)(2,1)S(1)}, u32[]{:S(2)}, u32[]{:S(2)}) collective-permute-start(bf16[2,128,128]{2,1,0:T(8,128)(2,1)S(1)} %get-tuple-element.70), channel_id=1, source_target_pairs={{0,20},{4,24},{8,28},{12,0},{16,4},{20,8},{24,12},{28,16},{1,21},{... | collective-permute-start | bytes 196616 | tf_op jit(solution)/shard_map/ppermute | solution.py:178
  30.3 1.2 %collective-permute-start.8 = (bf16[2,128,128]{2,1,0:T(8,128)(2,1)S(1)}, bf16[2,128,128]{2,1,0:T(8,128)(2,1)S(1)}, u32[]{:S(2)}, u32[]{:S(2)}) collective-permute-start(bf16[2,128,128]{2,1,0:T(8,128)(2,1)S(1)} %fusion.29), channel_id=1, source_target_pairs={{0,24},{4,28},{8,0},{12,4},{16,8},{20,12},{24,16},{28,20},{1,25},{... | collective-permute-start | bytes 196616 | tf_op jit(solution)/shard_map/ppermute | solution.py:178
  31.6 0.4 collective-permute-start.9
  32.1 5.0 %collective-permute-done.6 = bf16[2,128,128]{2,1,0:T(8,128)(2,1)S(1)} collective-permute-done((bf16[2,128,128]{2,1,0:T(8,128)(2,1)S(1)}, bf16[2,128,128]{2,1,0:T(8,128)(2,1)S(1)}, u32[]{:S(2)}, u32[]{:S(2)}) %collective-permute-start.6) | collective-permute-done | bytes 65568 | tf_op jit(solution)/shard_map/ppermute | solution.py:178
  37.1 2.1 %collective-permute-done.8 = bf16[2,128,128]{2,1,0:T(8,128)(2,1)S(1)} collective-permute-done((bf16[2,128,128]{2,1,0:T(8,128)(2,1)S(1)}, bf16[2,128,128]{2,1,0:T(8,128)(2,1)S(1)}, u32[]{:S(2)}, u32[]{:S(2)}) %collective-permute-start.8) | collective-permute-done | bytes 65568 | tf_op jit(solution)/shard_map/ppermute | solution.py:178
  39.6 0.1 pad_maximum_fusion.3
  39.7 0.1 pad_maximum_fusion.2
  39.8 0.6 copy-done.9
  40.4 0.7 convolution_bitcast_fusion
  41.1 0.1 copy-done.8
  41.2 0.6 convolution_bitcast_fusion.1
  41.8 0.6 slice_add_fusion.3
  42.5 0.2 fusion.11
  42.9 0.4 add_add_fusion.2
  43.3 0.4 subtract_add_fusion.1
  43.7 0.1 slice_bitcast_fusion.17
  43.8 0.4 add_add_fusion.1
  44.3 0.4 subtract_add_fusion
  44.7 0.2 fusion.40
  45.1 0.1 pad_maximum_fusion
  45.3 0.1 bitcast_convert_fusion
  45.4 0.3 fusion
  45.7 0.6 copy-done.2
  46.3 0.5 fusion.38
  46.8 0.5 fusion.39
  47.3 0.4 copy-done.7
  47.7 0.5 add_add_fusion
  48.1 0.2 copy-done.10
  48.4 0.3 multiply_add_fusion
  49.0 0.1 copy.60
  49.2 0.1 copy.55
  49.3 0.1 copy.56
  49.4 1.1 %collective-permute-start.10 = (f32[128,256]{1,0:T(8,128)S(1)}, f32[128,256]{1,0:T(8,128)S(1)}, u32[]{:S(2)}, u32[]{:S(2)}) collective-permute-start(f32[128,256]{1,0:T(8,128)S(1)} %bitcast.223), channel_id=1, source_target_pairs={{0,4},{4,8},{8,12},{12,16},{16,20},{20,24},{24,28},{28,0},{1,5},{5... | collective-permute-start | bytes 393224 | tf_op jit(solution)/shard_map/ppermute | solution.py:198
  50.6 0.1 copy.57
  50.7 1.9 %collective-permute-start.11 = (f32[128,256]{1,0:T(8,128)S(1)}, f32[128,256]{1,0:T(8,128)S(1)}, u32[]{:S(2)}, u32[]{:S(2)}) collective-permute-start(f32[128,256]{1,0:T(8,128)S(1)} %bitcast.222), channel_id=1, source_target_pairs={{0,8},{4,12},{8,16},{12,20},{16,24},{20,28},{24,0},{28,4},{1,9},{5... | collective-permute-start | bytes 393224 | tf_op jit(solution)/shard_map/ppermute | solution.py:198
  52.5 0.1 copy.58
  52.6 2.2 %collective-permute-start.12 = (f32[128,256]{1,0:T(8,128)S(1)}, f32[128,256]{1,0:T(8,128)S(1)}, u32[]{:S(2)}, u32[]{:S(2)}) collective-permute-start(f32[128,256]{1,0:T(8,128)S(1)} %bitcast.221), channel_id=1, source_target_pairs={{0,12},{4,16},{8,20},{12,24},{16,28},{20,0},{24,4},{28,8},{1,13},{... | collective-permute-start | bytes 393224 | tf_op jit(solution)/shard_map/ppermute | solution.py:198
  54.8 0.1 copy.59
  54.9 0.2 collective-permute-start.13
  55.1 0.1 copy.61
  55.2 0.1 copy.62
  55.5 0.8 %collective-permute-done.10 = f32[128,256]{1,0:T(8,128)S(1)} collective-permute-done((f32[128,256]{1,0:T(8,128)S(1)}, f32[128,256]{1,0:T(8,128)S(1)}, u32[]{:S(2)}, u32[]{:S(2)}) %collective-permute-start.10) | collective-permute-done | bytes 131104 | tf_op jit(solution)/shard_map/ppermute | solution.py:198
  56.3 0.4 collective-permute-start.15
  56.7 3.5 %collective-permute-done.11 = f32[128,256]{1,0:T(8,128)S(1)} collective-permute-done((f32[128,256]{1,0:T(8,128)S(1)}, f32[128,256]{1,0:T(8,128)S(1)}, u32[]{:S(2)}, u32[]{:S(2)}) %collective-permute-start.11) | collective-permute-done | bytes 131104 | tf_op jit(solution)/shard_map/ppermute | solution.py:198
  60.2 10.1 %collective-permute-done.12 = f32[128,256]{1,0:T(8,128)S(1)} collective-permute-done((f32[128,256]{1,0:T(8,128)S(1)}, f32[128,256]{1,0:T(8,128)S(1)}, u32[]{:S(2)}, u32[]{:S(2)}) %collective-permute-start.12) | collective-permute-done | bytes 131104 | tf_op jit(solution)/shard_map/ppermute | solution.py:198
  70.3 2.8 %collective-permute-done.13 = f32[128,256]{1,0:T(8,128)S(1)} collective-permute-done((f32[128,256]{1,0:T(8,128)S(1)}, f32[128,256]{1,0:T(8,128)S(1)}, u32[]{:S(2)}, u32[]{:S(2)}) %collective-permute-start.13) | collective-permute-done | bytes 131104 | tf_op jit(solution)/shard_map/ppermute | solution.py:198
  73.3 0.9 %multiply_convert_fusion = (bf16[128,1024]{1,0:T(8,128)(2,1)}, bf16[128,1024]{1,0:T(8,128)(2,1)}) fusion(f32[128,1024]{1,0:T(8,128)S(1)} %get-tuple-element.76, bf16[128,1024]{1,0:T(8,128)(2,1)S(1)} %copy-done.1, bf16[128,1024]{1,0:T(8,128)(2,1)S(1)} %copy-done), kind=kLoop, calls=%fused_computation.80 | loop fusion | flops 786432 | bytes 1572864 | tf_op jit(solution)/shard_map/convert_element_type | solution.py:236
  (82 shorter events, 1.6 us)
Async XLA Ops:
  0.6 13.7 %collective-permute-start = (bf16[128,1024]{1,0:T(8,128)(2,1)}, bf16[128,1024]{1,0:T(8,128)(2,1)S(1)}, u32[]{:S(2)}, u32[]{:S(2)}) collective-permute-start(bf16[128,1024]{1,0:T(8,128)(2,1)} %param.17), channel_id=1, source_target_pairs={{0,1},{1,0},{2,3},{3,2},{4,5},{5,4},{6,7},{7,6},{8,9},{9,8},{10,11... | collective-permute-start | bytes 786440 | tf_op jit(solution)/shard_map/ppermute | solution.py:26
  1.9 12.5 %collective-permute-start.1 = (bf16[128,1024]{1,0:T(8,128)(2,1)}, bf16[128,1024]{1,0:T(8,128)(2,1)S(1)}, u32[]{:S(2)}, u32[]{:S(2)}) collective-permute-start(bf16[128,1024]{1,0:T(8,128)(2,1)} %param.17), channel_id=1, source_target_pairs={{0,2},{1,3},{2,0},{3,1},{4,6},{5,7},{6,4},{7,5},{8,10},{9,11},{10,... | collective-permute-start | bytes 786440 | tf_op jit(solution)/shard_map/ppermute | solution.py:26
  3.1 11.6 %collective-permute-start.2 = (bf16[128,1024]{1,0:T(8,128)(2,1)}, bf16[128,1024]{1,0:T(8,128)(2,1)S(1)}, u32[]{:S(2)}, u32[]{:S(2)}) collective-permute-start(bf16[128,1024]{1,0:T(8,128)(2,1)} %param.17), channel_id=1, source_target_pairs={{0,3},{1,2},{2,1},{3,0},{4,7},{5,6},{6,5},{7,4},{8,11},{9,10},{10,... | collective-permute-start | bytes 786440 | tf_op jit(solution)/shard_map/ppermute | solution.py:26
  5.7 9.0 %copy-start.6 = (bf16[128,1024]{1,0:T(8,128)(2,1)S(1)}, bf16[128,1024]{1,0:T(8,128)(2,1)}, u32[]{:S(2)}) copy-start(bf16[128,1024]{1,0:T(8,128)(2,1)} %param.17) | copy-start | bytes 786436
  7.9 31.6 %all-to-all-start = ((bf16[8,2,128,128]{3,2,1,0:T(8,128)(2,1)}), bf16[8,2,128,128]{3,2,1,0:T(8,128)(2,1)S(1)}, u32[]{:S(2)}, u32[]{:S(2)}) async-start(bf16[8,2,128,128]{3,2,1,0:T(8,128)(2,1)} %copy.52), calls=%async_computation | async-start | bytes 1048576 | tf_op jit(solution)/shard_map/all_to_all | solution.py:149
  14.7 1.0 %copy-start.4 = (bf16[128,1024]{1,0:T(8,128)(2,1)S(1)}, bf16[128,1024]{1,0:T(8,128)(2,1)}, u32[]{:S(2)}) copy-start(bf16[128,1024]{1,0:T(8,128)(2,1)} %param.13) | copy-start | bytes 786436
  15.7 6.3 %copy-start.5 = (bf16[128,1024]{1,0:T(8,128)(2,1)S(1)}, bf16[128,1024]{1,0:T(8,128)(2,1)}, u32[]{:S(2)}) copy-start(bf16[128,1024]{1,0:T(8,128)(2,1)} %param.16) | copy-start | bytes 786436
  23.0 7.4 %collective-permute-start.3 = (bf16[2,128,128]{2,1,0:T(8,128)(2,1)S(1)}, bf16[2,128,128]{2,1,0:T(8,128)(2,1)S(1)}, u32[]{:S(2)}, u32[]{:S(2)}) collective-permute-start(bf16[2,128,128]{2,1,0:T(8,128)(2,1)S(1)} %get-tuple-element.66), channel_id=1, source_target_pairs={{0,4},{4,8},{8,12},{12,16},{16,20},{20,24},{24,28},{28,0},{1,5},{5... | collective-permute-start | bytes 196616 | tf_op jit(solution)/shard_map/ppermute | solution.py:178
  26.0 5.6 %collective-permute-start.4 = (bf16[2,128,128]{2,1,0:T(8,128)(2,1)S(1)}, bf16[2,128,128]{2,1,0:T(8,128)(2,1)S(1)}, u32[]{:S(2)}, u32[]{:S(2)}) collective-permute-start(bf16[2,128,128]{2,1,0:T(8,128)(2,1)S(1)} %get-tuple-element.67), channel_id=1, source_target_pairs={{0,8},{4,12},{8,16},{12,20},{16,24},{20,28},{24,0},{28,4},{1,9},{5... | collective-permute-start | bytes 196616 | tf_op jit(solution)/shard_map/ppermute | solution.py:178
  27.3 4.7 %collective-permute-start.5 = (bf16[2,128,128]{2,1,0:T(8,128)(2,1)S(1)}, bf16[2,128,128]{2,1,0:T(8,128)(2,1)S(1)}, u32[]{:S(2)}, u32[]{:S(2)}) collective-permute-start(bf16[2,128,128]{2,1,0:T(8,128)(2,1)S(1)} %get-tuple-element.68), channel_id=1, source_target_pairs={{0,12},{4,16},{8,20},{12,24},{16,28},{20,0},{24,4},{28,8},{1,13},{... | collective-permute-start | bytes 196616 | tf_op jit(solution)/shard_map/ppermute | solution.py:178
  27.3 9.8 %collective-permute-start.6 = (bf16[2,128,128]{2,1,0:T(8,128)(2,1)S(1)}, bf16[2,128,128]{2,1,0:T(8,128)(2,1)S(1)}, u32[]{:S(2)}, u32[]{:S(2)}) collective-permute-start(bf16[2,128,128]{2,1,0:T(8,128)(2,1)S(1)} %get-tuple-element.69), channel_id=1, source_target_pairs={{0,16},{4,20},{8,24},{12,28},{16,0},{20,4},{24,8},{28,12},{1,17},{... | collective-permute-start | bytes 196616 | tf_op jit(solution)/shard_map/ppermute | solution.py:178
  28.7 8.4 %collective-permute-start.7 = (bf16[2,128,128]{2,1,0:T(8,128)(2,1)S(1)}, bf16[2,128,128]{2,1,0:T(8,128)(2,1)S(1)}, u32[]{:S(2)}, u32[]{:S(2)}) collective-permute-start(bf16[2,128,128]{2,1,0:T(8,128)(2,1)S(1)} %get-tuple-element.70), channel_id=1, source_target_pairs={{0,20},{4,24},{8,28},{12,0},{16,4},{20,8},{24,12},{28,16},{1,21},{... | collective-permute-start | bytes 196616 | tf_op jit(solution)/shard_map/ppermute | solution.py:178
  30.3 8.9 %collective-permute-start.8 = (bf16[2,128,128]{2,1,0:T(8,128)(2,1)S(1)}, bf16[2,128,128]{2,1,0:T(8,128)(2,1)S(1)}, u32[]{:S(2)}, u32[]{:S(2)}) collective-permute-start(bf16[2,128,128]{2,1,0:T(8,128)(2,1)S(1)} %fusion.29), channel_id=1, source_target_pairs={{0,24},{4,28},{8,0},{12,4},{16,8},{20,12},{24,16},{28,20},{1,25},{... | collective-permute-start | bytes 196616 | tf_op jit(solution)/shard_map/ppermute | solution.py:178
  31.6 7.6 %collective-permute-start.9 = (bf16[2,128,128]{2,1,0:T(8,128)(2,1)S(1)}, bf16[2,128,128]{2,1,0:T(8,128)(2,1)S(1)}, u32[]{:S(2)}, u32[]{:S(2)}) collective-permute-start(bf16[2,128,128]{2,1,0:T(8,128)(2,1)S(1)} %get-tuple-element.65), channel_id=1, source_target_pairs={{0,28},{4,0},{8,4},{12,8},{16,12},{20,16},{24,20},{28,24},{1,29},{... | collective-permute-start | bytes 196616 | tf_op jit(solution)/shard_map/ppermute | solution.py:178
  39.6 0.8 %copy-start.9 = (bf16[256,128,1]{1,0,2:T(8,128)(2,1)S(1)}, bf16[256,128,1]{1,0,2:T(8,128)(2,1)}, u32[]{:S(2)}) copy-start(bf16[256,128,1]{1,0,2:T(8,128)(2,1)} %constant.244) | copy-start | bytes 196612
  40.4 0.8 %copy-start.8 = (bf16[256,128,1]{1,0,2:T(8,128)(2,1)S(1)}, bf16[256,128,1]{1,0,2:T(8,128)(2,1)}, u32[]{:S(2)}) copy-start(bf16[256,128,1]{1,0,2:T(8,128)(2,1)} %constant.245) | copy-start | bytes 196612
  43.8 0.8 %copy-start.11 = (bf16[128,1,1]{0,1,2:T(2,128)(2,1)S(1)}, bf16[128,1,1]{0,1,2:T(2,128)(2,1)}, u32[]{:S(2)}) copy-start(bf16[128,1,1]{0,1,2:T(2,128)(2,1)} %constant.248) | copy-start | bytes 772
  45.4 0.9 %copy-start.2 = (bf16[256,256,1]{1,0,2:T(8,128)(2,1)S(1)}, bf16[256,256,1]{1,0,2:T(8,128)(2,1)}, u32[]{:S(2)}) copy-start(bf16[256,256,1]{1,0,2:T(8,128)(2,1)} %constant.246) | copy-start | bytes 393220
  46.8 0.9 %copy-start.7 = (bf16[256,256,1]{1,0,2:T(8,128)(2,1)S(1)}, bf16[256,256,1]{1,0,2:T(8,128)(2,1)}, u32[]{:S(2)}) copy-start(bf16[256,256,1]{1,0,2:T(8,128)(2,1)} %constant.247) | copy-start | bytes 393220
  47.7 0.7 copy-start.10
  49.1 24.0 %collective-permute-start.14 = (f32[128,256]{1,0:T(8,128)S(1)}, f32[128,256]{1,0:T(8,128)S(1)}, u32[]{:S(2)}, u32[]{:S(2)}) collective-permute-start(f32[128,256]{1,0:T(8,128)S(1)} %bitcast.217), channel_id=1, source_target_pairs={{0,20},{4,24},{8,28},{12,0},{16,4},{20,8},{24,12},{28,16},{1,21},{... | collective-permute-start | bytes 393224 | tf_op jit(solution)/shard_map/ppermute | solution.py:198
  49.4 6.8 %collective-permute-start.10 = (f32[128,256]{1,0:T(8,128)S(1)}, f32[128,256]{1,0:T(8,128)S(1)}, u32[]{:S(2)}, u32[]{:S(2)}) collective-permute-start(f32[128,256]{1,0:T(8,128)S(1)} %bitcast.223), channel_id=1, source_target_pairs={{0,4},{4,8},{8,12},{12,16},{16,20},{20,24},{24,28},{28,0},{1,5},{5... | collective-permute-start | bytes 393224 | tf_op jit(solution)/shard_map/ppermute | solution.py:198
  50.7 9.5 %collective-permute-start.11 = (f32[128,256]{1,0:T(8,128)S(1)}, f32[128,256]{1,0:T(8,128)S(1)}, u32[]{:S(2)}, u32[]{:S(2)}) collective-permute-start(f32[128,256]{1,0:T(8,128)S(1)} %bitcast.222), channel_id=1, source_target_pairs={{0,8},{4,12},{8,16},{12,20},{16,24},{20,28},{24,0},{28,4},{1,9},{5... | collective-permute-start | bytes 393224 | tf_op jit(solution)/shard_map/ppermute | solution.py:198
  52.5 20.7 %copy-start = (bf16[128,1024]{1,0:T(8,128)(2,1)S(1)}, bf16[128,1024]{1,0:T(8,128)(2,1)}, u32[]{:S(2)}) copy-start(bf16[128,1024]{1,0:T(8,128)(2,1)} %param.15) | copy-start | bytes 786436
  52.5 20.7 %copy-start.1 = (bf16[128,1024]{1,0:T(8,128)(2,1)S(1)}, bf16[128,1024]{1,0:T(8,128)(2,1)}, u32[]{:S(2)}) copy-start(bf16[128,1024]{1,0:T(8,128)(2,1)} %param.14) | copy-start | bytes 786436
  52.6 17.7 %collective-permute-start.12 = (f32[128,256]{1,0:T(8,128)S(1)}, f32[128,256]{1,0:T(8,128)S(1)}, u32[]{:S(2)}, u32[]{:S(2)}) collective-permute-start(f32[128,256]{1,0:T(8,128)S(1)} %bitcast.221), channel_id=1, source_target_pairs={{0,12},{4,16},{8,20},{12,24},{16,28},{20,0},{24,4},{28,8},{1,13},{... | collective-permute-start | bytes 393224 | tf_op jit(solution)/shard_map/ppermute | solution.py:198
  54.9 18.2 %collective-permute-start.13 = (f32[128,256]{1,0:T(8,128)S(1)}, f32[128,256]{1,0:T(8,128)S(1)}, u32[]{:S(2)}, u32[]{:S(2)}) collective-permute-start(f32[128,256]{1,0:T(8,128)S(1)} %bitcast.220), channel_id=1, source_target_pairs={{0,16},{4,20},{8,24},{12,28},{16,0},{20,4},{24,8},{28,12},{1,17},{... | collective-permute-start | bytes 393224 | tf_op jit(solution)/shard_map/ppermute | solution.py:198
  56.3 16.9 %collective-permute-start.15 = (f32[128,256]{1,0:T(8,128)S(1)}, f32[128,256]{1,0:T(8,128)S(1)}, u32[]{:S(2)}, u32[]{:S(2)}) collective-permute-start(f32[128,256]{1,0:T(8,128)S(1)} %bitcast.219), channel_id=1, source_target_pairs={{0,24},{4,28},{8,0},{12,4},{16,8},{20,12},{24,16},{28,20},{1,25},{... | collective-permute-start | bytes 393224 | tf_op jit(solution)/shard_map/ppermute | solution.py:198
  60.2 13.0 %collective-permute-start.16 = (f32[128,256]{1,0:T(8,128)S(1)}, f32[128,256]{1,0:T(8,128)S(1)}, u32[]{:S(2)}, u32[]{:S(2)}) collective-permute-start(f32[128,256]{1,0:T(8,128)S(1)} %bitcast.218), channel_id=1, source_target_pairs={{0,28},{4,0},{8,4},{12,8},{16,12},{20,16},{24,20},{28,24},{1,29},{... | collective-permute-start | bytes 393224 | tf_op jit(solution)/shard_map/ppermute | solution.py:198
  73.2 1.0 %copy-start.3 = (f32[128,1024]{1,0:T(8,128)}, f32[128,1024]{1,0:T(8,128)S(1)}, u32[]{:S(2)}) copy-start(f32[128,1024]{1,0:T(8,128)S(1)} %get-tuple-element.75) | copy-start | bytes 1572868

commit v21 on v18

--- a/solution.py
+++ b/solution.py
@@ -215,11 +215,11 @@
     d_gated = gather_matmul(out_grad, out_weight)
     dq_grad = (d_gated * saved_conv.astype(jnp.float32)).astype(jnp.bfloat16)
     dz = d_gated * q_proj.astype(jnp.float32)
-    dz_hi, dz_lo = split_bf16(dz)
-    dz_t = scatter_lanes(jnp.stack([dz_hi, dz_lo]), sub)
+    dz_t = scatter_lanes(dz, sub)
+    dz_hi, dz_lo = split_bf16(dz_t.reshape(seq, sub))
     du_t, filter_t = long_correlations(
-        dz_t[:, 0].reshape(seq, sub),
-        dz_t[:, 1].reshape(seq, sub),
+        dz_hi,
+        dz_lo,
         inputs_t[:, 0].reshape(seq, sub),
         inputs_t[:, 1].reshape(seq, sub),
         float(seq) ** -0.5,

time: 75.6 us -> 75.6 us (level)
  other arithmetic: 6.18 us -> 5.26 us
    another operation x3 -> x0, other arithmetic: 1 us -> none  [body(): dz_t = scatter_lanes(jnp.stack([dz_hi, dz_lo]), sub)]
    unnamed x40 -> x41, local copies, waits for them, and re-layouts: 6.25 us -> 6.22 us
  transfers between devices with their start and end apart: 18 -> 18, of which waited for: 7 -> 10; matrix products, arithmetic and copies ran while one was open for 18% -> 17% of each run, Pallas kernels for 0% -> 0%
where the time goes in v21:
time: 75.6 us; the launch traced here: 74.3 us
  waiting for transfers between devices  25.2 us (33%)
  starting transfers between devices  23.8 us (31%)
  matrix products  9.96 us (13%)
  local copies, waits for them, and re-layouts  8.82 us (12%)
  other arithmetic  5.26 us (7%)
  between operations  1.27 us (2%)
    ppermute x7, waiting for transfers between devices, gather_lanes(): lax.ppermute(chunk, 'ctx', [(i, (i + shift) % count) for i in range(count)])  17.5 us
    ppermute x7, starting transfers between devices, scatter_lanes(): lax.ppermute(chunk, 'ctx', [(i, (i + shift) % count) for i in range(count)])  8.95 us
    ppermute x7, waiting for transfers between devices, scatter_lanes(): lax.ppermute(chunk, 'ctx', [(i, (i + shift) % count) for i in range(count)])  7.35 us
    dot_general x1, matrix products, gather_matmul(): lax.dot_general(gathered, out_weight, (((1,), (1,)), ((), ())), preferred...  6.99 us
    all_to_all x1, starting transfers between devices, all_to_all_ctx(): return lax.all_to_all(stacked, 'ctx', 0, 0, tiled=True)  6.44 us
    unnamed x41, local copies, waits for them, and re-layouts  6.22 us
    ppermute x7, starting transfers between devices, gather_lanes(): lax.ppermute(chunk, 'ctx', [(i, (i + shift) % count) for i in range(count)])  5.69 us
    dot_general x5, matrix products, table_times(): jnp.einsum('kn,snc->skc', table, signal, preferred_element_type=jnp.float32)  2.73 us
  transfers between devices with their start and end apart: 18, of which 10 were waited for; matrix products, arithmetic and copies ran while one was open for 17% of the time, Pallas kernels for 0%

profile of v21, /device:TPU:9, one launch (start us, length us, event | category | flops | bytes accessed | tf_op | source)
XLA Modules:
  0.0 74.3 jit_solution(12917146186083638315)
XLA Ops:
  0.6 1.3 %collective-permute-start = (bf16[128,1024]{1,0:T(8,128)(2,1)}, bf16[128,1024]{1,0:T(8,128)(2,1)S(1)}, u32[]{:S(2)}, u32[]{:S(2)}) collective-permute-start(bf16[128,1024]{1,0:T(8,128)(2,1)} %param.17), channel_id=1, source_target_pairs={{0,1},{1,0},{2,3},{3,2},{4,5},{5,4},{6,7},{7,6},{8,9},{9,8},{10,11... | collective-permute-start | bytes 786440 | tf_op jit(solution)/shard_map/ppermute | solution.py:26
  1.9 1.2 %collective-permute-start.1 = (bf16[128,1024]{1,0:T(8,128)(2,1)}, bf16[128,1024]{1,0:T(8,128)(2,1)S(1)}, u32[]{:S(2)}, u32[]{:S(2)}) collective-permute-start(bf16[128,1024]{1,0:T(8,128)(2,1)} %param.17), channel_id=1, source_target_pairs={{0,2},{1,3},{2,0},{3,1},{4,6},{5,7},{6,4},{7,5},{8,10},{9,11},{10,... | collective-permute-start | bytes 786440 | tf_op jit(solution)/shard_map/ppermute | solution.py:26
  3.1 0.2 collective-permute-start.2
  3.3 1.1 %copy.49 = bf16[128,1024]{0,1:T(8,128)(2,1)S(1)} copy(bf16[128,1024]{1,0:T(8,128)(2,1)} %param.14) | data formatting | bytes 524288 | tf_op args[1]
  4.5 1.1 %copy.50 = bf16[128,1024]{0,1:T(8,128)(2,1)S(1)} copy(bf16[128,1024]{1,0:T(8,128)(2,1)} %param.15) | data formatting | bytes 524288 | tf_op args[2]
  5.7 1.2 %copy.51 = bf16[128,1024]{0,1:T(8,128)(2,1)S(1)} copy(bf16[128,1024]{1,0:T(8,128)(2,1)} %param.19) | data formatting | bytes 524288 | tf_op args[6]
  6.9 1.0 %copy.52 = bf16[8,2,128,128]{3,2,1,0:T(8,128)(2,1)} copy(bf16[8,2,128,128]{2,3,0,1:T(8,128)(2,1)S(1)} %pad_maximum_fusion.4) | data formatting | bytes 1048576 | tf_op jit(solution)/shard_map/stack | solution.py:213
  7.9 6.4 %all-to-all-start = ((bf16[8,2,128,128]{3,2,1,0:T(8,128)(2,1)}), bf16[8,2,128,128]{3,2,1,0:T(8,128)(2,1)S(1)}, u32[]{:S(2)}, u32[]{:S(2)}) async-start(bf16[8,2,128,128]{3,2,1,0:T(8,128)(2,1)} %copy.52), calls=%async_computation | async-start | bytes 1048576 | tf_op jit(solution)/shard_map/all_to_all | solution.py:149
  14.4 0.3 collective-permute-done.2
  14.7 0.1 pad_maximum_fusion.1
  14.9 0.7 copy-done.10
  15.8 7.0 %convert_multiply_fusion = (f32[128,1024]{1,0:T(8,128)S(1)}, bf16[128,1024]{1,0:T(8,128)(2,1)}) fusion(bf16[128,1024]{1,0:T(8,128)(2,1)S(1)} %copy-done.10, bf16[128,1024]{1,0:T(8,128)(2,1)S(1)} %copy-done.11, bf16[1024,4096]{1,0:T(8,128)(2,1)} %param.18, bf16[128,1024]{1,0:T(8,128)(2,1)S(1)} %get-tuple-element.42, ...), kind=kOutput, calls=%fused_computation.74 | convolution fusion | flops 1078591488 | bytes 10747904 | tf_op jit(solution)/shard_map/dot_general | solution.py:35
  22.8 3.0 %collective-permute-start.3 = (f32[128,128]{1,0:T(8,128)S(1)}, f32[128,128]{1,0:T(8,128)S(1)}, u32[]{:S(2)}, u32[]{:S(2)}) collective-permute-start(f32[128,128]{1,0:T(8,128)S(1)} %get-tuple-element.69), channel_id=1, source_target_pairs={{0,4},{4,8},{8,12},{12,16},{16,20},{20,24},{24,28},{28,0},{1,5},{5... | collective-permute-start | bytes 196616 | tf_op jit(solution)/shard_map/ppermute | solution.py:178
  25.8 1.3 %collective-permute-start.4 = (f32[128,128]{1,0:T(8,128)S(1)}, f32[128,128]{1,0:T(8,128)S(1)}, u32[]{:S(2)}, u32[]{:S(2)}) collective-permute-start(f32[128,128]{1,0:T(8,128)S(1)} %get-tuple-element.68), channel_id=1, source_target_pairs={{0,8},{4,12},{8,16},{12,20},{16,24},{20,28},{24,0},{28,4},{1,9},{5... | collective-permute-start | bytes 196616 | tf_op jit(solution)/shard_map/ppermute | solution.py:178
  27.1 1.4 %collective-permute-start.6 = (f32[128,128]{1,0:T(8,128)S(1)}, f32[128,128]{1,0:T(8,128)S(1)}, u32[]{:S(2)}, u32[]{:S(2)}) collective-permute-start(f32[128,128]{1,0:T(8,128)S(1)} %get-tuple-element.66), channel_id=1, source_target_pairs={{0,16},{4,20},{8,24},{12,28},{16,0},{20,4},{24,8},{28,12},{1,17},{... | collective-permute-start | bytes 196616 | tf_op jit(solution)/shard_map/ppermute | solution.py:178
  28.5 1.6 %collective-permute-start.7 = (f32[128,128]{1,0:T(8,128)S(1)}, f32[128,128]{1,0:T(8,128)S(1)}, u32[]{:S(2)}, u32[]{:S(2)}) collective-permute-start(f32[128,128]{1,0:T(8,128)S(1)} %get-tuple-element.65), channel_id=1, source_target_pairs={{0,20},{4,24},{8,28},{12,0},{16,4},{20,8},{24,12},{28,16},{1,21},{... | collective-permute-start | bytes 196616 | tf_op jit(solution)/shard_map/ppermute | solution.py:178
  30.1 1.2 %collective-permute-start.8 = (f32[128,128]{1,0:T(8,128)S(1)}, f32[128,128]{1,0:T(8,128)S(1)}, u32[]{:S(2)}, u32[]{:S(2)}) collective-permute-start(f32[128,128]{1,0:T(8,128)S(1)} %get-tuple-element.64), channel_id=1, source_target_pairs={{0,24},{4,28},{8,0},{12,4},{16,8},{20,12},{24,16},{28,20},{1,25},{... | collective-permute-start | bytes 196616 | tf_op jit(solution)/shard_map/ppermute | solution.py:178
  31.3 0.5 collective-permute-start.9
  31.8 3.0 %collective-permute-done.5 = f32[128,128]{1,0:T(8,128)S(1)} collective-permute-done((f32[128,128]{1,0:T(8,128)S(1)}, f32[128,128]{1,0:T(8,128)S(1)}, u32[]{:S(2)}, u32[]{:S(2)}) %collective-permute-start.5) | collective-permute-done | bytes 65568 | tf_op jit(solution)/shard_map/ppermute | solution.py:178
  34.8 2.2 %collective-permute-done.6 = f32[128,128]{1,0:T(8,128)S(1)} collective-permute-done((f32[128,128]{1,0:T(8,128)S(1)}, f32[128,128]{1,0:T(8,128)S(1)}, u32[]{:S(2)}, u32[]{:S(2)}) %collective-permute-start.6) | collective-permute-done | bytes 65568 | tf_op jit(solution)/shard_map/ppermute | solution.py:178
  37.1 1.9 %collective-permute-done.8 = f32[128,128]{1,0:T(8,128)S(1)} collective-permute-done((f32[128,128]{1,0:T(8,128)S(1)}, f32[128,128]{1,0:T(8,128)S(1)}, u32[]{:S(2)}, u32[]{:S(2)}) %collective-permute-start.8) | collective-permute-done | bytes 65568 | tf_op jit(solution)/shard_map/ppermute | solution.py:178
  39.0 0.2 collective-permute-done.9
  39.6 0.1 pad_maximum_fusion.2
  39.8 0.6 copy-done.7
  40.4 0.7 convolution_bitcast_fusion
  41.1 0.1 copy-done.6
  41.2 0.6 convolution_bitcast_fusion.1
  41.8 0.6 slice_add_fusion.3
  42.5 0.2 fusion.12
  42.8 0.4 add_add_fusion.2
  43.3 0.4 subtract_add_fusion.1
  43.7 0.1 slice_bitcast_fusion.32
  43.8 0.4 add_add_fusion.1
  44.2 0.4 subtract_add_fusion
  44.6 0.2 fusion.47
  45.1 0.1 pad_maximum_fusion
  45.2 0.1 bitcast_convert_fusion
  45.4 0.3 fusion
  45.7 0.6 copy-done.2
  46.3 0.5 fusion.45
  46.7 0.5 fusion.46
  47.2 0.4 copy-done.5
  47.6 0.5 add_add_fusion
  48.1 0.2 copy-done.8
  48.3 0.3 multiply_add_fusion
  48.9 0.1 copy.60
  49.2 0.1 copy.55
  49.3 0.1 copy.56
  49.4 1.1 %collective-permute-start.10 = (f32[2,128,128]{2,1,0:T(8,128)S(1)}, f32[2,128,128]{2,1,0:T(8,128)S(1)}, u32[]{:S(2)}, u32[]{:S(2)}) collective-permute-start(f32[2,128,128]{2,1,0:T(8,128)S(1)} %bitcast.286), channel_id=1, source_target_pairs={{0,4},{4,8},{8,12},{12,16},{16,20},{20,24},{24,28},{28,0},{1,5},{5... | collective-permute-start | bytes 393224 | tf_op jit(solution)/shard_map/ppermute | solution.py:197
  50.5 0.1 copy.57
  50.6 1.9 %collective-permute-start.11 = (f32[2,128,128]{2,1,0:T(8,128)S(1)}, f32[2,128,128]{2,1,0:T(8,128)S(1)}, u32[]{:S(2)}, u32[]{:S(2)}) collective-permute-start(f32[2,128,128]{2,1,0:T(8,128)S(1)} %bitcast.285), channel_id=1, source_target_pairs={{0,8},{4,12},{8,16},{12,20},{16,24},{20,28},{24,0},{28,4},{1,9},{5... | collective-permute-start | bytes 393224 | tf_op jit(solution)/shard_map/ppermute | solution.py:197
  52.5 0.1 copy.58
  52.6 1.9 %collective-permute-start.12 = (f32[2,128,128]{2,1,0:T(8,128)S(1)}, f32[2,128,128]{2,1,0:T(8,128)S(1)}, u32[]{:S(2)}, u32[]{:S(2)}) collective-permute-start(f32[2,128,128]{2,1,0:T(8,128)S(1)} %bitcast.284), channel_id=1, source_target_pairs={{0,12},{4,16},{8,20},{12,24},{16,28},{20,0},{24,4},{28,8},{1,13},{... | collective-permute-start | bytes 393224 | tf_op jit(solution)/shard_map/ppermute | solution.py:197
  54.6 0.1 copy.59
  54.7 0.3 collective-permute-start.13
  55.0 0.1 copy.61
  55.1 0.1 copy.62
  55.3 0.8 %collective-permute-done.10 = f32[2,128,128]{2,1,0:T(8,128)S(1)} collective-permute-done((f32[2,128,128]{2,1,0:T(8,128)S(1)}, f32[2,128,128]{2,1,0:T(8,128)S(1)}, u32[]{:S(2)}, u32[]{:S(2)}) %collective-permute-start.10) | collective-permute-done | bytes 131104 | tf_op jit(solution)/shard_map/ppermute | solution.py:197
  56.1 0.4 collective-permute-start.15
  56.5 3.5 %collective-permute-done.11 = f32[2,128,128]{2,1,0:T(8,128)S(1)} collective-permute-done((f32[2,128,128]{2,1,0:T(8,128)S(1)}, f32[2,128,128]{2,1,0:T(8,128)S(1)}, u32[]{:S(2)}, u32[]{:S(2)}) %collective-permute-start.11) | collective-permute-done | bytes 131104 | tf_op jit(solution)/shard_map/ppermute | solution.py:197
  60.0 10.1 %collective-permute-done.12 = f32[2,128,128]{2,1,0:T(8,128)S(1)} collective-permute-done((f32[2,128,128]{2,1,0:T(8,128)S(1)}, f32[2,128,128]{2,1,0:T(8,128)S(1)}, u32[]{:S(2)}, u32[]{:S(2)}) %collective-permute-start.12) | collective-permute-done | bytes 131104 | tf_op jit(solution)/shard_map/ppermute | solution.py:197
  70.2 2.8 %collective-permute-done.13 = f32[2,128,128]{2,1,0:T(8,128)S(1)} collective-permute-done((f32[2,128,128]{2,1,0:T(8,128)S(1)}, f32[2,128,128]{2,1,0:T(8,128)S(1)}, u32[]{:S(2)}, u32[]{:S(2)}) %collective-permute-start.13) | collective-permute-done | bytes 131104 | tf_op jit(solution)/shard_map/ppermute | solution.py:197
  73.0 0.3 collective-permute-done.16
  73.4 0.9 %multiply_convert_fusion = (bf16[128,1024]{1,0:T(8,128)(2,1)}, bf16[128,1024]{1,0:T(8,128)(2,1)}) fusion(f32[128,1024]{1,0:T(8,128)S(1)} %get-tuple-element.75, bf16[128,1024]{1,0:T(8,128)(2,1)S(1)} %copy-done.1, bf16[128,1024]{1,0:T(8,128)(2,1)S(1)} %copy-done), kind=kLoop, calls=%fused_computation.67 | loop fusion | flops 786432 | bytes 1572864 | tf_op jit(solution)/shard_map/convert_element_type | solution.py:231
  (81 shorter events, 1.8 us)
Async XLA Ops:
  0.6 13.7 %collective-permute-start = (bf16[128,1024]{1,0:T(8,128)(2,1)}, bf16[128,1024]{1,0:T(8,128)(2,1)S(1)}, u32[]{:S(2)}, u32[]{:S(2)}) collective-permute-start(bf16[128,1024]{1,0:T(8,128)(2,1)} %param.17), channel_id=1, source_target_pairs={{0,1},{1,0},{2,3},{3,2},{4,5},{5,4},{6,7},{7,6},{8,9},{9,8},{10,11... | collective-permute-start | bytes 786440 | tf_op jit(solution)/shard_map/ppermute | solution.py:26
  1.9 12.5 %collective-permute-start.1 = (bf16[128,1024]{1,0:T(8,128)(2,1)}, bf16[128,1024]{1,0:T(8,128)(2,1)S(1)}, u32[]{:S(2)}, u32[]{:S(2)}) collective-permute-start(bf16[128,1024]{1,0:T(8,128)(2,1)} %param.17), channel_id=1, source_target_pairs={{0,2},{1,3},{2,0},{3,1},{4,6},{5,7},{6,4},{7,5},{8,10},{9,11},{10,... | collective-permute-start | bytes 786440 | tf_op jit(solution)/shard_map/ppermute | solution.py:26
  3.1 11.6 %collective-permute-start.2 = (bf16[128,1024]{1,0:T(8,128)(2,1)}, bf16[128,1024]{1,0:T(8,128)(2,1)S(1)}, u32[]{:S(2)}, u32[]{:S(2)}) collective-permute-start(bf16[128,1024]{1,0:T(8,128)(2,1)} %param.17), channel_id=1, source_target_pairs={{0,3},{1,2},{2,1},{3,0},{4,7},{5,6},{6,5},{7,4},{8,11},{9,10},{10,... | collective-permute-start | bytes 786440 | tf_op jit(solution)/shard_map/ppermute | solution.py:26
  5.7 9.0 %copy-start.4 = (bf16[128,1024]{1,0:T(8,128)(2,1)S(1)}, bf16[128,1024]{1,0:T(8,128)(2,1)}, u32[]{:S(2)}) copy-start(bf16[128,1024]{1,0:T(8,128)(2,1)} %param.17) | copy-start | bytes 786436
  7.9 31.5 %all-to-all-start = ((bf16[8,2,128,128]{3,2,1,0:T(8,128)(2,1)}), bf16[8,2,128,128]{3,2,1,0:T(8,128)(2,1)S(1)}, u32[]{:S(2)}, u32[]{:S(2)}) async-start(bf16[8,2,128,128]{3,2,1,0:T(8,128)(2,1)} %copy.52), calls=%async_computation | async-start | bytes 1048576 | tf_op jit(solution)/shard_map/all_to_all | solution.py:149
  14.7 1.0 %copy-start.10 = (bf16[128,1024]{1,0:T(8,128)(2,1)S(1)}, bf16[128,1024]{1,0:T(8,128)(2,1)}, u32[]{:S(2)}) copy-start(bf16[128,1024]{1,0:T(8,128)(2,1)} %param.13) | copy-start | bytes 786436
  14.7 1.0 %copy-start.11 = (bf16[128,1024]{1,0:T(8,128)(2,1)S(1)}, bf16[128,1024]{1,0:T(8,128)(2,1)}, u32[]{:S(2)}) copy-start(bf16[128,1024]{1,0:T(8,128)(2,1)} %param.16) | copy-start | bytes 786436
  22.8 7.3 %collective-permute-start.3 = (f32[128,128]{1,0:T(8,128)S(1)}, f32[128,128]{1,0:T(8,128)S(1)}, u32[]{:S(2)}, u32[]{:S(2)}) collective-permute-start(f32[128,128]{1,0:T(8,128)S(1)} %get-tuple-element.69), channel_id=1, source_target_pairs={{0,4},{4,8},{8,12},{12,16},{16,20},{20,24},{24,28},{28,0},{1,5},{5... | collective-permute-start | bytes 196616 | tf_op jit(solution)/shard_map/ppermute | solution.py:178
  25.8 5.5 %collective-permute-start.4 = (f32[128,128]{1,0:T(8,128)S(1)}, f32[128,128]{1,0:T(8,128)S(1)}, u32[]{:S(2)}, u32[]{:S(2)}) collective-permute-start(f32[128,128]{1,0:T(8,128)S(1)} %get-tuple-element.68), channel_id=1, source_target_pairs={{0,8},{4,12},{8,16},{12,20},{16,24},{20,28},{24,0},{28,4},{1,9},{5... | collective-permute-start | bytes 196616 | tf_op jit(solution)/shard_map/ppermute | solution.py:178
  27.1 7.7 %collective-permute-start.5 = (f32[128,128]{1,0:T(8,128)S(1)}, f32[128,128]{1,0:T(8,128)S(1)}, u32[]{:S(2)}, u32[]{:S(2)}) collective-permute-start(f32[128,128]{1,0:T(8,128)S(1)} %get-tuple-element.67), channel_id=1, source_target_pairs={{0,12},{4,16},{8,20},{12,24},{16,28},{20,0},{24,4},{28,8},{1,13},{... | collective-permute-start | bytes 196616 | tf_op jit(solution)/shard_map/ppermute | solution.py:178
  27.1 10.0 %collective-permute-start.6 = (f32[128,128]{1,0:T(8,128)S(1)}, f32[128,128]{1,0:T(8,128)S(1)}, u32[]{:S(2)}, u32[]{:S(2)}) collective-permute-start(f32[128,128]{1,0:T(8,128)S(1)} %get-tuple-element.66), channel_id=1, source_target_pairs={{0,16},{4,20},{8,24},{12,28},{16,0},{20,4},{24,8},{28,12},{1,17},{... | collective-permute-start | bytes 196616 | tf_op jit(solution)/shard_map/ppermute | solution.py:178
  28.5 8.6 %collective-permute-start.7 = (f32[128,128]{1,0:T(8,128)S(1)}, f32[128,128]{1,0:T(8,128)S(1)}, u32[]{:S(2)}, u32[]{:S(2)}) collective-permute-start(f32[128,128]{1,0:T(8,128)S(1)} %get-tuple-element.65), channel_id=1, source_target_pairs={{0,20},{4,24},{8,28},{12,0},{16,4},{20,8},{24,12},{28,16},{1,21},{... | collective-permute-start | bytes 196616 | tf_op jit(solution)/shard_map/ppermute | solution.py:178
  30.1 8.9 %collective-permute-start.8 = (f32[128,128]{1,0:T(8,128)S(1)}, f32[128,128]{1,0:T(8,128)S(1)}, u32[]{:S(2)}, u32[]{:S(2)}) collective-permute-start(f32[128,128]{1,0:T(8,128)S(1)} %get-tuple-element.64), channel_id=1, source_target_pairs={{0,24},{4,28},{8,0},{12,4},{16,8},{20,12},{24,16},{28,20},{1,25},{... | collective-permute-start | bytes 196616 | tf_op jit(solution)/shard_map/ppermute | solution.py:178
  31.3 7.9 %collective-permute-start.9 = (f32[128,128]{1,0:T(8,128)S(1)}, f32[128,128]{1,0:T(8,128)S(1)}, u32[]{:S(2)}, u32[]{:S(2)}) collective-permute-start(f32[128,128]{1,0:T(8,128)S(1)} %get-tuple-element.63), channel_id=1, source_target_pairs={{0,28},{4,0},{8,4},{12,8},{16,12},{20,16},{24,20},{28,24},{1,29},{... | collective-permute-start | bytes 196616 | tf_op jit(solution)/shard_map/ppermute | solution.py:178
  39.5 0.8 %copy-start.7 = (bf16[256,128,1]{1,0,2:T(8,128)(2,1)S(1)}, bf16[256,128,1]{1,0,2:T(8,128)(2,1)}, u32[]{:S(2)}) copy-start(bf16[256,128,1]{1,0,2:T(8,128)(2,1)} %constant.244) | copy-start | bytes 196612
  40.4 0.8 %copy-start.6 = (bf16[256,128,1]{1,0,2:T(8,128)(2,1)S(1)}, bf16[256,128,1]{1,0,2:T(8,128)(2,1)}, u32[]{:S(2)}) copy-start(bf16[256,128,1]{1,0,2:T(8,128)(2,1)} %constant.245) | copy-start | bytes 196612
  43.8 0.8 %copy-start.9 = (bf16[128,1,1]{0,1,2:T(2,128)(2,1)S(1)}, bf16[128,1,1]{0,1,2:T(2,128)(2,1)}, u32[]{:S(2)}) copy-start(bf16[128,1,1]{0,1,2:T(2,128)(2,1)} %constant.248) | copy-start | bytes 772
  45.4 0.9 %copy-start.2 = (bf16[256,256,1]{1,0,2:T(8,128)(2,1)S(1)}, bf16[256,256,1]{1,0,2:T(8,128)(2,1)}, u32[]{:S(2)}) copy-start(bf16[256,256,1]{1,0,2:T(8,128)(2,1)} %constant.246) | copy-start | bytes 393220
  46.7 0.9 %copy-start.5 = (bf16[256,256,1]{1,0,2:T(8,128)(2,1)S(1)}, bf16[256,256,1]{1,0,2:T(8,128)(2,1)}, u32[]{:S(2)}) copy-start(bf16[256,256,1]{1,0,2:T(8,128)(2,1)} %constant.247) | copy-start | bytes 393220
  47.6 0.7 copy-start.8
  49.0 23.9 %collective-permute-start.14 = (f32[2,128,128]{2,1,0:T(8,128)S(1)}, f32[2,128,128]{2,1,0:T(8,128)S(1)}, u32[]{:S(2)}, u32[]{:S(2)}) collective-permute-start(f32[2,128,128]{2,1,0:T(8,128)S(1)} %bitcast.280), channel_id=1, source_target_pairs={{0,20},{4,24},{8,28},{12,0},{16,4},{20,8},{24,12},{28,16},{1,21},{... | collective-permute-start | bytes 393224 | tf_op jit(solution)/shard_map/ppermute | solution.py:197
  49.4 6.7 %collective-permute-start.10 = (f32[2,128,128]{2,1,0:T(8,128)S(1)}, f32[2,128,128]{2,1,0:T(8,128)S(1)}, u32[]{:S(2)}, u32[]{:S(2)}) collective-permute-start(f32[2,128,128]{2,1,0:T(8,128)S(1)} %bitcast.286), channel_id=1, source_target_pairs={{0,4},{4,8},{8,12},{12,16},{16,20},{20,24},{24,28},{28,0},{1,5},{5... | collective-permute-start | bytes 393224 | tf_op jit(solution)/shard_map/ppermute | solution.py:197
  50.6 9.5 %collective-permute-start.11 = (f32[2,128,128]{2,1,0:T(8,128)S(1)}, f32[2,128,128]{2,1,0:T(8,128)S(1)}, u32[]{:S(2)}, u32[]{:S(2)}) collective-permute-start(f32[2,128,128]{2,1,0:T(8,128)S(1)} %bitcast.285), channel_id=1, source_target_pairs={{0,8},{4,12},{8,16},{12,20},{16,24},{20,28},{24,0},{28,4},{1,9},{5... | collective-permute-start | bytes 393224 | tf_op jit(solution)/shard_map/ppermute | solution.py:197
  52.5 20.9 %copy-start = (bf16[128,1024]{1,0:T(8,128)(2,1)S(1)}, bf16[128,1024]{1,0:T(8,128)(2,1)}, u32[]{:S(2)}) copy-start(bf16[128,1024]{1,0:T(8,128)(2,1)} %param.15) | copy-start | bytes 786436
  52.5 20.9 %copy-start.1 = (bf16[128,1024]{1,0:T(8,128)(2,1)S(1)}, bf16[128,1024]{1,0:T(8,128)(2,1)}, u32[]{:S(2)}) copy-start(bf16[128,1024]{1,0:T(8,128)(2,1)} %param.14) | copy-start | bytes 786436
  52.6 17.5 %collective-permute-start.12 = (f32[2,128,128]{2,1,0:T(8,128)S(1)}, f32[2,128,128]{2,1,0:T(8,128)S(1)}, u32[]{:S(2)}, u32[]{:S(2)}) collective-permute-start(f32[2,128,128]{2,1,0:T(8,128)S(1)} %bitcast.284), channel_id=1, source_target_pairs={{0,12},{4,16},{8,20},{12,24},{16,28},{20,0},{24,4},{28,8},{1,13},{... | collective-permute-start | bytes 393224 | tf_op jit(solution)/shard_map/ppermute | solution.py:197
  54.7 18.3 %collective-permute-start.13 = (f32[2,128,128]{2,1,0:T(8,128)S(1)}, f32[2,128,128]{2,1,0:T(8,128)S(1)}, u32[]{:S(2)}, u32[]{:S(2)}) collective-permute-start(f32[2,128,128]{2,1,0:T(8,128)S(1)} %bitcast.283), channel_id=1, source_target_pairs={{0,16},{4,20},{8,24},{12,28},{16,0},{20,4},{24,8},{28,12},{1,17},{... | collective-permute-start | bytes 393224 | tf_op jit(solution)/shard_map/ppermute | solution.py:197
  56.1 16.9 %collective-permute-start.15 = (f32[2,128,128]{2,1,0:T(8,128)S(1)}, f32[2,128,128]{2,1,0:T(8,128)S(1)}, u32[]{:S(2)}, u32[]{:S(2)}) collective-permute-start(f32[2,128,128]{2,1,0:T(8,128)S(1)} %bitcast.282), channel_id=1, source_target_pairs={{0,24},{4,28},{8,0},{12,4},{16,8},{20,12},{24,16},{28,20},{1,25},{... | collective-permute-start | bytes 393224 | tf_op jit(solution)/shard_map/ppermute | solution.py:197
  60.0 13.3 %collective-permute-start.16 = (f32[2,128,128]{2,1,0:T(8,128)S(1)}, f32[2,128,128]{2,1,0:T(8,128)S(1)}, u32[]{:S(2)}, u32[]{:S(2)}) collective-permute-start(f32[2,128,128]{2,1,0:T(8,128)S(1)} %bitcast.281), channel_id=1, source_target_pairs={{0,28},{4,0},{8,4},{12,8},{16,12},{20,16},{24,20},{28,24},{1,29},{... | collective-permute-start | bytes 393224 | tf_op jit(solution)/shard_map/ppermute | solution.py:197
  73.4 1.0 %copy-start.3 = (f32[128,1024]{1,0:T(8,128)}, f32[128,1024]{1,0:T(8,128)S(1)}, u32[]{:S(2)}) copy-start(f32[128,1024]{1,0:T(8,128)S(1)} %get-tuple-element.74) | copy-start | bytes 1572868
